TPU v7x, 128 devices: a whole 4x4x4 slice. The times are simulated.
128 devices in a mesh: group: 8 (over y, core), member: 16 (over z, x).
Axes of the slice: x: 4, y: 4, z: 4, core: 2. Of those that a mesh axis runs over, the one named last changes fastest.
Arguments:
- candidates: bfloat16 [512, 64, 1024], P('member', 'group'), may hold values from -6 to 6
- kv_cache: bfloat16 [64, 2048, 2048], P('group', 'member'), may hold values from -6 to 6
- cache_request: int32 [64], replicated, may hold values from 0 to 63, as said below
- rank_request: int32 [64], replicated, may hold values from 0 to 63, as said below
- hist_blocks: int32 [64], replicated, may hold values from 1 to 16, 544 in all
- w_uq: bfloat16 [1024, 2048], replicated, may hold values from -0.1875 to 0.1875
- w_out: bfloat16 [1024, 1024], replicated, may hold values from -0.1875 to 0.1875
Outputs:
- ranked: bfloat16 [512, 64, 1024], P('member', 'group')
Inputs may be any that keep to these rules, and one draw needn't show every extreme that they name: `cache_request`: A permutation; cache row q lies on group q // 8, events split over member. `rank_request`: A permutation; group g ranks positions g * 8 to (g + 1) * 8 - 1. The requests cached on one group are dealt out to the ranking groups in turn, so every pair of groups carries 8 // 8 or 1 requests and some pair carries exactly 1; the uneven part of the load is the live history lengths.
All inputs are finite; a program needn't handle non-finite values.
Results may differ from a plain program's by a relative error of at most 0.011.
Values may be sent and summed in bfloat16 or wider, within the bound.
No kernel may reach another device: no remote copies, remote signals or barrier semaphores. Data moves between devices by JAX's collectives and lax.ppermute only.
A program may use at most 320 MiB of HBM per device.

v0:
```python
import jax
import jax.numpy as jnp
from jax import lax
from jax.sharding import PartitionSpec as P

HEADS = 8
BLK = 128


def layer_norm(values):
    center = values - jnp.mean(values, axis=-1, keepdims=True)
    spread = jnp.mean(center * center, axis=-1, keepdims=True)
    return center * lax.rsqrt(spread + 1e-05)


def routing(cache_request, rank_request, per_group):
    slot_ids = jnp.arange(cache_request.shape[0], dtype=jnp.int32)
    match = cache_request[:, None] == rank_request[None, :]
    rank_pos = jnp.sum(jnp.where(match, slot_ids[None, :], 0), axis=1)
    target = rank_pos // per_group
    owner_grp = slot_ids // per_group
    earlier = (
        (owner_grp[:, None] == owner_grp[None, :])
        & (target[:, None] == target[None, :])
        & (slot_ids[None, :] < slot_ids[:, None])
    )
    arrival = jnp.sum(earlier.astype(jnp.int32), axis=1)
    slot_of_pos = jnp.sum(jnp.where(match, slot_ids[:, None], 0), axis=0)
    return (target, arrival, slot_of_pos)


def attend(piece, queries, live, scale):
    width = queries.shape[2] * queries.shape[3]
    count = piece.shape[1]
    keys = piece[:, :, :width].reshape(piece.shape[0], count, queries.shape[2], queries.shape[3])
    values = piece[:, :, width:].reshape(piece.shape[0], count, queries.shape[2], queries.shape[3])
    scores = jnp.einsum("crhd,rehd->rhce", queries, keys, preferred_element_type=jnp.float32)
    events = jnp.arange(count).astype(jnp.float32)
    keep = (events[None, :] < live[:, None]).astype(jnp.float32) / live[:, None]
    weights = (jax.nn.silu(scores * scale) * keep[:, None, None, :]).astype(jnp.bfloat16)
    return jnp.einsum("rhce,rehd->crhd", weights, values, preferred_element_type=jnp.float32)


def on_device(candidates, kv_cache, cache_request, rank_request, hist_blocks, w_uq, w_out):
    groups = lax.axis_size("group")
    per_group = kv_cache.shape[0]
    cand_rows = candidates.shape[0]
    width = candidates.shape[2]
    head_dim = width // HEADS
    capacity = (per_group + groups - 1) // groups
    group_now = lax.axis_index("group")
    target, arrival, slot_of_pos = routing(cache_request, rank_request, per_group)
    first_slot = group_now * per_group
    local_target = lax.dynamic_slice_in_dim(target, first_slot, per_group)
    local_arrival = lax.dynamic_slice_in_dim(arrival, first_slot, per_group)
    target_grid = jnp.arange(groups)[:, None, None]
    place_grid = jnp.arange(capacity)[None, :, None]
    hits = (local_target[None, None, :] == target_grid) & (
        local_arrival[None, None, :] == place_grid
    )
    chosen = jnp.sum(jnp.where(hits, jnp.arange(per_group)[None, None, :], 0), axis=2).reshape(-1)
    filled = jnp.any(hits, axis=2).reshape(-1)
    positions = first_slot + jnp.arange(per_group)
    source_slot = slot_of_pos[positions]
    receive_index = source_slot // per_group * capacity + arrival[source_slot]
    live = (hist_blocks[rank_request[positions]] * BLK).astype(jnp.float32)
    inputs = candidates.astype(jnp.float32)
    normed = layer_norm(inputs).astype(jnp.bfloat16).reshape(cand_rows * per_group, width)
    projected = jax.nn.silu(jnp.dot(normed, w_uq, preferred_element_type=jnp.float32))
    gates = projected[:, :width].reshape(cand_rows, per_group, width)
    queries = (
        projected[:, width:].astype(jnp.bfloat16).reshape(cand_rows, per_group, HEADS, head_dim)
    )
    scale = head_dim ** (-0.5)
    outgoing = jnp.where(filled[:, None, None], kv_cache[chosen], jnp.zeros((), jnp.bfloat16))
    incoming = lax.all_to_all(outgoing, "group", split_axis=0, concat_axis=0, tiled=True)
    panels = incoming[receive_index]
    attn = attend(lax.all_gather(panels, "member", axis=1, tiled=True), queries, live, scale)
    attn = attn.reshape(cand_rows, per_group, width)
    gated = (layer_norm(attn) * gates).astype(jnp.bfloat16).reshape(cand_rows * per_group, width)
    result = jnp.dot(gated, w_out, preferred_element_type=jnp.float32) + inputs.reshape(
        cand_rows * per_group, width
    )
    return result.astype(jnp.bfloat16).reshape(cand_rows, per_group, width)


def solution(mesh):
    return jax.shard_map(
        on_device,
        mesh=mesh,
        in_specs=(P("member", "group", None), P("group", "member", None), P(), P(), P(), P(), P()),
        out_specs=P("member", "group", None),
        check_vma=False,
    )
```

profile of v0, /device:TPU:1, one launch (start us, length us, event | category | flops | bytes accessed | tf_op | source)
XLA Modules:
  0.0 615.8 jit_solution(919087667570539489)
XLA Ops:
  6.5 0.0 copy-start
  6.5 1.0 fusion.26
  7.6 0.2 convert_reduce_fusion.1
  7.8 0.1 dynamic_slice.6
  7.8 0.1 dynamic-slice_compare_fusion
  7.9 0.1 select_reduce_fusion
  8.0 0.1 fusion.29
  8.2 5.0 gather_fusion
  13.1 4.5 broadcast_select_fusion
  17.6 6.0 all-to-all-start
  23.6 0.0 all-gather.3.cloned.1.call-start
  23.6 0.6 gather_fusion.1
  24.3 0.6 gather_fusion.2
  25.0 47.4 %all-to-all-done = bf16[8,128,2048]{2,1,0:T(8,128)(2,1)} async-done(((bf16[8,128,2048]{2,1,0:T(8,128)(2,1)}), bf16[8,128,2048]{2,1,0:T(8,128)(2,1)}, u32[]{:S(2)}, u32[]{:S(2)}) %all-to-all-start) | async-done | bytes 4194336 | tf_op jit(solution)/shard_map/all_to_all | solution.py:76
  72.4 5.0 gather_fusion.3
  77.4 0.0 copy-start.1
  77.4 0.0 copy-start.2
  77.4 0.0 copy-start.3
  77.4 0.0 all-gather.3.cloned.1.call-update
  77.4 0.6 copy-done.1
  78.0 0.6 gather_fusion.4
  78.7 0.0 copy-done.2
  78.7 0.6 gather_fusion.5
  79.3 0.0 copy-done.3
  79.3 0.1 convert_reduce_fusion
  79.5 0.3 fusion.8
  79.8 3.7 divide_multiply_fusion
  83.5 0.0 copy-start.4
  83.5 1.3 copy-done.4
  84.8 0.1 fusion.12
  84.9 0.1 convert_divide_fusion
  85.0 361.7 %all-gather.3.cloned.1.call-done = bf16[8,2048,2048]{2,1,0:T(8,128)(2,1)} async-done(((bf16[8,128,2048]{2,1,0:T(8,128)(2,1)}), bf16[8,2048,2048]{2,1,0:T(8,128)(2,1)}) %all-gather.3.cloned.1.call-update) | async-done | bytes 67108880 | tf_op jit(solution)/shard_map/all_gather | solution.py:78
  446.7 43.3 %fusion.37 = (bf16[8,2048,1024]{2,1,0:T(8,128)(2,1)}, bf16[8,2048,1024]{2,1,0:T(8,128)(2,1)}) fusion(bf16[8,2048,2048]{2,1,0:T(8,128)(2,1)} %all-gather.3.cloned.1.call-done), kind=kLoop, calls=%fused_computation.86 | loop fusion | bytes 134217728 | tf_op jit(solution)/shard_map/slice | solution.py:35
  490.0 42.2 %copy.44 = bf16[8,2048,1024]{1,2,0:T(8,128)(2,1)} copy(bf16[8,2048,1024]{2,1,0:T(8,128)(2,1)} %get-tuple-element.7) | data formatting | bytes 67108864 | tf_op jit(solution)/shard_map/slice | solution.py:35
  532.3 42.2 %copy.43 = bf16[8,2048,1024]{1,2,0:T(8,128)(2,1)} copy(bf16[8,2048,1024]{2,1,0:T(8,128)(2,1)} %get-tuple-element.8) | data formatting | bytes 67108864 | tf_op jit(solution)/shard_map/slice | solution.py:36
  574.5 29.0 %fusion.38 = (f32[32,8]{0,1:T(8,128)S(1)}, f32[32,8,8,128]{3,0,2,1:T(8,128)}) fusion(bf16[8,2048,8,128]{1,3,2,0:T(8,128)(2,1)} %bitcast.58, f32[8,2048]{1,0:T(8,128)S(1)} %convert_divide_fusion, bf16[8,2048,8,128]{1,3,2,0:T(8,128)(2,1)} %bitcast.57, bf16[32,8,8,128]{3,1,2,0:T(8,128)(2,1)S(1)} %fusion.12), kind=kOutput, calls=%fused_computation.87 | convolution fusion | flops 2177105664 | bytes 68748288 | tf_op jit(solution)/shard_map/rhce,rehd->crhd/dot_general | solution.py:41
  603.5 0.1 copy.49
  603.6 0.1 copy.50
  603.6 0.1 div.75
  603.7 1.5 multiply_reduce_fusion
  605.2 0.1 copy.51
  605.3 0.1 rsqrt.21
  605.4 0.0 copy-done
  605.4 3.5 fusion.7
  (17 shorter events, 0.1 us)
Async XLA Ops:
  6.5 598.9 %copy-start = (bf16[1024,1024]{1,0:T(8,128)(2,1)S(1)}, bf16[1024,1024]{1,0:T(8,128)(2,1)}, u32[]{:S(2)}) copy-start(bf16[1024,1024]{1,0:T(8,128)(2,1)} %param.13) | copy-start | bytes 6291460
  17.6 54.7 %all-to-all-start = ((bf16[8,128,2048]{2,1,0:T(8,128)(2,1)}), bf16[8,128,2048]{2,1,0:T(8,128)(2,1)}, u32[]{:S(2)}, u32[]{:S(2)}) async-start(bf16[8,128,2048]{2,1,0:T(8,128)(2,1)} %broadcast_select_fusion), calls=%async_computation | async-start | bytes 8388608 | tf_op jit(solution)/shard_map/all_to_all | solution.py:76
  23.6 423.1 %all-gather.3.cloned.1.call-start = ((), (), s32[]{:S(2)}) async-start(), calls=%async_computation.1 | async-start | bytes 71303168 | tf_op jit(solution)/shard_map/all_gather | solution.py:78
  77.4 0.7 copy-start.1
  77.4 1.3 copy-start.2
  77.4 2.0 copy-start.3
  83.5 1.4 copy-start.4
Sparse Core Ops, SparseCore 0:
  77.5 369.1 all-gather.2
where the time goes:
time: 618 us; the launch traced here: 616 us
  waiting for transfers between devices  409 us (66%)
  local copies, waits for them, and re-layouts  143 us (23%)
  matrix products  36.2 us (6%)
  between operations  13.5 us (2%)
  other arithmetic  8.11 us (1%)
    all_gather x1, waiting for transfers between devices, on_device(): lax.all_gather(panels, 'member', axis=1, tiled=True)  362 us
    slice x2, local copies, waits for them, and re-layouts, attend(): piece[:, :, :width]  85.6 us
    all_to_all x1, waiting for transfers between devices, on_device(): lax.all_to_all(outgoing, 'group', split_axis=0, concat_axis=0, tiled=True)  47.4 us
    slice x1, local copies, waits for them, and re-layouts, attend(): piece[:, :, width:]  42.2 us
    dot_general x1, matrix products, attend(): jnp.einsum('rhce,rehd->crhd', weights, values, preferred_element_type=jnp...  29 us
  transfers between devices with their start and end apart: 2, of which 2 were waited for; matrix products, arithmetic and copies ran while one was open for 1% of the time, Pallas kernels for 0%

commit v1 on v0

--- a/solution.py
+++ b/solution.py
@@ -29,16 +29,17 @@
     return (target, arrival, slot_of_pos)
 
 
-def attend(piece, queries, live, scale):
-    width = queries.shape[2] * queries.shape[3]
-    count = piece.shape[1]
-    keys = piece[:, :, :width].reshape(piece.shape[0], count, queries.shape[2], queries.shape[3])
-    values = piece[:, :, width:].reshape(piece.shape[0], count, queries.shape[2], queries.shape[3])
-    scores = jnp.einsum("crhd,rehd->rhce", queries, keys, preferred_element_type=jnp.float32)
-    events = jnp.arange(count).astype(jnp.float32)
+def attend_local(queries, piece, live, first_event, scale):
+    rows, count = piece.shape[0], piece.shape[1]
+    heads, head_dim = queries.shape[2], queries.shape[3]
+    width = heads * head_dim
+    keys = piece[:, :, :width].reshape(rows, count, heads, head_dim)
+    values = piece[:, :, width:].reshape(rows, count, heads, head_dim)
+    scores = jnp.einsum("rchd,rehd->rhce", queries, keys, preferred_element_type=jnp.float32)
+    events = (first_event + jnp.arange(count)).astype(jnp.float32)
     keep = (events[None, :] < live[:, None]).astype(jnp.float32) / live[:, None]
     weights = (jax.nn.silu(scores * scale) * keep[:, None, None, :]).astype(jnp.bfloat16)
-    return jnp.einsum("rhce,rehd->crhd", weights, values, preferred_element_type=jnp.float32)
+    return jnp.einsum("rhce,rehd->rchd", weights, values, preferred_element_type=jnp.float32)
 
 
 def on_device(candidates, kv_cache, cache_request, rank_request, hist_blocks, w_uq, w_out):
@@ -47,12 +48,15 @@
     cand_rows = candidates.shape[0]
     width = candidates.shape[2]
     head_dim = width // HEADS
+    count = kv_cache.shape[1]
     capacity = (per_group + groups - 1) // groups
     group_now = lax.axis_index("group")
+    member_now = lax.axis_index("member")
     target, arrival, slot_of_pos = routing(cache_request, rank_request, per_group)
     first_slot = group_now * per_group
     local_target = lax.dynamic_slice_in_dim(target, first_slot, per_group)
     local_arrival = lax.dynamic_slice_in_dim(arrival, first_slot, per_group)
+    row_index = local_target * capacity + local_arrival
     target_grid = jnp.arange(groups)[:, None, None]
     place_grid = jnp.arange(capacity)[None, :, None]
     hits = (local_target[None, None, :] == target_grid) & (
@@ -63,20 +67,35 @@
     positions = first_slot + jnp.arange(per_group)
     source_slot = slot_of_pos[positions]
     receive_index = source_slot // per_group * capacity + arrival[source_slot]
-    live = (hist_blocks[rank_request[positions]] * BLK).astype(jnp.float32)
+    send_hits = receive_index[None, :] == jnp.arange(groups * capacity)[:, None]
+    send_pos = jnp.sum(jnp.where(send_hits, jnp.arange(per_group)[None, :], 0), axis=1)
+    send_filled = jnp.any(send_hits, axis=1)
+    row_live = (hist_blocks[cache_request[first_slot + jnp.arange(per_group)]] * BLK).astype(
+        jnp.float32
+    )
+
     inputs = candidates.astype(jnp.float32)
     normed = layer_norm(inputs).astype(jnp.bfloat16).reshape(cand_rows * per_group, width)
     projected = jax.nn.silu(jnp.dot(normed, w_uq, preferred_element_type=jnp.float32))
     gates = projected[:, :width].reshape(cand_rows, per_group, width)
-    queries = (
-        projected[:, width:].astype(jnp.bfloat16).reshape(cand_rows, per_group, HEADS, head_dim)
-    )
+    queries = projected[:, width:].astype(jnp.bfloat16).reshape(cand_rows, per_group, width)
     scale = head_dim ** (-0.5)
-    outgoing = jnp.where(filled[:, None, None], kv_cache[chosen], jnp.zeros((), jnp.bfloat16))
-    incoming = lax.all_to_all(outgoing, "group", split_axis=0, concat_axis=0, tiled=True)
-    panels = incoming[receive_index]
-    attn = attend(lax.all_gather(panels, "member", axis=1, tiled=True), queries, live, scale)
-    attn = attn.reshape(cand_rows, per_group, width)
+
+    q_pos = jnp.swapaxes(queries, 0, 1)
+    q_out = jnp.where(send_filled[:, None, None], q_pos[send_pos], jnp.zeros((), jnp.bfloat16))
+    q_in = lax.all_to_all(q_out, "group", split_axis=0, concat_axis=0, tiled=True)
+    q_rows = q_in[row_index]
+    q_all = lax.all_gather(q_rows, "member", axis=1, tiled=True)
+    q_all = q_all.reshape(per_group, q_all.shape[1], HEADS, head_dim)
+
+    partial = attend_local(q_all, kv_cache, row_live, member_now * count, scale)
+    partial = partial.reshape(per_group, partial.shape[1], width)
+    summed = lax.psum_scatter(partial, "member", scatter_dimension=1, tiled=True)
+
+    a_out = jnp.where(filled[:, None, None], summed[chosen], jnp.zeros((), jnp.float32))
+    a_in = lax.all_to_all(a_out, "group", split_axis=0, concat_axis=0, tiled=True)
+    attn = jnp.swapaxes(a_in[receive_index], 0, 1)
+
     gated = (layer_norm(attn) * gates).astype(jnp.bfloat16).reshape(cand_rows * per_group, width)
     result = jnp.dot(gated, w_out, preferred_element_type=jnp.float32) + inputs.reshape(
         cand_rows * per_group, width

time: 618 us -> 298 us (0.48)
  waiting for transfers between devices: 409 us -> 189 us
  local copies, waits for them, and re-layouts: 143 us -> 52.7 us
  matrix products: 36.2 us -> 20.7 us
    all_gather x1, waiting for transfers between devices: 362 us -> 57.3 us  [on_device(): q_all = lax.all_gather(q_rows, 'member', axis=1, tiled=True)]
    slice x3 -> x2, local copies, waits for them, and re-layouts: 128 us -> 8.77 us  [the longest x1 4.86 us: attend_local(): keys = piece[:, :, :width].reshape(rows, count, heads, head_dim)]
    reduce_scatter x0 -> x1, waiting for transfers between devices: none -> 110 us  [on_device(): lax.psum_scatter(partial, 'member', scatter_dimension=1, tiled=True)]
    all_to_all x1 -> x2, waiting for transfers between devices: 47.4 us -> 21.9 us  [the longest x1 12.7 us: on_device(): lax.all_to_all(a_out, 'group', split_axis=0, concat_axis=0, tiled=True)]
    reshape x0 -> x2, local copies, waits for them, and re-layouts: none -> 18.8 us  [the longest x1 16.4 us: on_device(): partial = partial.reshape(per_group, partial.shape[1], width)]
    dot_general x1, matrix products: 29 us -> 15.3 us  [attend_local(): jnp.einsum('rhce,rehd->rchd', weights, values, preferred_element_type=jnp...]
    all_gather x0 -> x1, local copies, waits for them, and re-layouts: none -> 11.4 us  [on_device(): q_all = lax.all_gather(q_rows, 'member', axis=1, tiled=True)]
  transfers between devices with their start and end apart: 2 -> 4, of which waited for: 2 -> 4; matrix products, arithmetic and copies ran while one was open for 1% -> 6% of each run, Pallas kernels for 0% -> 0%
where the time goes in v1:
time: 298 us; the launch traced here: 297 us
  waiting for transfers between devices  189 us (63%)
  local copies, waits for them, and re-layouts  52.7 us (18%)
  matrix products  20.7 us (7%)
  between operations  13.6 us (5%)
  starting transfers between devices  11.2 us (4%)
  other arithmetic  8.88 us (3%)
    reduce_scatter x1, waiting for transfers between devices, on_device(): lax.psum_scatter(partial, 'member', scatter_dimension=1, tiled=True)  110 us
    all_gather x1, waiting for transfers between devices, on_device(): q_all = lax.all_gather(q_rows, 'member', axis=1, tiled=True)  57.3 us
    reshape x1, local copies, waits for them, and re-layouts, on_device(): partial = partial.reshape(per_group, partial.shape[1], width)  16.4 us
    dot_general x1, matrix products, attend_local(): jnp.einsum('rhce,rehd->rchd', weights, values, preferred_element_type=jnp...  15.3 us
    all_to_all x1, waiting for transfers between devices, on_device(): lax.all_to_all(a_out, 'group', split_axis=0, concat_axis=0, tiled=True)  12.7 us
    all_gather x1, local copies, waits for them, and re-layouts, on_device(): q_all = lax.all_gather(q_rows, 'member', axis=1, tiled=True)  11.4 us
    all_to_all x1, waiting for transfers between devices, on_device(): lax.all_to_all(q_out, 'group', split_axis=0, concat_axis=0, tiled=True)  9.26 us
  transfers between devices with their start and end apart: 4, of which 4 were waited for; matrix products, arithmetic and copies ran while one was open for 6% of the time, Pallas kernels for 0%

profile of v1, /device:TPU:1, one launch (start us, length us, event | category | flops | bytes accessed | tf_op | source)
XLA Modules:
  0.0 296.7 jit_solution(6112455092179821543)
XLA Ops:
  6.5 0.0 copy-start
  6.5 1.0 fusion.19
  7.6 0.6 gather_fusion
  8.3 0.2 convert_reduce_fusion.1
  8.4 0.6 gather_fusion.1
  9.1 0.1 select_reduce_fusion.1
  9.2 0.1 fusion.21
  9.3 1.2 convert_reduce_fusion
  10.5 0.1 copy.66
  10.6 0.1 copy.67
  10.7 1.3 fusion.5
  12.0 0.1 copy.68
  12.1 0.1 copy.69
  12.2 3.8 %divide_multiply_fusion = f32[256,2048]{1,0:T(8,128)S(1)} fusion(bf16[1024,2048]{1,0:T(8,128)(2,1)} %param.12, bf16[32,8,1024]{2,1,0:T(8,128)(2,1)} %param.7, f32[32,8]{1,0:T(8,128)S(1)} %copy.69, f32[32,8]{1,0:T(8,128)S(1)} %copy.67), kind=kOutput, calls=%fused_computation.10 | convolution fusion | flops 1076887552 | bytes 6817792 | tf_op jit(solution)/shard_map/dot_general | solution.py:79
  16.0 0.0 copy-start.4
  16.0 0.0 copy-start.1
  16.0 0.1 fusion.8
  16.1 0.3 copy.90
  16.4 0.9 copy-done.4
  17.3 0.6 gather_fusion.2
  17.9 0.9 broadcast_select_fusion.1
  18.8 6.0 %all-to-all-start = ((bf16[8,32,1024]{2,1,0:T(8,128)(2,1)}), bf16[8,32,1024]{2,1,0:T(8,128)(2,1)S(1)}, u32[]{:S(2)}, u32[]{:S(2)}) async-start(bf16[8,32,1024]{2,1,0:T(8,128)(2,1)} %broadcast_select_fusion.1), calls=%async_computation | async-start | bytes 1048576 | tf_op jit(solution)/shard_map/all_to_all | solution.py:86
  24.8 0.0 all-gather.3.cloned.1.call-start
  24.8 0.1 compare_select_fusion.5
  24.9 9.3 %all-to-all-done = bf16[8,32,1024]{2,1,0:T(8,128)(2,1)S(1)} async-done(((bf16[8,32,1024]{2,1,0:T(8,128)(2,1)}), bf16[8,32,1024]{2,1,0:T(8,128)(2,1)S(1)}, u32[]{:S(2)}, u32[]{:S(2)}) %all-to-all-start) | async-done | bytes 524320 | tf_op jit(solution)/shard_map/all_to_all | solution.py:86
  34.1 1.4 gather_fusion.3
  35.5 0.0 all-gather.3.cloned.1.call-update
  35.5 0.0 reduce-scatter.2.cloned.1.call-start
  35.6 0.0 copy-done.1
  35.6 0.6 gather_fusion.4
  36.2 4.9 %fusion.33 = (bf16[8,128,1024]{2,1,0:T(8,128)(2,1)}, bf16[8,128,1024]{2,1,0:T(8,128)(2,1)}) fusion(bf16[8,128,2048]{2,1,0:T(8,128)(2,1)} %param.8), kind=kLoop, calls=%fused_computation.101 | loop fusion | bytes 8388608 | tf_op jit(solution)/shard_map/slice | solution.py:36
  41.1 0.0 copy-start.2
  41.1 3.9 %copy.75 = bf16[8,128,1024]{1,2,0:T(8,128)(2,1)} copy(bf16[8,128,1024]{2,1,0:T(8,128)(2,1)} %get-tuple-element.10) | data formatting | bytes 4194304 | tf_op jit(solution)/shard_map/slice | solution.py:37
  45.0 4.0 %copy.81 = bf16[8,128,1024]{1,2,0:T(8,128)(2,1)} copy(bf16[8,128,1024]{2,1,0:T(8,128)(2,1)} %get-tuple-element.9) | data formatting | bytes 4194304
  49.0 0.0 copy-done.2
  49.0 0.6 gather_fusion.5
  49.7 0.1 convert_divide_fusion
  49.8 57.3 %all-gather.3.cloned.1.call-done = bf16[8,512,1024]{2,1,0:T(8,128)(2,1)} async-done(((bf16[8,32,1024]{2,1,0:T(8,128)(2,1)}), bf16[8,512,1024]{2,1,0:T(8,128)(2,1)}) %all-gather.3.cloned.1.call-update) | async-done | bytes 8388624 | tf_op jit(solution)/shard_map/all_gather | solution.py:88
  107.1 11.4 %copy.71 = bf16[8,512,1024]{1,2,0:T(8,128)(2,1)} copy(bf16[8,512,1024]{2,1,0:T(8,128)(2,1)} %all-gather.3.cloned.1.call-done) | data formatting | bytes 16777216 | tf_op jit(solution)/shard_map/all_gather | solution.py:88
  118.5 15.3 %fusion = f32[8,8,512,128]{2,3,1,0:T(8,128)} fusion(bf16[8,128,8,128]{1,3,2,0:T(8,128)(2,1)} %bitcast.74, bf16[8,512,8,128]{1,3,2,0:T(8,128)(2,1)} %bitcast.73, bf16[8,128,8,128]{1,3,2,0:T(8,128)(2,1)} %bitcast.75, f32[8,128]{1,0:T(8,128)S(1)} %convert_divide_fusion), kind=kOutput, calls=%fused_computation.9 | convolution fusion | flops 2176843776 | bytes 29364224 | tf_op jit(solution)/shard_map/rhce,rehd->rchd/dot_general | solution.py:42
  133.8 16.4 %copy.76 = f32[8,512,1024]{2,1,0:T(8,128)} copy(f32[8,512,1024]{1,2,0:T(8,128)} %bitcast.72) | data formatting | bytes 33554432 | tf_op jit(solution)/shard_map/reshape | solution.py:92
  150.2 0.0 reduce-scatter.2.cloned.1.call-update
  150.2 0.1 broadcast_compare_fusion
  150.3 0.1 select_reduce_fusion
  150.4 0.1 fusion.23
  150.5 110.2 %reduce-scatter.2.cloned.1.call-done = f32[8,32,1024]{2,1,0:T(8,128)} async-done(((f32[8,512,1024]{2,1,0:T(8,128)}), f32[8,32,1024]{2,1,0:T(8,128)}) %reduce-scatter.2.cloned.1.call-update) | async-done | bytes 1048592 | tf_op jit(solution)/shard_map/reduce_scatter | solution.py:93
  260.7 1.8 gather_fusion.6
  262.6 1.2 broadcast_select_fusion
  263.7 5.2 %all-to-all-start.1 = ((f32[8,32,1024]{2,1,0:T(8,128)}), f32[8,32,1024]{2,1,0:T(8,128)}, u32[]{:S(2)}, u32[]{:S(2)}) async-start(f32[8,32,1024]{2,1,0:T(8,128)} %broadcast_select_fusion), calls=%async_computation.2 | async-start | bytes 2097152 | tf_op jit(solution)/shard_map/all_to_all | solution.py:96
  269.0 2.4 slice_bitcast_fusion
  271.3 12.7 %all-to-all-done.1 = f32[8,32,1024]{2,1,0:T(8,128)} async-done(((f32[8,32,1024]{2,1,0:T(8,128)}), f32[8,32,1024]{2,1,0:T(8,128)}, u32[]{:S(2)}, u32[]{:S(2)}) %all-to-all-start.1) | async-done | bytes 1048608 | tf_op jit(solution)/shard_map/all_to_all | solution.py:96
  284.0 1.8 gather_fusion.7
  285.9 0.0 copy-start.3
  285.9 0.1 bitcast_reduce_fusion
  286.0 0.2 multiply_reduce_fusion
  286.3 1.9 fusion.7
  288.2 0.0 copy-done
  288.2 0.0 copy-done.3
  288.2 1.6 fusion.4
  (21 shorter events, 0.1 us)
Async XLA Ops:
  6.5 281.6 %copy-start = (bf16[1024,1024]{1,0:T(8,128)(2,1)S(1)}, bf16[1024,1024]{1,0:T(8,128)(2,1)}, u32[]{:S(2)}) copy-start(bf16[1024,1024]{1,0:T(8,128)(2,1)} %param.13) | copy-start | bytes 6291460
  16.0 1.3 copy-start.4
  16.0 19.6 %copy-start.1 = (s32[64]{0:T(128)S(1)}, s32[64]{0:T(128)}, u32[]{:S(2)}) copy-start(s32[64]{0:T(128)} %param.9) | copy-start | bytes 772
  18.8 15.3 %all-to-all-start = ((bf16[8,32,1024]{2,1,0:T(8,128)(2,1)}), bf16[8,32,1024]{2,1,0:T(8,128)(2,1)S(1)}, u32[]{:S(2)}, u32[]{:S(2)}) async-start(bf16[8,32,1024]{2,1,0:T(8,128)(2,1)} %broadcast_select_fusion.1), calls=%async_computation | async-start | bytes 1048576 | tf_op jit(solution)/shard_map/all_to_all | solution.py:86
  24.8 82.3 %all-gather.3.cloned.1.call-start = ((), (), s32[]{:S(2)}) async-start(), calls=%async_computation.4 | async-start | bytes 8912896 | tf_op jit(solution)/shard_map/all_gather | solution.py:88
  35.5 225.2 %reduce-scatter.2.cloned.1.call-start = ((), (), s32[]{:S(2)}) async-start(), calls=%async_computation.3 | async-start | bytes 17825792 | tf_op jit(solution)/shard_map/reduce_scatter | solution.py:93
  41.1 7.9 %copy-start.2 = (s32[64]{0:T(128)S(1)}, s32[64]{0:T(128)}, u32[]{:S(2)}) copy-start(s32[64]{0:T(128)} %param.11) | copy-start | bytes 772
  263.7 20.3 %all-to-all-start.1 = ((f32[8,32,1024]{2,1,0:T(8,128)}), f32[8,32,1024]{2,1,0:T(8,128)}, u32[]{:S(2)}, u32[]{:S(2)}) async-start(f32[8,32,1024]{2,1,0:T(8,128)} %broadcast_select_fusion), calls=%async_computation.2 | async-start | bytes 2097152 | tf_op jit(solution)/shard_map/all_to_all | solution.py:96
  285.9 2.3 copy-start.3
Sparse Core Ops, SparseCore 0:
  35.6 71.4 all-gather.2
  150.3 110.3 reduce-scatter.1

commit v2 on v1

--- a/solution.py
+++ b/solution.py
@@ -1,6 +1,10 @@
+import functools
+
 import jax
 import jax.numpy as jnp
 from jax import lax
+from jax.experimental import pallas as pl
+from jax.experimental.pallas import tpu as pltpu
 from jax.sharding import PartitionSpec as P
 
 HEADS = 8
@@ -29,17 +33,56 @@
     return (target, arrival, slot_of_pos)
 
 
-def attend_local(queries, piece, live, first_event, scale):
-    rows, count = piece.shape[0], piece.shape[1]
-    heads, head_dim = queries.shape[2], queries.shape[3]
+def attend_kernel(n_live_ref, q_ref, kv_ref, keep_ref, o_ref, *, heads, head_dim, scale):
+    row = pl.program_id(0)
     width = heads * head_dim
-    keys = piece[:, :, :width].reshape(rows, count, heads, head_dim)
-    values = piece[:, :, width:].reshape(rows, count, heads, head_dim)
-    scores = jnp.einsum("rchd,rehd->rhce", queries, keys, preferred_element_type=jnp.float32)
+
+    @pl.when(n_live_ref[row] <= 0)
+    def _():
+        o_ref[...] = jnp.zeros(o_ref.shape, o_ref.dtype)
+
+    @pl.when(n_live_ref[row] > 0)
+    def _():
+        keep = keep_ref[0]
+        for h in range(heads):
+            lo = h * head_dim
+            q = q_ref[0, :, lo:lo + head_dim]
+            k = kv_ref[0, :, lo:lo + head_dim]
+            v = kv_ref[0, :, width + lo:width + lo + head_dim]
+            s = lax.dot_general(q, k, (((1,), (1,)), ((), ())), preferred_element_type=jnp.float32)
+            w = (jax.nn.silu(s * scale) * keep).astype(jnp.bfloat16)
+            o = jnp.dot(w, v, preferred_element_type=jnp.float32)
+            o_ref[0, :, lo:lo + head_dim] = o.astype(o_ref.dtype)
+
+
+def attend_local(queries, piece, live, first_event, scale, heads, out_dtype):
+    rows, cands, width = queries.shape
+    count = piece.shape[1]
+    head_dim = width // heads
     events = (first_event + jnp.arange(count)).astype(jnp.float32)
-    keep = (events[None, :] < live[:, None]).astype(jnp.float32) / live[:, None]
-    weights = (jax.nn.silu(scores * scale) * keep[:, None, None, :]).astype(jnp.bfloat16)
-    return jnp.einsum("rhce,rehd->rchd", weights, values, preferred_element_type=jnp.float32)
+    keep = ((events[None, :] < live[:, None]).astype(jnp.float32) / live[:, None])[:, None, :]
+    n_live = jnp.clip(live.astype(jnp.int32) - first_event, 0, count).astype(jnp.int32)
+    kernel = functools.partial(attend_kernel, heads=heads, head_dim=head_dim, scale=scale)
+    flops = 4 * rows * cands * count * width
+    return pl.pallas_call(
+        kernel,
+        out_shape=jax.ShapeDtypeStruct((rows, cands, width), out_dtype),
+        grid_spec=pltpu.PrefetchScalarGridSpec(
+            num_scalar_prefetch=1,
+            grid=(rows,),
+            in_specs=[
+                pl.BlockSpec((1, cands, width), lambda r, n: (r, 0, 0)),
+                pl.BlockSpec((1, count, 2 * width), lambda r, n: (r, 0, 0)),
+                pl.BlockSpec((1, 1, count), lambda r, n: (r, 0, 0)),
+            ],
+            out_specs=pl.BlockSpec((1, cands, width), lambda r, n: (r, 0, 0)),
+        ),
+        cost_estimate=pl.CostEstimate(
+            flops=flops,
+            transcendentals=rows * cands * count * heads,
+            bytes_accessed=rows * (cands * width * 4 + count * width * 4),
+        ),
+    )(n_live, queries, piece, keep)
 
 
 def on_device(candidates, kv_cache, cache_request, rank_request, hist_blocks, w_uq, w_out):
@@ -86,15 +129,13 @@
     q_in = lax.all_to_all(q_out, "group", split_axis=0, concat_axis=0, tiled=True)
     q_rows = q_in[row_index]
     q_all = lax.all_gather(q_rows, "member", axis=1, tiled=True)
-    q_all = q_all.reshape(per_group, q_all.shape[1], HEADS, head_dim)
 
-    partial = attend_local(q_all, kv_cache, row_live, member_now * count, scale)
-    partial = partial.reshape(per_group, partial.shape[1], width)
+    partial = attend_local(q_all, kv_cache, row_live, member_now * count, scale, HEADS, jnp.bfloat16)
     summed = lax.psum_scatter(partial, "member", scatter_dimension=1, tiled=True)
 
-    a_out = jnp.where(filled[:, None, None], summed[chosen], jnp.zeros((), jnp.float32))
+    a_out = jnp.where(filled[:, None, None], summed[chosen], jnp.zeros((), summed.dtype))
     a_in = lax.all_to_all(a_out, "group", split_axis=0, concat_axis=0, tiled=True)
-    attn = jnp.swapaxes(a_in[receive_index], 0, 1)
+    attn = jnp.swapaxes(a_in[receive_index], 0, 1).astype(jnp.float32)
 
     gated = (layer_norm(attn) * gates).astype(jnp.bfloat16).reshape(cand_rows * per_group, width)
     result = jnp.dot(gated, w_out, preferred_element_type=jnp.float32) + inputs.reshape(

time: 298 us -> 239 us (0.80)
  local copies, waits for them, and re-layouts: 52.7 us -> 13.6 us
  waiting for transfers between devices: 189 us -> 169 us
  matrix products: 20.7 us -> 5.27 us
  Pallas kernels: 0 us -> 13.5 us
    reduce_scatter x1, waiting for transfers between devices: 110 us -> 83 us  [on_device(): lax.psum_scatter(partial, 'member', scatter_dimension=1, tiled=True)]
    reshape x1 -> x0, local copies, waits for them, and re-layouts: 16.4 us -> none  [on_device(): partial = partial.reshape(per_group, partial.shape[1], width)]
    dot_general x1 -> x0, matrix products: 15.3 us -> none  [attend_local(): jnp.einsum('rhce,rehd->rchd', weights, values, preferred_element_type=jnp...]
    pallas_call x0 -> x1, Pallas kernels: none -> 13.5 us  [attend_local(): pl.pallas_call(kernel, out_shape=jax.ShapeDtypeStruct((rows, cands, width...]
    all_gather x1, waiting for transfers between devices: 57.3 us -> 69 us  [on_device(): q_all = lax.all_gather(q_rows, 'member', axis=1, tiled=True)]
    all_gather x1 -> x0, local copies, waits for them, and re-layouts: 11.4 us -> none  [on_device(): q_all = lax.all_gather(q_rows, 'member', axis=1, tiled=True)]
    slice x2 -> x0, local copies, waits for them, and re-layouts: 8.77 us -> none  [the longest x1 4.86 us: attend_local(): keys = piece[:, :, :width].reshape(rows, count, heads, head_dim)]
    all_to_all x1, waiting for transfers between devices: 12.7 us -> 7.1 us  [on_device(): lax.all_to_all(a_out, 'group', split_axis=0, concat_axis=0, tiled=True)]
  transfers between devices with their start and end apart: 4 -> 4, of which waited for: 4 -> 4; matrix products, arithmetic and copies ran while one was open for 6% -> 2% of each run, Pallas kernels for 0% -> 0%
where the time goes in v2:
time: 239 us; the launch traced here: 238 us
  waiting for transfers between devices  169 us (71%)
  local copies, waits for them, and re-layouts  13.6 us (6%)
  between operations  13.6 us (6%)
  Pallas kernels  13.5 us (6%)
  starting transfers between devices  12.4 us (5%)
  other arithmetic  10.8 us (5%)
  matrix products  5.27 us (2%)
    reduce_scatter x1, waiting for transfers between devices, on_device(): lax.psum_scatter(partial, 'member', scatter_dimension=1, tiled=True)  83 us
    all_gather x1, waiting for transfers between devices, on_device(): q_all = lax.all_gather(q_rows, 'member', axis=1, tiled=True)  69 us
    pallas_call x1, Pallas kernels, attend_local(): pl.pallas_call(kernel, out_shape=jax.ShapeDtypeStruct((rows, cands, width...  13.5 us
    all_to_all x1, waiting for transfers between devices, on_device(): lax.all_to_all(q_out, 'group', split_axis=0, concat_axis=0, tiled=True)  9.37 us
    all_to_all x1, waiting for transfers between devices, on_device(): lax.all_to_all(a_out, 'group', split_axis=0, concat_axis=0, tiled=True)  7.1 us
    all_to_all x1, starting transfers between devices, on_device(): lax.all_to_all(a_out, 'group', split_axis=0, concat_axis=0, tiled=True)  6.41 us
    all_to_all x1, starting transfers between devices, on_device(): lax.all_to_all(q_out, 'group', split_axis=0, concat_axis=0, tiled=True)  5.96 us
  transfers between devices with their start and end apart: 4, of which 4 were waited for; matrix products, arithmetic and copies ran while one was open for 2% of the time, Pallas kernels for 0%

profile of v2, /device:TPU:1, one launch (start us, length us, event | category | flops | bytes accessed | tf_op | source)
XLA Modules:
  0.0 237.7 jit_solution(3797273370483689482)
XLA Ops:
  6.5 0.0 copy-start
  6.5 0.0 copy-start.3
  6.5 1.0 fusion.22
  7.6 0.6 gather_fusion.2
  8.3 0.2 convert_reduce_fusion.1
  8.5 0.6 gather_fusion.3
  9.1 0.1 select_reduce_fusion.1
  9.2 0.1 fusion.25
  9.4 1.2 convert_reduce_fusion
  10.6 0.1 copy.34
  10.6 0.1 copy.35
  10.7 1.3 fusion.4
  12.0 0.1 copy.36
  12.1 0.1 copy.37
  12.2 0.0 copy-done.3
  12.2 3.7 %divide_multiply_fusion = f32[256,2048]{1,0:T(8,128)S(1)} fusion(bf16[1024,2048]{1,0:T(8,128)(2,1)} %param.12, bf16[32,8,1024]{2,1,0:T(8,128)(2,1)S(1)} %copy-done.3, f32[32,8]{1,0:T(8,128)S(1)} %copy.37, f32[32,8]{1,0:T(8,128)S(1)} %copy.35), kind=kOutput, calls=%fused_computation.8 | convolution fusion | flops 1076887552 | bytes 6817792 | tf_op jit(solution)/shard_map/dot_general | solution.py:122
  15.9 0.0 copy-start.4
  15.9 0.1 fusion.11
  15.9 0.3 copy.48
  16.2 1.0 copy-done.4
  17.2 1.4 gather_fusion.4
  18.6 0.0 copy-start.1
  18.6 0.0 copy-start.2
  18.6 2.0 broadcast_select_fusion
  20.6 6.0 %all-to-all-start = ((bf16[8,32,1024]{2,1,0:T(8,128)(2,1)}), bf16[8,32,1024]{2,1,0:T(8,128)(2,1)}, u32[]{:S(2)}, u32[]{:S(2)}) async-start(bf16[8,32,1024]{2,1,0:T(8,128)(2,1)} %broadcast_select_fusion), calls=%async_computation | async-start | bytes 1048576 | tf_op jit(solution)/shard_map/all_to_all | solution.py:129
  26.5 0.0 all-gather.3.cloned.1.call-start
  26.5 0.1 compare_select_fusion.4
  26.6 9.4 %all-to-all-done = bf16[8,32,1024]{2,1,0:T(8,128)(2,1)} async-done(((bf16[8,32,1024]{2,1,0:T(8,128)(2,1)}), bf16[8,32,1024]{2,1,0:T(8,128)(2,1)}, u32[]{:S(2)}, u32[]{:S(2)}) %all-to-all-start) | async-done | bytes 524320 | tf_op jit(solution)/shard_map/all_to_all | solution.py:129
  36.0 2.4 %gather_fusion.5 = bf16[8,32,1024]{2,1,0:T(8,128)(2,1)} fusion(bf16[8,32,1024]{2,1,0:T(8,128)(2,1)} %all-to-all-done, s32[1024]{0:T(1024)S(1)} %pad_clamp_fusion.2), kind=kCustom, calls=%fused_computation.5 | custom fusion | bytes 1048608 | tf_op jit(solution)/shard_map/gather | solution.py:130
  38.4 0.0 all-gather.3.cloned.1.call-update
  38.4 0.0 reduce-scatter.2.cloned.1.call-start
  38.5 0.0 copy-done.1
  38.5 0.6 gather_fusion
  39.1 0.0 copy-done.2
  39.1 0.6 gather_fusion.1
  39.8 0.5 multiply_convert_fusion
  40.3 0.7 fusion.24.keep_ref
  41.0 69.0 %all-gather.3.cloned.1.call-done.q_ref = bf16[8,512,1024]{2,1,0:T(8,128)(2,1)} async-done(((bf16[8,32,1024]{2,1,0:T(8,128)(2,1)}), bf16[8,512,1024]{2,1,0:T(8,128)(2,1)}) %all-gather.3.cloned.1.call-update) | async-done | bytes 8388624 | tf_op jit(solution)/shard_map/all_gather | solution.py:131
  110.0 13.5 %shard_map.73 = bf16[8,512,1024]{2,1,0:T(8,128)(2,1)} custom-call(s32[8]{0:T(128)} %get-tuple-element.10.n_live_ref, bf16[8,512,1024]{2,1,0:T(8,128)(2,1)} %all-gather.3.cloned.1.call-done.q_ref, bf16[8,128,2048]{2,1,0:T(8,128)(2,1)} %kv_ref.1, f32[8,1,128]{2,1,0:T(1,128)} %fusion.24.keep_ref), custom_call_target="tpu_custom_call" | custom-call | flops 2147483648 | bytes 20971520 | tf_op jit(solution)/shard_map/pallas_call | solution.py:67
  123.5 0.0 reduce-scatter.2.cloned.1.call-update
  123.5 0.1 broadcast_compare_fusion
  123.6 0.1 select_reduce_fusion
  123.8 0.1 fusion.27
  123.9 83.0 %reduce-scatter.2.cloned.1.call-done = bf16[8,32,1024]{2,1,0:T(8,128)(2,1)} async-done(((bf16[8,512,1024]{2,1,0:T(8,128)(2,1)}), bf16[8,32,1024]{2,1,0:T(8,128)(2,1)}) %reduce-scatter.2.cloned.1.call-update) | async-done | bytes 524304 | tf_op jit(solution)/shard_map/reduce_scatter | solution.py:134
  206.9 1.6 gather_fusion.6
  208.5 0.9 broadcast_select_fusion.1
  209.4 6.4 %all-to-all-start.1 = ((bf16[8,32,1024]{2,1,0:T(8,128)(2,1)}), bf16[8,32,1024]{2,1,0:T(8,128)(2,1)}, u32[]{:S(2)}, u32[]{:S(2)}) async-start(bf16[8,32,1024]{2,1,0:T(8,128)(2,1)} %broadcast_select_fusion.1), calls=%async_computation.2 | async-start | bytes 1048576 | tf_op jit(solution)/shard_map/all_to_all | solution.py:137
  215.9 2.3 slice_bitcast_fusion
  218.2 7.1 %all-to-all-done.1 = bf16[8,32,1024]{2,1,0:T(8,128)(2,1)} async-done(((bf16[8,32,1024]{2,1,0:T(8,128)(2,1)}), bf16[8,32,1024]{2,1,0:T(8,128)(2,1)}, u32[]{:S(2)}, u32[]{:S(2)}) %all-to-all-start.1) | async-done | bytes 524320 | tf_op jit(solution)/shard_map/all_to_all | solution.py:137
  225.3 1.6 gather_fusion.7
  226.9 0.1 bitcast_reduce_fusion
  227.1 0.3 fusion.8
  227.4 1.9 fusion.10
  229.3 0.0 copy-done
  229.3 1.6 fusion.3
  (21 shorter events, 0.1 us)
Async XLA Ops:
  6.5 222.7 %copy-start = (bf16[1024,1024]{1,0:T(8,128)(2,1)S(1)}, bf16[1024,1024]{1,0:T(8,128)(2,1)}, u32[]{:S(2)}) copy-start(bf16[1024,1024]{1,0:T(8,128)(2,1)} %param.13) | copy-start | bytes 6291460
  6.5 5.7 %copy-start.3 = (bf16[32,8,1024]{2,1,0:T(8,128)(2,1)S(1)}, bf16[32,8,1024]{2,1,0:T(8,128)(2,1)}, u32[]{:S(2)}) copy-start(bf16[32,8,1024]{2,1,0:T(8,128)(2,1)} %param.7) | copy-start | bytes 1572868
  15.9 1.4 copy-start.4
  18.6 19.9 %copy-start.1 = (s32[64]{0:T(128)S(1)}, s32[64]{0:T(128)}, u32[]{:S(2)}) copy-start(s32[64]{0:T(128)} %param.9) | copy-start | bytes 772
  18.6 20.6 %copy-start.2 = (s32[64]{0:T(128)S(1)}, s32[64]{0:T(128)}, u32[]{:S(2)}) copy-start(s32[64]{0:T(128)} %param.11) | copy-start | bytes 772
  20.6 15.4 %all-to-all-start = ((bf16[8,32,1024]{2,1,0:T(8,128)(2,1)}), bf16[8,32,1024]{2,1,0:T(8,128)(2,1)}, u32[]{:S(2)}, u32[]{:S(2)}) async-start(bf16[8,32,1024]{2,1,0:T(8,128)(2,1)} %broadcast_select_fusion), calls=%async_computation | async-start | bytes 1048576 | tf_op jit(solution)/shard_map/all_to_all | solution.py:129
  26.5 83.5 %all-gather.3.cloned.1.call-start = ((), (), s32[]{:S(2)}) async-start(), calls=%async_computation.4 | async-start | bytes 8912896 | tf_op jit(solution)/shard_map/all_gather | solution.py:131
  38.4 168.5 %reduce-scatter.2.cloned.1.call-start = ((), (), s32[]{:S(2)}) async-start(), calls=%async_computation.3 | async-start | bytes 8912896 | tf_op jit(solution)/shard_map/reduce_scatter | solution.py:134
  209.4 15.9 %all-to-all-start.1 = ((bf16[8,32,1024]{2,1,0:T(8,128)(2,1)}), bf16[8,32,1024]{2,1,0:T(8,128)(2,1)}, u32[]{:S(2)}, u32[]{:S(2)}) async-start(bf16[8,32,1024]{2,1,0:T(8,128)(2,1)} %broadcast_select_fusion.1), calls=%async_computation.2 | async-start | bytes 1048576 | tf_op jit(solution)/shard_map/all_to_all | solution.py:137
Sparse Core Ops, SparseCore 0:
  38.5 71.4 all-gather.2
  123.7 83.2 reduce-scatter.1

commit v3 on v2

--- a/solution.py
+++ b/solution.py
@@ -85,7 +85,82 @@
     )(n_live, queries, piece, keep)
 
 
-def on_device(candidates, kv_cache, cache_request, rank_request, hist_blocks, w_uq, w_out):
+def shift_perm(grid, axis, shift):
+    rows, cols = grid
+    pairs = []
+    for zi in range(rows):
+        for xi in range(cols):
+            if axis == 0:
+                dst = ((zi + shift) % rows) * cols + xi
+            else:
+                dst = zi * cols + (xi + shift) % cols
+            pairs.append((zi * cols + xi, dst))
+    return pairs
+
+
+def send(value, grid, axis, shift):
+    return lax.ppermute(value, "member", shift_perm(grid, axis, shift))
+
+
+def ring_gather(block, grid, axis):
+    n = grid[axis]
+    slots = {0: block}
+    ahead, behind = block, block
+    for k in range(1, (n - 1) // 2 + 1):
+        ahead = send(ahead, grid, axis, -1)
+        behind = send(behind, grid, axis, 1)
+        slots[k], slots[n - k] = ahead, behind
+    if n % 2 == 0:
+        if n == 2:
+            slots[1] = send(block, grid, axis, -1)
+        else:
+            half = block.shape[1] // 2
+            first = send(behind[:, :half], grid, axis, 1)
+            second = send(ahead[:, half:], grid, axis, -1)
+            slots[n // 2] = jnp.concatenate([first, second], axis=1)
+    return jnp.concatenate([slots[r] for r in range(n)], axis=1)
+
+
+def ring_reduce(parts, grid, axis):
+    n = grid[axis]
+    rows, total, width = parts.shape
+    m = total // n
+    slots = [parts[:, r * m:(r + 1) * m].astype(jnp.float32) for r in range(n)]
+    if n == 1:
+        return slots[0]
+    if n == 2:
+        return slots[0] + send(slots[1].astype(jnp.bfloat16), grid, axis, 1).astype(jnp.float32)
+    top = (n - 1) // 2
+    acc_ahead, acc_behind = slots[top], slots[n - top]
+    if n % 2 == 0:
+        half = m // 2
+        far = slots[n // 2].astype(jnp.bfloat16)
+        got_first = send(far[:, :half], grid, axis, 1).astype(jnp.float32)
+        got_second = send(far[:, half:], grid, axis, -1).astype(jnp.float32)
+        acc_ahead = acc_ahead + jnp.concatenate([got_first, jnp.zeros_like(got_first)], axis=1)
+        acc_behind = acc_behind + jnp.concatenate([jnp.zeros_like(got_second), got_second], axis=1)
+    for k in range(top, 0, -1):
+        got_ahead = send(acc_ahead.astype(jnp.bfloat16), grid, axis, 1).astype(jnp.float32)
+        got_behind = send(acc_behind.astype(jnp.bfloat16), grid, axis, -1).astype(jnp.float32)
+        if k > 1:
+            acc_ahead = slots[k - 1] + got_ahead
+            acc_behind = slots[n - k + 1] + got_behind
+        else:
+            return slots[0] + got_ahead + got_behind
+
+
+def torus_gather(block, grid, order):
+    rows, m, width = block.shape
+    out = ring_gather(block, grid, order[1])
+    return ring_gather(out, grid, order[0])
+
+
+def torus_reduce(parts, grid, order):
+    out = ring_reduce(parts, grid, order[0])
+    return ring_reduce(out, grid, order[1])
+
+
+def on_device(grid, candidates, kv_cache, cache_request, rank_request, hist_blocks, w_uq, w_out):
     groups = lax.axis_size("group")
     per_group = kv_cache.shape[0]
     cand_rows = candidates.shape[0]
@@ -128,10 +203,16 @@
     q_out = jnp.where(send_filled[:, None, None], q_pos[send_pos], jnp.zeros((), jnp.bfloat16))
     q_in = lax.all_to_all(q_out, "group", split_axis=0, concat_axis=0, tiled=True)
     q_rows = q_in[row_index]
-    q_all = lax.all_gather(q_rows, "member", axis=1, tiled=True)
-
-    partial = attend_local(q_all, kv_cache, row_live, member_now * count, scale, HEADS, jnp.bfloat16)
-    summed = lax.psum_scatter(partial, "member", scatter_dimension=1, tiled=True)
+    split = per_group // 2
+    halves = ((slice(0, split), (0, 1)), (slice(split, per_group), (1, 0)))
+    sums = []
+    for rows_of, order in halves:
+        q_all = torus_gather(q_rows[rows_of], grid, order)
+        partial = attend_local(
+            q_all, kv_cache[rows_of], row_live[rows_of], member_now * count, scale, HEADS, jnp.bfloat16
+        )
+        sums.append(torus_reduce(partial, grid, order))
+    summed = jnp.concatenate(sums, axis=0).astype(jnp.bfloat16)
 
     a_out = jnp.where(filled[:, None, None], summed[chosen], jnp.zeros((), summed.dtype))
     a_in = lax.all_to_all(a_out, "group", split_axis=0, concat_axis=0, tiled=True)
@@ -144,9 +225,21 @@
     return result.astype(jnp.bfloat16).reshape(cand_rows, per_group, width)
 
 
+def member_grid(mesh):
+    members = mesh.shape["member"]
+    try:
+        line = mesh.devices[0]
+        cols = len({d.coords[0] for d in line})
+    except (AttributeError, TypeError, IndexError):
+        cols = int(round(members ** 0.5))
+    if cols < 1 or members % cols:
+        cols = members
+    return (members // cols, cols)
+
+
 def solution(mesh):
     return jax.shard_map(
-        on_device,
+        functools.partial(on_device, member_grid(mesh)),
         mesh=mesh,
         in_specs=(P("member", "group", None), P("group", "member", None), P(), P(), P(), P(), P()),
         out_specs=P("member", "group", None),

time: 239 us -> 193 us (0.81)
  waiting for transfers between devices: 169 us -> 55 us
  starting transfers between devices: 12.4 us -> 64.5 us
  local copies, waits for them, and re-layouts: 13.6 us -> 35.8 us
  between operations: 13.6 us -> 0.47 us
  other arithmetic: 10.8 us -> 15.7 us
    reduce_scatter x1 -> x0, waiting for transfers between devices: 83 us -> none  [on_device(): lax.psum_scatter(partial, 'member', scatter_dimension=1, tiled=True)]
    all_gather x1 -> x0, waiting for transfers between devices: 69 us -> none  [on_device(): q_all = lax.all_gather(q_rows, 'member', axis=1, tiled=True)]
    ppermute x0 -> x32, starting transfers between devices: none -> 41.4 us  [send(): return lax.ppermute(value, 'member', shift_perm(grid, axis, shift))]
    ppermute x0 -> x32, waiting for transfers between devices: none -> 39.2 us  [send(): return lax.ppermute(value, 'member', shift_perm(grid, axis, shift))]
    unnamed x10 -> x25, local copies, waits for them, and re-layouts: 0.98 us -> 14.3 us
    all_to_all x1, starting transfers between devices: 6.41 us -> 17.1 us  [on_device(): lax.all_to_all(a_out, 'group', split_axis=0, concat_axis=0, tiled=True)]
    slice x0 -> x14, local copies, waits for them, and re-layouts: none -> 8.07 us  [the longest x4 3.74 us: ring_reduce(): got_first = send(far[:, :half], grid, axis, 1).astype(jnp.float32)]
    concatenate x0 -> x4, local copies, waits for them, and re-layouts: none -> 3.85 us  [ring_gather(): return jnp.concatenate([slots[r] for r in range(n)], axis=1)]
  transfers between devices with their start and end apart: 4 -> 34, of which waited for: 4 -> 11; matrix products, arithmetic and copies ran while one was open for 2% -> 18% of each run, Pallas kernels for 0% -> 8%
where the time goes in v3:
time: 193 us
  starting transfers between devices  64.5 us (33%)
  waiting for transfers between devices  55 us (28%)
  local copies, waits for them, and re-layouts  35.8 us (19%)
  other arithmetic  15.7 us (8%)
  Pallas kernels  15.7 us (8%)
  matrix products  5.45 us (3%)
    ppermute x32, starting transfers between devices, send(): return lax.ppermute(value, 'member', shift_perm(grid, axis, shift))  41.4 us
    ppermute x32, waiting for transfers between devices, send(): return lax.ppermute(value, 'member', shift_perm(grid, axis, shift))  39.2 us
    all_to_all x1, starting transfers between devices, on_device(): lax.all_to_all(a_out, 'group', split_axis=0, concat_axis=0, tiled=True)  17.1 us
    pallas_call x2, Pallas kernels, attend_local(): pl.pallas_call(kernel, out_shape=jax.ShapeDtypeStruct((rows, cands, width...  15.7 us
    unnamed x25, local copies, waits for them, and re-layouts  14.3 us
    all_to_all x1, waiting for transfers between devices, on_device(): lax.all_to_all(q_out, 'group', split_axis=0, concat_axis=0, tiled=True)  8.62 us
    all_to_all x1, waiting for transfers between devices, on_device(): lax.all_to_all(a_out, 'group', split_axis=0, concat_axis=0, tiled=True)  7.14 us
    all_to_all x1, starting transfers between devices, on_device(): lax.all_to_all(q_out, 'group', split_axis=0, concat_axis=0, tiled=True)  5.96 us
  transfers between devices with their start and end apart: 34, of which 11 were waited for; matrix products, arithmetic and copies ran while one was open for 18% of the time, Pallas kernels for 8%

profile of v3, /device:TPU:1, one launch (start us, length us, event | category | flops | bytes accessed | tf_op | source)
XLA Modules:
  0.0 192.6 jit_solution(6646084688967088385)
XLA Ops:
  0.0 1.0 fusion.30
  1.0 1.3 gather_fusion
  4.1 1.2 convert_reduce_fusion
  5.5 1.3 fusion.4
  7.0 3.8 %divide_multiply_fusion = f32[256,2048]{1,0:T(8,128)S(1)} fusion(bf16[1024,2048]{1,0:T(8,128)(2,1)} %param.12, bf16[32,8,1024]{2,1,0:T(8,128)(2,1)} %param.7, f32[32,8]{1,0:T(8,128)S(1)} %copy.37, f32[32,8]{1,0:T(8,128)S(1)} %copy.35), kind=kOutput, calls=%fused_computation.14 | convolution fusion | flops 1076887552 | bytes 6817792 | tf_op jit(solution)/shard_map/dot_general | solution.py:197
  11.2 0.9 copy-done.5
  12.7 0.9 broadcast_select_fusion
  13.6 6.0 %all-to-all-start = ((bf16[8,32,1024]{2,1,0:T(8,128)(2,1)}), bf16[8,32,1024]{2,1,0:T(8,128)(2,1)S(1)}, u32[]{:S(2)}, u32[]{:S(2)}) async-start(bf16[8,32,1024]{2,1,0:T(8,128)(2,1)} %broadcast_select_fusion), calls=%async_computation | async-start | bytes 1048576 | tf_op jit(solution)/shard_map/all_to_all | solution.py:204
  20.3 8.6 %all-to-all-done = bf16[8,32,1024]{2,1,0:T(8,128)(2,1)S(1)} async-done(((bf16[8,32,1024]{2,1,0:T(8,128)(2,1)}), bf16[8,32,1024]{2,1,0:T(8,128)(2,1)S(1)}, u32[]{:S(2)}, u32[]{:S(2)}) %all-to-all-start) | async-done | bytes 524320 | tf_op jit(solution)/shard_map/all_to_all | solution.py:204
  29.5 1.1 constant_dynamic-update-slice_fusion.4
  30.6 1.2 collective-permute-start.1
  31.8 1.5 collective-permute-start
  33.3 3.8 %collective-permute-start.16 = (bf16[4,32,1024]{2,1,0:T(8,128)(2,1)S(1)}, bf16[4,32,1024]{2,1,0:T(8,128)(2,1)S(1)}, u32[]{:S(2)}, u32[]{:S(2)}) collective-permute-start(bf16[4,32,1024]{2,1,0:T(8,128)(2,1)S(1)} %get-tuple-element.36), channel_id=1, source_target_pairs={{0,12},{1,13},{2,14},{3,15},{4,0},{5,1},{6,2},{7,3},{8,4},{9,5},{1... | collective-permute-start | bytes 786440 | tf_op jit(solution)/shard_map/ppermute | solution.py:102
  37.1 1.6 collective-permute-done.1
  38.9 2.7 %collective-permute-start.3 = (bf16[4,16,1024]{2,1,0:T(8,128)(2,1)S(1)}, bf16[4,16,1024]{2,1,0:T(8,128)(2,1)S(1)}, u32[]{:S(2)}, u32[]{:S(2)}) collective-permute-start(bf16[4,16,1024]{2,1,0:T(8,128)(2,1)S(1)} %slice.178), channel_id=1, source_target_pairs={{0,3},{1,0},{2,1},{3,2},{4,7},{5,4},{6,5},{7,6},{8,11},{9,8},{10,9... | collective-permute-start | bytes 393224 | tf_op jit(solution)/shard_map/ppermute | solution.py:102
  41.6 2.8 %collective-permute-done.17 = bf16[4,32,1024]{2,1,0:T(8,128)(2,1)S(1)} collective-permute-done((bf16[4,32,1024]{2,1,0:T(8,128)(2,1)S(1)}, bf16[4,32,1024]{2,1,0:T(8,128)(2,1)S(1)}, u32[]{:S(2)}, u32[]{:S(2)}) %collective-permute-start.17) | collective-permute-done | bytes 262176 | tf_op jit(solution)/shard_map/ppermute | solution.py:102
  44.4 2.7 %collective-permute-start.19 = (bf16[4,16,1024]{2,1,0:T(8,128)(2,1)S(1)}, bf16[4,16,1024]{2,1,0:T(8,128)(2,1)S(1)}, u32[]{:S(2)}, u32[]{:S(2)}) collective-permute-start(bf16[4,16,1024]{2,1,0:T(8,128)(2,1)S(1)} %slice.193), channel_id=1, source_target_pairs={{0,12},{1,13},{2,14},{3,15},{4,0},{5,1},{6,2},{7,3},{8,4},{9,5},{1... | collective-permute-start | bytes 393224 | tf_op jit(solution)/shard_map/ppermute | solution.py:102
  47.2 0.8 constant_dynamic-update-slice_fusion.3
  48.7 0.7 constant_dynamic-update-slice_fusion.1
  49.5 0.9 constant_dynamic-update-slice_fusion
  50.3 0.9 constant_dynamic-update-slice_fusion.17
  51.2 2.7 %collective-permute-start.4 = (bf16[4,128,1024]{2,1,0:T(8,128)(2,1)}, bf16[4,128,1024]{2,1,0:T(8,128)(2,1)S(1)}, u32[]{:S(2)}, u32[]{:S(2)}) collective-permute-start(bf16[4,128,1024]{2,1,0:T(8,128)(2,1)} %get-tuple-element.37), channel_id=1, source_target_pairs={{0,12},{1,13},{2,14},{3,15},{4,0},{5,1},{6,2},{7,3},{8,4},{9,5},{1... | collective-permute-start | bytes 3145736 | tf_op jit(solution)/shard_map/ppermute | solution.py:102
  55.3 0.8 constant_dynamic-update-slice_fusion.14
  56.2 1.3 collective-permute-start.20
  57.7 2.5 %fusion.47 = (bf16[4,128,2048]{2,1,0:T(8,128)(2,1)}, bf16[4,128,2048]{2,1,0:T(8,128)(2,1)}) fusion(bf16[8,128,2048]{2,1,0:T(8,128)(2,1)S(1)} %copy-done.3), kind=kLoop, calls=%fused_computation.156 | loop fusion | bytes 8388608 | tf_op jit(solution)/shard_map/slice | solution.py:212
  60.2 13.1 %collective-permute-done.5 = bf16[4,128,1024]{2,1,0:T(8,128)(2,1)S(1)} collective-permute-done((bf16[4,128,1024]{2,1,0:T(8,128)(2,1)}, bf16[4,128,1024]{2,1,0:T(8,128)(2,1)S(1)}, u32[]{:S(2)}, u32[]{:S(2)}) %collective-permute-start.5) | collective-permute-done | bytes 1048608 | tf_op jit(solution)/shard_map/ppermute | solution.py:102
  74.1 2.7 %collective-permute-start.7 = (bf16[4,64,1024]{2,1,0:T(8,128)(2,1)S(1)}, bf16[4,64,1024]{2,1,0:T(8,128)(2,1)S(1)}, u32[]{:S(2)}, u32[]{:S(2)}) collective-permute-start(bf16[4,64,1024]{2,1,0:T(8,128)(2,1)S(1)} %slice.180), channel_id=1, source_target_pairs={{0,12},{1,13},{2,14},{3,15},{4,0},{5,1},{6,2},{7,3},{8,4},{9,5},{1... | collective-permute-start | bytes 1572872 | tf_op jit(solution)/shard_map/ppermute | solution.py:102
  77.4 2.1 %collective-permute-done.21 = bf16[4,128,1024]{2,1,0:T(8,128)(2,1)S(1)} collective-permute-done((bf16[4,128,1024]{2,1,0:T(8,128)(2,1)}, bf16[4,128,1024]{2,1,0:T(8,128)(2,1)S(1)}, u32[]{:S(2)}, u32[]{:S(2)}) %collective-permute-start.21) | collective-permute-done | bytes 1048608 | tf_op jit(solution)/shard_map/ppermute | solution.py:102
  79.5 0.8 slice.194
  80.4 0.8 slice.195
  81.2 2.7 %collective-permute-start.23 = (bf16[4,64,1024]{2,1,0:T(8,128)(2,1)}, bf16[4,64,1024]{2,1,0:T(8,128)(2,1)}, u32[]{:S(2)}, u32[]{:S(2)}) collective-permute-start(bf16[4,64,1024]{2,1,0:T(8,128)(2,1)} %slice.195), channel_id=1, source_target_pairs={{0,3},{1,0},{2,1},{3,2},{4,7},{5,4},{6,5},{7,6},{8,11},{9,8},{10,9... | collective-permute-start | bytes 1572872 | tf_op jit(solution)/shard_map/ppermute | solution.py:102
  83.9 1.1 constant_dynamic-update-slice_fusion.8
  84.9 1.1 constant_dynamic-update-slice_fusion.22
  86.0 0.8 constant_dynamic-update-slice_fusion.7
  86.8 0.9 constant_dynamic-update-slice_fusion.6
  87.7 1.1 constant_dynamic-update-slice_fusion.5.q_ref
  88.8 7.8 %shard_map.73 = bf16[4,512,1024]{2,1,0:T(8,128)(2,1)} custom-call(s32[4]{0:T(128)} %get-tuple-element.57.n_live_ref, bf16[4,512,1024]{2,1,0:T(8,128)(2,1)} %constant_dynamic-update-slice_fusion.5.q_ref, bf16[4,128,2048]{2,1,0:T(8,128)(2,1)} %get-tuple-element.17.kv_ref, f32[4,1,128]{2,1,0:T(1,128)} %get-tuple-element.53.keep_ref), custom_call_target="tpu_custom_call" | custom-call | flops 1073741824 | bytes 10485760 | tf_op jit(solution)/shard_map/pallas_call | solution.py:67
  96.6 2.2 %fusion.46 = (bf16[4,64,1024]{2,1,0:T(8,128)(2,1)}, bf16[4,64,1024]{2,1,0:T(8,128)(2,1)}) fusion(bf16[4,512,1024]{2,1,0:T(8,128)(2,1)} %shard_map.73), kind=kLoop, calls=%fused_computation.155 | loop fusion | bytes 2097152 | tf_op jit(solution)/shard_map/slice | solution.py:138
  99.1 1.3 collective-permute-start.8
  100.3 1.9 constant_dynamic-update-slice_fusion.21
  102.2 1.9 constant_dynamic-update-slice_fusion.20
  104.1 1.1 constant_dynamic-update-slice_fusion.19.q_ref
  105.2 7.9 %shard_map.74 = bf16[4,512,1024]{2,1,0:T(8,128)(2,1)} custom-call(s32[4]{0:T(128)} %get-tuple-element.58.n_live_ref, bf16[4,512,1024]{2,1,0:T(8,128)(2,1)} %constant_dynamic-update-slice_fusion.19.q_ref, bf16[4,128,2048]{2,1,0:T(8,128)(2,1)} %get-tuple-element.18.kv_ref, f32[4,1,128]{2,1,0:T(1,128)} %get-tuple-element.54.keep_ref), custom_call_target="tpu_custom_call" | custom-call | flops 1073741824 | bytes 10485760 | tf_op jit(solution)/shard_map/pallas_call | solution.py:67
  113.0 1.5 fusion.48
  114.6 2.7 %collective-permute-start.26 = (bf16[4,64,1024]{2,1,0:T(8,128)(2,1)S(1)}, bf16[4,64,1024]{2,1,0:T(8,128)(2,1)S(1)}, u32[]{:S(2)}, u32[]{:S(2)}) collective-permute-start(bf16[4,64,1024]{2,1,0:T(8,128)(2,1)S(1)} %get-tuple-element.22), channel_id=1, source_target_pairs={{0,3},{1,0},{2,1},{3,2},{4,7},{5,4},{6,5},{7,6},{8,11},{9,8},{10,9... | collective-permute-start | bytes 1572872 | tf_op jit(solution)/shard_map/ppermute | solution.py:102
  117.2 2.4 %add_convert_fusion.3 = (bf16[4,128,1024]{2,1,0:T(8,128)(2,1)S(1)}, bf16[4,128,1024]{2,1,0:T(8,128)(2,1)S(1)}) fusion(bf16[4,512,1024]{2,1,0:T(8,128)(2,1)} %shard_map.73, bf16[4,64,1024]{2,1,0:T(8,128)(2,1)} %collective-permute-done.8, bf16[4,64,1024]{2,1,0:T(8,128)(2,1)} %collective-permute-done.10), kind=kLoop, calls=%fused_computation.13 | loop fusion | flops 4194304 | bytes 5242880 | tf_op jit(solution)/shard_map/convert_element_type | solution.py:143
  120.2 0.9 collective-permute-start.9
  121.2 2.6 %collective-permute-done.24 = bf16[4,64,1024]{2,1,0:T(8,128)(2,1)S(1)} collective-permute-done((bf16[4,64,1024]{2,1,0:T(8,128)(2,1)S(1)}, bf16[4,64,1024]{2,1,0:T(8,128)(2,1)S(1)}, u32[]{:S(2)}, u32[]{:S(2)}) %collective-permute-start.24) | collective-permute-done | bytes 524320 | tf_op jit(solution)/shard_map/ppermute | solution.py:102
  124.6 2.7 %collective-permute-start.27 = (bf16[4,128,1024]{2,1,0:T(8,128)(2,1)S(1)}, bf16[4,128,1024]{2,1,0:T(8,128)(2,1)S(1)}, u32[]{:S(2)}, u32[]{:S(2)}) collective-permute-start(bf16[4,128,1024]{2,1,0:T(8,128)(2,1)S(1)} %get-tuple-element.20), channel_id=1, source_target_pairs={{0,3},{1,0},{2,1},{3,2},{4,7},{5,4},{6,5},{7,6},{8,11},{9,8},{10,9... | collective-permute-start | bytes 3145736 | tf_op jit(solution)/shard_map/ppermute | solution.py:102
  127.6 10.2 %collective-permute-done.11 = bf16[4,128,1024]{2,1,0:T(8,128)(2,1)S(1)} collective-permute-done((bf16[4,128,1024]{2,1,0:T(8,128)(2,1)S(1)}, bf16[4,128,1024]{2,1,0:T(8,128)(2,1)S(1)}, u32[]{:S(2)}, u32[]{:S(2)}) %collective-permute-start.11) | collective-permute-done | bytes 1048608 | tf_op jit(solution)/shard_map/ppermute | solution.py:102
  137.8 2.2 %collective-permute-done.9 = bf16[4,128,1024]{2,1,0:T(8,128)(2,1)S(1)} collective-permute-done((bf16[4,128,1024]{2,1,0:T(8,128)(2,1)S(1)}, bf16[4,128,1024]{2,1,0:T(8,128)(2,1)S(1)}, u32[]{:S(2)}, u32[]{:S(2)}) %collective-permute-start.9) | collective-permute-done | bytes 1048608 | tf_op jit(solution)/shard_map/ppermute | solution.py:102
  140.0 1.7 fusion.44
  141.8 2.7 %collective-permute-start.14 = (bf16[4,16,1024]{2,1,0:T(8,128)(2,1)S(1)}, bf16[4,16,1024]{2,1,0:T(8,128)(2,1)S(1)}, u32[]{:S(2)}, u32[]{:S(2)}) collective-permute-start(bf16[4,16,1024]{2,1,0:T(8,128)(2,1)S(1)} %get-tuple-element.28), channel_id=1, source_target_pairs={{0,3},{1,0},{2,1},{3,2},{4,7},{5,4},{6,5},{7,6},{8,11},{9,8},{10,9... | collective-permute-start | bytes 393224 | tf_op jit(solution)/shard_map/ppermute | solution.py:102
  146.0 2.7 %collective-permute-start.30 = (bf16[4,16,1024]{2,1,0:T(8,128)(2,1)S(1)}, bf16[4,16,1024]{2,1,0:T(8,128)(2,1)S(1)}, u32[]{:S(2)}, u32[]{:S(2)}) collective-permute-start(bf16[4,16,1024]{2,1,0:T(8,128)(2,1)S(1)} %get-tuple-element.30), channel_id=1, source_target_pairs={{0,12},{1,13},{2,14},{3,15},{4,0},{5,1},{6,2},{7,3},{8,4},{9,5},{1... | collective-permute-start | bytes 393224 | tf_op jit(solution)/shard_map/ppermute | solution.py:102
  149.2 2.6 %collective-permute-start.15 = (bf16[4,32,1024]{2,1,0:T(8,128)(2,1)S(1)}, bf16[4,32,1024]{2,1,0:T(8,128)(2,1)S(1)}, u32[]{:S(2)}, u32[]{:S(2)}) collective-permute-start(bf16[4,32,1024]{2,1,0:T(8,128)(2,1)S(1)} %get-tuple-element.24), channel_id=1, source_target_pairs={{0,3},{1,0},{2,1},{3,2},{4,7},{5,4},{6,5},{7,6},{8,11},{9,8},{10,9... | collective-permute-start | bytes 786440 | tf_op jit(solution)/shard_map/ppermute | solution.py:102
  152.0 2.7 %collective-permute-start.31 = (bf16[4,32,1024]{2,1,0:T(8,128)(2,1)S(1)}, bf16[4,32,1024]{2,1,0:T(8,128)(2,1)S(1)}, u32[]{:S(2)}, u32[]{:S(2)}) collective-permute-start(bf16[4,32,1024]{2,1,0:T(8,128)(2,1)S(1)} %get-tuple-element.26), channel_id=1, source_target_pairs={{0,12},{1,13},{2,14},{3,15},{4,0},{5,1},{6,2},{7,3},{8,4},{9,5},{1... | collective-permute-start | bytes 786440 | tf_op jit(solution)/shard_map/ppermute | solution.py:102
  154.7 3.9 %collective-permute-done.13 = bf16[4,32,1024]{2,1,0:T(8,128)(2,1)S(1)} collective-permute-done((bf16[4,32,1024]{2,1,0:T(8,128)(2,1)S(1)}, bf16[4,32,1024]{2,1,0:T(8,128)(2,1)S(1)}, u32[]{:S(2)}, u32[]{:S(2)}) %collective-permute-start.13) | collective-permute-done | bytes 262176 | tf_op jit(solution)/shard_map/ppermute | solution.py:102
  159.5 0.9 broadcast_select_fusion.1
  160.4 17.1 %all-to-all-start.1 = ((bf16[8,32,1024]{2,1,0:T(8,128)(2,1)}), bf16[8,32,1024]{2,1,0:T(8,128)(2,1)}, u32[]{:S(2)}, u32[]{:S(2)}) async-start(bf16[8,32,1024]{2,1,0:T(8,128)(2,1)} %broadcast_select_fusion.1), calls=%async_computation.1 | async-start | bytes 1048576 | tf_op jit(solution)/shard_map/all_to_all | solution.py:218
  177.6 2.3 %slice_bitcast_fusion = f32[32,8,1024]{2,1,0:T(8,128)} fusion(f32[256,2048]{1,0:T(8,128)} %copy-done.5), kind=kLoop, calls=%fused_computation.25 | loop fusion | bytes 2097152 | tf_op jit(solution)/shard_map/reshape | solution.py:198
  179.9 7.1 %all-to-all-done.1 = bf16[8,32,1024]{2,1,0:T(8,128)(2,1)} async-done(((bf16[8,32,1024]{2,1,0:T(8,128)(2,1)}), bf16[8,32,1024]{2,1,0:T(8,128)(2,1)}, u32[]{:S(2)}, u32[]{:S(2)}) %all-to-all-start.1) | async-done | bytes 524320 | tf_op jit(solution)/shard_map/all_to_all | solution.py:218
  187.0 1.6 gather_fusion.7
  189.1 1.9 fusion.10
  191.0 1.6 fusion.3
  (114 shorter events, 14.0 us)
Async XLA Ops:
  0.0 191.0 %copy-start = (bf16[1024,1024]{1,0:T(8,128)(2,1)S(1)}, bf16[1024,1024]{1,0:T(8,128)(2,1)}, u32[]{:S(2)}) copy-start(bf16[1024,1024]{1,0:T(8,128)(2,1)} %param.13) | copy-start | bytes 6291460
  10.8 1.3 copy-start.5
  10.8 8.7 %copy-start.1 = (s32[64]{0:T(128)S(1)}, s32[64]{0:T(128)}, u32[]{:S(2)}) copy-start(s32[64]{0:T(128)} %param.11) | copy-start | bytes 772
  13.6 15.3 %all-to-all-start = ((bf16[8,32,1024]{2,1,0:T(8,128)(2,1)}), bf16[8,32,1024]{2,1,0:T(8,128)(2,1)S(1)}, u32[]{:S(2)}, u32[]{:S(2)}) async-start(bf16[8,32,1024]{2,1,0:T(8,128)(2,1)} %broadcast_select_fusion), calls=%async_computation | async-start | bytes 1048576 | tf_op jit(solution)/shard_map/all_to_all | solution.py:204
  30.6 8.1 %collective-permute-start.1 = (bf16[4,32,1024]{2,1,0:T(8,128)(2,1)S(1)}, bf16[4,32,1024]{2,1,0:T(8,128)(2,1)S(1)}, u32[]{:S(2)}, u32[]{:S(2)}) collective-permute-start(bf16[4,32,1024]{2,1,0:T(8,128)(2,1)S(1)} %get-tuple-element.35), channel_id=1, source_target_pairs={{0,1},{1,2},{2,3},{3,0},{4,5},{5,6},{6,7},{7,4},{8,9},{9,10},{10,1... | collective-permute-start | bytes 786440 | tf_op jit(solution)/shard_map/ppermute | solution.py:102
  31.8 25.8 %copy-start.3 = (bf16[8,128,2048]{2,1,0:T(8,128)(2,1)S(1)}, bf16[8,128,2048]{2,1,0:T(8,128)(2,1)}, u32[]{:S(2)}) copy-start(bf16[8,128,2048]{2,1,0:T(8,128)(2,1)} %param.8) | copy-start | bytes 12582916
  31.8 7.0 %collective-permute-start = (bf16[4,32,1024]{2,1,0:T(8,128)(2,1)S(1)}, bf16[4,32,1024]{2,1,0:T(8,128)(2,1)S(1)}, u32[]{:S(2)}, u32[]{:S(2)}) collective-permute-start(bf16[4,32,1024]{2,1,0:T(8,128)(2,1)S(1)} %get-tuple-element.35), channel_id=1, source_target_pairs={{0,3},{1,0},{2,1},{3,2},{4,7},{5,4},{6,5},{7,6},{8,11},{9,8},{10,9... | collective-permute-start | bytes 786440 | tf_op jit(solution)/shard_map/ppermute | solution.py:102
  33.3 11.1 %collective-permute-start.16 = (bf16[4,32,1024]{2,1,0:T(8,128)(2,1)S(1)}, bf16[4,32,1024]{2,1,0:T(8,128)(2,1)S(1)}, u32[]{:S(2)}, u32[]{:S(2)}) collective-permute-start(bf16[4,32,1024]{2,1,0:T(8,128)(2,1)S(1)} %get-tuple-element.36), channel_id=1, source_target_pairs={{0,12},{1,13},{2,14},{3,15},{4,0},{5,1},{6,2},{7,3},{8,4},{9,5},{1... | collective-permute-start | bytes 786440 | tf_op jit(solution)/shard_map/ppermute | solution.py:102
  37.1 7.3 %collective-permute-start.17 = (bf16[4,32,1024]{2,1,0:T(8,128)(2,1)S(1)}, bf16[4,32,1024]{2,1,0:T(8,128)(2,1)S(1)}, u32[]{:S(2)}, u32[]{:S(2)}) collective-permute-start(bf16[4,32,1024]{2,1,0:T(8,128)(2,1)S(1)} %get-tuple-element.36), channel_id=1, source_target_pairs={{0,4},{1,5},{2,6},{3,7},{4,8},{5,9},{6,10},{7,11},{8,12},{9,13},{1... | collective-permute-start | bytes 786440 | tf_op jit(solution)/shard_map/ppermute | solution.py:102
  38.7 9.3 %collective-permute-start.2 = (bf16[4,16,1024]{2,1,0:T(8,128)(2,1)S(1)}, bf16[4,16,1024]{2,1,0:T(8,128)(2,1)S(1)}, u32[]{:S(2)}, u32[]{:S(2)}) collective-permute-start(bf16[4,16,1024]{2,1,0:T(8,128)(2,1)S(1)} %slice.177), channel_id=1, source_target_pairs={{0,1},{1,2},{2,3},{3,0},{4,5},{5,6},{6,7},{7,4},{8,9},{9,10},{10,1... | collective-permute-start | bytes 393224 | tf_op jit(solution)/shard_map/ppermute | solution.py:102
  38.9 9.9 %collective-permute-start.3 = (bf16[4,16,1024]{2,1,0:T(8,128)(2,1)S(1)}, bf16[4,16,1024]{2,1,0:T(8,128)(2,1)S(1)}, u32[]{:S(2)}, u32[]{:S(2)}) collective-permute-start(bf16[4,16,1024]{2,1,0:T(8,128)(2,1)S(1)} %slice.178), channel_id=1, source_target_pairs={{0,3},{1,0},{2,1},{3,2},{4,7},{5,4},{6,5},{7,6},{8,11},{9,8},{10,9... | collective-permute-start | bytes 393224 | tf_op jit(solution)/shard_map/ppermute | solution.py:102
  44.3 9.6 %collective-permute-start.18 = (bf16[4,16,1024]{2,1,0:T(8,128)(2,1)S(1)}, bf16[4,16,1024]{2,1,0:T(8,128)(2,1)S(1)}, u32[]{:S(2)}, u32[]{:S(2)}) collective-permute-start(bf16[4,16,1024]{2,1,0:T(8,128)(2,1)S(1)} %slice.192), channel_id=1, source_target_pairs={{0,4},{1,5},{2,6},{3,7},{4,8},{5,9},{6,10},{7,11},{8,12},{9,13},{1... | collective-permute-start | bytes 393224 | tf_op jit(solution)/shard_map/ppermute | solution.py:102
  44.4 10.2 %collective-permute-start.19 = (bf16[4,16,1024]{2,1,0:T(8,128)(2,1)S(1)}, bf16[4,16,1024]{2,1,0:T(8,128)(2,1)S(1)}, u32[]{:S(2)}, u32[]{:S(2)}) collective-permute-start(bf16[4,16,1024]{2,1,0:T(8,128)(2,1)S(1)} %slice.193), channel_id=1, source_target_pairs={{0,12},{1,13},{2,14},{3,15},{4,0},{5,1},{6,2},{7,3},{8,4},{9,5},{1... | collective-permute-start | bytes 393224 | tf_op jit(solution)/shard_map/ppermute | solution.py:102
  50.3 22.9 %collective-permute-start.5 = (bf16[4,128,1024]{2,1,0:T(8,128)(2,1)}, bf16[4,128,1024]{2,1,0:T(8,128)(2,1)S(1)}, u32[]{:S(2)}, u32[]{:S(2)}) collective-permute-start(bf16[4,128,1024]{2,1,0:T(8,128)(2,1)} %get-tuple-element.37), channel_id=1, source_target_pairs={{0,4},{1,5},{2,6},{3,7},{4,8},{5,9},{6,10},{7,11},{8,12},{9,13},{1... | collective-permute-start | bytes 3145736 | tf_op jit(solution)/shard_map/ppermute | solution.py:102
  51.2 22.8 %collective-permute-start.4 = (bf16[4,128,1024]{2,1,0:T(8,128)(2,1)}, bf16[4,128,1024]{2,1,0:T(8,128)(2,1)S(1)}, u32[]{:S(2)}, u32[]{:S(2)}) collective-permute-start(bf16[4,128,1024]{2,1,0:T(8,128)(2,1)} %get-tuple-element.37), channel_id=1, source_target_pairs={{0,12},{1,13},{2,14},{3,15},{4,0},{5,1},{6,2},{7,3},{8,4},{9,5},{1... | collective-permute-start | bytes 3145736 | tf_op jit(solution)/shard_map/ppermute | solution.py:102
  56.2 24.2 %collective-permute-start.20 = (bf16[4,128,1024]{2,1,0:T(8,128)(2,1)}, bf16[4,128,1024]{2,1,0:T(8,128)(2,1)S(1)}, u32[]{:S(2)}, u32[]{:S(2)}) collective-permute-start(bf16[4,128,1024]{2,1,0:T(8,128)(2,1)} %get-tuple-element.41), channel_id=1, source_target_pairs={{0,3},{1,0},{2,1},{3,2},{4,7},{5,4},{6,5},{7,6},{8,11},{9,8},{10,9... | collective-permute-start | bytes 3145736 | tf_op jit(solution)/shard_map/ppermute | solution.py:102
  57.5 22.1 %collective-permute-start.21 = (bf16[4,128,1024]{2,1,0:T(8,128)(2,1)}, bf16[4,128,1024]{2,1,0:T(8,128)(2,1)S(1)}, u32[]{:S(2)}, u32[]{:S(2)}) collective-permute-start(bf16[4,128,1024]{2,1,0:T(8,128)(2,1)} %get-tuple-element.41), channel_id=1, source_target_pairs={{0,1},{1,2},{2,3},{3,0},{4,5},{5,6},{6,7},{7,4},{8,9},{9,10},{10,1... | collective-permute-start | bytes 3145736 | tf_op jit(solution)/shard_map/ppermute | solution.py:102
  73.3 12.7 %collective-permute-start.6 = (bf16[4,64,1024]{2,1,0:T(8,128)(2,1)S(1)}, bf16[4,64,1024]{2,1,0:T(8,128)(2,1)S(1)}, u32[]{:S(2)}, u32[]{:S(2)}) collective-permute-start(bf16[4,64,1024]{2,1,0:T(8,128)(2,1)S(1)} %slice.179), channel_id=1, source_target_pairs={{0,4},{1,5},{2,6},{3,7},{4,8},{5,9},{6,10},{7,11},{8,12},{9,13},{1... | collective-permute-start | bytes 1572872 | tf_op jit(solution)/shard_map/ppermute | solution.py:102
  74.1 12.7 %collective-permute-start.7 = (bf16[4,64,1024]{2,1,0:T(8,128)(2,1)S(1)}, bf16[4,64,1024]{2,1,0:T(8,128)(2,1)S(1)}, u32[]{:S(2)}, u32[]{:S(2)}) collective-permute-start(bf16[4,64,1024]{2,1,0:T(8,128)(2,1)S(1)} %slice.180), channel_id=1, source_target_pairs={{0,12},{1,13},{2,14},{3,15},{4,0},{5,1},{6,2},{7,3},{8,4},{9,5},{1... | collective-permute-start | bytes 1572872 | tf_op jit(solution)/shard_map/ppermute | solution.py:102
  80.4 20.0 %collective-permute-start.22 = (bf16[4,64,1024]{2,1,0:T(8,128)(2,1)}, bf16[4,64,1024]{2,1,0:T(8,128)(2,1)}, u32[]{:S(2)}, u32[]{:S(2)}) collective-permute-start(bf16[4,64,1024]{2,1,0:T(8,128)(2,1)} %slice.194), channel_id=1, source_target_pairs={{0,1},{1,2},{2,3},{3,0},{4,5},{5,6},{6,7},{7,4},{8,9},{9,10},{10,1... | collective-permute-start | bytes 1572872 | tf_op jit(solution)/shard_map/ppermute | solution.py:102
  81.2 21.0 %collective-permute-start.23 = (bf16[4,64,1024]{2,1,0:T(8,128)(2,1)}, bf16[4,64,1024]{2,1,0:T(8,128)(2,1)}, u32[]{:S(2)}, u32[]{:S(2)}) collective-permute-start(bf16[4,64,1024]{2,1,0:T(8,128)(2,1)} %slice.195), channel_id=1, source_target_pairs={{0,3},{1,0},{2,1},{3,2},{4,7},{5,4},{6,5},{7,6},{8,11},{9,8},{10,9... | collective-permute-start | bytes 1572872 | tf_op jit(solution)/shard_map/ppermute | solution.py:102
  98.9 18.4 %collective-permute-start.10 = (bf16[4,64,1024]{2,1,0:T(8,128)(2,1)}, bf16[4,64,1024]{2,1,0:T(8,128)(2,1)}, u32[]{:S(2)}, u32[]{:S(2)}) collective-permute-start(bf16[4,64,1024]{2,1,0:T(8,128)(2,1)} %get-tuple-element.16), channel_id=1, source_target_pairs={{0,12},{1,13},{2,14},{3,15},{4,0},{5,1},{6,2},{7,3},{8,4},{9,5},{1... | collective-permute-start | bytes 1572872 | tf_op jit(solution)/shard_map/ppermute | solution.py:102
  99.1 18.2 %collective-permute-start.8 = (bf16[4,64,1024]{2,1,0:T(8,128)(2,1)}, bf16[4,64,1024]{2,1,0:T(8,128)(2,1)}, u32[]{:S(2)}, u32[]{:S(2)}) collective-permute-start(bf16[4,64,1024]{2,1,0:T(8,128)(2,1)} %get-tuple-element.15), channel_id=1, source_target_pairs={{0,4},{1,5},{2,6},{3,7},{4,8},{5,9},{6,10},{7,11},{8,12},{9,13},{1... | collective-permute-start | bytes 1572872 | tf_op jit(solution)/shard_map/ppermute | solution.py:102
  113.0 10.8 %copy-start.2 = (bf16[4,512,1024]{2,1,0:T(8,128)(2,1)S(1)}, bf16[4,512,1024]{2,1,0:T(8,128)(2,1)}, u32[]{:S(2)}) copy-start(bf16[4,512,1024]{2,1,0:T(8,128)(2,1)} %shard_map.74) | copy-start | bytes 12582916
  114.5 9.3 %collective-permute-start.24 = (bf16[4,64,1024]{2,1,0:T(8,128)(2,1)S(1)}, bf16[4,64,1024]{2,1,0:T(8,128)(2,1)S(1)}, u32[]{:S(2)}, u32[]{:S(2)}) collective-permute-start(bf16[4,64,1024]{2,1,0:T(8,128)(2,1)S(1)} %get-tuple-element.21), channel_id=1, source_target_pairs={{0,1},{1,2},{2,3},{3,0},{4,5},{5,6},{6,7},{7,4},{8,9},{9,10},{10,1... | collective-permute-start | bytes 1572872 | tf_op jit(solution)/shard_map/ppermute | solution.py:102
  114.6 9.2 %collective-permute-start.26 = (bf16[4,64,1024]{2,1,0:T(8,128)(2,1)S(1)}, bf16[4,64,1024]{2,1,0:T(8,128)(2,1)S(1)}, u32[]{:S(2)}, u32[]{:S(2)}) collective-permute-start(bf16[4,64,1024]{2,1,0:T(8,128)(2,1)S(1)} %get-tuple-element.22), channel_id=1, source_target_pairs={{0,3},{1,0},{2,1},{3,2},{4,7},{5,4},{6,5},{7,6},{8,11},{9,8},{10,9... | collective-permute-start | bytes 1572872 | tf_op jit(solution)/shard_map/ppermute | solution.py:102
  119.6 18.2 %collective-permute-start.11 = (bf16[4,128,1024]{2,1,0:T(8,128)(2,1)S(1)}, bf16[4,128,1024]{2,1,0:T(8,128)(2,1)S(1)}, u32[]{:S(2)}, u32[]{:S(2)}) collective-permute-start(bf16[4,128,1024]{2,1,0:T(8,128)(2,1)S(1)} %get-tuple-element.14), channel_id=1, source_target_pairs={{0,12},{1,13},{2,14},{3,15},{4,0},{5,1},{6,2},{7,3},{8,4},{9,5},{1... | collective-permute-start | bytes 3145736 | tf_op jit(solution)/shard_map/ppermute | solution.py:102
  120.2 19.8 %collective-permute-start.9 = (bf16[4,128,1024]{2,1,0:T(8,128)(2,1)S(1)}, bf16[4,128,1024]{2,1,0:T(8,128)(2,1)S(1)}, u32[]{:S(2)}, u32[]{:S(2)}) collective-permute-start(bf16[4,128,1024]{2,1,0:T(8,128)(2,1)S(1)} %get-tuple-element.13), channel_id=1, source_target_pairs={{0,4},{1,5},{2,6},{3,7},{4,8},{5,9},{6,10},{7,11},{8,12},{9,13},{1... | collective-permute-start | bytes 3145736 | tf_op jit(solution)/shard_map/ppermute | solution.py:102
  124.5 20.7 %collective-permute-start.25 = (bf16[4,128,1024]{2,1,0:T(8,128)(2,1)S(1)}, bf16[4,128,1024]{2,1,0:T(8,128)(2,1)S(1)}, u32[]{:S(2)}, u32[]{:S(2)}) collective-permute-start(bf16[4,128,1024]{2,1,0:T(8,128)(2,1)S(1)} %get-tuple-element.19), channel_id=1, source_target_pairs={{0,1},{1,2},{2,3},{3,0},{4,5},{5,6},{6,7},{7,4},{8,9},{9,10},{10,1... | collective-permute-start | bytes 3145736 | tf_op jit(solution)/shard_map/ppermute | solution.py:102
  124.6 20.6 %collective-permute-start.27 = (bf16[4,128,1024]{2,1,0:T(8,128)(2,1)S(1)}, bf16[4,128,1024]{2,1,0:T(8,128)(2,1)S(1)}, u32[]{:S(2)}, u32[]{:S(2)}) collective-permute-start(bf16[4,128,1024]{2,1,0:T(8,128)(2,1)S(1)} %get-tuple-element.20), channel_id=1, source_target_pairs={{0,3},{1,0},{2,1},{3,2},{4,7},{5,4},{6,5},{7,6},{8,11},{9,8},{10,9... | collective-permute-start | bytes 3145736 | tf_op jit(solution)/shard_map/ppermute | solution.py:102
  141.8 6.9 %collective-permute-start.12 = (bf16[4,16,1024]{2,1,0:T(8,128)(2,1)S(1)}, bf16[4,16,1024]{2,1,0:T(8,128)(2,1)S(1)}, u32[]{:S(2)}, u32[]{:S(2)}) collective-permute-start(bf16[4,16,1024]{2,1,0:T(8,128)(2,1)S(1)} %get-tuple-element.27), channel_id=1, source_target_pairs={{0,1},{1,2},{2,3},{3,0},{4,5},{5,6},{6,7},{7,4},{8,9},{9,10},{10,1... | collective-permute-start | bytes 393224 | tf_op jit(solution)/shard_map/ppermute | solution.py:102
  141.8 6.9 %collective-permute-start.14 = (bf16[4,16,1024]{2,1,0:T(8,128)(2,1)S(1)}, bf16[4,16,1024]{2,1,0:T(8,128)(2,1)S(1)}, u32[]{:S(2)}, u32[]{:S(2)}) collective-permute-start(bf16[4,16,1024]{2,1,0:T(8,128)(2,1)S(1)} %get-tuple-element.28), channel_id=1, source_target_pairs={{0,3},{1,0},{2,1},{3,2},{4,7},{5,4},{6,5},{7,6},{8,11},{9,8},{10,9... | collective-permute-start | bytes 393224 | tf_op jit(solution)/shard_map/ppermute | solution.py:102
  145.9 5.9 %collective-permute-start.28 = (bf16[4,16,1024]{2,1,0:T(8,128)(2,1)S(1)}, bf16[4,16,1024]{2,1,0:T(8,128)(2,1)S(1)}, u32[]{:S(2)}, u32[]{:S(2)}) collective-permute-start(bf16[4,16,1024]{2,1,0:T(8,128)(2,1)S(1)} %get-tuple-element.29), channel_id=1, source_target_pairs={{0,4},{1,5},{2,6},{3,7},{4,8},{5,9},{6,10},{7,11},{8,12},{9,13},{1... | collective-permute-start | bytes 393224 | tf_op jit(solution)/shard_map/ppermute | solution.py:102
  146.0 5.8 %collective-permute-start.30 = (bf16[4,16,1024]{2,1,0:T(8,128)(2,1)S(1)}, bf16[4,16,1024]{2,1,0:T(8,128)(2,1)S(1)}, u32[]{:S(2)}, u32[]{:S(2)}) collective-permute-start(bf16[4,16,1024]{2,1,0:T(8,128)(2,1)S(1)} %get-tuple-element.30), channel_id=1, source_target_pairs={{0,12},{1,13},{2,14},{3,15},{4,0},{5,1},{6,2},{7,3},{8,4},{9,5},{1... | collective-permute-start | bytes 393224 | tf_op jit(solution)/shard_map/ppermute | solution.py:102
  148.8 9.8 %collective-permute-start.13 = (bf16[4,32,1024]{2,1,0:T(8,128)(2,1)S(1)}, bf16[4,32,1024]{2,1,0:T(8,128)(2,1)S(1)}, u32[]{:S(2)}, u32[]{:S(2)}) collective-permute-start(bf16[4,32,1024]{2,1,0:T(8,128)(2,1)S(1)} %get-tuple-element.23), channel_id=1, source_target_pairs={{0,1},{1,2},{2,3},{3,0},{4,5},{5,6},{6,7},{7,4},{8,9},{9,10},{10,1... | collective-permute-start | bytes 786440 | tf_op jit(solution)/shard_map/ppermute | solution.py:102
  149.2 9.4 %collective-permute-start.15 = (bf16[4,32,1024]{2,1,0:T(8,128)(2,1)S(1)}, bf16[4,32,1024]{2,1,0:T(8,128)(2,1)S(1)}, u32[]{:S(2)}, u32[]{:S(2)}) collective-permute-start(bf16[4,32,1024]{2,1,0:T(8,128)(2,1)S(1)} %get-tuple-element.24), channel_id=1, source_target_pairs={{0,3},{1,0},{2,1},{3,2},{4,7},{5,4},{6,5},{7,6},{8,11},{9,8},{10,9... | collective-permute-start | bytes 786440 | tf_op jit(solution)/shard_map/ppermute | solution.py:102
  152.0 6.8 %collective-permute-start.29 = (bf16[4,32,1024]{2,1,0:T(8,128)(2,1)S(1)}, bf16[4,32,1024]{2,1,0:T(8,128)(2,1)S(1)}, u32[]{:S(2)}, u32[]{:S(2)}) collective-permute-start(bf16[4,32,1024]{2,1,0:T(8,128)(2,1)S(1)} %get-tuple-element.25), channel_id=1, source_target_pairs={{0,4},{1,5},{2,6},{3,7},{4,8},{5,9},{6,10},{7,11},{8,12},{9,13},{1... | collective-permute-start | bytes 786440 | tf_op jit(solution)/shard_map/ppermute | solution.py:102
  152.0 6.7 %collective-permute-start.31 = (bf16[4,32,1024]{2,1,0:T(8,128)(2,1)S(1)}, bf16[4,32,1024]{2,1,0:T(8,128)(2,1)S(1)}, u32[]{:S(2)}, u32[]{:S(2)}) collective-permute-start(bf16[4,32,1024]{2,1,0:T(8,128)(2,1)S(1)} %get-tuple-element.26), channel_id=1, source_target_pairs={{0,12},{1,13},{2,14},{3,15},{4,0},{5,1},{6,2},{7,3},{8,4},{9,5},{1... | collective-permute-start | bytes 786440 | tf_op jit(solution)/shard_map/ppermute | solution.py:102
  159.5 31.5 %copy-start.4 = (bf16[32,8,1024]{2,1,0:T(8,128)(2,1)S(1)}, bf16[32,8,1024]{2,1,0:T(8,128)(2,1)}, u32[]{:S(2)}) copy-start(bf16[32,8,1024]{2,1,0:T(8,128)(2,1)} %param.7) | copy-start | bytes 1572868
  160.4 26.6 %all-to-all-start.1 = ((bf16[8,32,1024]{2,1,0:T(8,128)(2,1)}), bf16[8,32,1024]{2,1,0:T(8,128)(2,1)}, u32[]{:S(2)}, u32[]{:S(2)}) async-start(bf16[8,32,1024]{2,1,0:T(8,128)(2,1)} %broadcast_select_fusion.1), calls=%async_computation.1 | async-start | bytes 1048576 | tf_op jit(solution)/shard_map/all_to_all | solution.py:218

commit v4 on v3

--- a/solution.py
+++ b/solution.py
@@ -102,7 +102,7 @@
     return lax.ppermute(value, "member", shift_perm(grid, axis, shift))
 
 
-def ring_gather(block, grid, axis):
+def ring_gather_slots(block, grid, axis):
     n = grid[axis]
     slots = {0: block}
     ahead, behind = block, block
@@ -118,23 +118,26 @@
             first = send(behind[:, :half], grid, axis, 1)
             second = send(ahead[:, half:], grid, axis, -1)
             slots[n // 2] = jnp.concatenate([first, second], axis=1)
-    return jnp.concatenate([slots[r] for r in range(n)], axis=1)
-
-
-def ring_reduce(parts, grid, axis):
+    return [slots[r] for r in range(n)]
+
+
+def ring_gather(block, grid, axis):
+    return jnp.concatenate(ring_gather_slots(block, grid, axis), axis=1)
+
+
+def ring_reduce_slots(parts, grid, axis):
     n = grid[axis]
-    rows, total, width = parts.shape
-    m = total // n
-    slots = [parts[:, r * m:(r + 1) * m].astype(jnp.float32) for r in range(n)]
+    m = parts[0].shape[1]
+    slots = [p.astype(jnp.float32) for p in parts]
     if n == 1:
         return slots[0]
     if n == 2:
-        return slots[0] + send(slots[1].astype(jnp.bfloat16), grid, axis, 1).astype(jnp.float32)
+        return slots[0] + send(parts[1].astype(jnp.bfloat16), grid, axis, 1).astype(jnp.float32)
     top = (n - 1) // 2
     acc_ahead, acc_behind = slots[top], slots[n - top]
     if n % 2 == 0:
         half = m // 2
-        far = slots[n // 2].astype(jnp.bfloat16)
+        far = parts[n // 2].astype(jnp.bfloat16)
         got_first = send(far[:, :half], grid, axis, 1).astype(jnp.float32)
         got_second = send(far[:, half:], grid, axis, -1).astype(jnp.float32)
         acc_ahead = acc_ahead + jnp.concatenate([got_first, jnp.zeros_like(got_first)], axis=1)
@@ -147,6 +150,12 @@
             acc_behind = slots[n - k + 1] + got_behind
         else:
             return slots[0] + got_ahead + got_behind
+
+
+def ring_reduce(parts, grid, axis):
+    n = grid[axis]
+    m = parts.shape[1] // n
+    return ring_reduce_slots([parts[:, r * m:(r + 1) * m] for r in range(n)], grid, axis)
 
 
 def torus_gather(block, grid, order):
@@ -207,11 +216,15 @@
     halves = ((slice(0, split), (0, 1)), (slice(split, per_group), (1, 0)))
     sums = []
     for rows_of, order in halves:
-        q_all = torus_gather(q_rows[rows_of], grid, order)
-        partial = attend_local(
-            q_all, kv_cache[rows_of], row_live[rows_of], member_now * count, scale, HEADS, jnp.bfloat16
-        )
-        sums.append(torus_reduce(partial, grid, order))
+        inner = ring_gather(q_rows[rows_of], grid, order[1])
+        partials = [
+            attend_local(
+                q_slot, kv_cache[rows_of], row_live[rows_of], member_now * count, scale, HEADS, jnp.bfloat16
+            )
+            for q_slot in ring_gather_slots(inner, grid, order[0])
+        ]
+        outer = ring_reduce_slots(partials, grid, order[0]).astype(jnp.bfloat16)
+        sums.append(ring_reduce(outer, grid, order[1]))
     summed = jnp.concatenate(sums, axis=0).astype(jnp.bfloat16)
 
     a_out = jnp.where(filled[:, None, None], summed[chosen], jnp.zeros((), summed.dtype))

time: 193 us -> 245 us (1.27)
  Pallas kernels: 15.7 us -> 66.9 us
  local copies, waits for them, and re-layouts: 35.8 us -> 28.9 us
  other arithmetic: 15.7 us -> 22 us
  waiting for transfers between devices: 55 us -> 58 us
  starting transfers between devices: 64.5 us -> 61.6 us
    pallas_call x2 -> x8, Pallas kernels: 15.7 us -> 66.9 us  [attend_local(): pl.pallas_call(kernel, out_shape=jax.ShapeDtypeStruct((rows, cands, width...]
    unnamed x25 -> x36, local copies, waits for them, and re-layouts: 14.3 us -> 6.15 us
    convert_element_type x4 -> x8, other arithmetic: 3.25 us -> 9.65 us  [the longest x2 4.41 us: on_device(): outer = ring_reduce_slots(partials, grid, order[0]).astype(jnp.bfloat16)]
    all_to_all x1, starting transfers between devices: 17.1 us -> 12.8 us  [on_device(): lax.all_to_all(a_out, 'group', split_axis=0, concat_axis=0, tiled=True)]
    slice x12 -> x13, local copies, waits for them, and re-layouts: 5.5 us -> 9.14 us  [the longest x4 3.81 us: ring_reduce_slots(): got_first = send(far[:, :half], grid, axis, 1).astype(jnp.float32)]
    concatenate x0 -> x2, other arithmetic: none -> 3.3 us  [ring_gather_slots(): slots[n // 2] = jnp.concatenate([first, second], axis=1)]
  transfers between devices with their start and end apart: 34 -> 34, of which waited for: 11 -> 9; matrix products, arithmetic and copies ran while one was open for 18% -> 14% of each run, Pallas kernels for 8% -> 27%
where the time goes in v4:
time: 245 us; the launch traced here: 243 us
  Pallas kernels  66.9 us (27%)
  starting transfers between devices  61.6 us (25%)
  waiting for transfers between devices  58 us (24%)
  local copies, waits for them, and re-layouts  28.9 us (12%)
  other arithmetic  22 us (9%)
  matrix products  5.29 us (2%)
    pallas_call x8, Pallas kernels, attend_local(): pl.pallas_call(kernel, out_shape=jax.ShapeDtypeStruct((rows, cands, width...  66.9 us
    ppermute x32, starting transfers between devices, send(): return lax.ppermute(value, 'member', shift_perm(grid, axis, shift))  42.7 us
    ppermute x32, waiting for transfers between devices, send(): return lax.ppermute(value, 'member', shift_perm(grid, axis, shift))  41.6 us
    all_to_all x1, starting transfers between devices, on_device(): lax.all_to_all(a_out, 'group', split_axis=0, concat_axis=0, tiled=True)  12.8 us
    all_to_all x1, waiting for transfers between devices, on_device(): lax.all_to_all(q_out, 'group', split_axis=0, concat_axis=0, tiled=True)  9.26 us
    all_to_all x1, waiting for transfers between devices, on_device(): lax.all_to_all(a_out, 'group', split_axis=0, concat_axis=0, tiled=True)  7.13 us
    unnamed x36, local copies, waits for them, and re-layouts  6.15 us
    all_to_all x1, starting transfers between devices, on_device(): lax.all_to_all(q_out, 'group', split_axis=0, concat_axis=0, tiled=True)  6.09 us
  transfers between devices with their start and end apart: 34, of which 9 were waited for; matrix products, arithmetic and copies ran while one was open for 14% of the time, Pallas kernels for 27%

profile of v4, /device:TPU:1, one launch (start us, length us, event | category | flops | bytes accessed | tf_op | source)
XLA Modules:
  0.0 243.2 jit_solution(16466649156874599196)
XLA Ops:
  0.0 1.0 fusion.22
  1.1 1.3 gather_fusion
  4.2 1.2 convert_reduce_fusion
  6.0 3.7 %divide_multiply_fusion = f32[256,2048]{1,0:T(8,128)S(1)} fusion(bf16[1024,2048]{1,0:T(8,128)(2,1)} %param.12, bf16[32,8,1024]{2,1,0:T(8,128)(2,1)S(1)} %copy-done.12, f32[32,8]{1,0:T(8,128)S(1)} %copy.37, f32[32,8]{1,0:T(8,128)S(1)} %copy.35), kind=kOutput, calls=%fused_computation.14 | convolution fusion | flops 1076887552 | bytes 6817792 | tf_op jit(solution)/shard_map/dot_general | solution.py:206
  10.0 1.0 copy-done.14
  11.6 0.9 broadcast_select_fusion
  12.5 6.1 %all-to-all-start = ((bf16[8,32,1024]{2,1,0:T(8,128)(2,1)}), bf16[8,32,1024]{2,1,0:T(8,128)(2,1)S(1)}, u32[]{:S(2)}, u32[]{:S(2)}) async-start(bf16[8,32,1024]{2,1,0:T(8,128)(2,1)} %broadcast_select_fusion), calls=%async_computation | async-start | bytes 1048576 | tf_op jit(solution)/shard_map/all_to_all | solution.py:213
  18.7 9.3 %all-to-all-done = bf16[8,32,1024]{2,1,0:T(8,128)(2,1)S(1)} async-done(((bf16[8,32,1024]{2,1,0:T(8,128)(2,1)}), bf16[8,32,1024]{2,1,0:T(8,128)(2,1)S(1)}, u32[]{:S(2)}, u32[]{:S(2)}) %all-to-all-start) | async-done | bytes 524320 | tf_op jit(solution)/shard_map/all_to_all | solution.py:213
  28.5 1.1 fusion.41
  29.6 1.2 collective-permute-start.1
  31.5 1.5 collective-permute-start
  33.0 4.9 %collective-permute-done.1 = bf16[4,32,1024]{2,1,0:T(8,128)(2,1)S(1)} collective-permute-done((bf16[4,32,1024]{2,1,0:T(8,128)(2,1)}, bf16[4,32,1024]{2,1,0:T(8,128)(2,1)S(1)}, u32[]{:S(2)}, u32[]{:S(2)}) %collective-permute-start.1) | collective-permute-done | bytes 262176 | tf_op jit(solution)/shard_map/ppermute | solution.py:102
  38.1 3.8 %collective-permute-start.16 = (bf16[4,32,1024]{2,1,0:T(8,128)(2,1)}, bf16[4,32,1024]{2,1,0:T(8,128)(2,1)}, u32[]{:S(2)}, u32[]{:S(2)}) collective-permute-start(bf16[4,32,1024]{2,1,0:T(8,128)(2,1)} %get-tuple-element.26), channel_id=1, source_target_pairs={{0,12},{1,13},{2,14},{3,15},{4,0},{5,1},{6,2},{7,3},{8,4},{9,5},{1... | collective-permute-start | bytes 786440 | tf_op jit(solution)/shard_map/ppermute | solution.py:102
  41.9 2.7 %collective-permute-start.3 = (bf16[4,16,1024]{2,1,0:T(8,128)(2,1)S(1)}, bf16[4,16,1024]{2,1,0:T(8,128)(2,1)S(1)}, u32[]{:S(2)}, u32[]{:S(2)}) collective-permute-start(bf16[4,16,1024]{2,1,0:T(8,128)(2,1)S(1)} %slice.158), channel_id=1, source_target_pairs={{0,3},{1,0},{2,1},{3,2},{4,7},{5,4},{6,5},{7,6},{8,11},{9,8},{10,9... | collective-permute-start | bytes 393224 | tf_op jit(solution)/shard_map/ppermute | solution.py:102
  48.0 2.7 %collective-permute-start.4 = (bf16[4,128,1024]{2,1,0:T(8,128)(2,1)}, bf16[4,128,1024]{2,1,0:T(8,128)(2,1)}, u32[]{:S(2)}, u32[]{:S(2)}) collective-permute-start(bf16[4,128,1024]{2,1,0:T(8,128)(2,1)} %constant_dynamic-update-slice_fusion.q_ref), channel_id=1, source_target_pairs={{0,12},{1,13},{2,14},{3,15},{4,0},{5,1},{6,2},{7,3},{8,4},{9,5},{1... | collective-permute-start | bytes 3145736 | tf_op jit(solution)/shard_map/ppermute | solution.py:102
  50.8 1.1 slice.170
  51.9 2.6 %collective-permute-start.19 = (bf16[4,16,1024]{2,1,0:T(8,128)(2,1)S(1)}, bf16[4,16,1024]{2,1,0:T(8,128)(2,1)S(1)}, u32[]{:S(2)}, u32[]{:S(2)}) collective-permute-start(bf16[4,16,1024]{2,1,0:T(8,128)(2,1)S(1)} %slice.170), channel_id=1, source_target_pairs={{0,12},{1,13},{2,14},{3,15},{4,0},{5,1},{6,2},{7,3},{8,4},{9,5},{1... | collective-permute-start | bytes 393224 | tf_op jit(solution)/shard_map/ppermute | solution.py:102
  54.5 1.7 constant_dynamic-update-slice_fusion.8
  56.2 17.5 %collective-permute-done.18 = bf16[4,16,1024]{2,1,0:T(8,128)(2,1)S(1)} collective-permute-done((bf16[4,16,1024]{2,1,0:T(8,128)(2,1)S(1)}, bf16[4,16,1024]{2,1,0:T(8,128)(2,1)S(1)}, u32[]{:S(2)}, u32[]{:S(2)}) %collective-permute-start.18) | collective-permute-done | bytes 131104 | tf_op jit(solution)/shard_map/ppermute | solution.py:102
  75.8 0.9 collective-permute-start.21
  76.7 2.7 %collective-permute-start.20 = (bf16[4,128,1024]{2,1,0:T(8,128)(2,1)}, bf16[4,128,1024]{2,1,0:T(8,128)(2,1)S(1)}, u32[]{:S(2)}, u32[]{:S(2)}) collective-permute-start(bf16[4,128,1024]{2,1,0:T(8,128)(2,1)} %constant_dynamic-update-slice_fusion.5.q_ref), channel_id=1, source_target_pairs={{0,3},{1,0},{2,1},{3,2},{4,7},{5,4},{6,5},{7,6},{8,11},{9,8},{10,9... | collective-permute-start | bytes 3145736 | tf_op jit(solution)/shard_map/ppermute | solution.py:102
  80.8 1.3 slice.160
  82.1 2.5 %collective-permute-start.7 = (bf16[4,64,1024]{2,1,0:T(8,128)(2,1)S(1)}, bf16[4,64,1024]{2,1,0:T(8,128)(2,1)S(1)}, u32[]{:S(2)}, u32[]{:S(2)}) collective-permute-start(bf16[4,64,1024]{2,1,0:T(8,128)(2,1)S(1)} %slice.160), channel_id=1, source_target_pairs={{0,12},{1,13},{2,14},{3,15},{4,0},{5,1},{6,2},{7,3},{8,4},{9,5},{1... | collective-permute-start | bytes 1572872 | tf_op jit(solution)/shard_map/ppermute | solution.py:102
  84.6 2.5 %fusion.36 = (bf16[4,128,2048]{2,1,0:T(8,128)(2,1)}, bf16[4,128,2048]{2,1,0:T(8,128)(2,1)}) fusion(bf16[8,128,2048]{2,1,0:T(8,128)(2,1)S(1)} %copy-done.2), kind=kLoop, calls=%fused_computation.129 | loop fusion | bytes 8388608 | tf_op jit(solution)/shard_map/slice | solution.py:222
  87.1 12.0 %collective-permute-done.21.q_ref = bf16[4,128,1024]{2,1,0:T(8,128)(2,1)S(1)} collective-permute-done((bf16[4,128,1024]{2,1,0:T(8,128)(2,1)}, bf16[4,128,1024]{2,1,0:T(8,128)(2,1)S(1)}, u32[]{:S(2)}, u32[]{:S(2)}) %collective-permute-start.21) | collective-permute-done | bytes 1048608 | tf_op jit(solution)/shard_map/ppermute | solution.py:102
  99.1 0.9 slice.171
  100.0 0.9 slice.172
  100.9 2.7 %collective-permute-start.23 = (bf16[4,64,1024]{2,1,0:T(8,128)(2,1)}, bf16[4,64,1024]{2,1,0:T(8,128)(2,1)}, u32[]{:S(2)}, u32[]{:S(2)}) collective-permute-start(bf16[4,64,1024]{2,1,0:T(8,128)(2,1)} %slice.172), channel_id=1, source_target_pairs={{0,3},{1,0},{2,1},{3,2},{4,7},{5,4},{6,5},{7,6},{8,11},{9,8},{10,9... | collective-permute-start | bytes 1572872 | tf_op jit(solution)/shard_map/ppermute | solution.py:102
  103.6 1.1 pad_maximum_fusion.q_ref
  104.7 8.4 %shard_map.75 = bf16[4,128,1024]{2,1,0:T(8,128)(2,1)} custom-call(s32[4]{0:T(128)} %get-tuple-element.31.n_live_ref, bf16[4,128,1024]{2,1,0:T(8,128)(2,1)} %pad_maximum_fusion.q_ref, bf16[4,128,2048]{2,1,0:T(8,128)(2,1)} %get-tuple-element.9.kv_ref, f32[4,1,128]{2,1,0:T(1,128)} %get-tuple-element.27.keep_ref), custom_call_target="tpu_custom_call" | custom-call | flops 268435456 | bytes 4194304 | tf_op jit(solution)/shard_map/pallas_call | solution.py:67
  113.0 2.3 fusion.38
  115.3 8.3 %shard_map.74 = bf16[4,128,1024]{2,1,0:T(8,128)(2,1)} custom-call(s32[4]{0:T(128)} %get-tuple-element.31.n_live_ref, bf16[4,128,1024]{2,1,0:T(8,128)(2,1)} %collective-permute-done.4.q_ref, bf16[4,128,2048]{2,1,0:T(8,128)(2,1)} %get-tuple-element.9.kv_ref, f32[4,1,128]{2,1,0:T(1,128)} %get-tuple-element.27.keep_ref), custom_call_target="tpu_custom_call" | custom-call | flops 268435456 | bytes 4194304 | tf_op jit(solution)/shard_map/pallas_call | solution.py:67
  123.7 8.4 %shard_map.76 = bf16[4,128,1024]{2,1,0:T(8,128)(2,1)} custom-call(s32[4]{0:T(128)} %get-tuple-element.31.n_live_ref, bf16[4,128,1024]{2,1,0:T(8,128)(2,1)} %copy-done.9, bf16[4,128,2048]{2,1,0:T(8,128)(2,1)} %get-tuple-element.9.kv_ref, f32[4,1,128]{2,1,0:T(1,128)} %get-tuple-element.27.keep_ref), custom_call_target="tpu_custom_call" | custom-call | flops 268435456 | bytes 4194304 | tf_op jit(solution)/shard_map/pallas_call | solution.py:67
  132.1 8.3 %shard_map.78 = bf16[4,128,1024]{2,1,0:T(8,128)(2,1)} custom-call(s32[4]{0:T(128)} %get-tuple-element.32.n_live_ref, bf16[4,128,1024]{2,1,0:T(8,128)(2,1)} %copy-done.11, bf16[4,128,2048]{2,1,0:T(8,128)(2,1)} %get-tuple-element.10.kv_ref, f32[4,1,128]{2,1,0:T(1,128)} %get-tuple-element.28.keep_ref), custom_call_target="tpu_custom_call" | custom-call | flops 268435456 | bytes 4194304 | tf_op jit(solution)/shard_map/pallas_call | solution.py:67
  140.4 8.3 %shard_map.80 = bf16[4,128,1024]{2,1,0:T(8,128)(2,1)} custom-call(s32[4]{0:T(128)} %get-tuple-element.32.n_live_ref, bf16[4,128,1024]{2,1,0:T(8,128)(2,1)} %copy-done.10, bf16[4,128,2048]{2,1,0:T(8,128)(2,1)} %get-tuple-element.10.kv_ref, f32[4,1,128]{2,1,0:T(1,128)} %get-tuple-element.28.keep_ref), custom_call_target="tpu_custom_call" | custom-call | flops 268435456 | bytes 4194304 | tf_op jit(solution)/shard_map/pallas_call | solution.py:67
  148.7 2.2 pad_maximum_fusion.1.q_ref
  151.0 8.3 %shard_map.79 = bf16[4,128,1024]{2,1,0:T(8,128)(2,1)} custom-call(s32[4]{0:T(128)} %get-tuple-element.32.n_live_ref, bf16[4,128,1024]{2,1,0:T(8,128)(2,1)} %pad_maximum_fusion.1.q_ref, bf16[4,128,2048]{2,1,0:T(8,128)(2,1)} %get-tuple-element.10.kv_ref, f32[4,1,128]{2,1,0:T(1,128)} %get-tuple-element.28.keep_ref), custom_call_target="tpu_custom_call" | custom-call | flops 268435456 | bytes 4194304 | tf_op jit(solution)/shard_map/pallas_call | solution.py:67
  159.3 1.5 fusion.40
  160.9 2.7 %collective-permute-start.26 = (bf16[4,64,1024]{2,1,0:T(8,128)(2,1)S(1)}, bf16[4,64,1024]{2,1,0:T(8,128)(2,1)S(1)}, u32[]{:S(2)}, u32[]{:S(2)}) collective-permute-start(bf16[4,64,1024]{2,1,0:T(8,128)(2,1)S(1)} %get-tuple-element.22), channel_id=1, source_target_pairs={{0,3},{1,0},{2,1},{3,2},{4,7},{5,4},{6,5},{7,6},{8,11},{9,8},{10,9... | collective-permute-start | bytes 1572872 | tf_op jit(solution)/shard_map/ppermute | solution.py:102
  163.5 1.3 add_convert_fusion.5
  164.9 1.2 add_convert_fusion.4
  166.1 2.6 %collective-permute-start.11 = (bf16[4,128,1024]{2,1,0:T(8,128)(2,1)}, bf16[4,128,1024]{2,1,0:T(8,128)(2,1)}, u32[]{:S(2)}, u32[]{:S(2)}) collective-permute-start(bf16[4,128,1024]{2,1,0:T(8,128)(2,1)} %add_convert_fusion.4), channel_id=1, source_target_pairs={{0,12},{1,13},{2,14},{3,15},{4,0},{5,1},{6,2},{7,3},{8,4},{9,5},{1... | collective-permute-start | bytes 3145736 | tf_op jit(solution)/shard_map/ppermute | solution.py:102
  168.7 1.7 collective-permute-done.24
  170.4 1.3 add_convert_fusion.2
  172.3 1.3 add_convert_fusion.1
  173.6 2.0 collective-permute-start.27
  175.9 8.3 %shard_map.73 = bf16[4,128,1024]{2,1,0:T(8,128)(2,1)} custom-call(s32[4]{0:T(128)} %get-tuple-element.31.n_live_ref, bf16[4,128,1024]{2,1,0:T(8,128)(2,1)} %constant_dynamic-update-slice_fusion.q_ref, bf16[4,128,2048]{2,1,0:T(8,128)(2,1)} %get-tuple-element.9.kv_ref, f32[4,1,128]{2,1,0:T(1,128)} %get-tuple-element.27.keep_ref), custom_call_target="tpu_custom_call" | custom-call | flops 268435456 | bytes 4194304 | tf_op jit(solution)/shard_map/pallas_call | solution.py:67
  184.2 8.5 %shard_map.77 = bf16[4,128,1024]{2,1,0:T(8,128)(2,1)} custom-call(s32[4]{0:T(128)} %get-tuple-element.32.n_live_ref, bf16[4,128,1024]{2,1,0:T(8,128)(2,1)} %constant_dynamic-update-slice_fusion.5.q_ref, bf16[4,128,2048]{2,1,0:T(8,128)(2,1)} %get-tuple-element.10.kv_ref, f32[4,1,128]{2,1,0:T(1,128)} %get-tuple-element.28.keep_ref), custom_call_target="tpu_custom_call" | custom-call | flops 268435456 | bytes 4194304 | tf_op jit(solution)/shard_map/pallas_call | solution.py:67
  192.7 2.2 add_convert_fusion.3
  195.3 2.4 collective-permute-start.14
  197.7 2.2 add_convert_fusion
  200.0 2.7 %collective-permute-start.30 = (bf16[4,16,1024]{2,1,0:T(8,128)(2,1)S(1)}, bf16[4,16,1024]{2,1,0:T(8,128)(2,1)S(1)}, u32[]{:S(2)}, u32[]{:S(2)}) collective-permute-start(bf16[4,16,1024]{2,1,0:T(8,128)(2,1)S(1)} %get-tuple-element.20), channel_id=1, source_target_pairs={{0,12},{1,13},{2,14},{3,15},{4,0},{5,1},{6,2},{7,3},{8,4},{9,5},{1... | collective-permute-start | bytes 393224 | tf_op jit(solution)/shard_map/ppermute | solution.py:102
  202.8 1.4 collective-permute-start.13
  204.2 1.4 collective-permute-start.15
  205.9 2.7 %collective-permute-start.31 = (bf16[4,32,1024]{2,1,0:T(8,128)(2,1)S(1)}, bf16[4,32,1024]{2,1,0:T(8,128)(2,1)S(1)}, u32[]{:S(2)}, u32[]{:S(2)}) collective-permute-start(bf16[4,32,1024]{2,1,0:T(8,128)(2,1)S(1)} %get-tuple-element.18), channel_id=1, source_target_pairs={{0,12},{1,13},{2,14},{3,15},{4,0},{5,1},{6,2},{7,3},{8,4},{9,5},{1... | collective-permute-start | bytes 786440 | tf_op jit(solution)/shard_map/ppermute | solution.py:102
  208.6 1.5 collective-permute-done.13
  210.2 3.4 %collective-permute-done.29 = bf16[4,32,1024]{2,1,0:T(8,128)(2,1)S(1)} collective-permute-done((bf16[4,32,1024]{2,1,0:T(8,128)(2,1)S(1)}, bf16[4,32,1024]{2,1,0:T(8,128)(2,1)S(1)}, u32[]{:S(2)}, u32[]{:S(2)}) %collective-permute-start.29) | collective-permute-done | bytes 262176 | tf_op jit(solution)/shard_map/ppermute | solution.py:102
  214.4 0.9 broadcast_select_fusion.1
  215.3 12.8 %all-to-all-start.1 = ((bf16[8,32,1024]{2,1,0:T(8,128)(2,1)}), bf16[8,32,1024]{2,1,0:T(8,128)(2,1)}, u32[]{:S(2)}, u32[]{:S(2)}) async-start(bf16[8,32,1024]{2,1,0:T(8,128)(2,1)} %broadcast_select_fusion.1), calls=%async_computation.1 | async-start | bytes 1048576 | tf_op jit(solution)/shard_map/all_to_all | solution.py:231
  228.1 2.3 slice_bitcast_fusion
  230.5 7.1 %all-to-all-done.1 = bf16[8,32,1024]{2,1,0:T(8,128)(2,1)} async-done(((bf16[8,32,1024]{2,1,0:T(8,128)(2,1)}), bf16[8,32,1024]{2,1,0:T(8,128)(2,1)}, u32[]{:S(2)}, u32[]{:S(2)}) %all-to-all-start.1) | async-done | bytes 524320 | tf_op jit(solution)/shard_map/all_to_all | solution.py:231
  237.6 1.6 gather_fusion.7
  239.7 1.9 fusion.10
  241.5 1.6 fusion.3
  (133 shorter events, 15.2 us)
Async XLA Ops:
  0.0 241.5 %copy-start = (bf16[1024,1024]{1,0:T(8,128)(2,1)S(1)}, bf16[1024,1024]{1,0:T(8,128)(2,1)}, u32[]{:S(2)}) copy-start(bf16[1024,1024]{1,0:T(8,128)(2,1)} %param.13) | copy-start | bytes 6291460
  0.0 5.5 %copy-start.12 = (bf16[32,8,1024]{2,1,0:T(8,128)(2,1)S(1)}, bf16[32,8,1024]{2,1,0:T(8,128)(2,1)}, u32[]{:S(2)}) copy-start(bf16[32,8,1024]{2,1,0:T(8,128)(2,1)} %param.7) | copy-start | bytes 1572868
  9.6 1.4 copy-start.14
  12.5 18.3 %copy-start.1 = (s32[64]{0:T(128)S(1)}, s32[64]{0:T(128)}, u32[]{:S(2)}) copy-start(s32[64]{0:T(128)} %param.11) | copy-start | bytes 772
  12.5 15.4 %all-to-all-start = ((bf16[8,32,1024]{2,1,0:T(8,128)(2,1)}), bf16[8,32,1024]{2,1,0:T(8,128)(2,1)S(1)}, u32[]{:S(2)}, u32[]{:S(2)}) async-start(bf16[8,32,1024]{2,1,0:T(8,128)(2,1)} %broadcast_select_fusion), calls=%async_computation | async-start | bytes 1048576 | tf_op jit(solution)/shard_map/all_to_all | solution.py:213
  29.6 8.3 %collective-permute-start.1 = (bf16[4,32,1024]{2,1,0:T(8,128)(2,1)}, bf16[4,32,1024]{2,1,0:T(8,128)(2,1)S(1)}, u32[]{:S(2)}, u32[]{:S(2)}) collective-permute-start(bf16[4,32,1024]{2,1,0:T(8,128)(2,1)} %get-tuple-element.23), channel_id=1, source_target_pairs={{0,1},{1,2},{2,3},{3,0},{4,5},{5,6},{6,7},{7,4},{8,9},{9,10},{10,1... | collective-permute-start | bytes 786440 | tf_op jit(solution)/shard_map/ppermute | solution.py:102
  31.5 10.4 %collective-permute-start = (bf16[4,32,1024]{2,1,0:T(8,128)(2,1)}, bf16[4,32,1024]{2,1,0:T(8,128)(2,1)S(1)}, u32[]{:S(2)}, u32[]{:S(2)}) collective-permute-start(bf16[4,32,1024]{2,1,0:T(8,128)(2,1)} %get-tuple-element.23), channel_id=1, source_target_pairs={{0,3},{1,0},{2,1},{3,2},{4,7},{5,4},{6,5},{7,6},{8,11},{9,8},{10,9... | collective-permute-start | bytes 786440 | tf_op jit(solution)/shard_map/ppermute | solution.py:102
  37.9 7.4 %collective-permute-start.2 = (bf16[4,16,1024]{2,1,0:T(8,128)(2,1)S(1)}, bf16[4,16,1024]{2,1,0:T(8,128)(2,1)S(1)}, u32[]{:S(2)}, u32[]{:S(2)}) collective-permute-start(bf16[4,16,1024]{2,1,0:T(8,128)(2,1)S(1)} %slice.157), channel_id=1, source_target_pairs={{0,1},{1,2},{2,3},{3,0},{4,5},{5,6},{6,7},{7,4},{8,9},{9,10},{10,1... | collective-permute-start | bytes 393224 | tf_op jit(solution)/shard_map/ppermute | solution.py:102
  38.1 12.7 %collective-permute-start.16 = (bf16[4,32,1024]{2,1,0:T(8,128)(2,1)}, bf16[4,32,1024]{2,1,0:T(8,128)(2,1)}, u32[]{:S(2)}, u32[]{:S(2)}) collective-permute-start(bf16[4,32,1024]{2,1,0:T(8,128)(2,1)} %get-tuple-element.26), channel_id=1, source_target_pairs={{0,12},{1,13},{2,14},{3,15},{4,0},{5,1},{6,2},{7,3},{8,4},{9,5},{1... | collective-permute-start | bytes 786440 | tf_op jit(solution)/shard_map/ppermute | solution.py:102
  41.9 8.9 %collective-permute-start.17 = (bf16[4,32,1024]{2,1,0:T(8,128)(2,1)}, bf16[4,32,1024]{2,1,0:T(8,128)(2,1)S(1)}, u32[]{:S(2)}, u32[]{:S(2)}) collective-permute-start(bf16[4,32,1024]{2,1,0:T(8,128)(2,1)} %get-tuple-element.26), channel_id=1, source_target_pairs={{0,4},{1,5},{2,6},{3,7},{4,8},{5,9},{6,10},{7,11},{8,12},{9,13},{1... | collective-permute-start | bytes 786440 | tf_op jit(solution)/shard_map/ppermute | solution.py:102
  41.9 4.7 %collective-permute-start.3 = (bf16[4,16,1024]{2,1,0:T(8,128)(2,1)S(1)}, bf16[4,16,1024]{2,1,0:T(8,128)(2,1)S(1)}, u32[]{:S(2)}, u32[]{:S(2)}) collective-permute-start(bf16[4,16,1024]{2,1,0:T(8,128)(2,1)S(1)} %slice.158), channel_id=1, source_target_pairs={{0,3},{1,0},{2,1},{3,2},{4,7},{5,4},{6,5},{7,6},{8,11},{9,8},{10,9... | collective-permute-start | bytes 393224 | tf_op jit(solution)/shard_map/ppermute | solution.py:102
  48.0 32.7 %collective-permute-start.5 = (bf16[4,128,1024]{2,1,0:T(8,128)(2,1)}, bf16[4,128,1024]{2,1,0:T(8,128)(2,1)S(1)}, u32[]{:S(2)}, u32[]{:S(2)}) collective-permute-start(bf16[4,128,1024]{2,1,0:T(8,128)(2,1)} %constant_dynamic-update-slice_fusion.q_ref), channel_id=1, source_target_pairs={{0,4},{1,5},{2,6},{3,7},{4,8},{5,9},{6,10},{7,11},{8,12},{9,13},{1... | collective-permute-start | bytes 3145736 | tf_op jit(solution)/shard_map/ppermute | solution.py:102
  48.0 32.8 %collective-permute-start.4 = (bf16[4,128,1024]{2,1,0:T(8,128)(2,1)}, bf16[4,128,1024]{2,1,0:T(8,128)(2,1)}, u32[]{:S(2)}, u32[]{:S(2)}) collective-permute-start(bf16[4,128,1024]{2,1,0:T(8,128)(2,1)} %constant_dynamic-update-slice_fusion.q_ref), channel_id=1, source_target_pairs={{0,12},{1,13},{2,14},{3,15},{4,0},{5,1},{6,2},{7,3},{8,4},{9,5},{1... | collective-permute-start | bytes 3145736 | tf_op jit(solution)/shard_map/ppermute | solution.py:102
  50.7 33.9 %copy-start.2 = (bf16[8,128,2048]{2,1,0:T(8,128)(2,1)S(1)}, bf16[8,128,2048]{2,1,0:T(8,128)(2,1)}, u32[]{:S(2)}) copy-start(bf16[8,128,2048]{2,1,0:T(8,128)(2,1)} %param.8) | copy-start | bytes 12582916
  50.7 22.9 %collective-permute-start.18 = (bf16[4,16,1024]{2,1,0:T(8,128)(2,1)S(1)}, bf16[4,16,1024]{2,1,0:T(8,128)(2,1)S(1)}, u32[]{:S(2)}, u32[]{:S(2)}) collective-permute-start(bf16[4,16,1024]{2,1,0:T(8,128)(2,1)S(1)} %slice.169), channel_id=1, source_target_pairs={{0,4},{1,5},{2,6},{3,7},{4,8},{5,9},{6,10},{7,11},{8,12},{9,13},{1... | collective-permute-start | bytes 393224 | tf_op jit(solution)/shard_map/ppermute | solution.py:102
  51.9 22.4 %collective-permute-start.19 = (bf16[4,16,1024]{2,1,0:T(8,128)(2,1)S(1)}, bf16[4,16,1024]{2,1,0:T(8,128)(2,1)S(1)}, u32[]{:S(2)}, u32[]{:S(2)}) collective-permute-start(bf16[4,16,1024]{2,1,0:T(8,128)(2,1)S(1)} %slice.170), channel_id=1, source_target_pairs={{0,12},{1,13},{2,14},{3,15},{4,0},{5,1},{6,2},{7,3},{8,4},{9,5},{1... | collective-permute-start | bytes 393224 | tf_op jit(solution)/shard_map/ppermute | solution.py:102
  75.8 23.3 %collective-permute-start.21 = (bf16[4,128,1024]{2,1,0:T(8,128)(2,1)}, bf16[4,128,1024]{2,1,0:T(8,128)(2,1)S(1)}, u32[]{:S(2)}, u32[]{:S(2)}) collective-permute-start(bf16[4,128,1024]{2,1,0:T(8,128)(2,1)} %constant_dynamic-update-slice_fusion.5.q_ref), channel_id=1, source_target_pairs={{0,1},{1,2},{2,3},{3,0},{4,5},{5,6},{6,7},{7,4},{8,9},{9,10},{10,1... | collective-permute-start | bytes 3145736 | tf_op jit(solution)/shard_map/ppermute | solution.py:102
  76.7 23.3 %collective-permute-start.20 = (bf16[4,128,1024]{2,1,0:T(8,128)(2,1)}, bf16[4,128,1024]{2,1,0:T(8,128)(2,1)S(1)}, u32[]{:S(2)}, u32[]{:S(2)}) collective-permute-start(bf16[4,128,1024]{2,1,0:T(8,128)(2,1)} %constant_dynamic-update-slice_fusion.5.q_ref), channel_id=1, source_target_pairs={{0,3},{1,0},{2,1},{3,2},{4,7},{5,4},{6,5},{7,6},{8,11},{9,8},{10,9... | collective-permute-start | bytes 3145736 | tf_op jit(solution)/shard_map/ppermute | solution.py:102
  80.6 6.4 %copy-start.9 = (bf16[4,128,1024]{2,1,0:T(8,128)(2,1)}, bf16[4,128,1024]{2,1,0:T(8,128)(2,1)S(1)}, u32[]{:S(2)}) copy-start(bf16[4,128,1024]{2,1,0:T(8,128)(2,1)S(1)} %collective-permute-done.5.q_ref) | copy-start | bytes 3145732
  80.7 22.9 %collective-permute-start.6 = (bf16[4,64,1024]{2,1,0:T(8,128)(2,1)S(1)}, bf16[4,64,1024]{2,1,0:T(8,128)(2,1)S(1)}, u32[]{:S(2)}, u32[]{:S(2)}) collective-permute-start(bf16[4,64,1024]{2,1,0:T(8,128)(2,1)S(1)} %slice.159), channel_id=1, source_target_pairs={{0,4},{1,5},{2,6},{3,7},{4,8},{5,9},{6,10},{7,11},{8,12},{9,13},{1... | collective-permute-start | bytes 1572872 | tf_op jit(solution)/shard_map/ppermute | solution.py:102
  82.1 21.5 %collective-permute-start.7 = (bf16[4,64,1024]{2,1,0:T(8,128)(2,1)S(1)}, bf16[4,64,1024]{2,1,0:T(8,128)(2,1)S(1)}, u32[]{:S(2)}, u32[]{:S(2)}) collective-permute-start(bf16[4,64,1024]{2,1,0:T(8,128)(2,1)S(1)} %slice.160), channel_id=1, source_target_pairs={{0,12},{1,13},{2,14},{3,15},{4,0},{5,1},{6,2},{7,3},{8,4},{9,5},{1... | collective-permute-start | bytes 1572872 | tf_op jit(solution)/shard_map/ppermute | solution.py:102
  99.1 5.6 %copy-start.10 = (bf16[4,128,1024]{2,1,0:T(8,128)(2,1)}, bf16[4,128,1024]{2,1,0:T(8,128)(2,1)S(1)}, u32[]{:S(2)}) copy-start(bf16[4,128,1024]{2,1,0:T(8,128)(2,1)S(1)} %collective-permute-done.21.q_ref) | copy-start | bytes 3145732
  100.0 48.7 %collective-permute-start.22 = (bf16[4,64,1024]{2,1,0:T(8,128)(2,1)}, bf16[4,64,1024]{2,1,0:T(8,128)(2,1)}, u32[]{:S(2)}, u32[]{:S(2)}) collective-permute-start(bf16[4,64,1024]{2,1,0:T(8,128)(2,1)} %slice.171), channel_id=1, source_target_pairs={{0,1},{1,2},{2,3},{3,0},{4,5},{5,6},{6,7},{7,4},{8,9},{9,10},{10,1... | collective-permute-start | bytes 1572872 | tf_op jit(solution)/shard_map/ppermute | solution.py:102
  100.0 4.7 %copy-start.11 = (bf16[4,128,1024]{2,1,0:T(8,128)(2,1)}, bf16[4,128,1024]{2,1,0:T(8,128)(2,1)S(1)}, u32[]{:S(2)}) copy-start(bf16[4,128,1024]{2,1,0:T(8,128)(2,1)S(1)} %collective-permute-done.20.q_ref) | copy-start | bytes 3145732
  100.9 47.8 %collective-permute-start.23 = (bf16[4,64,1024]{2,1,0:T(8,128)(2,1)}, bf16[4,64,1024]{2,1,0:T(8,128)(2,1)}, u32[]{:S(2)}, u32[]{:S(2)}) collective-permute-start(bf16[4,64,1024]{2,1,0:T(8,128)(2,1)} %slice.172), channel_id=1, source_target_pairs={{0,3},{1,0},{2,1},{3,2},{4,7},{5,4},{6,5},{7,6},{8,11},{9,8},{10,9... | collective-permute-start | bytes 1572872 | tf_op jit(solution)/shard_map/ppermute | solution.py:102
  115.3 48.2 %collective-permute-start.8 = (bf16[4,64,1024]{2,1,0:T(8,128)(2,1)}, bf16[4,64,1024]{2,1,0:T(8,128)(2,1)S(1)}, u32[]{:S(2)}, u32[]{:S(2)}) collective-permute-start(bf16[4,64,1024]{2,1,0:T(8,128)(2,1)} %get-tuple-element.15), channel_id=1, source_target_pairs={{0,4},{1,5},{2,6},{3,7},{4,8},{5,9},{6,10},{7,11},{8,12},{9,13},{1... | collective-permute-start | bytes 1572872 | tf_op jit(solution)/shard_map/ppermute | solution.py:102
  148.7 16.2 %collective-permute-start.10 = (bf16[4,64,1024]{2,1,0:T(8,128)(2,1)}, bf16[4,64,1024]{2,1,0:T(8,128)(2,1)S(1)}, u32[]{:S(2)}, u32[]{:S(2)}) collective-permute-start(bf16[4,64,1024]{2,1,0:T(8,128)(2,1)} %get-tuple-element.16), channel_id=1, source_target_pairs={{0,12},{1,13},{2,14},{3,15},{4,0},{5,1},{6,2},{7,3},{8,4},{9,5},{1... | collective-permute-start | bytes 1572872 | tf_op jit(solution)/shard_map/ppermute | solution.py:102
  159.3 4.2 %copy-start.6 = (bf16[4,128,1024]{2,1,0:T(8,128)(2,1)S(1)}, bf16[4,128,1024]{2,1,0:T(8,128)(2,1)}, u32[]{:S(2)}) copy-start(bf16[4,128,1024]{2,1,0:T(8,128)(2,1)} %shard_map.74) | copy-start | bytes 3145732
  159.3 5.6 %copy-start.5 = (bf16[4,128,1024]{2,1,0:T(8,128)(2,1)S(1)}, bf16[4,128,1024]{2,1,0:T(8,128)(2,1)}, u32[]{:S(2)}) copy-start(bf16[4,128,1024]{2,1,0:T(8,128)(2,1)} %shard_map.76) | copy-start | bytes 3145732
  160.8 9.6 %collective-permute-start.24 = (bf16[4,64,1024]{2,1,0:T(8,128)(2,1)S(1)}, bf16[4,64,1024]{2,1,0:T(8,128)(2,1)S(1)}, u32[]{:S(2)}, u32[]{:S(2)}) collective-permute-start(bf16[4,64,1024]{2,1,0:T(8,128)(2,1)S(1)} %get-tuple-element.21), channel_id=1, source_target_pairs={{0,1},{1,2},{2,3},{3,0},{4,5},{5,6},{6,7},{7,4},{8,9},{9,10},{10,1... | collective-permute-start | bytes 1572872 | tf_op jit(solution)/shard_map/ppermute | solution.py:102
  160.9 9.6 %copy-start.4 = (bf16[4,128,1024]{2,1,0:T(8,128)(2,1)S(1)}, bf16[4,128,1024]{2,1,0:T(8,128)(2,1)}, u32[]{:S(2)}) copy-start(bf16[4,128,1024]{2,1,0:T(8,128)(2,1)} %shard_map.78) | copy-start | bytes 3145732
  160.9 11.5 %collective-permute-start.26 = (bf16[4,64,1024]{2,1,0:T(8,128)(2,1)S(1)}, bf16[4,64,1024]{2,1,0:T(8,128)(2,1)S(1)}, u32[]{:S(2)}, u32[]{:S(2)}) collective-permute-start(bf16[4,64,1024]{2,1,0:T(8,128)(2,1)S(1)} %get-tuple-element.22), channel_id=1, source_target_pairs={{0,3},{1,0},{2,1},{3,2},{4,7},{5,4},{6,5},{7,6},{8,11},{9,8},{10,9... | collective-permute-start | bytes 1572872 | tf_op jit(solution)/shard_map/ppermute | solution.py:102
  164.8 7.5 %copy-start.3 = (bf16[4,128,1024]{2,1,0:T(8,128)(2,1)S(1)}, bf16[4,128,1024]{2,1,0:T(8,128)(2,1)}, u32[]{:S(2)}) copy-start(bf16[4,128,1024]{2,1,0:T(8,128)(2,1)} %shard_map.80) | copy-start | bytes 3145732
  164.8 27.9 %collective-permute-start.9 = (bf16[4,128,1024]{2,1,0:T(8,128)(2,1)}, bf16[4,128,1024]{2,1,0:T(8,128)(2,1)}, u32[]{:S(2)}, u32[]{:S(2)}) collective-permute-start(bf16[4,128,1024]{2,1,0:T(8,128)(2,1)} %add_convert_fusion.5), channel_id=1, source_target_pairs={{0,4},{1,5},{2,6},{3,7},{4,8},{5,9},{6,10},{7,11},{8,12},{9,13},{1... | collective-permute-start | bytes 3145736 | tf_op jit(solution)/shard_map/ppermute | solution.py:102
  166.1 26.5 %collective-permute-start.11 = (bf16[4,128,1024]{2,1,0:T(8,128)(2,1)}, bf16[4,128,1024]{2,1,0:T(8,128)(2,1)}, u32[]{:S(2)}, u32[]{:S(2)}) collective-permute-start(bf16[4,128,1024]{2,1,0:T(8,128)(2,1)} %add_convert_fusion.4), channel_id=1, source_target_pairs={{0,12},{1,13},{2,14},{3,15},{4,0},{5,1},{6,2},{7,3},{8,4},{9,5},{1... | collective-permute-start | bytes 3145736 | tf_op jit(solution)/shard_map/ppermute | solution.py:102
  171.7 26.0 %collective-permute-start.25 = (bf16[4,128,1024]{2,1,0:T(8,128)(2,1)}, bf16[4,128,1024]{2,1,0:T(8,128)(2,1)}, u32[]{:S(2)}, u32[]{:S(2)}) collective-permute-start(bf16[4,128,1024]{2,1,0:T(8,128)(2,1)} %add_convert_fusion.2), channel_id=1, source_target_pairs={{0,1},{1,2},{2,3},{3,0},{4,5},{5,6},{6,7},{7,4},{8,9},{9,10},{10,1... | collective-permute-start | bytes 3145736 | tf_op jit(solution)/shard_map/ppermute | solution.py:102
  173.6 24.1 %collective-permute-start.27 = (bf16[4,128,1024]{2,1,0:T(8,128)(2,1)}, bf16[4,128,1024]{2,1,0:T(8,128)(2,1)}, u32[]{:S(2)}, u32[]{:S(2)}) collective-permute-start(bf16[4,128,1024]{2,1,0:T(8,128)(2,1)} %add_convert_fusion.1), channel_id=1, source_target_pairs={{0,3},{1,0},{2,1},{3,2},{4,7},{5,4},{6,5},{7,6},{8,11},{9,8},{10,9... | collective-permute-start | bytes 3145736 | tf_op jit(solution)/shard_map/ppermute | solution.py:102
  184.2 8.5 %copy-start.8 = (bf16[4,128,1024]{2,1,0:T(8,128)(2,1)S(1)}, bf16[4,128,1024]{2,1,0:T(8,128)(2,1)}, u32[]{:S(2)}) copy-start(bf16[4,128,1024]{2,1,0:T(8,128)(2,1)} %shard_map.73) | copy-start | bytes 3145732
  192.7 5.1 %copy-start.7 = (bf16[4,128,1024]{2,1,0:T(8,128)(2,1)S(1)}, bf16[4,128,1024]{2,1,0:T(8,128)(2,1)}, u32[]{:S(2)}) copy-start(bf16[4,128,1024]{2,1,0:T(8,128)(2,1)} %shard_map.77) | copy-start | bytes 3145732
  195.0 7.7 %collective-permute-start.12 = (bf16[4,16,1024]{2,1,0:T(8,128)(2,1)S(1)}, bf16[4,16,1024]{2,1,0:T(8,128)(2,1)S(1)}, u32[]{:S(2)}, u32[]{:S(2)}) collective-permute-start(bf16[4,16,1024]{2,1,0:T(8,128)(2,1)S(1)} %get-tuple-element.13), channel_id=1, source_target_pairs={{0,1},{1,2},{2,3},{3,0},{4,5},{5,6},{6,7},{7,4},{8,9},{9,10},{10,1... | collective-permute-start | bytes 393224 | tf_op jit(solution)/shard_map/ppermute | solution.py:102
  195.3 7.4 %collective-permute-start.14 = (bf16[4,16,1024]{2,1,0:T(8,128)(2,1)S(1)}, bf16[4,16,1024]{2,1,0:T(8,128)(2,1)S(1)}, u32[]{:S(2)}, u32[]{:S(2)}) collective-permute-start(bf16[4,16,1024]{2,1,0:T(8,128)(2,1)S(1)} %get-tuple-element.14), channel_id=1, source_target_pairs={{0,3},{1,0},{2,1},{3,2},{4,7},{5,4},{6,5},{7,6},{8,11},{9,8},{10,9... | collective-permute-start | bytes 393224 | tf_op jit(solution)/shard_map/ppermute | solution.py:102
  199.9 5.6 %collective-permute-start.28 = (bf16[4,16,1024]{2,1,0:T(8,128)(2,1)S(1)}, bf16[4,16,1024]{2,1,0:T(8,128)(2,1)S(1)}, u32[]{:S(2)}, u32[]{:S(2)}) collective-permute-start(bf16[4,16,1024]{2,1,0:T(8,128)(2,1)S(1)} %get-tuple-element.19), channel_id=1, source_target_pairs={{0,4},{1,5},{2,6},{3,7},{4,8},{5,9},{6,10},{7,11},{8,12},{9,13},{1... | collective-permute-start | bytes 393224 | tf_op jit(solution)/shard_map/ppermute | solution.py:102
  200.0 5.5 %collective-permute-start.30 = (bf16[4,16,1024]{2,1,0:T(8,128)(2,1)S(1)}, bf16[4,16,1024]{2,1,0:T(8,128)(2,1)S(1)}, u32[]{:S(2)}, u32[]{:S(2)}) collective-permute-start(bf16[4,16,1024]{2,1,0:T(8,128)(2,1)S(1)} %get-tuple-element.20), channel_id=1, source_target_pairs={{0,12},{1,13},{2,14},{3,15},{4,0},{5,1},{6,2},{7,3},{8,4},{9,5},{1... | collective-permute-start | bytes 393224 | tf_op jit(solution)/shard_map/ppermute | solution.py:102
  202.8 7.3 %collective-permute-start.13 = (bf16[4,32,1024]{2,1,0:T(8,128)(2,1)S(1)}, bf16[4,32,1024]{2,1,0:T(8,128)(2,1)S(1)}, u32[]{:S(2)}, u32[]{:S(2)}) collective-permute-start(bf16[4,32,1024]{2,1,0:T(8,128)(2,1)S(1)} %get-tuple-element.11), channel_id=1, source_target_pairs={{0,1},{1,2},{2,3},{3,0},{4,5},{5,6},{6,7},{7,4},{8,9},{9,10},{10,1... | collective-permute-start | bytes 786440 | tf_op jit(solution)/shard_map/ppermute | solution.py:102
  204.2 5.9 %collective-permute-start.15 = (bf16[4,32,1024]{2,1,0:T(8,128)(2,1)S(1)}, bf16[4,32,1024]{2,1,0:T(8,128)(2,1)S(1)}, u32[]{:S(2)}, u32[]{:S(2)}) collective-permute-start(bf16[4,32,1024]{2,1,0:T(8,128)(2,1)S(1)} %get-tuple-element.12), channel_id=1, source_target_pairs={{0,3},{1,0},{2,1},{3,2},{4,7},{5,4},{6,5},{7,6},{8,11},{9,8},{10,9... | collective-permute-start | bytes 786440 | tf_op jit(solution)/shard_map/ppermute | solution.py:102
  205.6 8.0 %collective-permute-start.29 = (bf16[4,32,1024]{2,1,0:T(8,128)(2,1)S(1)}, bf16[4,32,1024]{2,1,0:T(8,128)(2,1)S(1)}, u32[]{:S(2)}, u32[]{:S(2)}) collective-permute-start(bf16[4,32,1024]{2,1,0:T(8,128)(2,1)S(1)} %get-tuple-element.17), channel_id=1, source_target_pairs={{0,4},{1,5},{2,6},{3,7},{4,8},{5,9},{6,10},{7,11},{8,12},{9,13},{1... | collective-permute-start | bytes 786440 | tf_op jit(solution)/shard_map/ppermute | solution.py:102
  205.9 7.7 %collective-permute-start.31 = (bf16[4,32,1024]{2,1,0:T(8,128)(2,1)S(1)}, bf16[4,32,1024]{2,1,0:T(8,128)(2,1)S(1)}, u32[]{:S(2)}, u32[]{:S(2)}) collective-permute-start(bf16[4,32,1024]{2,1,0:T(8,128)(2,1)S(1)} %get-tuple-element.18), channel_id=1, source_target_pairs={{0,12},{1,13},{2,14},{3,15},{4,0},{5,1},{6,2},{7,3},{8,4},{9,5},{1... | collective-permute-start | bytes 786440 | tf_op jit(solution)/shard_map/ppermute | solution.py:102
  215.3 22.3 %all-to-all-start.1 = ((bf16[8,32,1024]{2,1,0:T(8,128)(2,1)}), bf16[8,32,1024]{2,1,0:T(8,128)(2,1)}, u32[]{:S(2)}, u32[]{:S(2)}) async-start(bf16[8,32,1024]{2,1,0:T(8,128)(2,1)} %broadcast_select_fusion.1), calls=%async_computation.1 | async-start | bytes 1048576 | tf_op jit(solution)/shard_map/all_to_all | solution.py:231
  230.5 11.1 %copy-start.13 = (bf16[32,8,1024]{2,1,0:T(8,128)(2,1)S(1)}, bf16[32,8,1024]{2,1,0:T(8,128)(2,1)}, u32[]{:S(2)}) copy-start(bf16[32,8,1024]{2,1,0:T(8,128)(2,1)} %param.7) | copy-start | bytes 1572868

commit v5 on v3

--- a/solution.py
+++ b/solution.py
@@ -121,20 +121,19 @@
     return jnp.concatenate([slots[r] for r in range(n)], axis=1)
 
 
-def ring_reduce(parts, grid, axis):
+def ring_reduce_slots(parts, grid, axis):
     n = grid[axis]
-    rows, total, width = parts.shape
-    m = total // n
-    slots = [parts[:, r * m:(r + 1) * m].astype(jnp.float32) for r in range(n)]
+    m = parts[0].shape[1]
+    slots = [p.astype(jnp.float32) for p in parts]
     if n == 1:
         return slots[0]
     if n == 2:
-        return slots[0] + send(slots[1].astype(jnp.bfloat16), grid, axis, 1).astype(jnp.float32)
+        return slots[0] + send(parts[1].astype(jnp.bfloat16), grid, axis, 1).astype(jnp.float32)
     top = (n - 1) // 2
     acc_ahead, acc_behind = slots[top], slots[n - top]
     if n % 2 == 0:
         half = m // 2
-        far = slots[n // 2].astype(jnp.bfloat16)
+        far = parts[n // 2].astype(jnp.bfloat16)
         got_first = send(far[:, :half], grid, axis, 1).astype(jnp.float32)
         got_second = send(far[:, half:], grid, axis, -1).astype(jnp.float32)
         acc_ahead = acc_ahead + jnp.concatenate([got_first, jnp.zeros_like(got_first)], axis=1)
@@ -147,6 +146,31 @@
             acc_behind = slots[n - k + 1] + got_behind
         else:
             return slots[0] + got_ahead + got_behind
+
+
+def ring_reduce(parts, grid, axis):
+    n = grid[axis]
+    m = parts.shape[1] // n
+    return ring_reduce_slots([parts[:, r * m:(r + 1) * m] for r in range(n)], grid, axis)
+
+
+def torus_reduce_abs(parts, grid, coords, order):
+    rr, total, width = parts.shape
+    m = total // (grid[0] * grid[1])
+    grid_parts = parts.reshape(rr, grid[0], grid[1], m, width)
+    first, second = order
+    n = grid[first]
+    slots = [
+        lax.dynamic_index_in_dim(grid_parts, (coords[first] + r) % n, 1 + first, keepdims=False).reshape(
+            rr, -1, width
+        )
+        for r in range(n)
+    ]
+    out = ring_reduce_slots(slots, grid, first).astype(jnp.bfloat16)
+    n = grid[second]
+    out = out.reshape(rr, n, m, width)
+    slots = [lax.dynamic_index_in_dim(out, (coords[second] + r) % n, 1, keepdims=False) for r in range(n)]
+    return ring_reduce_slots(slots, grid, second)
 
 
 def torus_gather(block, grid, order):
@@ -203,15 +227,16 @@
     q_out = jnp.where(send_filled[:, None, None], q_pos[send_pos], jnp.zeros((), jnp.bfloat16))
     q_in = lax.all_to_all(q_out, "group", split_axis=0, concat_axis=0, tiled=True)
     q_rows = q_in[row_index]
+    coords = (member_now // grid[1], member_now % grid[1])
     split = per_group // 2
     halves = ((slice(0, split), (0, 1)), (slice(split, per_group), (1, 0)))
     sums = []
     for rows_of, order in halves:
-        q_all = torus_gather(q_rows[rows_of], grid, order)
+        q_all = lax.all_gather(q_rows[rows_of], "member", axis=1, tiled=True)
         partial = attend_local(
             q_all, kv_cache[rows_of], row_live[rows_of], member_now * count, scale, HEADS, jnp.bfloat16
         )
-        sums.append(torus_reduce(partial, grid, order))
+        sums.append(torus_reduce_abs(partial, grid, coords, order))
     summed = jnp.concatenate(sums, axis=0).astype(jnp.bfloat16)
 
     a_out = jnp.where(filled[:, None, None], summed[chosen], jnp.zeros((), summed.dtype))

time: 193 us -> 246 us (1.27)
  waiting for transfers between devices: 55 us -> 135 us
  starting transfers between devices: 64.5 us -> 36.1 us
  between operations: 0.47 us -> 14 us
  local copies, waits for them, and re-layouts: 35.8 us -> 24 us
    all_gather x0 -> x2, waiting for transfers between devices: none -> 83.1 us  [on_device(): q_all = lax.all_gather(q_rows[rows_of], 'member', axis=1, tiled=True)]
    ppermute x32 -> x16, starting transfers between devices: 41.4 us -> 19.5 us  [send(): return lax.ppermute(value, 'member', shift_perm(grid, axis, shift))]
    unnamed x25 -> x16, local copies, waits for them, and re-layouts: 14.3 us -> 0.97 us
    dynamic_slice x0 -> x2, local copies, waits for them, and re-layouts: none -> 7.22 us  [torus_reduce_abs(): lax.dynamic_index_in_dim(grid_parts, (coords[first] + r) % n, 1 + first,...]
    all_to_all x1, starting transfers between devices: 17.1 us -> 10.4 us  [on_device(): lax.all_to_all(a_out, 'group', split_axis=0, concat_axis=0, tiled=True)]
    ppermute x32 -> x16, waiting for transfers between devices: 39.2 us -> 34.6 us  [send(): return lax.ppermute(value, 'member', shift_perm(grid, axis, shift))]
    concatenate x4 -> x0, local copies, waits for them, and re-layouts: 3.85 us -> none  [ring_gather(): return jnp.concatenate([slots[r] for r in range(n)], axis=1)]
    slice x12 -> x5, local copies, waits for them, and re-layouts: 5.5 us -> 1.98 us  [the longest x4 1.16 us: ring_reduce_slots(): got_first = send(far[:, :half], grid, axis, 1).astype(jnp.float32)]
  transfers between devices with their start and end apart: 34 -> 20, of which waited for: 11 -> 14; matrix products, arithmetic and copies ran while one was open for 18% -> 10% of each run, Pallas kernels for 8% -> 6%
where the time goes in v5:
time: 246 us; the launch traced here: 245 us
  waiting for transfers between devices  135 us (55%)
  starting transfers between devices  36.1 us (15%)
  local copies, waits for them, and re-layouts  24 us (10%)
  Pallas kernels  15.8 us (6%)
  other arithmetic  15.1 us (6%)
  between operations  14 us (6%)
  matrix products  5.3 us (2%)
    all_gather x2, waiting for transfers between devices, on_device(): q_all = lax.all_gather(q_rows[rows_of], 'member', axis=1, tiled=True)  83.1 us
    ppermute x16, waiting for transfers between devices, send(): return lax.ppermute(value, 'member', shift_perm(grid, axis, shift))  34.6 us
    ppermute x16, starting transfers between devices, send(): return lax.ppermute(value, 'member', shift_perm(grid, axis, shift))  19.5 us
    pallas_call x2, Pallas kernels, attend_local(): pl.pallas_call(kernel, out_shape=jax.ShapeDtypeStruct((rows, cands, width...  15.8 us
    all_to_all x1, starting transfers between devices, on_device(): lax.all_to_all(a_out, 'group', split_axis=0, concat_axis=0, tiled=True)  10.4 us
    all_to_all x1, waiting for transfers between devices, on_device(): lax.all_to_all(q_out, 'group', split_axis=0, concat_axis=0, tiled=True)  9.34 us
    dynamic_slice x2, local copies, waits for them, and re-layouts, torus_reduce_abs(): lax.dynamic_index_in_dim(grid_parts, (coords[first] + r) % n, 1 + first,...  7.22 us
    all_to_all x1, waiting for transfers between devices, on_device(): lax.all_to_all(a_out, 'group', split_axis=0, concat_axis=0, tiled=True)  7.12 us
  transfers between devices with their start and end apart: 20, of which 14 were waited for; matrix products, arithmetic and copies ran while one was open for 10% of the time, Pallas kernels for 6%

profile of v5, /device:TPU:1, one launch (start us, length us, event | category | flops | bytes accessed | tf_op | source)
XLA Modules:
  0.0 245.0 jit_solution(15316880368613088124)
XLA Ops:
  6.6 1.0 fusion.38
  7.6 0.6 gather_fusion.2
  8.3 0.2 convert_reduce_fusion.1
  8.5 0.6 gather_fusion.3
  9.4 1.2 convert_reduce_fusion
  10.8 1.3 fusion.12
  12.3 3.7 %divide_multiply_fusion = f32[256,2048]{1,0:T(8,128)S(1)} fusion(bf16[1024,2048]{1,0:T(8,128)(2,1)} %param.12, bf16[32,8,1024]{2,1,0:T(8,128)(2,1)S(1)} %copy-done.5, f32[32,8]{1,0:T(8,128)S(1)} %copy.68, f32[32,8]{1,0:T(8,128)S(1)} %copy.66), kind=kOutput, calls=%fused_computation.22 | convolution fusion | flops 1076887552 | bytes 6817792 | tf_op jit(solution)/shard_map/dot_general | solution.py:221
  16.0 0.3 copy.92
  16.3 0.9 copy-done.7
  17.3 0.6 gather_fusion.4
  17.9 0.9 broadcast_select_fusion
  18.8 6.1 %all-to-all-start = ((bf16[8,32,1024]{2,1,0:T(8,128)(2,1)}), bf16[8,32,1024]{2,1,0:T(8,128)(2,1)S(1)}, u32[]{:S(2)}, u32[]{:S(2)}) async-start(bf16[8,32,1024]{2,1,0:T(8,128)(2,1)} %broadcast_select_fusion), calls=%async_computation | async-start | bytes 1048576 | tf_op jit(solution)/shard_map/all_to_all | solution.py:228
  24.9 9.3 %all-to-all-done = bf16[8,32,1024]{2,1,0:T(8,128)(2,1)S(1)} async-done(((bf16[8,32,1024]{2,1,0:T(8,128)(2,1)}), bf16[8,32,1024]{2,1,0:T(8,128)(2,1)S(1)}, u32[]{:S(2)}, u32[]{:S(2)}) %all-to-all-start) | async-done | bytes 524320 | tf_op jit(solution)/shard_map/all_to_all | solution.py:228
  34.2 0.6 gather_fusion.5
  34.8 0.8 fusion.55
  35.7 0.7 all-gather.3.cloned.1.call-update
  36.4 0.6 gather_fusion
  37.2 0.6 gather_fusion.1
  38.0 0.7 subtract_clamp_fusion.1
  38.7 0.7 fusion.43
  39.4 4.8 %fusion.52 = (bf16[4,128,2048]{2,1,0:T(8,128)(2,1)}, bf16[4,128,2048]{2,1,0:T(8,128)(2,1)}) fusion(bf16[8,128,2048]{2,1,0:T(8,128)(2,1)} %param.8), kind=kLoop, calls=%fused_computation.143 | loop fusion | bytes 8388608 | tf_op jit(solution)/shard_map/slice | solution.py:237
  44.1 43.6 %all-gather.5.cloned.1.call-done.q_ref = bf16[4,512,1024]{2,1,0:T(8,128)(2,1)} async-done(((bf16[4,32,1024]{2,1,0:T(8,128)(2,1)}), bf16[4,512,1024]{2,1,0:T(8,128)(2,1)}) %all-gather.5.cloned.1.call-update) | async-done | bytes 4194320 | tf_op jit(solution)/shard_map/all_gather | solution.py:235
  87.8 7.9 %shard_map.74 = bf16[4,512,1024]{2,1,0:T(8,128)(2,1)} custom-call(s32[4]{0:T(128)} %get-tuple-element.38.n_live_ref, bf16[4,512,1024]{2,1,0:T(8,128)(2,1)} %all-gather.5.cloned.1.call-done.q_ref, bf16[4,128,2048]{2,1,0:T(8,128)(2,1)} %get-tuple-element.14.kv_ref, f32[4,1,128]{2,1,0:T(1,128)} %get-tuple-element.34.keep_ref), custom_call_target="tpu_custom_call" | custom-call | flops 1073741824 | bytes 10485760 | tf_op jit(solution)/shard_map/pallas_call | solution.py:67
  95.6 4.2 %constant_dynamic-slice_fusion.3 = (bf16[4,4,1,32,1024]{4,3,2,1,0:T(8,128)(2,1)}, bf16[4,4,1,32,1024]{4,3,2,1,0:T(8,128)(2,1)}, bf16[4,4,1,32,1024]{4,3,2,1,0:T(8,128)(2,1)S(1)}, bf16[4,4,1,32,1024]{4,3,2,1,0:T(8,128)(2,1)S(1)}) fusion(bf16[4,4,4,32,1024]{4,3,2,1,0:T(8,128)(2,1)} %bitcast.129, s32[]{:T(128)S(6)} %select_n.259, s32[]{:T(128)S(6)} %select_n.265, ...), kind=kLoop, calls=%fused_computation.95 | loop fusion | bytes 8388624 | tf_op jit(solution)/shard_map/jit(dynamic_index_in_dim)/dynamic_slice | solution.py:164
  99.9 1.0 fusion.54
  100.9 2.4 collective-permute-start.10
  103.3 39.5 %all-gather.3.cloned.1.call-done.q_ref = bf16[4,512,1024]{2,1,0:T(8,128)(2,1)} async-done(((bf16[4,32,1024]{2,1,0:T(8,128)(2,1)}), bf16[4,512,1024]{2,1,0:T(8,128)(2,1)}) %all-gather.3.cloned.1.call-update) | async-done | bytes 4194320 | tf_op jit(solution)/shard_map/all_gather | solution.py:235
  142.8 7.9 %shard_map.73 = bf16[4,512,1024]{2,1,0:T(8,128)(2,1)} custom-call(s32[4]{0:T(128)} %get-tuple-element.37.n_live_ref, bf16[4,512,1024]{2,1,0:T(8,128)(2,1)} %all-gather.3.cloned.1.call-done.q_ref, bf16[4,128,2048]{2,1,0:T(8,128)(2,1)} %get-tuple-element.13.kv_ref, f32[4,1,128]{2,1,0:T(1,128)} %get-tuple-element.33.keep_ref), custom_call_target="tpu_custom_call" | custom-call | flops 1073741824 | bytes 10485760 | tf_op jit(solution)/shard_map/pallas_call | solution.py:67
  150.7 3.0 %constant_dynamic-slice_fusion.7 = (bf16[4,1,4,32,1024]{4,3,2,1,0:T(8,128)(2,1)S(1)}, bf16[4,1,4,32,1024]{4,3,2,1,0:T(8,128)(2,1)S(1)}, bf16[4,1,4,32,1024]{4,3,...) fusion(bf16[4,4,4,32,1024]{4,3,2,1,0:T(8,128)(2,1)} %bitcast.130, s32[]{:T(128)S(6)} %select_n.250, s32[]{:T(128)S(6)} %select_n.256, ...), kind=kLoop, calls=%fused_computation.99 | loop fusion | bytes 8388624 | tf_op jit(solution)/shard_map/jit(dynamic_index_in_dim)/dynamic_slice | solution.py:164
  153.8 1.5 collective-permute-start.2
  155.3 1.4 fusion
  156.7 2.0 collective-permute-start.11
  158.6 1.3 fusion.1
  160.1 6.5 %collective-permute-done.2 = bf16[4,64,1024]{2,1,0:T(8,128)(2,1)S(1)} collective-permute-done((bf16[4,64,1024]{2,1,0:T(8,128)(2,1)S(1)}, bf16[4,64,1024]{2,1,0:T(8,128)(2,1)S(1)}, u32[]{:S(2)}, u32[]{:S(2)}) %collective-permute-start.2) | collective-permute-done | bytes 524320 | tf_op jit(solution)/shard_map/ppermute | solution.py:102
  166.6 0.3 fusion.4
  167.0 3.5 %collective-permute-start.3 = (bf16[4,128,1024]{2,1,0:T(8,128)(2,1)S(1)}, bf16[4,128,1024]{2,1,0:T(8,128)(2,1)S(1)}, u32[]{:S(2)}, u32[]{:S(2)}) collective-permute-start(bf16[4,128,1024]{2,1,0:T(8,128)(2,1)S(1)} %fusion.4), channel_id=1, source_target_pairs={{0,12},{1,13},{2,14},{3,15},{4,0},{5,1},{6,2},{7,3},{8,4},{9,5},{1... | collective-permute-start | bytes 3145736 | tf_op jit(solution)/shard_map/ppermute | solution.py:102
  170.4 0.3 fusion.5
  170.8 0.3 collective-permute-start.1
  171.2 8.8 %collective-permute-done.11 = bf16[4,128,1024]{2,1,0:T(8,128)(2,1)S(1)} collective-permute-done((bf16[4,128,1024]{2,1,0:T(8,128)(2,1)S(1)}, bf16[4,128,1024]{2,1,0:T(8,128)(2,1)S(1)}, u32[]{:S(2)}, u32[]{:S(2)}) %collective-permute-start.11) | collective-permute-done | bytes 1048608 | tf_op jit(solution)/shard_map/ppermute | solution.py:102
  180.1 4.5 %collective-permute-done.9 = bf16[4,128,1024]{2,1,0:T(8,128)(2,1)S(1)} collective-permute-done((bf16[4,128,1024]{2,1,0:T(8,128)(2,1)S(1)}, bf16[4,128,1024]{2,1,0:T(8,128)(2,1)S(1)}, u32[]{:S(2)}, u32[]{:S(2)}) %collective-permute-start.9) | collective-permute-done | bytes 1048608 | tf_op jit(solution)/shard_map/ppermute | solution.py:102
  184.6 0.7 fusion.3
  185.4 0.4 collective-permute-start.12
  185.7 2.4 collective-permute-start.14
  188.1 4.1 %collective-permute-done.3 = bf16[4,128,1024]{2,1,0:T(8,128)(2,1)S(1)} collective-permute-done((bf16[4,128,1024]{2,1,0:T(8,128)(2,1)S(1)}, bf16[4,128,1024]{2,1,0:T(8,128)(2,1)S(1)}, u32[]{:S(2)}, u32[]{:S(2)}) %collective-permute-start.3) | collective-permute-done | bytes 1048608 | tf_op jit(solution)/shard_map/ppermute | solution.py:102
  192.2 3.7 %collective-permute-done.1 = bf16[4,128,1024]{2,1,0:T(8,128)(2,1)S(1)} collective-permute-done((bf16[4,128,1024]{2,1,0:T(8,128)(2,1)S(1)}, bf16[4,128,1024]{2,1,0:T(8,128)(2,1)S(1)}, u32[]{:S(2)}, u32[]{:S(2)}) %collective-permute-start.1) | collective-permute-done | bytes 1048608 | tf_op jit(solution)/shard_map/ppermute | solution.py:102
  195.9 0.7 fusion.7
  196.8 2.7 %collective-permute-start.6 = (bf16[4,16,1024]{2,1,0:T(8,128)(2,1)S(1)}, bf16[4,16,1024]{2,1,0:T(8,128)(2,1)S(1)}, u32[]{:S(2)}, u32[]{:S(2)}) collective-permute-start(bf16[4,16,1024]{2,1,0:T(8,128)(2,1)S(1)} %get-tuple-element.30), channel_id=1, source_target_pairs={{0,3},{1,0},{2,1},{3,2},{4,7},{5,4},{6,5},{7,6},{8,11},{9,8},{10,9... | collective-permute-start | bytes 393224 | tf_op jit(solution)/shard_map/ppermute | solution.py:102
  199.6 1.5 collective-permute-start.13
  201.2 0.6 collective-permute-done.4
  201.9 2.7 %collective-permute-start.7 = (bf16[4,32,1024]{2,1,0:T(8,128)(2,1)S(1)}, bf16[4,32,1024]{2,1,0:T(8,128)(2,1)S(1)}, u32[]{:S(2)}, u32[]{:S(2)}) collective-permute-start(bf16[4,32,1024]{2,1,0:T(8,128)(2,1)S(1)} %get-tuple-element.20), channel_id=1, source_target_pairs={{0,3},{1,0},{2,1},{3,2},{4,7},{5,4},{6,5},{7,6},{8,11},{9,8},{10,9... | collective-permute-start | bytes 786440 | tf_op jit(solution)/shard_map/ppermute | solution.py:102
  204.6 0.5 collective-permute-done.15
  205.1 1.0 collective-permute-done.13
  206.2 1.9 collective-permute-done.7
  208.2 2.9 %collective-permute-done.5 = bf16[4,32,1024]{2,1,0:T(8,128)(2,1)S(1)} collective-permute-done((bf16[4,32,1024]{2,1,0:T(8,128)(2,1)S(1)}, bf16[4,32,1024]{2,1,0:T(8,128)(2,1)S(1)}, u32[]{:S(2)}, u32[]{:S(2)}) %collective-permute-start.5) | collective-permute-done | bytes 262176 | tf_op jit(solution)/shard_map/ppermute | solution.py:102
  211.2 0.6 gather_fusion.6
  211.8 0.9 broadcast_select_fusion.1
  212.7 10.4 %all-to-all-start.1 = ((bf16[8,32,1024]{2,1,0:T(8,128)(2,1)}), bf16[8,32,1024]{2,1,0:T(8,128)(2,1)}, u32[]{:S(2)}, u32[]{:S(2)}) async-start(bf16[8,32,1024]{2,1,0:T(8,128)(2,1)} %broadcast_select_fusion.1), calls=%async_computation.1 | async-start | bytes 1048576 | tf_op jit(solution)/shard_map/all_to_all | solution.py:243
  223.2 2.3 slice_bitcast_fusion
  225.5 7.1 %all-to-all-done.1 = bf16[8,32,1024]{2,1,0:T(8,128)(2,1)} async-done(((bf16[8,32,1024]{2,1,0:T(8,128)(2,1)}), bf16[8,32,1024]{2,1,0:T(8,128)(2,1)}, u32[]{:S(2)}, u32[]{:S(2)}) %all-to-all-start.1) | async-done | bytes 524320 | tf_op jit(solution)/shard_map/all_to_all | solution.py:243
  232.6 1.6 gather_fusion.7
  234.2 0.1 bitcast_reduce_fusion
  234.4 0.3 fusion.16
  234.7 1.9 fusion.18
  236.6 1.6 fusion.11
  (74 shorter events, 2.2 us)
Async XLA Ops:
  6.5 230.0 %copy-start = (bf16[1024,1024]{1,0:T(8,128)(2,1)S(1)}, bf16[1024,1024]{1,0:T(8,128)(2,1)}, u32[]{:S(2)}) copy-start(bf16[1024,1024]{1,0:T(8,128)(2,1)} %param.13) | copy-start | bytes 6291460
  6.5 5.7 %copy-start.5 = (bf16[32,8,1024]{2,1,0:T(8,128)(2,1)S(1)}, bf16[32,8,1024]{2,1,0:T(8,128)(2,1)}, u32[]{:S(2)}) copy-start(bf16[32,8,1024]{2,1,0:T(8,128)(2,1)} %param.7) | copy-start | bytes 1572868
  15.9 1.4 copy-start.7
  18.8 17.6 %copy-start.1 = (s32[64]{0:T(128)S(1)}, s32[64]{0:T(128)}, u32[]{:S(2)}) copy-start(s32[64]{0:T(128)} %param.9) | copy-start | bytes 772
  18.8 18.5 %copy-start.2 = (s32[64]{0:T(128)S(1)}, s32[64]{0:T(128)}, u32[]{:S(2)}) copy-start(s32[64]{0:T(128)} %param.11) | copy-start | bytes 772
  18.8 15.4 %all-to-all-start = ((bf16[8,32,1024]{2,1,0:T(8,128)(2,1)}), bf16[8,32,1024]{2,1,0:T(8,128)(2,1)S(1)}, u32[]{:S(2)}, u32[]{:S(2)}) async-start(bf16[8,32,1024]{2,1,0:T(8,128)(2,1)} %broadcast_select_fusion), calls=%async_computation | async-start | bytes 1048576 | tf_op jit(solution)/shard_map/all_to_all | solution.py:228
  24.9 62.9 %all-gather.5.cloned.1.call-start = ((), (), s32[]{:S(2)}) async-start(), calls=%async_computation.3 | async-start | bytes 4456448 | tf_op jit(solution)/shard_map/all_gather | solution.py:235
  35.6 107.2 %all-gather.3.cloned.1.call-start = ((), (), s32[]{:S(2)}) async-start(), calls=%async_computation.2 | async-start | bytes 4456448 | tf_op jit(solution)/shard_map/all_gather | solution.py:235
  100.9 54.4 %collective-permute-start.10 = (bf16[4,64,1024]{2,1,0:T(8,128)(2,1)}, bf16[4,64,1024]{2,1,0:T(8,128)(2,1)}, u32[]{:S(2)}, u32[]{:S(2)}) collective-permute-start(bf16[4,64,1024]{2,1,0:T(8,128)(2,1)} %get-tuple-element.26), channel_id=1, source_target_pairs={{0,3},{1,0},{2,1},{3,2},{4,7},{5,4},{6,5},{7,6},{8,11},{9,8},{10,9... | collective-permute-start | bytes 1572872 | tf_op jit(solution)/shard_map/ppermute | solution.py:102
  103.3 55.3 %collective-permute-start.8 = (bf16[4,64,1024]{2,1,0:T(8,128)(2,1)}, bf16[4,64,1024]{2,1,0:T(8,128)(2,1)}, u32[]{:S(2)}, u32[]{:S(2)}) collective-permute-start(bf16[4,64,1024]{2,1,0:T(8,128)(2,1)} %get-tuple-element.25), channel_id=1, source_target_pairs={{0,1},{1,2},{2,3},{3,0},{4,5},{5,6},{6,7},{7,4},{8,9},{9,10},{10,1... | collective-permute-start | bytes 1572872 | tf_op jit(solution)/shard_map/ppermute | solution.py:102
  153.7 1.6 copy-start.3
  153.8 12.9 %collective-permute-start.2 = (bf16[4,64,1024]{2,1,0:T(8,128)(2,1)S(1)}, bf16[4,64,1024]{2,1,0:T(8,128)(2,1)S(1)}, u32[]{:S(2)}, u32[]{:S(2)}) collective-permute-start(bf16[4,64,1024]{2,1,0:T(8,128)(2,1)S(1)} %get-tuple-element.22), channel_id=1, source_target_pairs={{0,12},{1,13},{2,14},{3,15},{4,0},{5,1},{6,2},{7,3},{8,4},{9,5},{1... | collective-permute-start | bytes 1572872 | tf_op jit(solution)/shard_map/ppermute | solution.py:102
  155.2 15.2 %collective-permute-start = (bf16[4,64,1024]{2,1,0:T(8,128)(2,1)S(1)}, bf16[4,64,1024]{2,1,0:T(8,128)(2,1)S(1)}, u32[]{:S(2)}, u32[]{:S(2)}) collective-permute-start(bf16[4,64,1024]{2,1,0:T(8,128)(2,1)S(1)} %get-tuple-element.21), channel_id=1, source_target_pairs={{0,4},{1,5},{2,6},{3,7},{4,8},{5,9},{6,10},{7,11},{8,12},{9,13},{1... | collective-permute-start | bytes 1572872 | tf_op jit(solution)/shard_map/ppermute | solution.py:102
  156.7 23.4 %collective-permute-start.11 = (bf16[4,128,1024]{2,1,0:T(8,128)(2,1)S(1)}, bf16[4,128,1024]{2,1,0:T(8,128)(2,1)S(1)}, u32[]{:S(2)}, u32[]{:S(2)}) collective-permute-start(bf16[4,128,1024]{2,1,0:T(8,128)(2,1)S(1)} %fusion), channel_id=1, source_target_pairs={{0,3},{1,0},{2,1},{3,2},{4,7},{5,4},{6,5},{7,6},{8,11},{9,8},{10,9... | collective-permute-start | bytes 3145736 | tf_op jit(solution)/shard_map/ppermute | solution.py:102
  160.0 24.6 %collective-permute-start.9 = (bf16[4,128,1024]{2,1,0:T(8,128)(2,1)S(1)}, bf16[4,128,1024]{2,1,0:T(8,128)(2,1)S(1)}, u32[]{:S(2)}, u32[]{:S(2)}) collective-permute-start(bf16[4,128,1024]{2,1,0:T(8,128)(2,1)S(1)} %fusion.1), channel_id=1, source_target_pairs={{0,1},{1,2},{2,3},{3,0},{4,5},{5,6},{6,7},{7,4},{8,9},{9,10},{10,1... | collective-permute-start | bytes 3145736 | tf_op jit(solution)/shard_map/ppermute | solution.py:102
  166.6 18.0 %copy-start.4 = (bf16[4,4,1,32,1024]{4,3,2,1,0:T(8,128)(2,1)S(1)}, bf16[4,4,1,32,1024]{4,3,2,1,0:T(8,128)(2,1)}, u32[]{:S(2)}) copy-start(bf16[4,4,1,32,1024]{4,3,2,1,0:T(8,128)(2,1)} %get-tuple-element.15) | copy-start | bytes 3145732
  167.0 25.3 %collective-permute-start.3 = (bf16[4,128,1024]{2,1,0:T(8,128)(2,1)S(1)}, bf16[4,128,1024]{2,1,0:T(8,128)(2,1)S(1)}, u32[]{:S(2)}, u32[]{:S(2)}) collective-permute-start(bf16[4,128,1024]{2,1,0:T(8,128)(2,1)S(1)} %fusion.4), channel_id=1, source_target_pairs={{0,12},{1,13},{2,14},{3,15},{4,0},{5,1},{6,2},{7,3},{8,4},{9,5},{1... | collective-permute-start | bytes 3145736 | tf_op jit(solution)/shard_map/ppermute | solution.py:102
  170.8 25.2 %collective-permute-start.1 = (bf16[4,128,1024]{2,1,0:T(8,128)(2,1)S(1)}, bf16[4,128,1024]{2,1,0:T(8,128)(2,1)S(1)}, u32[]{:S(2)}, u32[]{:S(2)}) collective-permute-start(bf16[4,128,1024]{2,1,0:T(8,128)(2,1)S(1)} %fusion.5), channel_id=1, source_target_pairs={{0,4},{1,5},{2,6},{3,7},{4,8},{5,9},{6,10},{7,11},{8,12},{9,13},{1... | collective-permute-start | bytes 3145736 | tf_op jit(solution)/shard_map/ppermute | solution.py:102
  185.4 14.1 %collective-permute-start.12 = (bf16[4,16,1024]{2,1,0:T(8,128)(2,1)S(1)}, bf16[4,16,1024]{2,1,0:T(8,128)(2,1)S(1)}, u32[]{:S(2)}, u32[]{:S(2)}) collective-permute-start(bf16[4,16,1024]{2,1,0:T(8,128)(2,1)S(1)} %get-tuple-element.31), channel_id=1, source_target_pairs={{0,4},{1,5},{2,6},{3,7},{4,8},{5,9},{6,10},{7,11},{8,12},{9,13},{1... | collective-permute-start | bytes 393224 | tf_op jit(solution)/shard_map/ppermute | solution.py:102
  185.7 13.7 %collective-permute-start.14 = (bf16[4,16,1024]{2,1,0:T(8,128)(2,1)S(1)}, bf16[4,16,1024]{2,1,0:T(8,128)(2,1)S(1)}, u32[]{:S(2)}, u32[]{:S(2)}) collective-permute-start(bf16[4,16,1024]{2,1,0:T(8,128)(2,1)S(1)} %get-tuple-element.32), channel_id=1, source_target_pairs={{0,12},{1,13},{2,14},{3,15},{4,0},{5,1},{6,2},{7,3},{8,4},{9,5},{1... | collective-permute-start | bytes 393224 | tf_op jit(solution)/shard_map/ppermute | solution.py:102
  196.7 5.1 %collective-permute-start.4 = (bf16[4,16,1024]{2,1,0:T(8,128)(2,1)S(1)}, bf16[4,16,1024]{2,1,0:T(8,128)(2,1)S(1)}, u32[]{:S(2)}, u32[]{:S(2)}) collective-permute-start(bf16[4,16,1024]{2,1,0:T(8,128)(2,1)S(1)} %get-tuple-element.29), channel_id=1, source_target_pairs={{0,1},{1,2},{2,3},{3,0},{4,5},{5,6},{6,7},{7,4},{8,9},{9,10},{10,1... | collective-permute-start | bytes 393224 | tf_op jit(solution)/shard_map/ppermute | solution.py:102
  196.8 5.0 %collective-permute-start.6 = (bf16[4,16,1024]{2,1,0:T(8,128)(2,1)S(1)}, bf16[4,16,1024]{2,1,0:T(8,128)(2,1)S(1)}, u32[]{:S(2)}, u32[]{:S(2)}) collective-permute-start(bf16[4,16,1024]{2,1,0:T(8,128)(2,1)S(1)} %get-tuple-element.30), channel_id=1, source_target_pairs={{0,3},{1,0},{2,1},{3,2},{4,7},{5,4},{6,5},{7,6},{8,11},{9,8},{10,9... | collective-permute-start | bytes 393224 | tf_op jit(solution)/shard_map/ppermute | solution.py:102
  199.5 5.6 %collective-permute-start.15 = (bf16[4,32,1024]{2,1,0:T(8,128)(2,1)S(1)}, bf16[4,32,1024]{2,1,0:T(8,128)(2,1)S(1)}, u32[]{:S(2)}, u32[]{:S(2)}) collective-permute-start(bf16[4,32,1024]{2,1,0:T(8,128)(2,1)S(1)} %get-tuple-element.24), channel_id=1, source_target_pairs={{0,12},{1,13},{2,14},{3,15},{4,0},{5,1},{6,2},{7,3},{8,4},{9,5},{1... | collective-permute-start | bytes 786440 | tf_op jit(solution)/shard_map/ppermute | solution.py:102
  199.6 6.5 %collective-permute-start.13 = (bf16[4,32,1024]{2,1,0:T(8,128)(2,1)S(1)}, bf16[4,32,1024]{2,1,0:T(8,128)(2,1)S(1)}, u32[]{:S(2)}, u32[]{:S(2)}) collective-permute-start(bf16[4,32,1024]{2,1,0:T(8,128)(2,1)S(1)} %get-tuple-element.23), channel_id=1, source_target_pairs={{0,4},{1,5},{2,6},{3,7},{4,8},{5,9},{6,10},{7,11},{8,12},{9,13},{1... | collective-permute-start | bytes 786440 | tf_op jit(solution)/shard_map/ppermute | solution.py:102
  201.9 6.3 %collective-permute-start.7 = (bf16[4,32,1024]{2,1,0:T(8,128)(2,1)S(1)}, bf16[4,32,1024]{2,1,0:T(8,128)(2,1)S(1)}, u32[]{:S(2)}, u32[]{:S(2)}) collective-permute-start(bf16[4,32,1024]{2,1,0:T(8,128)(2,1)S(1)} %get-tuple-element.20), channel_id=1, source_target_pairs={{0,3},{1,0},{2,1},{3,2},{4,7},{5,4},{6,5},{7,6},{8,11},{9,8},{10,9... | collective-permute-start | bytes 786440 | tf_op jit(solution)/shard_map/ppermute | solution.py:102
  204.6 6.4 %collective-permute-start.5 = (bf16[4,32,1024]{2,1,0:T(8,128)(2,1)S(1)}, bf16[4,32,1024]{2,1,0:T(8,128)(2,1)S(1)}, u32[]{:S(2)}, u32[]{:S(2)}) collective-permute-start(bf16[4,32,1024]{2,1,0:T(8,128)(2,1)S(1)} %get-tuple-element.19), channel_id=1, source_target_pairs={{0,1},{1,2},{2,3},{3,0},{4,5},{5,6},{6,7},{7,4},{8,9},{9,10},{10,1... | collective-permute-start | bytes 786440 | tf_op jit(solution)/shard_map/ppermute | solution.py:102
  212.7 19.9 %all-to-all-start.1 = ((bf16[8,32,1024]{2,1,0:T(8,128)(2,1)}), bf16[8,32,1024]{2,1,0:T(8,128)(2,1)}, u32[]{:S(2)}, u32[]{:S(2)}) async-start(bf16[8,32,1024]{2,1,0:T(8,128)(2,1)} %broadcast_select_fusion.1), calls=%async_computation.1 | async-start | bytes 1048576 | tf_op jit(solution)/shard_map/all_to_all | solution.py:243
  225.5 11.1 %copy-start.6 = (bf16[32,8,1024]{2,1,0:T(8,128)(2,1)S(1)}, bf16[32,8,1024]{2,1,0:T(8,128)(2,1)}, u32[]{:S(2)}) copy-start(bf16[32,8,1024]{2,1,0:T(8,128)(2,1)} %param.7) | copy-start | bytes 1572868
Sparse Core Ops, SparseCore 0:
  35.8 51.9 all-gather.4
  89.9 52.8 all-gather.2

commit v6 on v3

--- a/solution.py
+++ b/solution.py
@@ -33,56 +33,65 @@
     return (target, arrival, slot_of_pos)
 
 
-def attend_kernel(n_live_ref, q_ref, kv_ref, keep_ref, o_ref, *, heads, head_dim, scale):
+def attend_kernel(n_live_ref, *refs, pieces, heads, head_dim, scale):
+    q_refs = refs[:pieces]
+    kv_ref, keep_ref = refs[pieces], refs[pieces + 1]
+    o_refs = refs[pieces + 2:]
     row = pl.program_id(0)
     width = heads * head_dim
 
     @pl.when(n_live_ref[row] <= 0)
     def _():
-        o_ref[...] = jnp.zeros(o_ref.shape, o_ref.dtype)
+        for o_ref in o_refs:
+            o_ref[...] = jnp.zeros(o_ref.shape, o_ref.dtype)
 
     @pl.when(n_live_ref[row] > 0)
     def _():
         keep = keep_ref[0]
         for h in range(heads):
             lo = h * head_dim
-            q = q_ref[0, :, lo:lo + head_dim]
             k = kv_ref[0, :, lo:lo + head_dim]
             v = kv_ref[0, :, width + lo:width + lo + head_dim]
-            s = lax.dot_general(q, k, (((1,), (1,)), ((), ())), preferred_element_type=jnp.float32)
-            w = (jax.nn.silu(s * scale) * keep).astype(jnp.bfloat16)
-            o = jnp.dot(w, v, preferred_element_type=jnp.float32)
-            o_ref[0, :, lo:lo + head_dim] = o.astype(o_ref.dtype)
-
-
-def attend_local(queries, piece, live, first_event, scale, heads, out_dtype):
-    rows, cands, width = queries.shape
+            for q_ref, o_ref in zip(q_refs, o_refs):
+                q = q_ref[0, :, lo:lo + head_dim]
+                s = lax.dot_general(q, k, (((1,), (1,)), ((), ())), preferred_element_type=jnp.float32)
+                w = (jax.nn.silu(s * scale) * keep).astype(jnp.bfloat16)
+                o = jnp.dot(w, v, preferred_element_type=jnp.float32)
+                o_ref[0, :, lo:lo + head_dim] = o.astype(o_ref.dtype)
+
+
+def attend_local(q_pieces, piece, live, first_event, scale, heads, out_dtype):
+    rows, _, width = q_pieces[0].shape
     count = piece.shape[1]
     head_dim = width // heads
+    cands = sum(q.shape[1] for q in q_pieces)
     events = (first_event + jnp.arange(count)).astype(jnp.float32)
     keep = ((events[None, :] < live[:, None]).astype(jnp.float32) / live[:, None])[:, None, :]
     n_live = jnp.clip(live.astype(jnp.int32) - first_event, 0, count).astype(jnp.int32)
-    kernel = functools.partial(attend_kernel, heads=heads, head_dim=head_dim, scale=scale)
+    kernel = functools.partial(
+        attend_kernel, pieces=len(q_pieces), heads=heads, head_dim=head_dim, scale=scale
+    )
     flops = 4 * rows * cands * count * width
+    q_specs = [pl.BlockSpec((1, q.shape[1], width), lambda r, n: (r, 0, 0)) for q in q_pieces]
     return pl.pallas_call(
         kernel,
-        out_shape=jax.ShapeDtypeStruct((rows, cands, width), out_dtype),
+        out_shape=[jax.ShapeDtypeStruct(q.shape, out_dtype) for q in q_pieces],
         grid_spec=pltpu.PrefetchScalarGridSpec(
             num_scalar_prefetch=1,
             grid=(rows,),
-            in_specs=[
-                pl.BlockSpec((1, cands, width), lambda r, n: (r, 0, 0)),
+            in_specs=q_specs
+            + [
                 pl.BlockSpec((1, count, 2 * width), lambda r, n: (r, 0, 0)),
                 pl.BlockSpec((1, 1, count), lambda r, n: (r, 0, 0)),
             ],
-            out_specs=pl.BlockSpec((1, cands, width), lambda r, n: (r, 0, 0)),
+            out_specs=[pl.BlockSpec((1, q.shape[1], width), lambda r, n: (r, 0, 0)) for q in q_pieces],
         ),
         cost_estimate=pl.CostEstimate(
             flops=flops,
             transcendentals=rows * cands * count * heads,
             bytes_accessed=rows * (cands * width * 4 + count * width * 4),
         ),
-    )(n_live, queries, piece, keep)
+    )(n_live, *q_pieces, piece, keep)
 
 
 def shift_perm(grid, axis, shift):
@@ -100,6 +109,46 @@
 
 def send(value, grid, axis, shift):
     return lax.ppermute(value, "member", shift_perm(grid, axis, shift))
+
+
+def ring_gather_pieces(block, grid, axis):
+    n = grid[axis]
+    if n % 2 or n < 4:
+        return ring_gather_slots(block, grid, axis)
+    slots = {0: block}
+    ahead, behind = block, block
+    for k in range(1, (n - 1) // 2 + 1):
+        ahead = send(ahead, grid, axis, -1)
+        behind = send(behind, grid, axis, 1)
+        slots[k], slots[n - k] = ahead, behind
+    half = block.shape[1] // 2
+    first = send(behind[:, :half], grid, axis, 1)
+    second = send(ahead[:, half:], grid, axis, -1)
+    return [slots[r] for r in range(n // 2)] + [first, second] + [slots[r] for r in range(n // 2 + 1, n)]
+
+
+def ring_reduce_pieces(parts, grid, axis):
+    n = grid[axis]
+    if n % 2 or n < 4:
+        return ring_reduce_slots(parts, grid, axis)
+    parts = list(parts)
+    far_first, far_second = parts[n // 2], parts[n // 2 + 1]
+    slots = parts[: n // 2] + [None] + parts[n // 2 + 2:]
+    half = far_first.shape[1]
+    got_first = send(far_first.astype(jnp.bfloat16), grid, axis, 1).astype(jnp.float32)
+    got_second = send(far_second.astype(jnp.bfloat16), grid, axis, -1).astype(jnp.float32)
+    top = (n - 1) // 2
+    lead, tail = slots[top].astype(jnp.float32), slots[n - top].astype(jnp.float32)
+    acc_ahead = jnp.concatenate([lead[:, :half] + got_first, lead[:, half:]], axis=1)
+    acc_behind = jnp.concatenate([tail[:, :half], tail[:, half:] + got_second], axis=1)
+    for k in range(top, 0, -1):
+        got_ahead = send(acc_ahead.astype(jnp.bfloat16), grid, axis, 1).astype(jnp.float32)
+        got_behind = send(acc_behind.astype(jnp.bfloat16), grid, axis, -1).astype(jnp.float32)
+        if k > 1:
+            acc_ahead = slots[k - 1].astype(jnp.float32) + got_ahead
+            acc_behind = slots[n - k + 1].astype(jnp.float32) + got_behind
+        else:
+            return slots[0].astype(jnp.float32) + got_ahead + got_behind
 
 
 def ring_gather(block, grid, axis):
@@ -194,9 +243,8 @@
 
     inputs = candidates.astype(jnp.float32)
     normed = layer_norm(inputs).astype(jnp.bfloat16).reshape(cand_rows * per_group, width)
-    projected = jax.nn.silu(jnp.dot(normed, w_uq, preferred_element_type=jnp.float32))
-    gates = projected[:, :width].reshape(cand_rows, per_group, width)
-    queries = projected[:, width:].astype(jnp.bfloat16).reshape(cand_rows, per_group, width)
+    queries = jax.nn.silu(jnp.dot(normed, w_uq[:, width:], preferred_element_type=jnp.float32))
+    queries = queries.astype(jnp.bfloat16).reshape(cand_rows, per_group, width)
     scale = head_dim ** (-0.5)
 
     q_pos = jnp.swapaxes(queries, 0, 1)
@@ -207,17 +255,26 @@
     halves = ((slice(0, split), (0, 1)), (slice(split, per_group), (1, 0)))
     sums = []
     for rows_of, order in halves:
-        q_all = torus_gather(q_rows[rows_of], grid, order)
-        partial = attend_local(
-            q_all, kv_cache[rows_of], row_live[rows_of], member_now * count, scale, HEADS, jnp.bfloat16
+        inner = ring_gather(q_rows[rows_of], grid, order[1])
+        partials = attend_local(
+            ring_gather_pieces(inner, grid, order[0]),
+            kv_cache[rows_of],
+            row_live[rows_of],
+            member_now * count,
+            scale,
+            HEADS,
+            jnp.bfloat16,
         )
-        sums.append(torus_reduce(partial, grid, order))
+        outer = ring_reduce_pieces(partials, grid, order[0]).astype(jnp.bfloat16)
+        sums.append(ring_reduce(outer, grid, order[1]))
     summed = jnp.concatenate(sums, axis=0).astype(jnp.bfloat16)
 
     a_out = jnp.where(filled[:, None, None], summed[chosen], jnp.zeros((), summed.dtype))
     a_in = lax.all_to_all(a_out, "group", split_axis=0, concat_axis=0, tiled=True)
     attn = jnp.swapaxes(a_in[receive_index], 0, 1).astype(jnp.float32)
 
+    gates = jax.nn.silu(jnp.dot(normed, w_uq[:, :width], preferred_element_type=jnp.float32))
+    gates = gates.reshape(cand_rows, per_group, width)
     gated = (layer_norm(attn) * gates).astype(jnp.bfloat16).reshape(cand_rows * per_group, width)
     result = jnp.dot(gated, w_out, preferred_element_type=jnp.float32) + inputs.reshape(
         cand_rows * per_group, width

time: 193 us -> 228 us (1.18)
  Pallas kernels: 15.7 us -> 59.3 us
  waiting for transfers between devices: 55 us -> 48.1 us
  local copies, waits for them, and re-layouts: 35.8 us -> 29 us
    pallas_call x2, Pallas kernels: 15.7 us -> 59.3 us  [attend_local(): pl.pallas_call(kernel, out_shape=[jax.ShapeDtypeStruct(q.shape, out_dtype...]
    slice x0 -> x9, local copies, waits for them, and re-layouts: none -> 10.4 us  [the longest x2 2.99 us: ring_gather_pieces(): second = send(ahead[:, half:], grid, axis, -1)]
    unnamed x25 -> x28, local copies, waits for them, and re-layouts: 14.3 us -> 4.29 us
    ppermute x32, starting transfers between devices: 41.4 us -> 50.6 us  [send(): return lax.ppermute(value, 'member', shift_perm(grid, axis, shift))]
    all_to_all x1, starting transfers between devices: 17.1 us -> 9.45 us  [on_device(): lax.all_to_all(a_out, 'group', split_axis=0, concat_axis=0, tiled=True)]
    ppermute x32, waiting for transfers between devices: 39.2 us -> 32.8 us  [send(): return lax.ppermute(value, 'member', shift_perm(grid, axis, shift))]
    slice x4 -> x2, local copies, waits for them, and re-layouts: 3.74 us -> 0.04 us  [ring_reduce(): got_first = send(far[:, :half], grid, axis, 1).astype(jnp.float32)]
    convert_element_type x4 -> x2, other arithmetic: 3.25 us -> 0.16 us  [ring_reduce(): acc_ahead.astype(jnp.bfloat16)]
  transfers between devices with their start and end apart: 34 -> 34, of which waited for: 11 -> 13; matrix products, arithmetic and copies ran while one was open for 18% -> 14% of each run, Pallas kernels for 8% -> 26%
where the time goes in v6:
time: 228 us; the launch traced here: 226 us
  starting transfers between devices  66.1 us (29%)
  Pallas kernels  59.3 us (26%)
  waiting for transfers between devices  48.1 us (21%)
  local copies, waits for them, and re-layouts  29 us (13%)
  other arithmetic  14.9 us (7%)
  matrix products  7.58 us (3%)
    pallas_call x2, Pallas kernels, attend_local(): pl.pallas_call(kernel, out_shape=[jax.ShapeDtypeStruct(q.shape, out_dtype...  59.3 us
    ppermute x32, starting transfers between devices, send(): return lax.ppermute(value, 'member', shift_perm(grid, axis, shift))  50.6 us
    ppermute x32, waiting for transfers between devices, send(): return lax.ppermute(value, 'member', shift_perm(grid, axis, shift))  32.8 us
    all_to_all x1, starting transfers between devices, on_device(): lax.all_to_all(a_out, 'group', split_axis=0, concat_axis=0, tiled=True)  9.45 us
    all_to_all x1, waiting for transfers between devices, on_device(): lax.all_to_all(q_out, 'group', split_axis=0, concat_axis=0, tiled=True)  9.26 us
    all_to_all x1, starting transfers between devices, on_device(): lax.all_to_all(q_out, 'group', split_axis=0, concat_axis=0, tiled=True)  6.08 us
    all_to_all x1, waiting for transfers between devices, on_device(): lax.all_to_all(a_out, 'group', split_axis=0, concat_axis=0, tiled=True)  6.01 us
    slice x1, local copies, waits for them, and re-layouts, on_device(): kv_cache[rows_of]  4.8 us
  transfers between devices with their start and end apart: 34, of which 13 were waited for; matrix products, arithmetic and copies ran while one was open for 14% of the time, Pallas kernels for 26%

profile of v6, /device:TPU:1, one launch (start us, length us, event | category | flops | bytes accessed | tf_op | source)
XLA Modules:
  0.0 225.5 jit_solution(10070589690998901667)
XLA Ops:
  0.0 1.0 fusion.28
  1.1 1.3 gather_fusion
  4.2 1.2 convert_reduce_fusion
  6.0 2.5 %fusion.19 = bf16[32,8,1024]{2,1,0:T(8,128)(2,1)S(1)} fusion(bf16[1024,2048]{1,0:T(8,128)(2,1)} %param.12, bf16[32,8,1024]{2,1,0:T(8,128)(2,1)S(1)} %copy-done.3, f32[32,8]{1,0:T(8,128)S(1)} %copy.37, f32[32,8]{1,0:T(8,128)S(1)} %copy.35), kind=kOutput, calls=%fused_computation.41 | convolution fusion | flops 539230208 | bytes 3147776 | tf_op jit(solution)/shard_map/dot_general | solution.py:246
  9.3 0.9 broadcast_select_fusion
  10.2 6.1 %all-to-all-start = ((bf16[8,32,1024]{2,1,0:T(8,128)(2,1)}), bf16[8,32,1024]{2,1,0:T(8,128)(2,1)S(1)}, u32[]{:S(2)}, u32[]{:S(2)}) async-start(bf16[8,32,1024]{2,1,0:T(8,128)(2,1)} %broadcast_select_fusion), calls=%async_computation | async-start | bytes 1048576 | tf_op jit(solution)/shard_map/all_to_all | solution.py:252
  16.4 9.3 %all-to-all-done = bf16[8,32,1024]{2,1,0:T(8,128)(2,1)S(1)} async-done(((bf16[8,32,1024]{2,1,0:T(8,128)(2,1)}), bf16[8,32,1024]{2,1,0:T(8,128)(2,1)S(1)}, u32[]{:S(2)}, u32[]{:S(2)}) %all-to-all-start) | async-done | bytes 524320 | tf_op jit(solution)/shard_map/all_to_all | solution.py:252
  26.3 1.0 fusion.45
  27.3 1.2 collective-permute-start.1
  28.5 1.5 collective-permute-start
  30.0 1.6 collective-permute-start.17
  31.6 2.1 collective-permute-start.16
  34.4 1.2 collective-permute-done.1
  35.7 2.7 %collective-permute-start.3 = (bf16[4,16,1024]{2,1,0:T(8,128)(2,1)S(1)}, bf16[4,16,1024]{2,1,0:T(8,128)(2,1)S(1)}, u32[]{:S(2)}, u32[]{:S(2)}) collective-permute-start(bf16[4,16,1024]{2,1,0:T(8,128)(2,1)S(1)} %slice.180), channel_id=1, source_target_pairs={{0,3},{1,0},{2,1},{3,2},{4,7},{5,4},{6,5},{7,6},{8,11},{9,8},{10,9... | collective-permute-start | bytes 393224 | tf_op jit(solution)/shard_map/ppermute | solution.py:111
  38.9 1.3 collective-permute-start.18
  40.2 2.2 collective-permute-start.19
  42.4 0.8 constant_dynamic-update-slice_fusion.3
  43.2 0.8 constant_dynamic-update-slice_fusion.8
  43.9 0.7 constant_dynamic-update-slice_fusion.2
  45.3 0.7 constant_dynamic-update-slice_fusion.refs_0_
  46.0 2.7 %collective-permute-start.4 = (bf16[4,128,1024]{2,1,0:T(8,128)(2,1)}, bf16[4,128,1024]{2,1,0:T(8,128)(2,1)}, u32[]{:S(2)}, u32[]{:S(2)}) collective-permute-start(bf16[4,128,1024]{2,1,0:T(8,128)(2,1)} %constant_dynamic-update-slice_fusion.refs_0_), channel_id=1, source_target_pairs={{0,12},{1,13},{2,14},{3,15},{4,0},{5,1},{6,2},{7,3},{8,4},{9,5},{1... | collective-permute-start | bytes 3145736 | tf_op jit(solution)/shard_map/ppermute | solution.py:111
  49.4 0.7 constant_dynamic-update-slice_fusion.6
  50.1 0.7 constant_dynamic-update-slice_fusion.5.refs_0_
  50.8 2.7 %collective-permute-start.20 = (bf16[4,128,1024]{2,1,0:T(8,128)(2,1)}, bf16[4,128,1024]{2,1,0:T(8,128)(2,1)}, u32[]{:S(2)}, u32[]{:S(2)}) collective-permute-start(bf16[4,128,1024]{2,1,0:T(8,128)(2,1)} %constant_dynamic-update-slice_fusion.5.refs_0_), channel_id=1, source_target_pairs={{0,3},{1,0},{2,1},{3,2},{4,7},{5,4},{6,5},{7,6},{8,11},{9,8},{10,9... | collective-permute-start | bytes 3145736 | tf_op jit(solution)/shard_map/ppermute | solution.py:111
  53.5 4.8 %fusion.42 = (bf16[4,128,2048]{2,1,0:T(8,128)(2,1)}, bf16[4,128,2048]{2,1,0:T(8,128)(2,1)}) fusion(bf16[8,128,2048]{2,1,0:T(8,128)(2,1)} %param.8), kind=kLoop, calls=%fused_computation.131 | loop fusion | bytes 8388608 | tf_op jit(solution)/shard_map/slice | solution.py:261
  58.3 11.3 %collective-permute-done.5.refs_4_ = bf16[4,128,1024]{2,1,0:T(8,128)(2,1)} collective-permute-done((bf16[4,128,1024]{2,1,0:T(8,128)(2,1)}, bf16[4,128,1024]{2,1,0:T(8,128)(2,1)}, u32[]{:S(2)}, u32[]{:S(2)}) %collective-permute-start.5) | collective-permute-done | bytes 1048608 | tf_op jit(solution)/shard_map/ppermute | solution.py:111
  69.6 1.1 slice.181
  70.8 1.1 slice.182
  71.9 2.7 %collective-permute-start.7 = (bf16[4,64,1024]{2,1,0:T(8,128)(2,1)S(1)}, bf16[4,64,1024]{2,1,0:T(8,128)(2,1)}, u32[]{:S(2)}, u32[]{:S(2)}) collective-permute-start(bf16[4,64,1024]{2,1,0:T(8,128)(2,1)S(1)} %slice.182), channel_id=1, source_target_pairs={{0,12},{1,13},{2,14},{3,15},{4,0},{5,1},{6,2},{7,3},{8,4},{9,5},{1... | collective-permute-start | bytes 1572872 | tf_op jit(solution)/shard_map/ppermute | solution.py:111
  74.6 0.7 fusion.33
  75.3 0.9 slice.191
  76.2 1.9 slice.192
  78.1 2.7 %collective-permute-start.23 = (bf16[4,64,1024]{2,1,0:T(8,128)(2,1)}, bf16[4,64,1024]{2,1,0:T(8,128)(2,1)}, u32[]{:S(2)}, u32[]{:S(2)}) collective-permute-start(bf16[4,64,1024]{2,1,0:T(8,128)(2,1)} %slice.192), channel_id=1, source_target_pairs={{0,3},{1,0},{2,1},{3,2},{4,7},{5,4},{6,5},{7,6},{8,11},{9,8},{10,9... | collective-permute-start | bytes 1572872 | tf_op jit(solution)/shard_map/ppermute | solution.py:111
  81.4 0.7 collective-permute-done.6.refs_2_
  82.1 29.7 %shard_map.73 = (bf16[4,128,1024]{2,1,0:T(8,128)(2,1)}, bf16[4,128,1024]{2,1,0:T(8,128)(2,1)}, bf16[4,64,1024]{2,1,0:T(8,128)(2,1)}, bf16[4,64,1024]{2,1,0:T(8,128)(2,1)}, bf16[4,128,1024]{2,1,0:T(8,128)(2,1)}) custom-call(s32[4]{0:T(128)} %get-tuple-element.47.n_live_ref, bf16[4,128,1024]{2,1,0:T(8,128)(2,1)} %constant_dynamic-update-slice_fusion.refs_0_, ...), custom_call_target="tpu_custom_call" | custom-call | flops 1073741824 | bytes 10485760 | tf_op jit(solution)/shard_map/pallas_call | solution.py:76
  112.1 2.7 %collective-permute-start.10 = (bf16[4,64,1024]{2,1,0:T(8,128)(2,1)}, bf16[4,64,1024]{2,1,0:T(8,128)(2,1)}, u32[]{:S(2)}, u32[]{:S(2)}) collective-permute-start(bf16[4,64,1024]{2,1,0:T(8,128)(2,1)} %get-tuple-element.19), channel_id=1, source_target_pairs={{0,12},{1,13},{2,14},{3,15},{4,0},{5,1},{6,2},{7,3},{8,4},{9,5},{1... | collective-permute-start | bytes 1572872 | tf_op jit(solution)/shard_map/ppermute | solution.py:111
  114.9 1.1 slice.134
  116.0 1.1 slice.135
  117.1 29.6 %shard_map.74 = (bf16[4,128,1024]{2,1,0:T(8,128)(2,1)}, bf16[4,128,1024]{2,1,0:T(8,128)(2,1)}, bf16[4,64,1024]{2,1,0:T(8,128)(2,1)}, bf16[4,64,1024]{2,1,0:T(8,128)(2,1)}, bf16[4,128,1024]{2,1,0:T(8,128)(2,1)}) custom-call(s32[4]{0:T(128)} %get-tuple-element.48.n_live_ref, bf16[4,128,1024]{2,1,0:T(8,128)(2,1)} %constant_dynamic-update-slice_fusion.5.refs_0_, ...), custom_call_target="tpu_custom_call" | custom-call | flops 1073741824 | bytes 10485760 | tf_op jit(solution)/shard_map/pallas_call | solution.py:76
  146.7 1.2 slice.152
  147.9 2.7 %collective-permute-start.26 = (bf16[4,64,1024]{2,1,0:T(8,128)(2,1)}, bf16[4,64,1024]{2,1,0:T(8,128)(2,1)S(1)}, u32[]{:S(2)}, u32[]{:S(2)}) collective-permute-start(bf16[4,64,1024]{2,1,0:T(8,128)(2,1)} %get-tuple-element.24), channel_id=1, source_target_pairs={{0,3},{1,0},{2,1},{3,2},{4,7},{5,4},{6,5},{7,6},{8,11},{9,8},{10,9... | collective-permute-start | bytes 1572872 | tf_op jit(solution)/shard_map/ppermute | solution.py:111
  150.6 1.1 slice.153
  151.7 1.3 add_convert_fusion.5
  153.2 1.3 add_convert_fusion.4
  154.6 2.6 %collective-permute-start.11 = (bf16[4,128,1024]{2,1,0:T(8,128)(2,1)S(1)}, bf16[4,128,1024]{2,1,0:T(8,128)(2,1)S(1)}, u32[]{:S(2)}, u32[]{:S(2)}) collective-permute-start(bf16[4,128,1024]{2,1,0:T(8,128)(2,1)S(1)} %pad_maximum_fusion.1), channel_id=1, source_target_pairs={{0,12},{1,13},{2,14},{3,15},{4,0},{5,1},{6,2},{7,3},{8,4},{9,5},{1... | collective-permute-start | bytes 3145736 | tf_op jit(solution)/shard_map/ppermute | solution.py:111
  157.9 2.7 %collective-permute-start.27 = (bf16[4,128,1024]{2,1,0:T(8,128)(2,1)S(1)}, bf16[4,128,1024]{2,1,0:T(8,128)(2,1)S(1)}, u32[]{:S(2)}, u32[]{:S(2)}) collective-permute-start(bf16[4,128,1024]{2,1,0:T(8,128)(2,1)S(1)} %pad_maximum_fusion.3), channel_id=1, source_target_pairs={{0,3},{1,0},{2,1},{3,2},{4,7},{5,4},{6,5},{7,6},{8,11},{9,8},{10,9... | collective-permute-start | bytes 3145736 | tf_op jit(solution)/shard_map/ppermute | solution.py:111
  160.8 12.5 %collective-permute-done.9 = bf16[4,128,1024]{2,1,0:T(8,128)(2,1)S(1)} collective-permute-done((bf16[4,128,1024]{2,1,0:T(8,128)(2,1)S(1)}, bf16[4,128,1024]{2,1,0:T(8,128)(2,1)S(1)}, u32[]{:S(2)}, u32[]{:S(2)}) %collective-permute-start.9) | collective-permute-done | bytes 1048608 | tf_op jit(solution)/shard_map/ppermute | solution.py:111
  174.5 2.7 %collective-permute-start.14 = (bf16[4,16,1024]{2,1,0:T(8,128)(2,1)S(1)}, bf16[4,16,1024]{2,1,0:T(8,128)(2,1)S(1)}, u32[]{:S(2)}, u32[]{:S(2)}) collective-permute-start(bf16[4,16,1024]{2,1,0:T(8,128)(2,1)S(1)} %get-tuple-element.34), channel_id=1, source_target_pairs={{0,3},{1,0},{2,1},{3,2},{4,7},{5,4},{6,5},{7,6},{8,11},{9,8},{10,9... | collective-permute-start | bytes 393224 | tf_op jit(solution)/shard_map/ppermute | solution.py:111
  177.1 1.3 collective-permute-done.25
  179.2 6.8 %collective-permute-start.28 = (bf16[4,16,1024]{2,1,0:T(8,128)(2,1)S(1)}, bf16[4,16,1024]{2,1,0:T(8,128)(2,1)S(1)}, u32[]{:S(2)}, u32[]{:S(2)}) collective-permute-start(bf16[4,16,1024]{2,1,0:T(8,128)(2,1)S(1)} %get-tuple-element.37), channel_id=1, source_target_pairs={{0,4},{1,5},{2,6},{3,7},{4,8},{5,9},{6,10},{7,11},{8,12},{9,13},{1... | collective-permute-start | bytes 393224 | tf_op jit(solution)/shard_map/ppermute | solution.py:111
  186.2 3.5 %collective-permute-start.15 = (bf16[4,32,1024]{2,1,0:T(8,128)(2,1)S(1)}, bf16[4,32,1024]{2,1,0:T(8,128)(2,1)S(1)}, u32[]{:S(2)}, u32[]{:S(2)}) collective-permute-start(bf16[4,32,1024]{2,1,0:T(8,128)(2,1)S(1)} %get-tuple-element.32), channel_id=1, source_target_pairs={{0,3},{1,0},{2,1},{3,2},{4,7},{5,4},{6,5},{7,6},{8,11},{9,8},{10,9... | collective-permute-start | bytes 786440 | tf_op jit(solution)/shard_map/ppermute | solution.py:111
  189.9 2.0 collective-permute-start.29
  191.9 0.8 collective-permute-start.31
  192.7 1.0 collective-permute-done.13
  193.8 2.9 %collective-permute-done.29 = bf16[4,32,1024]{2,1,0:T(8,128)(2,1)S(1)} collective-permute-done((bf16[4,32,1024]{2,1,0:T(8,128)(2,1)S(1)}, bf16[4,32,1024]{2,1,0:T(8,128)(2,1)S(1)}, u32[]{:S(2)}, u32[]{:S(2)}) %collective-permute-start.29) | collective-permute-done | bytes 262176 | tf_op jit(solution)/shard_map/ppermute | solution.py:111
  196.7 0.8 collective-permute-done.31
  197.7 1.4 gather_fusion.6
  199.1 1.9 broadcast_select_fusion.1
  201.0 9.4 %all-to-all-start.1 = ((bf16[8,32,1024]{2,1,0:T(8,128)(2,1)}), bf16[8,32,1024]{2,1,0:T(8,128)(2,1)}, u32[]{:S(2)}, u32[]{:S(2)}) async-start(bf16[8,32,1024]{2,1,0:T(8,128)(2,1)} %broadcast_select_fusion.1), calls=%async_computation.1 | async-start | bytes 1048576 | tf_op jit(solution)/shard_map/all_to_all | solution.py:273
  210.5 3.5 %multiply_bitcast_fusion = f32[32,8,1024]{2,1,0:T(8,128)} fusion(bf16[1024,2048]{1,0:T(8,128)(2,1)} %param.12, bf16[32,8,1024]{2,1,0:T(8,128)(2,1)S(1)} %copy-done.4, f32[32,8]{1,0:T(8,128)S(1)} %copy.37, f32[32,8]{1,0:T(8,128)S(1)} %copy.35), kind=kOutput, calls=%fused_computation.35 | convolution fusion | flops 538968064 | bytes 3672064 | tf_op jit(solution)/shard_map/dot_general | solution.py:276
  213.9 6.0 %all-to-all-done.1 = bf16[8,32,1024]{2,1,0:T(8,128)(2,1)} async-done(((bf16[8,32,1024]{2,1,0:T(8,128)(2,1)}), bf16[8,32,1024]{2,1,0:T(8,128)(2,1)}, u32[]{:S(2)}, u32[]{:S(2)}) %all-to-all-start.1) | async-done | bytes 524320 | tf_op jit(solution)/shard_map/all_to_all | solution.py:273
  219.9 1.6 gather_fusion.7
  222.0 1.9 fusion.14
  223.9 1.6 fusion.7
  (123 shorter events, 11.8 us)
Async XLA Ops:
  0.0 223.9 %copy-start = (bf16[1024,1024]{1,0:T(8,128)(2,1)S(1)}, bf16[1024,1024]{1,0:T(8,128)(2,1)}, u32[]{:S(2)}) copy-start(bf16[1024,1024]{1,0:T(8,128)(2,1)} %param.13) | copy-start | bytes 6291460
  0.0 5.5 %copy-start.3 = (bf16[32,8,1024]{2,1,0:T(8,128)(2,1)S(1)}, bf16[32,8,1024]{2,1,0:T(8,128)(2,1)}, u32[]{:S(2)}) copy-start(bf16[32,8,1024]{2,1,0:T(8,128)(2,1)} %param.7) | copy-start | bytes 1572868
  10.2 23.5 %copy-start.1 = (s32[64]{0:T(128)S(1)}, s32[64]{0:T(128)}, u32[]{:S(2)}) copy-start(s32[64]{0:T(128)} %param.11) | copy-start | bytes 772
  10.2 15.4 %all-to-all-start = ((bf16[8,32,1024]{2,1,0:T(8,128)(2,1)}), bf16[8,32,1024]{2,1,0:T(8,128)(2,1)S(1)}, u32[]{:S(2)}, u32[]{:S(2)}) async-start(bf16[8,32,1024]{2,1,0:T(8,128)(2,1)} %broadcast_select_fusion), calls=%async_computation | async-start | bytes 1048576 | tf_op jit(solution)/shard_map/all_to_all | solution.py:252
  27.3 8.3 %collective-permute-start.1 = (bf16[4,32,1024]{2,1,0:T(8,128)(2,1)}, bf16[4,32,1024]{2,1,0:T(8,128)(2,1)S(1)}, u32[]{:S(2)}, u32[]{:S(2)}) collective-permute-start(bf16[4,32,1024]{2,1,0:T(8,128)(2,1)} %get-tuple-element.39), channel_id=1, source_target_pairs={{0,1},{1,2},{2,3},{3,0},{4,5},{5,6},{6,7},{7,4},{8,9},{9,10},{10,1... | collective-permute-start | bytes 786440 | tf_op jit(solution)/shard_map/ppermute | solution.py:111
  28.5 7.2 %collective-permute-start = (bf16[4,32,1024]{2,1,0:T(8,128)(2,1)}, bf16[4,32,1024]{2,1,0:T(8,128)(2,1)S(1)}, u32[]{:S(2)}, u32[]{:S(2)}) collective-permute-start(bf16[4,32,1024]{2,1,0:T(8,128)(2,1)} %get-tuple-element.39), channel_id=1, source_target_pairs={{0,3},{1,0},{2,1},{3,2},{4,7},{5,4},{6,5},{7,6},{8,11},{9,8},{10,9... | collective-permute-start | bytes 786440 | tf_op jit(solution)/shard_map/ppermute | solution.py:111
  30.0 8.9 %collective-permute-start.17 = (bf16[4,32,1024]{2,1,0:T(8,128)(2,1)S(1)}, bf16[4,32,1024]{2,1,0:T(8,128)(2,1)S(1)}, u32[]{:S(2)}, u32[]{:S(2)}) collective-permute-start(bf16[4,32,1024]{2,1,0:T(8,128)(2,1)S(1)} %get-tuple-element.42), channel_id=1, source_target_pairs={{0,4},{1,5},{2,6},{3,7},{4,8},{5,9},{6,10},{7,11},{8,12},{9,13},{1... | collective-permute-start | bytes 786440 | tf_op jit(solution)/shard_map/ppermute | solution.py:111
  31.6 8.6 %collective-permute-start.16 = (bf16[4,32,1024]{2,1,0:T(8,128)(2,1)S(1)}, bf16[4,32,1024]{2,1,0:T(8,128)(2,1)S(1)}, u32[]{:S(2)}, u32[]{:S(2)}) collective-permute-start(bf16[4,32,1024]{2,1,0:T(8,128)(2,1)S(1)} %get-tuple-element.42), channel_id=1, source_target_pairs={{0,12},{1,13},{2,14},{3,15},{4,0},{5,1},{6,2},{7,3},{8,4},{9,5},{1... | collective-permute-start | bytes 786440 | tf_op jit(solution)/shard_map/ppermute | solution.py:111
  35.6 8.3 %collective-permute-start.2 = (bf16[4,16,1024]{2,1,0:T(8,128)(2,1)S(1)}, bf16[4,16,1024]{2,1,0:T(8,128)(2,1)S(1)}, u32[]{:S(2)}, u32[]{:S(2)}) collective-permute-start(bf16[4,16,1024]{2,1,0:T(8,128)(2,1)S(1)} %slice.179), channel_id=1, source_target_pairs={{0,1},{1,2},{2,3},{3,0},{4,5},{5,6},{6,7},{7,4},{8,9},{9,10},{10,1... | collective-permute-start | bytes 393224 | tf_op jit(solution)/shard_map/ppermute | solution.py:111
  35.7 8.9 %collective-permute-start.3 = (bf16[4,16,1024]{2,1,0:T(8,128)(2,1)S(1)}, bf16[4,16,1024]{2,1,0:T(8,128)(2,1)S(1)}, u32[]{:S(2)}, u32[]{:S(2)}) collective-permute-start(bf16[4,16,1024]{2,1,0:T(8,128)(2,1)S(1)} %slice.180), channel_id=1, source_target_pairs={{0,3},{1,0},{2,1},{3,2},{4,7},{5,4},{6,5},{7,6},{8,11},{9,8},{10,9... | collective-permute-start | bytes 393224 | tf_op jit(solution)/shard_map/ppermute | solution.py:111
  38.9 9.8 %collective-permute-start.18 = (bf16[4,16,1024]{2,1,0:T(8,128)(2,1)S(1)}, bf16[4,16,1024]{2,1,0:T(8,128)(2,1)S(1)}, u32[]{:S(2)}, u32[]{:S(2)}) collective-permute-start(bf16[4,16,1024]{2,1,0:T(8,128)(2,1)S(1)} %slice.189), channel_id=1, source_target_pairs={{0,4},{1,5},{2,6},{3,7},{4,8},{5,9},{6,10},{7,11},{8,12},{9,13},{1... | collective-permute-start | bytes 393224 | tf_op jit(solution)/shard_map/ppermute | solution.py:111
  40.2 9.2 %collective-permute-start.19 = (bf16[4,16,1024]{2,1,0:T(8,128)(2,1)S(1)}, bf16[4,16,1024]{2,1,0:T(8,128)(2,1)S(1)}, u32[]{:S(2)}, u32[]{:S(2)}) collective-permute-start(bf16[4,16,1024]{2,1,0:T(8,128)(2,1)S(1)} %slice.190), channel_id=1, source_target_pairs={{0,12},{1,13},{2,14},{3,15},{4,0},{5,1},{6,2},{7,3},{8,4},{9,5},{1... | collective-permute-start | bytes 393224 | tf_op jit(solution)/shard_map/ppermute | solution.py:111
  46.0 23.6 %collective-permute-start.5 = (bf16[4,128,1024]{2,1,0:T(8,128)(2,1)}, bf16[4,128,1024]{2,1,0:T(8,128)(2,1)}, u32[]{:S(2)}, u32[]{:S(2)}) collective-permute-start(bf16[4,128,1024]{2,1,0:T(8,128)(2,1)} %constant_dynamic-update-slice_fusion.refs_0_), channel_id=1, source_target_pairs={{0,4},{1,5},{2,6},{3,7},{4,8},{5,9},{6,10},{7,11},{8,12},{9,13},{1... | collective-permute-start | bytes 3145736 | tf_op jit(solution)/shard_map/ppermute | solution.py:111
  46.0 24.7 %collective-permute-start.4 = (bf16[4,128,1024]{2,1,0:T(8,128)(2,1)}, bf16[4,128,1024]{2,1,0:T(8,128)(2,1)}, u32[]{:S(2)}, u32[]{:S(2)}) collective-permute-start(bf16[4,128,1024]{2,1,0:T(8,128)(2,1)} %constant_dynamic-update-slice_fusion.refs_0_), channel_id=1, source_target_pairs={{0,12},{1,13},{2,14},{3,15},{4,0},{5,1},{6,2},{7,3},{8,4},{9,5},{1... | collective-permute-start | bytes 3145736 | tf_op jit(solution)/shard_map/ppermute | solution.py:111
  50.8 24.5 %collective-permute-start.21 = (bf16[4,128,1024]{2,1,0:T(8,128)(2,1)}, bf16[4,128,1024]{2,1,0:T(8,128)(2,1)S(1)}, u32[]{:S(2)}, u32[]{:S(2)}) collective-permute-start(bf16[4,128,1024]{2,1,0:T(8,128)(2,1)} %constant_dynamic-update-slice_fusion.5.refs_0_), channel_id=1, source_target_pairs={{0,1},{1,2},{2,3},{3,0},{4,5},{5,6},{6,7},{7,4},{8,9},{9,10},{10,1... | collective-permute-start | bytes 3145736 | tf_op jit(solution)/shard_map/ppermute | solution.py:111
  50.8 25.4 %collective-permute-start.20 = (bf16[4,128,1024]{2,1,0:T(8,128)(2,1)}, bf16[4,128,1024]{2,1,0:T(8,128)(2,1)}, u32[]{:S(2)}, u32[]{:S(2)}) collective-permute-start(bf16[4,128,1024]{2,1,0:T(8,128)(2,1)} %constant_dynamic-update-slice_fusion.5.refs_0_), channel_id=1, source_target_pairs={{0,3},{1,0},{2,1},{3,2},{4,7},{5,4},{6,5},{7,6},{8,11},{9,8},{10,9... | collective-permute-start | bytes 3145736 | tf_op jit(solution)/shard_map/ppermute | solution.py:111
  70.7 11.3 %collective-permute-start.6 = (bf16[4,64,1024]{2,1,0:T(8,128)(2,1)S(1)}, bf16[4,64,1024]{2,1,0:T(8,128)(2,1)}, u32[]{:S(2)}, u32[]{:S(2)}) collective-permute-start(bf16[4,64,1024]{2,1,0:T(8,128)(2,1)S(1)} %slice.181), channel_id=1, source_target_pairs={{0,4},{1,5},{2,6},{3,7},{4,8},{5,9},{6,10},{7,11},{8,12},{9,13},{1... | collective-permute-start | bytes 1572872 | tf_op jit(solution)/shard_map/ppermute | solution.py:111
  71.9 10.2 %collective-permute-start.7 = (bf16[4,64,1024]{2,1,0:T(8,128)(2,1)S(1)}, bf16[4,64,1024]{2,1,0:T(8,128)(2,1)}, u32[]{:S(2)}, u32[]{:S(2)}) collective-permute-start(bf16[4,64,1024]{2,1,0:T(8,128)(2,1)S(1)} %slice.182), channel_id=1, source_target_pairs={{0,12},{1,13},{2,14},{3,15},{4,0},{5,1},{6,2},{7,3},{8,4},{9,5},{1... | collective-permute-start | bytes 1572872 | tf_op jit(solution)/shard_map/ppermute | solution.py:111
  75.3 36.5 %copy-start.2 = (bf16[4,128,1024]{2,1,0:T(8,128)(2,1)}, bf16[4,128,1024]{2,1,0:T(8,128)(2,1)S(1)}, u32[]{:S(2)}) copy-start(bf16[4,128,1024]{2,1,0:T(8,128)(2,1)S(1)} %collective-permute-done.21.refs_4_) | copy-start | bytes 3145732
  76.2 40.9 %collective-permute-start.22 = (bf16[4,64,1024]{2,1,0:T(8,128)(2,1)}, bf16[4,64,1024]{2,1,0:T(8,128)(2,1)}, u32[]{:S(2)}, u32[]{:S(2)}) collective-permute-start(bf16[4,64,1024]{2,1,0:T(8,128)(2,1)} %slice.191), channel_id=1, source_target_pairs={{0,1},{1,2},{2,3},{3,0},{4,5},{5,6},{6,7},{7,4},{8,9},{9,10},{10,1... | collective-permute-start | bytes 1572872 | tf_op jit(solution)/shard_map/ppermute | solution.py:111
  78.1 39.0 %collective-permute-start.23 = (bf16[4,64,1024]{2,1,0:T(8,128)(2,1)}, bf16[4,64,1024]{2,1,0:T(8,128)(2,1)}, u32[]{:S(2)}, u32[]{:S(2)}) collective-permute-start(bf16[4,64,1024]{2,1,0:T(8,128)(2,1)} %slice.192), channel_id=1, source_target_pairs={{0,3},{1,0},{2,1},{3,2},{4,7},{5,4},{6,5},{7,6},{8,11},{9,8},{10,9... | collective-permute-start | bytes 1572872 | tf_op jit(solution)/shard_map/ppermute | solution.py:111
  111.8 39.9 %collective-permute-start.8 = (bf16[4,64,1024]{2,1,0:T(8,128)(2,1)}, bf16[4,64,1024]{2,1,0:T(8,128)(2,1)}, u32[]{:S(2)}, u32[]{:S(2)}) collective-permute-start(bf16[4,64,1024]{2,1,0:T(8,128)(2,1)} %get-tuple-element.17), channel_id=1, source_target_pairs={{0,4},{1,5},{2,6},{3,7},{4,8},{5,9},{6,10},{7,11},{8,12},{9,13},{1... | collective-permute-start | bytes 1572872 | tf_op jit(solution)/shard_map/ppermute | solution.py:111
  112.1 41.1 %collective-permute-start.10 = (bf16[4,64,1024]{2,1,0:T(8,128)(2,1)}, bf16[4,64,1024]{2,1,0:T(8,128)(2,1)}, u32[]{:S(2)}, u32[]{:S(2)}) collective-permute-start(bf16[4,64,1024]{2,1,0:T(8,128)(2,1)} %get-tuple-element.19), channel_id=1, source_target_pairs={{0,12},{1,13},{2,14},{3,15},{4,0},{5,1},{6,2},{7,3},{8,4},{9,5},{1... | collective-permute-start | bytes 1572872 | tf_op jit(solution)/shard_map/ppermute | solution.py:111
  146.7 5.0 %copy-start.6 = (bf16[4,128,1024]{2,1,0:T(8,128)(2,1)S(1)}, bf16[4,128,1024]{2,1,0:T(8,128)(2,1)}, u32[]{:S(2)}) copy-start(bf16[4,128,1024]{2,1,0:T(8,128)(2,1)} %get-tuple-element.16) | copy-start | bytes 3145732
  146.7 10.6 %collective-permute-start.24 = (bf16[4,64,1024]{2,1,0:T(8,128)(2,1)}, bf16[4,64,1024]{2,1,0:T(8,128)(2,1)S(1)}, u32[]{:S(2)}, u32[]{:S(2)}) collective-permute-start(bf16[4,64,1024]{2,1,0:T(8,128)(2,1)} %get-tuple-element.22), channel_id=1, source_target_pairs={{0,1},{1,2},{2,3},{3,0},{4,5},{5,6},{6,7},{7,4},{8,9},{9,10},{10,1... | collective-permute-start | bytes 1572872 | tf_op jit(solution)/shard_map/ppermute | solution.py:111
  147.9 9.7 %collective-permute-start.26 = (bf16[4,64,1024]{2,1,0:T(8,128)(2,1)}, bf16[4,64,1024]{2,1,0:T(8,128)(2,1)S(1)}, u32[]{:S(2)}, u32[]{:S(2)}) collective-permute-start(bf16[4,64,1024]{2,1,0:T(8,128)(2,1)} %get-tuple-element.24), channel_id=1, source_target_pairs={{0,3},{1,0},{2,1},{3,2},{4,7},{5,4},{6,5},{7,6},{8,11},{9,8},{10,9... | collective-permute-start | bytes 1572872 | tf_op jit(solution)/shard_map/ppermute | solution.py:111
  151.6 1.6 copy-start.5
  153.1 4.2 %copy-start.8 = (bf16[4,128,1024]{2,1,0:T(8,128)(2,1)S(1)}, bf16[4,128,1024]{2,1,0:T(8,128)(2,1)}, u32[]{:S(2)}) copy-start(bf16[4,128,1024]{2,1,0:T(8,128)(2,1)} %get-tuple-element.21) | copy-start | bytes 3145732
  153.1 20.2 %collective-permute-start.9 = (bf16[4,128,1024]{2,1,0:T(8,128)(2,1)S(1)}, bf16[4,128,1024]{2,1,0:T(8,128)(2,1)S(1)}, u32[]{:S(2)}, u32[]{:S(2)}) collective-permute-start(bf16[4,128,1024]{2,1,0:T(8,128)(2,1)S(1)} %pad_maximum_fusion), channel_id=1, source_target_pairs={{0,4},{1,5},{2,6},{3,7},{4,8},{5,9},{6,10},{7,11},{8,12},{9,13},{1... | collective-permute-start | bytes 3145736 | tf_op jit(solution)/shard_map/ppermute | solution.py:111
  154.6 3.0 %copy-start.7 = (bf16[4,128,1024]{2,1,0:T(8,128)(2,1)S(1)}, bf16[4,128,1024]{2,1,0:T(8,128)(2,1)}, u32[]{:S(2)}) copy-start(bf16[4,128,1024]{2,1,0:T(8,128)(2,1)} %get-tuple-element.23) | copy-start | bytes 3145732
  154.6 19.1 %collective-permute-start.11 = (bf16[4,128,1024]{2,1,0:T(8,128)(2,1)S(1)}, bf16[4,128,1024]{2,1,0:T(8,128)(2,1)S(1)}, u32[]{:S(2)}, u32[]{:S(2)}) collective-permute-start(bf16[4,128,1024]{2,1,0:T(8,128)(2,1)S(1)} %pad_maximum_fusion.1), channel_id=1, source_target_pairs={{0,12},{1,13},{2,14},{3,15},{4,0},{5,1},{6,2},{7,3},{8,4},{9,5},{1... | collective-permute-start | bytes 3145736 | tf_op jit(solution)/shard_map/ppermute | solution.py:111
  157.5 16.2 %copy-start.9 = (bf16[4,128,1024]{2,1,0:T(8,128)(2,1)S(1)}, bf16[4,128,1024]{2,1,0:T(8,128)(2,1)}, u32[]{:S(2)}) copy-start(bf16[4,128,1024]{2,1,0:T(8,128)(2,1)} %get-tuple-element.15) | copy-start | bytes 3145732
  157.5 20.9 %collective-permute-start.25 = (bf16[4,128,1024]{2,1,0:T(8,128)(2,1)S(1)}, bf16[4,128,1024]{2,1,0:T(8,128)(2,1)S(1)}, u32[]{:S(2)}, u32[]{:S(2)}) collective-permute-start(bf16[4,128,1024]{2,1,0:T(8,128)(2,1)S(1)} %pad_maximum_fusion.2), channel_id=1, source_target_pairs={{0,1},{1,2},{2,3},{3,0},{4,5},{5,6},{6,7},{7,4},{8,9},{9,10},{10,1... | collective-permute-start | bytes 3145736 | tf_op jit(solution)/shard_map/ppermute | solution.py:111
  157.9 20.6 %collective-permute-start.27 = (bf16[4,128,1024]{2,1,0:T(8,128)(2,1)S(1)}, bf16[4,128,1024]{2,1,0:T(8,128)(2,1)S(1)}, u32[]{:S(2)}, u32[]{:S(2)}) collective-permute-start(bf16[4,128,1024]{2,1,0:T(8,128)(2,1)S(1)} %pad_maximum_fusion.3), channel_id=1, source_target_pairs={{0,3},{1,0},{2,1},{3,2},{4,7},{5,4},{6,5},{7,6},{8,11},{9,8},{10,9... | collective-permute-start | bytes 3145736 | tf_op jit(solution)/shard_map/ppermute | solution.py:111
  173.7 4.8 %copy-start.10 = (bf16[4,128,1024]{2,1,0:T(8,128)(2,1)S(1)}, bf16[4,128,1024]{2,1,0:T(8,128)(2,1)}, u32[]{:S(2)}) copy-start(bf16[4,128,1024]{2,1,0:T(8,128)(2,1)} %get-tuple-element.20) | copy-start | bytes 3145732
  174.4 11.6 %collective-permute-start.12 = (bf16[4,16,1024]{2,1,0:T(8,128)(2,1)S(1)}, bf16[4,16,1024]{2,1,0:T(8,128)(2,1)S(1)}, u32[]{:S(2)}, u32[]{:S(2)}) collective-permute-start(bf16[4,16,1024]{2,1,0:T(8,128)(2,1)S(1)} %get-tuple-element.33), channel_id=1, source_target_pairs={{0,1},{1,2},{2,3},{3,0},{4,5},{5,6},{6,7},{7,4},{8,9},{9,10},{10,1... | collective-permute-start | bytes 393224 | tf_op jit(solution)/shard_map/ppermute | solution.py:111
  174.5 11.5 %collective-permute-start.14 = (bf16[4,16,1024]{2,1,0:T(8,128)(2,1)S(1)}, bf16[4,16,1024]{2,1,0:T(8,128)(2,1)S(1)}, u32[]{:S(2)}, u32[]{:S(2)}) collective-permute-start(bf16[4,16,1024]{2,1,0:T(8,128)(2,1)S(1)} %get-tuple-element.34), channel_id=1, source_target_pairs={{0,3},{1,0},{2,1},{3,2},{4,7},{5,4},{6,5},{7,6},{8,11},{9,8},{10,9... | collective-permute-start | bytes 393224 | tf_op jit(solution)/shard_map/ppermute | solution.py:111
  179.2 10.5 %collective-permute-start.28 = (bf16[4,16,1024]{2,1,0:T(8,128)(2,1)S(1)}, bf16[4,16,1024]{2,1,0:T(8,128)(2,1)S(1)}, u32[]{:S(2)}, u32[]{:S(2)}) collective-permute-start(bf16[4,16,1024]{2,1,0:T(8,128)(2,1)S(1)} %get-tuple-element.37), channel_id=1, source_target_pairs={{0,4},{1,5},{2,6},{3,7},{4,8},{5,9},{6,10},{7,11},{8,12},{9,13},{1... | collective-permute-start | bytes 393224 | tf_op jit(solution)/shard_map/ppermute | solution.py:111
  186.0 3.8 %collective-permute-start.30 = (bf16[4,16,1024]{2,1,0:T(8,128)(2,1)S(1)}, bf16[4,16,1024]{2,1,0:T(8,128)(2,1)S(1)}, u32[]{:S(2)}, u32[]{:S(2)}) collective-permute-start(bf16[4,16,1024]{2,1,0:T(8,128)(2,1)S(1)} %get-tuple-element.38), channel_id=1, source_target_pairs={{0,12},{1,13},{2,14},{3,15},{4,0},{5,1},{6,2},{7,3},{8,4},{9,5},{1... | collective-permute-start | bytes 393224 | tf_op jit(solution)/shard_map/ppermute | solution.py:111
  186.1 7.5 %collective-permute-start.13 = (bf16[4,32,1024]{2,1,0:T(8,128)(2,1)S(1)}, bf16[4,32,1024]{2,1,0:T(8,128)(2,1)S(1)}, u32[]{:S(2)}, u32[]{:S(2)}) collective-permute-start(bf16[4,32,1024]{2,1,0:T(8,128)(2,1)S(1)} %get-tuple-element.31), channel_id=1, source_target_pairs={{0,1},{1,2},{2,3},{3,0},{4,5},{5,6},{6,7},{7,4},{8,9},{9,10},{10,1... | collective-permute-start | bytes 786440 | tf_op jit(solution)/shard_map/ppermute | solution.py:111
  186.2 7.5 %collective-permute-start.15 = (bf16[4,32,1024]{2,1,0:T(8,128)(2,1)S(1)}, bf16[4,32,1024]{2,1,0:T(8,128)(2,1)S(1)}, u32[]{:S(2)}, u32[]{:S(2)}) collective-permute-start(bf16[4,32,1024]{2,1,0:T(8,128)(2,1)S(1)} %get-tuple-element.32), channel_id=1, source_target_pairs={{0,3},{1,0},{2,1},{3,2},{4,7},{5,4},{6,5},{7,6},{8,11},{9,8},{10,9... | collective-permute-start | bytes 786440 | tf_op jit(solution)/shard_map/ppermute | solution.py:111
  189.9 6.8 %collective-permute-start.29 = (bf16[4,32,1024]{2,1,0:T(8,128)(2,1)S(1)}, bf16[4,32,1024]{2,1,0:T(8,128)(2,1)S(1)}, u32[]{:S(2)}, u32[]{:S(2)}) collective-permute-start(bf16[4,32,1024]{2,1,0:T(8,128)(2,1)S(1)} %get-tuple-element.35), channel_id=1, source_target_pairs={{0,4},{1,5},{2,6},{3,7},{4,8},{5,9},{6,10},{7,11},{8,12},{9,13},{1... | collective-permute-start | bytes 786440 | tf_op jit(solution)/shard_map/ppermute | solution.py:111
  191.9 5.6 %collective-permute-start.31 = (bf16[4,32,1024]{2,1,0:T(8,128)(2,1)S(1)}, bf16[4,32,1024]{2,1,0:T(8,128)(2,1)S(1)}, u32[]{:S(2)}, u32[]{:S(2)}) collective-permute-start(bf16[4,32,1024]{2,1,0:T(8,128)(2,1)S(1)} %get-tuple-element.36), channel_id=1, source_target_pairs={{0,12},{1,13},{2,14},{3,15},{4,0},{5,1},{6,2},{7,3},{8,4},{9,5},{1... | collective-permute-start | bytes 786440 | tf_op jit(solution)/shard_map/ppermute | solution.py:111
  197.6 12.8 %copy-start.4 = (bf16[32,8,1024]{2,1,0:T(8,128)(2,1)S(1)}, bf16[32,8,1024]{2,1,0:T(8,128)(2,1)}, u32[]{:S(2)}) copy-start(bf16[32,8,1024]{2,1,0:T(8,128)(2,1)} %param.7) | copy-start | bytes 1572868
  201.0 18.9 %all-to-all-start.1 = ((bf16[8,32,1024]{2,1,0:T(8,128)(2,1)}), bf16[8,32,1024]{2,1,0:T(8,128)(2,1)}, u32[]{:S(2)}, u32[]{:S(2)}) async-start(bf16[8,32,1024]{2,1,0:T(8,128)(2,1)} %broadcast_select_fusion.1), calls=%async_computation.1 | async-start | bytes 1048576 | tf_op jit(solution)/shard_map/all_to_all | solution.py:273

commit v7 on v3

--- a/solution.py
+++ b/solution.py
@@ -33,9 +33,8 @@
     return (target, arrival, slot_of_pos)
 
 
-def attend_kernel(n_live_ref, q_ref, kv_ref, keep_ref, o_ref, *, heads, head_dim, scale):
+def attend_kernel(n_live_ref, q_ref, kt_ref, v_ref, keep_ref, o_ref, *, heads, head_dim, scale):
     row = pl.program_id(0)
-    width = heads * head_dim
 
     @pl.when(n_live_ref[row] <= 0)
     def _():
@@ -47,9 +46,9 @@
         for h in range(heads):
             lo = h * head_dim
             q = q_ref[0, :, lo:lo + head_dim]
-            k = kv_ref[0, :, lo:lo + head_dim]
-            v = kv_ref[0, :, width + lo:width + lo + head_dim]
-            s = lax.dot_general(q, k, (((1,), (1,)), ((), ())), preferred_element_type=jnp.float32)
+            kt = kt_ref[0, lo:lo + head_dim, :]
+            v = v_ref[0, :, lo:lo + head_dim]
+            s = jnp.dot(q, kt, preferred_element_type=jnp.float32)
             w = (jax.nn.silu(s * scale) * keep).astype(jnp.bfloat16)
             o = jnp.dot(w, v, preferred_element_type=jnp.float32)
             o_ref[0, :, lo:lo + head_dim] = o.astype(o_ref.dtype)
@@ -59,6 +58,7 @@
     rows, cands, width = queries.shape
     count = piece.shape[1]
     head_dim = width // heads
+    keys_t = jnp.swapaxes(piece[:, :, :width], 1, 2)
     events = (first_event + jnp.arange(count)).astype(jnp.float32)
     keep = ((events[None, :] < live[:, None]).astype(jnp.float32) / live[:, None])[:, None, :]
     n_live = jnp.clip(live.astype(jnp.int32) - first_event, 0, count).astype(jnp.int32)
@@ -72,7 +72,8 @@
             grid=(rows,),
             in_specs=[
                 pl.BlockSpec((1, cands, width), lambda r, n: (r, 0, 0)),
-                pl.BlockSpec((1, count, 2 * width), lambda r, n: (r, 0, 0)),
+                pl.BlockSpec((1, width, count), lambda r, n: (r, 0, 0)),
+                pl.BlockSpec((1, count, width), lambda r, n: (r, 0, 1)),
                 pl.BlockSpec((1, 1, count), lambda r, n: (r, 0, 0)),
             ],
             out_specs=pl.BlockSpec((1, cands, width), lambda r, n: (r, 0, 0)),
@@ -82,7 +83,7 @@
             transcendentals=rows * cands * count * heads,
             bytes_accessed=rows * (cands * width * 4 + count * width * 4),
         ),
-    )(n_live, queries, piece, keep)
+    )(n_live, queries, keys_t, piece, keep)
 
 
 def shift_perm(grid, axis, shift):

time: 193 us -> 209 us (1.083)
  local copies, waits for them, and re-layouts: 35.8 us -> 56.1 us
  waiting for transfers between devices: 55 us -> 50.2 us
    unnamed x25 -> x31, local copies, waits for them, and re-layouts: 14.3 us -> 23.8 us
    slice x0 -> x1, local copies, waits for them, and re-layouts: none -> 2.74 us  [attend_local(): keys_t = jnp.swapaxes(piece[:, :, :width], 1, 2)]
    all_to_all x1, waiting for transfers between devices: 8.62 us -> 5.98 us  [on_device(): lax.all_to_all(q_out, 'group', split_axis=0, concat_axis=0, tiled=True)]
    ppermute x32, waiting for transfers between devices: 39.2 us -> 37.1 us  [send(): return lax.ppermute(value, 'member', shift_perm(grid, axis, shift))]
    slice x4, local copies, waits for them, and re-layouts: 0.88 us -> 2.99 us  [ring_gather(): second = send(ahead[:, half:], grid, axis, -1)]
  transfers between devices with their start and end apart: 34 -> 34, of which waited for: 11 -> 11; matrix products, arithmetic and copies ran while one was open for 18% -> 24% of each run, Pallas kernels for 8% -> 7%
where the time goes in v7:
time: 209 us; the launch traced here: 208 us
  starting transfers between devices  64 us (31%)
  local copies, waits for them, and re-layouts  56.1 us (27%)
  waiting for transfers between devices  50.2 us (24%)
  other arithmetic  16.7 us (8%)
  Pallas kernels  14.7 us (7%)
  matrix products  5.47 us (3%)
    ppermute x32, starting transfers between devices, send(): return lax.ppermute(value, 'member', shift_perm(grid, axis, shift))  41.4 us
    ppermute x32, waiting for transfers between devices, send(): return lax.ppermute(value, 'member', shift_perm(grid, axis, shift))  37.1 us
    unnamed x31, local copies, waits for them, and re-layouts  23.8 us
    all_to_all x1, starting transfers between devices, on_device(): lax.all_to_all(a_out, 'group', split_axis=0, concat_axis=0, tiled=True)  16.6 us
    pallas_call x2, Pallas kernels, attend_local(): pl.pallas_call(kernel, out_shape=jax.ShapeDtypeStruct((rows, cands, width...  14.7 us
    all_to_all x1, waiting for transfers between devices, on_device(): lax.all_to_all(a_out, 'group', split_axis=0, concat_axis=0, tiled=True)  7.15 us
    all_to_all x1, waiting for transfers between devices, on_device(): lax.all_to_all(q_out, 'group', split_axis=0, concat_axis=0, tiled=True)  5.98 us
    all_to_all x1, starting transfers between devices, on_device(): lax.all_to_all(q_out, 'group', split_axis=0, concat_axis=0, tiled=True)  5.96 us
  transfers between devices with their start and end apart: 34, of which 11 were waited for; matrix products, arithmetic and copies ran while one was open for 24% of the time, Pallas kernels for 7%

profile of v7, /device:TPU:1, one launch (start us, length us, event | category | flops | bytes accessed | tf_op | source)
XLA Modules:
  0.0 207.6 jit_solution(15294076062187315960)
XLA Ops:
  0.0 1.0 fusion.30
  1.0 1.3 gather_fusion
  4.1 1.2 convert_reduce_fusion
  5.5 1.3 fusion.4
  7.0 3.8 %divide_multiply_fusion = f32[256,2048]{1,0:T(8,128)S(1)} fusion(bf16[1024,2048]{1,0:T(8,128)(2,1)} %param.12, bf16[32,8,1024]{2,1,0:T(8,128)(2,1)} %param.7, f32[32,8]{1,0:T(8,128)S(1)} %copy.47, f32[32,8]{1,0:T(8,128)S(1)} %copy.45), kind=kOutput, calls=%fused_computation.14 | convolution fusion | flops 1076887552 | bytes 6817792 | tf_op jit(solution)/shard_map/dot_general | solution.py:198
  13.6 6.0 %all-to-all-start = ((bf16[8,32,1024]{2,1,0:T(8,128)(2,1)}), bf16[8,32,1024]{2,1,0:T(8,128)(2,1)}, u32[]{:S(2)}, u32[]{:S(2)}) async-start(bf16[8,32,1024]{2,1,0:T(8,128)(2,1)} %broadcast_select_fusion), calls=%async_computation | async-start | bytes 1048576 | tf_op jit(solution)/shard_map/all_to_all | solution.py:205
  20.3 2.7 %fusion.48 = (bf16[4,128,1024]{2,1,0:T(8,128)(2,1)}, bf16[4,128,1024]{2,1,0:T(8,128)(2,1)S(1)}) fusion(bf16[8,128,2048]{2,1,0:T(8,128)(2,1)} %param.8), kind=kLoop, calls=%fused_computation.157 | loop fusion | bytes 4194304 | tf_op jit(solution)/shard_map/slice | solution.py:61
  23.0 6.0 %all-to-all-done = bf16[8,32,1024]{2,1,0:T(8,128)(2,1)} async-done(((bf16[8,32,1024]{2,1,0:T(8,128)(2,1)}), bf16[8,32,1024]{2,1,0:T(8,128)(2,1)}, u32[]{:S(2)}, u32[]{:S(2)}) %all-to-all-start) | async-done | bytes 524320 | tf_op jit(solution)/shard_map/all_to_all | solution.py:205
  29.0 2.4 %gather_fusion.5 = bf16[8,32,1024]{2,1,0:T(8,128)(2,1)} fusion(bf16[8,32,1024]{2,1,0:T(8,128)(2,1)} %all-to-all-done, s32[1024]{0:T(1024)S(1)} %pad_clamp_fusion.2), kind=kCustom, calls=%fused_computation.5 | custom fusion | bytes 1048608 | tf_op jit(solution)/shard_map/gather | solution.py:206
  31.4 2.4 %constant_dynamic-update-slice_fusion.4 = (bf16[4,128,1024]{2,1,0:T(8,128)(2,1)}, bf16[4,512,1024]{2,1,0:T(8,128)(2,1)}, bf16[4,128,1024]{2,1,0:T(8,128)(2,1)}, ...) fusion(bf16[8,32,1024]{2,1,0:T(8,128)(2,1)} %gather_fusion.5), kind=kLoop, calls=%fused_computation.63 | loop fusion | bytes 2097152
  33.8 1.2 collective-permute-start.1
  35.0 1.5 collective-permute-start
  36.4 3.8 %collective-permute-start.16 = (bf16[4,32,1024]{2,1,0:T(8,128)(2,1)}, bf16[4,32,1024]{2,1,0:T(8,128)(2,1)S(1)}, u32[]{:S(2)}, u32[]{:S(2)}) collective-permute-start(bf16[4,32,1024]{2,1,0:T(8,128)(2,1)} %get-tuple-element.38), channel_id=1, source_target_pairs={{0,12},{1,13},{2,14},{3,15},{4,0},{5,1},{6,2},{7,3},{8,4},{9,5},{1... | collective-permute-start | bytes 786440 | tf_op jit(solution)/shard_map/ppermute | solution.py:103
  40.3 1.8 collective-permute-done.1
  42.2 2.7 %collective-permute-start.3 = (bf16[4,16,1024]{2,1,0:T(8,128)(2,1)S(1)}, bf16[4,16,1024]{2,1,0:T(8,128)(2,1)S(1)}, u32[]{:S(2)}, u32[]{:S(2)}) collective-permute-start(bf16[4,16,1024]{2,1,0:T(8,128)(2,1)S(1)} %slice.188), channel_id=1, source_target_pairs={{0,3},{1,0},{2,1},{3,2},{4,7},{5,4},{6,5},{7,6},{8,11},{9,8},{10,9... | collective-permute-start | bytes 393224 | tf_op jit(solution)/shard_map/ppermute | solution.py:103
  44.9 2.8 %collective-permute-done.17 = bf16[4,32,1024]{2,1,0:T(8,128)(2,1)S(1)} collective-permute-done((bf16[4,32,1024]{2,1,0:T(8,128)(2,1)}, bf16[4,32,1024]{2,1,0:T(8,128)(2,1)S(1)}, u32[]{:S(2)}, u32[]{:S(2)}) %collective-permute-start.17) | collective-permute-done | bytes 262176 | tf_op jit(solution)/shard_map/ppermute | solution.py:103
  47.8 2.7 %collective-permute-start.19 = (bf16[4,16,1024]{2,1,0:T(8,128)(2,1)S(1)}, bf16[4,16,1024]{2,1,0:T(8,128)(2,1)S(1)}, u32[]{:S(2)}, u32[]{:S(2)}) collective-permute-start(bf16[4,16,1024]{2,1,0:T(8,128)(2,1)S(1)} %slice.203), channel_id=1, source_target_pairs={{0,12},{1,13},{2,14},{3,15},{4,0},{5,1},{6,2},{7,3},{8,4},{9,5},{1... | collective-permute-start | bytes 393224 | tf_op jit(solution)/shard_map/ppermute | solution.py:103
  54.8 2.7 %collective-permute-start.4 = (bf16[4,128,1024]{2,1,0:T(8,128)(2,1)}, bf16[4,128,1024]{2,1,0:T(8,128)(2,1)}, u32[]{:S(2)}, u32[]{:S(2)}) collective-permute-start(bf16[4,128,1024]{2,1,0:T(8,128)(2,1)} %get-tuple-element.39), channel_id=1, source_target_pairs={{0,12},{1,13},{2,14},{3,15},{4,0},{5,1},{6,2},{7,3},{8,4},{9,5},{1... | collective-permute-start | bytes 3145736 | tf_op jit(solution)/shard_map/ppermute | solution.py:103
  59.0 0.9 constant_dynamic-update-slice_fusion.14
  59.9 1.3 collective-permute-start.20
  61.4 2.5 %fusion.47 = (bf16[4,128,2048]{2,1,0:T(8,128)(2,1)}, bf16[4,128,2048]{2,1,0:T(8,128)(2,1)}) fusion(bf16[8,128,2048]{2,1,0:T(8,128)(2,1)S(1)} %copy-done.3), kind=kLoop, calls=%fused_computation.156 | loop fusion | bytes 8388608 | tf_op jit(solution)/shard_map/slice | solution.py:213
  63.9 13.0 %collective-permute-done.5 = bf16[4,128,1024]{2,1,0:T(8,128)(2,1)S(1)} collective-permute-done((bf16[4,128,1024]{2,1,0:T(8,128)(2,1)}, bf16[4,128,1024]{2,1,0:T(8,128)(2,1)S(1)}, u32[]{:S(2)}, u32[]{:S(2)}) %collective-permute-start.5) | collective-permute-done | bytes 1048608 | tf_op jit(solution)/shard_map/ppermute | solution.py:103
  76.9 1.0 copy-done.4
  79.4 2.3 %copy.55 = bf16[4,128,1024]{1,2,0:T(8,128)(2,1)} copy(bf16[4,128,1024]{2,1,0:T(8,128)(2,1)} %get-tuple-element.19) | data formatting | bytes 2097152
  81.7 1.3 copy.56
  83.0 1.1 slice.190
  84.1 2.7 %collective-permute-start.7 = (bf16[4,64,1024]{2,1,0:T(8,128)(2,1)S(1)}, bf16[4,64,1024]{2,1,0:T(8,128)(2,1)S(1)}, u32[]{:S(2)}, u32[]{:S(2)}) collective-permute-start(bf16[4,64,1024]{2,1,0:T(8,128)(2,1)S(1)} %slice.190), channel_id=1, source_target_pairs={{0,12},{1,13},{2,14},{3,15},{4,0},{5,1},{6,2},{7,3},{8,4},{9,5},{1... | collective-permute-start | bytes 1572872 | tf_op jit(solution)/shard_map/ppermute | solution.py:103
  87.4 2.0 slice.204
  89.4 1.9 slice.205
  91.3 2.7 %collective-permute-start.23 = (bf16[4,64,1024]{2,1,0:T(8,128)(2,1)}, bf16[4,64,1024]{2,1,0:T(8,128)(2,1)}, u32[]{:S(2)}, u32[]{:S(2)}) collective-permute-start(bf16[4,64,1024]{2,1,0:T(8,128)(2,1)} %slice.205), channel_id=1, source_target_pairs={{0,3},{1,0},{2,1},{3,2},{4,7},{5,4},{6,5},{7,6},{8,11},{9,8},{10,9... | collective-permute-start | bytes 1572872 | tf_op jit(solution)/shard_map/ppermute | solution.py:103
  94.0 2.3 %constant_dynamic-update-slice_fusion.8 = bf16[4,512,1024]{2,1,0:T(8,128)(2,1)} fusion(bf16[4,512,1024]{2,1,0:T(8,128)(2,1)} %get-tuple-element.40, bf16[4,128,1024]{2,1,0:T(8,128)(2,1)} %collective-permute-done.4), kind=kLoop, calls=%fused_computation.67 | loop fusion | bytes 2097152
  96.2 2.3 %constant_dynamic-update-slice_fusion.22 = bf16[4,512,1024]{2,1,0:T(8,128)(2,1)} fusion(bf16[4,512,1024]{2,1,0:T(8,128)(2,1)} %get-tuple-element.44, bf16[4,128,1024]{2,1,0:T(8,128)(2,1)} %collective-permute-done.20), kind=kLoop, calls=%fused_computation.81 | loop fusion | bytes 2097152
  98.5 1.9 constant_dynamic-update-slice_fusion.7
  101.2 1.1 constant_dynamic-update-slice_fusion.5.q_ref
  102.3 7.3 %shard_map.73 = bf16[4,512,1024]{2,1,0:T(8,128)(2,1)} custom-call(s32[4]{0:T(128)} %get-tuple-element.59.n_live_ref, bf16[4,512,1024]{2,1,0:T(8,128)(2,1)} %constant_dynamic-update-slice_fusion.5.q_ref, bf16[4,1024,128]{2,1,0:T(8,128)(2,1)} %bitcast.74, bf16[4,128,2048]{2,1,0:T(8,128)(2,1)} %get-tuple-element.17.v_ref, f32[4,1,128]{2,1,0:T(1,128)} %get-tuple-element.55.keep_ref), custom_call_target="tpu_custom_call" | custom-call | flops 1073741824 | bytes 10485760 | tf_op jit(solution)/shard_map/pallas_call | solution.py:67
  109.6 2.3 %fusion.46 = (bf16[4,64,1024]{2,1,0:T(8,128)(2,1)}, bf16[4,64,1024]{2,1,0:T(8,128)(2,1)}) fusion(bf16[4,512,1024]{2,1,0:T(8,128)(2,1)} %shard_map.73), kind=kLoop, calls=%fused_computation.155 | loop fusion | bytes 2097152 | tf_op jit(solution)/shard_map/slice | solution.py:139
  111.9 1.5 collective-permute-start.8
  113.4 1.9 constant_dynamic-update-slice_fusion.21
  115.3 1.9 constant_dynamic-update-slice_fusion.20
  117.2 2.3 %constant_dynamic-update-slice_fusion.19.q_ref = bf16[4,512,1024]{2,1,0:T(8,128)(2,1)} fusion(bf16[4,512,1024]{2,1,0:T(8,128)(2,1)} %constant_dynamic-update-slice_fusion.20, bf16[4,128,1024]{2,1,0:T(8,128)(2,1)} %collective-permute-done.21), kind=kLoop, calls=%fused_computation.78 | loop fusion | bytes 2097152 | tf_op jit(solution)/shard_map/concatenate | solution.py:122
  119.5 7.4 %shard_map.74 = bf16[4,512,1024]{2,1,0:T(8,128)(2,1)} custom-call(s32[4]{0:T(128)} %get-tuple-element.60.n_live_ref, bf16[4,512,1024]{2,1,0:T(8,128)(2,1)} %constant_dynamic-update-slice_fusion.19.q_ref, bf16[4,1024,128]{2,1,0:T(8,128)(2,1)} %bitcast.73, bf16[4,128,2048]{2,1,0:T(8,128)(2,1)} %get-tuple-element.18.v_ref, f32[4,1,128]{2,1,0:T(1,128)} %get-tuple-element.56.keep_ref), custom_call_target="tpu_custom_call" | custom-call | flops 1073741824 | bytes 10485760 | tf_op jit(solution)/shard_map/pallas_call | solution.py:67
  126.8 1.5 fusion.49
  128.4 2.7 %collective-permute-start.26 = (bf16[4,64,1024]{2,1,0:T(8,128)(2,1)S(1)}, bf16[4,64,1024]{2,1,0:T(8,128)(2,1)S(1)}, u32[]{:S(2)}, u32[]{:S(2)}) collective-permute-start(bf16[4,64,1024]{2,1,0:T(8,128)(2,1)S(1)} %get-tuple-element.24), channel_id=1, source_target_pairs={{0,3},{1,0},{2,1},{3,2},{4,7},{5,4},{6,5},{7,6},{8,11},{9,8},{10,9... | collective-permute-start | bytes 1572872 | tf_op jit(solution)/shard_map/ppermute | solution.py:103
  131.1 2.1 add_convert_fusion.3
  133.3 1.4 collective-permute-start.9
  134.7 2.9 %collective-permute-done.24 = bf16[4,64,1024]{2,1,0:T(8,128)(2,1)S(1)} collective-permute-done((bf16[4,64,1024]{2,1,0:T(8,128)(2,1)S(1)}, bf16[4,64,1024]{2,1,0:T(8,128)(2,1)S(1)}, u32[]{:S(2)}, u32[]{:S(2)}) %collective-permute-start.24) | collective-permute-done | bytes 524320 | tf_op jit(solution)/shard_map/ppermute | solution.py:103
  138.4 2.7 %collective-permute-start.27 = (bf16[4,128,1024]{2,1,0:T(8,128)(2,1)S(1)}, bf16[4,128,1024]{2,1,0:T(8,128)(2,1)S(1)}, u32[]{:S(2)}, u32[]{:S(2)}) collective-permute-start(bf16[4,128,1024]{2,1,0:T(8,128)(2,1)S(1)} %get-tuple-element.22), channel_id=1, source_target_pairs={{0,3},{1,0},{2,1},{3,2},{4,7},{5,4},{6,5},{7,6},{8,11},{9,8},{10,9... | collective-permute-start | bytes 3145736 | tf_op jit(solution)/shard_map/ppermute | solution.py:103
  141.4 10.3 %collective-permute-done.11 = bf16[4,128,1024]{2,1,0:T(8,128)(2,1)S(1)} collective-permute-done((bf16[4,128,1024]{2,1,0:T(8,128)(2,1)S(1)}, bf16[4,128,1024]{2,1,0:T(8,128)(2,1)S(1)}, u32[]{:S(2)}, u32[]{:S(2)}) %collective-permute-start.11) | collective-permute-done | bytes 1048608 | tf_op jit(solution)/shard_map/ppermute | solution.py:103
  151.7 1.0 collective-permute-done.9
  152.7 1.9 fusion.44
  154.7 2.7 %collective-permute-start.14 = (bf16[4,16,1024]{2,1,0:T(8,128)(2,1)S(1)}, bf16[4,16,1024]{2,1,0:T(8,128)(2,1)S(1)}, u32[]{:S(2)}, u32[]{:S(2)}) collective-permute-start(bf16[4,16,1024]{2,1,0:T(8,128)(2,1)S(1)} %get-tuple-element.30), channel_id=1, source_target_pairs={{0,3},{1,0},{2,1},{3,2},{4,7},{5,4},{6,5},{7,6},{8,11},{9,8},{10,9... | collective-permute-start | bytes 393224 | tf_op jit(solution)/shard_map/ppermute | solution.py:103
  157.4 1.6 collective-permute-done.25
  159.8 2.7 %collective-permute-start.30 = (bf16[4,16,1024]{2,1,0:T(8,128)(2,1)S(1)}, bf16[4,16,1024]{2,1,0:T(8,128)(2,1)S(1)}, u32[]{:S(2)}, u32[]{:S(2)}) collective-permute-start(bf16[4,16,1024]{2,1,0:T(8,128)(2,1)S(1)} %get-tuple-element.32), channel_id=1, source_target_pairs={{0,12},{1,13},{2,14},{3,15},{4,0},{5,1},{6,2},{7,3},{8,4},{9,5},{1... | collective-permute-start | bytes 393224 | tf_op jit(solution)/shard_map/ppermute | solution.py:103
  162.7 2.9 %collective-permute-start.15 = (bf16[4,32,1024]{2,1,0:T(8,128)(2,1)S(1)}, bf16[4,32,1024]{2,1,0:T(8,128)(2,1)S(1)}, u32[]{:S(2)}, u32[]{:S(2)}) collective-permute-start(bf16[4,32,1024]{2,1,0:T(8,128)(2,1)S(1)} %get-tuple-element.26), channel_id=1, source_target_pairs={{0,3},{1,0},{2,1},{3,2},{4,7},{5,4},{6,5},{7,6},{8,11},{9,8},{10,9... | collective-permute-start | bytes 786440 | tf_op jit(solution)/shard_map/ppermute | solution.py:103
  165.9 2.7 %collective-permute-start.31 = (bf16[4,32,1024]{2,1,0:T(8,128)(2,1)S(1)}, bf16[4,32,1024]{2,1,0:T(8,128)(2,1)S(1)}, u32[]{:S(2)}, u32[]{:S(2)}) collective-permute-start(bf16[4,32,1024]{2,1,0:T(8,128)(2,1)S(1)} %get-tuple-element.28), channel_id=1, source_target_pairs={{0,12},{1,13},{2,14},{3,15},{4,0},{5,1},{6,2},{7,3},{8,4},{9,5},{1... | collective-permute-start | bytes 786440 | tf_op jit(solution)/shard_map/ppermute | solution.py:103
  168.5 3.3 %collective-permute-done.13 = bf16[4,32,1024]{2,1,0:T(8,128)(2,1)S(1)} collective-permute-done((bf16[4,32,1024]{2,1,0:T(8,128)(2,1)S(1)}, bf16[4,32,1024]{2,1,0:T(8,128)(2,1)S(1)}, u32[]{:S(2)}, u32[]{:S(2)}) %collective-permute-start.13) | collective-permute-done | bytes 262176 | tf_op jit(solution)/shard_map/ppermute | solution.py:103
  172.4 1.4 gather_fusion.6
  173.8 2.0 broadcast_select_fusion.1
  175.8 16.6 %all-to-all-start.1 = ((bf16[8,32,1024]{2,1,0:T(8,128)(2,1)}), bf16[8,32,1024]{2,1,0:T(8,128)(2,1)}, u32[]{:S(2)}, u32[]{:S(2)}) async-start(bf16[8,32,1024]{2,1,0:T(8,128)(2,1)} %broadcast_select_fusion.1), calls=%async_computation.1 | async-start | bytes 1048576 | tf_op jit(solution)/shard_map/all_to_all | solution.py:219
  192.5 2.3 %slice_bitcast_fusion = f32[32,8,1024]{2,1,0:T(8,128)} fusion(f32[256,2048]{1,0:T(8,128)} %copy-done.7), kind=kLoop, calls=%fused_computation.25 | loop fusion | bytes 2097152 | tf_op jit(solution)/shard_map/reshape | solution.py:199
  194.8 7.2 %all-to-all-done.1 = bf16[8,32,1024]{2,1,0:T(8,128)(2,1)} async-done(((bf16[8,32,1024]{2,1,0:T(8,128)(2,1)}), bf16[8,32,1024]{2,1,0:T(8,128)(2,1)}, u32[]{:S(2)}, u32[]{:S(2)}) %all-to-all-start.1) | async-done | bytes 524320 | tf_op jit(solution)/shard_map/all_to_all | solution.py:219
  201.9 1.6 gather_fusion.7
  204.0 1.9 fusion.10
  205.9 1.7 fusion.3
  (121 shorter events, 18.5 us)
Async XLA Ops:
  0.0 205.9 %copy-start = (bf16[1024,1024]{1,0:T(8,128)(2,1)S(1)}, bf16[1024,1024]{1,0:T(8,128)(2,1)}, u32[]{:S(2)}) copy-start(bf16[1024,1024]{1,0:T(8,128)(2,1)} %param.13) | copy-start | bytes 6291460
  10.8 1.3 copy-start.7
  10.8 8.8 %copy-start.1 = (s32[64]{0:T(128)S(1)}, s32[64]{0:T(128)}, u32[]{:S(2)}) copy-start(s32[64]{0:T(128)} %param.11) | copy-start | bytes 772
  13.6 15.4 %all-to-all-start = ((bf16[8,32,1024]{2,1,0:T(8,128)(2,1)}), bf16[8,32,1024]{2,1,0:T(8,128)(2,1)}, u32[]{:S(2)}, u32[]{:S(2)}) async-start(bf16[8,32,1024]{2,1,0:T(8,128)(2,1)} %broadcast_select_fusion), calls=%async_computation | async-start | bytes 1048576 | tf_op jit(solution)/shard_map/all_to_all | solution.py:205
  33.8 8.3 %collective-permute-start.1 = (bf16[4,32,1024]{2,1,0:T(8,128)(2,1)}, bf16[4,32,1024]{2,1,0:T(8,128)(2,1)S(1)}, u32[]{:S(2)}, u32[]{:S(2)}) collective-permute-start(bf16[4,32,1024]{2,1,0:T(8,128)(2,1)} %get-tuple-element.37), channel_id=1, source_target_pairs={{0,1},{1,2},{2,3},{3,0},{4,5},{5,6},{6,7},{7,4},{8,9},{9,10},{10,1... | collective-permute-start | bytes 786440 | tf_op jit(solution)/shard_map/ppermute | solution.py:103
  35.0 26.4 %copy-start.3 = (bf16[8,128,2048]{2,1,0:T(8,128)(2,1)S(1)}, bf16[8,128,2048]{2,1,0:T(8,128)(2,1)}, u32[]{:S(2)}) copy-start(bf16[8,128,2048]{2,1,0:T(8,128)(2,1)} %param.8) | copy-start | bytes 12582916
  35.0 7.2 %collective-permute-start = (bf16[4,32,1024]{2,1,0:T(8,128)(2,1)}, bf16[4,32,1024]{2,1,0:T(8,128)(2,1)S(1)}, u32[]{:S(2)}, u32[]{:S(2)}) collective-permute-start(bf16[4,32,1024]{2,1,0:T(8,128)(2,1)} %get-tuple-element.37), channel_id=1, source_target_pairs={{0,3},{1,0},{2,1},{3,2},{4,7},{5,4},{6,5},{7,6},{8,11},{9,8},{10,9... | collective-permute-start | bytes 786440 | tf_op jit(solution)/shard_map/ppermute | solution.py:103
  36.4 11.3 %collective-permute-start.16 = (bf16[4,32,1024]{2,1,0:T(8,128)(2,1)}, bf16[4,32,1024]{2,1,0:T(8,128)(2,1)S(1)}, u32[]{:S(2)}, u32[]{:S(2)}) collective-permute-start(bf16[4,32,1024]{2,1,0:T(8,128)(2,1)} %get-tuple-element.38), channel_id=1, source_target_pairs={{0,12},{1,13},{2,14},{3,15},{4,0},{5,1},{6,2},{7,3},{8,4},{9,5},{1... | collective-permute-start | bytes 786440 | tf_op jit(solution)/shard_map/ppermute | solution.py:103
  40.2 7.5 %collective-permute-start.17 = (bf16[4,32,1024]{2,1,0:T(8,128)(2,1)}, bf16[4,32,1024]{2,1,0:T(8,128)(2,1)S(1)}, u32[]{:S(2)}, u32[]{:S(2)}) collective-permute-start(bf16[4,32,1024]{2,1,0:T(8,128)(2,1)} %get-tuple-element.38), channel_id=1, source_target_pairs={{0,4},{1,5},{2,6},{3,7},{4,8},{5,9},{6,10},{7,11},{8,12},{9,13},{1... | collective-permute-start | bytes 786440 | tf_op jit(solution)/shard_map/ppermute | solution.py:103
  42.1 9.3 %collective-permute-start.2 = (bf16[4,16,1024]{2,1,0:T(8,128)(2,1)S(1)}, bf16[4,16,1024]{2,1,0:T(8,128)(2,1)S(1)}, u32[]{:S(2)}, u32[]{:S(2)}) collective-permute-start(bf16[4,16,1024]{2,1,0:T(8,128)(2,1)S(1)} %slice.187), channel_id=1, source_target_pairs={{0,1},{1,2},{2,3},{3,0},{4,5},{5,6},{6,7},{7,4},{8,9},{9,10},{10,1... | collective-permute-start | bytes 393224 | tf_op jit(solution)/shard_map/ppermute | solution.py:103
  42.2 10.0 %collective-permute-start.3 = (bf16[4,16,1024]{2,1,0:T(8,128)(2,1)S(1)}, bf16[4,16,1024]{2,1,0:T(8,128)(2,1)S(1)}, u32[]{:S(2)}, u32[]{:S(2)}) collective-permute-start(bf16[4,16,1024]{2,1,0:T(8,128)(2,1)S(1)} %slice.188), channel_id=1, source_target_pairs={{0,3},{1,0},{2,1},{3,2},{4,7},{5,4},{6,5},{7,6},{8,11},{9,8},{10,9... | collective-permute-start | bytes 393224 | tf_op jit(solution)/shard_map/ppermute | solution.py:103
  47.7 9.7 %collective-permute-start.18 = (bf16[4,16,1024]{2,1,0:T(8,128)(2,1)S(1)}, bf16[4,16,1024]{2,1,0:T(8,128)(2,1)S(1)}, u32[]{:S(2)}, u32[]{:S(2)}) collective-permute-start(bf16[4,16,1024]{2,1,0:T(8,128)(2,1)S(1)} %slice.202), channel_id=1, source_target_pairs={{0,4},{1,5},{2,6},{3,7},{4,8},{5,9},{6,10},{7,11},{8,12},{9,13},{1... | collective-permute-start | bytes 393224 | tf_op jit(solution)/shard_map/ppermute | solution.py:103
  47.8 10.4 %collective-permute-start.19 = (bf16[4,16,1024]{2,1,0:T(8,128)(2,1)S(1)}, bf16[4,16,1024]{2,1,0:T(8,128)(2,1)S(1)}, u32[]{:S(2)}, u32[]{:S(2)}) collective-permute-start(bf16[4,16,1024]{2,1,0:T(8,128)(2,1)S(1)} %slice.203), channel_id=1, source_target_pairs={{0,12},{1,13},{2,14},{3,15},{4,0},{5,1},{6,2},{7,3},{8,4},{9,5},{1... | collective-permute-start | bytes 393224 | tf_op jit(solution)/shard_map/ppermute | solution.py:103
  53.9 23.0 %collective-permute-start.5 = (bf16[4,128,1024]{2,1,0:T(8,128)(2,1)}, bf16[4,128,1024]{2,1,0:T(8,128)(2,1)S(1)}, u32[]{:S(2)}, u32[]{:S(2)}) collective-permute-start(bf16[4,128,1024]{2,1,0:T(8,128)(2,1)} %get-tuple-element.39), channel_id=1, source_target_pairs={{0,4},{1,5},{2,6},{3,7},{4,8},{5,9},{6,10},{7,11},{8,12},{9,13},{1... | collective-permute-start | bytes 3145736 | tf_op jit(solution)/shard_map/ppermute | solution.py:103
  54.8 28.2 %collective-permute-start.4 = (bf16[4,128,1024]{2,1,0:T(8,128)(2,1)}, bf16[4,128,1024]{2,1,0:T(8,128)(2,1)}, u32[]{:S(2)}, u32[]{:S(2)}) collective-permute-start(bf16[4,128,1024]{2,1,0:T(8,128)(2,1)} %get-tuple-element.39), channel_id=1, source_target_pairs={{0,12},{1,13},{2,14},{3,15},{4,0},{5,1},{6,2},{7,3},{8,4},{9,5},{1... | collective-permute-start | bytes 3145736 | tf_op jit(solution)/shard_map/ppermute | solution.py:103
  59.9 29.5 %collective-permute-start.20 = (bf16[4,128,1024]{2,1,0:T(8,128)(2,1)}, bf16[4,128,1024]{2,1,0:T(8,128)(2,1)}, u32[]{:S(2)}, u32[]{:S(2)}) collective-permute-start(bf16[4,128,1024]{2,1,0:T(8,128)(2,1)} %get-tuple-element.43), channel_id=1, source_target_pairs={{0,3},{1,0},{2,1},{3,2},{4,7},{5,4},{6,5},{7,6},{8,11},{9,8},{10,9... | collective-permute-start | bytes 3145736 | tf_op jit(solution)/shard_map/ppermute | solution.py:103
  61.2 26.2 %collective-permute-start.21 = (bf16[4,128,1024]{2,1,0:T(8,128)(2,1)}, bf16[4,128,1024]{2,1,0:T(8,128)(2,1)}, u32[]{:S(2)}, u32[]{:S(2)}) collective-permute-start(bf16[4,128,1024]{2,1,0:T(8,128)(2,1)} %get-tuple-element.43), channel_id=1, source_target_pairs={{0,1},{1,2},{2,3},{3,0},{4,5},{5,6},{6,7},{7,4},{8,9},{9,10},{10,1... | collective-permute-start | bytes 3145736 | tf_op jit(solution)/shard_map/ppermute | solution.py:103
  76.9 1.0 copy-start.4
  78.7 19.8 %collective-permute-start.6 = (bf16[4,64,1024]{2,1,0:T(8,128)(2,1)}, bf16[4,64,1024]{2,1,0:T(8,128)(2,1)}, u32[]{:S(2)}, u32[]{:S(2)}) collective-permute-start(bf16[4,64,1024]{2,1,0:T(8,128)(2,1)} %slice.189), channel_id=1, source_target_pairs={{0,4},{1,5},{2,6},{3,7},{4,8},{5,9},{6,10},{7,11},{8,12},{9,13},{1... | collective-permute-start | bytes 1572872 | tf_op jit(solution)/shard_map/ppermute | solution.py:103
  84.1 16.3 %collective-permute-start.7 = (bf16[4,64,1024]{2,1,0:T(8,128)(2,1)S(1)}, bf16[4,64,1024]{2,1,0:T(8,128)(2,1)S(1)}, u32[]{:S(2)}, u32[]{:S(2)}) collective-permute-start(bf16[4,64,1024]{2,1,0:T(8,128)(2,1)S(1)} %slice.190), channel_id=1, source_target_pairs={{0,12},{1,13},{2,14},{3,15},{4,0},{5,1},{6,2},{7,3},{8,4},{9,5},{1... | collective-permute-start | bytes 1572872 | tf_op jit(solution)/shard_map/ppermute | solution.py:103
  87.4 13.8 %copy-start.5 = (bf16[4,128,1024]{2,1,0:T(8,128)(2,1)S(1)}, bf16[4,128,1024]{2,1,0:T(8,128)(2,1)}, u32[]{:S(2)}) copy-start(bf16[4,128,1024]{2,1,0:T(8,128)(2,1)} %copy-done.4) | copy-start | bytes 3145732
  89.4 24.0 %collective-permute-start.22 = (bf16[4,64,1024]{2,1,0:T(8,128)(2,1)}, bf16[4,64,1024]{2,1,0:T(8,128)(2,1)}, u32[]{:S(2)}, u32[]{:S(2)}) collective-permute-start(bf16[4,64,1024]{2,1,0:T(8,128)(2,1)} %slice.204), channel_id=1, source_target_pairs={{0,1},{1,2},{2,3},{3,0},{4,5},{5,6},{6,7},{7,4},{8,9},{9,10},{10,1... | collective-permute-start | bytes 1572872 | tf_op jit(solution)/shard_map/ppermute | solution.py:103
  91.3 24.0 %collective-permute-start.23 = (bf16[4,64,1024]{2,1,0:T(8,128)(2,1)}, bf16[4,64,1024]{2,1,0:T(8,128)(2,1)}, u32[]{:S(2)}, u32[]{:S(2)}) collective-permute-start(bf16[4,64,1024]{2,1,0:T(8,128)(2,1)} %slice.205), channel_id=1, source_target_pairs={{0,3},{1,0},{2,1},{3,2},{4,7},{5,4},{6,5},{7,6},{8,11},{9,8},{10,9... | collective-permute-start | bytes 1572872 | tf_op jit(solution)/shard_map/ppermute | solution.py:103
  111.9 19.1 %collective-permute-start.10 = (bf16[4,64,1024]{2,1,0:T(8,128)(2,1)}, bf16[4,64,1024]{2,1,0:T(8,128)(2,1)S(1)}, u32[]{:S(2)}, u32[]{:S(2)}) collective-permute-start(bf16[4,64,1024]{2,1,0:T(8,128)(2,1)} %get-tuple-element.16), channel_id=1, source_target_pairs={{0,12},{1,13},{2,14},{3,15},{4,0},{5,1},{6,2},{7,3},{8,4},{9,5},{1... | collective-permute-start | bytes 1572872 | tf_op jit(solution)/shard_map/ppermute | solution.py:103
  111.9 19.1 %collective-permute-start.8 = (bf16[4,64,1024]{2,1,0:T(8,128)(2,1)}, bf16[4,64,1024]{2,1,0:T(8,128)(2,1)S(1)}, u32[]{:S(2)}, u32[]{:S(2)}) collective-permute-start(bf16[4,64,1024]{2,1,0:T(8,128)(2,1)} %get-tuple-element.15), channel_id=1, source_target_pairs={{0,4},{1,5},{2,6},{3,7},{4,8},{5,9},{6,10},{7,11},{8,12},{9,13},{1... | collective-permute-start | bytes 1572872 | tf_op jit(solution)/shard_map/ppermute | solution.py:103
  126.8 10.8 %copy-start.2 = (bf16[4,512,1024]{2,1,0:T(8,128)(2,1)S(1)}, bf16[4,512,1024]{2,1,0:T(8,128)(2,1)}, u32[]{:S(2)}) copy-start(bf16[4,512,1024]{2,1,0:T(8,128)(2,1)} %shard_map.74) | copy-start | bytes 12582916
  128.3 9.3 %collective-permute-start.24 = (bf16[4,64,1024]{2,1,0:T(8,128)(2,1)S(1)}, bf16[4,64,1024]{2,1,0:T(8,128)(2,1)S(1)}, u32[]{:S(2)}, u32[]{:S(2)}) collective-permute-start(bf16[4,64,1024]{2,1,0:T(8,128)(2,1)S(1)} %get-tuple-element.23), channel_id=1, source_target_pairs={{0,1},{1,2},{2,3},{3,0},{4,5},{5,6},{6,7},{7,4},{8,9},{9,10},{10,1... | collective-permute-start | bytes 1572872 | tf_op jit(solution)/shard_map/ppermute | solution.py:103
  128.4 9.2 %collective-permute-start.26 = (bf16[4,64,1024]{2,1,0:T(8,128)(2,1)S(1)}, bf16[4,64,1024]{2,1,0:T(8,128)(2,1)S(1)}, u32[]{:S(2)}, u32[]{:S(2)}) collective-permute-start(bf16[4,64,1024]{2,1,0:T(8,128)(2,1)S(1)} %get-tuple-element.24), channel_id=1, source_target_pairs={{0,3},{1,0},{2,1},{3,2},{4,7},{5,4},{6,5},{7,6},{8,11},{9,8},{10,9... | collective-permute-start | bytes 1572872 | tf_op jit(solution)/shard_map/ppermute | solution.py:103
  133.1 18.6 %collective-permute-start.11 = (bf16[4,128,1024]{2,1,0:T(8,128)(2,1)S(1)}, bf16[4,128,1024]{2,1,0:T(8,128)(2,1)S(1)}, u32[]{:S(2)}, u32[]{:S(2)}) collective-permute-start(bf16[4,128,1024]{2,1,0:T(8,128)(2,1)S(1)} %get-tuple-element.14), channel_id=1, source_target_pairs={{0,12},{1,13},{2,14},{3,15},{4,0},{5,1},{6,2},{7,3},{8,4},{9,5},{1... | collective-permute-start | bytes 3145736 | tf_op jit(solution)/shard_map/ppermute | solution.py:103
  133.3 19.4 %collective-permute-start.9 = (bf16[4,128,1024]{2,1,0:T(8,128)(2,1)S(1)}, bf16[4,128,1024]{2,1,0:T(8,128)(2,1)S(1)}, u32[]{:S(2)}, u32[]{:S(2)}) collective-permute-start(bf16[4,128,1024]{2,1,0:T(8,128)(2,1)S(1)} %get-tuple-element.13), channel_id=1, source_target_pairs={{0,4},{1,5},{2,6},{3,7},{4,8},{5,9},{6,10},{7,11},{8,12},{9,13},{1... | collective-permute-start | bytes 3145736 | tf_op jit(solution)/shard_map/ppermute | solution.py:103
  138.3 20.7 %collective-permute-start.25 = (bf16[4,128,1024]{2,1,0:T(8,128)(2,1)S(1)}, bf16[4,128,1024]{2,1,0:T(8,128)(2,1)S(1)}, u32[]{:S(2)}, u32[]{:S(2)}) collective-permute-start(bf16[4,128,1024]{2,1,0:T(8,128)(2,1)S(1)} %get-tuple-element.21), channel_id=1, source_target_pairs={{0,1},{1,2},{2,3},{3,0},{4,5},{5,6},{6,7},{7,4},{8,9},{9,10},{10,1... | collective-permute-start | bytes 3145736 | tf_op jit(solution)/shard_map/ppermute | solution.py:103
  138.4 20.6 %collective-permute-start.27 = (bf16[4,128,1024]{2,1,0:T(8,128)(2,1)S(1)}, bf16[4,128,1024]{2,1,0:T(8,128)(2,1)S(1)}, u32[]{:S(2)}, u32[]{:S(2)}) collective-permute-start(bf16[4,128,1024]{2,1,0:T(8,128)(2,1)S(1)} %get-tuple-element.22), channel_id=1, source_target_pairs={{0,3},{1,0},{2,1},{3,2},{4,7},{5,4},{6,5},{7,6},{8,11},{9,8},{10,9... | collective-permute-start | bytes 3145736 | tf_op jit(solution)/shard_map/ppermute | solution.py:103
  154.7 7.8 %collective-permute-start.12 = (bf16[4,16,1024]{2,1,0:T(8,128)(2,1)S(1)}, bf16[4,16,1024]{2,1,0:T(8,128)(2,1)S(1)}, u32[]{:S(2)}, u32[]{:S(2)}) collective-permute-start(bf16[4,16,1024]{2,1,0:T(8,128)(2,1)S(1)} %get-tuple-element.29), channel_id=1, source_target_pairs={{0,1},{1,2},{2,3},{3,0},{4,5},{5,6},{6,7},{7,4},{8,9},{9,10},{10,1... | collective-permute-start | bytes 393224 | tf_op jit(solution)/shard_map/ppermute | solution.py:103
  154.7 7.8 %collective-permute-start.14 = (bf16[4,16,1024]{2,1,0:T(8,128)(2,1)S(1)}, bf16[4,16,1024]{2,1,0:T(8,128)(2,1)S(1)}, u32[]{:S(2)}, u32[]{:S(2)}) collective-permute-start(bf16[4,16,1024]{2,1,0:T(8,128)(2,1)S(1)} %get-tuple-element.30), channel_id=1, source_target_pairs={{0,3},{1,0},{2,1},{3,2},{4,7},{5,4},{6,5},{7,6},{8,11},{9,8},{10,9... | collective-permute-start | bytes 393224 | tf_op jit(solution)/shard_map/ppermute | solution.py:103
  159.7 5.9 %collective-permute-start.28 = (bf16[4,16,1024]{2,1,0:T(8,128)(2,1)S(1)}, bf16[4,16,1024]{2,1,0:T(8,128)(2,1)S(1)}, u32[]{:S(2)}, u32[]{:S(2)}) collective-permute-start(bf16[4,16,1024]{2,1,0:T(8,128)(2,1)S(1)} %get-tuple-element.31), channel_id=1, source_target_pairs={{0,4},{1,5},{2,6},{3,7},{4,8},{5,9},{6,10},{7,11},{8,12},{9,13},{1... | collective-permute-start | bytes 393224 | tf_op jit(solution)/shard_map/ppermute | solution.py:103
  159.8 5.8 %collective-permute-start.30 = (bf16[4,16,1024]{2,1,0:T(8,128)(2,1)S(1)}, bf16[4,16,1024]{2,1,0:T(8,128)(2,1)S(1)}, u32[]{:S(2)}, u32[]{:S(2)}) collective-permute-start(bf16[4,16,1024]{2,1,0:T(8,128)(2,1)S(1)} %get-tuple-element.32), channel_id=1, source_target_pairs={{0,12},{1,13},{2,14},{3,15},{4,0},{5,1},{6,2},{7,3},{8,4},{9,5},{1... | collective-permute-start | bytes 393224 | tf_op jit(solution)/shard_map/ppermute | solution.py:103
  162.6 9.2 %collective-permute-start.13 = (bf16[4,32,1024]{2,1,0:T(8,128)(2,1)S(1)}, bf16[4,32,1024]{2,1,0:T(8,128)(2,1)S(1)}, u32[]{:S(2)}, u32[]{:S(2)}) collective-permute-start(bf16[4,32,1024]{2,1,0:T(8,128)(2,1)S(1)} %get-tuple-element.25), channel_id=1, source_target_pairs={{0,1},{1,2},{2,3},{3,0},{4,5},{5,6},{6,7},{7,4},{8,9},{9,10},{10,1... | collective-permute-start | bytes 786440 | tf_op jit(solution)/shard_map/ppermute | solution.py:103
  162.7 9.1 %collective-permute-start.15 = (bf16[4,32,1024]{2,1,0:T(8,128)(2,1)S(1)}, bf16[4,32,1024]{2,1,0:T(8,128)(2,1)S(1)}, u32[]{:S(2)}, u32[]{:S(2)}) collective-permute-start(bf16[4,32,1024]{2,1,0:T(8,128)(2,1)S(1)} %get-tuple-element.26), channel_id=1, source_target_pairs={{0,3},{1,0},{2,1},{3,2},{4,7},{5,4},{6,5},{7,6},{8,11},{9,8},{10,9... | collective-permute-start | bytes 786440 | tf_op jit(solution)/shard_map/ppermute | solution.py:103
  165.8 6.5 %collective-permute-start.29 = (bf16[4,32,1024]{2,1,0:T(8,128)(2,1)S(1)}, bf16[4,32,1024]{2,1,0:T(8,128)(2,1)S(1)}, u32[]{:S(2)}, u32[]{:S(2)}) collective-permute-start(bf16[4,32,1024]{2,1,0:T(8,128)(2,1)S(1)} %get-tuple-element.27), channel_id=1, source_target_pairs={{0,4},{1,5},{2,6},{3,7},{4,8},{5,9},{6,10},{7,11},{8,12},{9,13},{1... | collective-permute-start | bytes 786440 | tf_op jit(solution)/shard_map/ppermute | solution.py:103
  165.9 6.4 %collective-permute-start.31 = (bf16[4,32,1024]{2,1,0:T(8,128)(2,1)S(1)}, bf16[4,32,1024]{2,1,0:T(8,128)(2,1)S(1)}, u32[]{:S(2)}, u32[]{:S(2)}) collective-permute-start(bf16[4,32,1024]{2,1,0:T(8,128)(2,1)S(1)} %get-tuple-element.28), channel_id=1, source_target_pairs={{0,12},{1,13},{2,14},{3,15},{4,0},{5,1},{6,2},{7,3},{8,4},{9,5},{1... | collective-permute-start | bytes 786440 | tf_op jit(solution)/shard_map/ppermute | solution.py:103
  173.8 32.1 %copy-start.6 = (bf16[32,8,1024]{2,1,0:T(8,128)(2,1)S(1)}, bf16[32,8,1024]{2,1,0:T(8,128)(2,1)}, u32[]{:S(2)}) copy-start(bf16[32,8,1024]{2,1,0:T(8,128)(2,1)} %param.7) | copy-start | bytes 1572868
  175.8 26.1 %all-to-all-start.1 = ((bf16[8,32,1024]{2,1,0:T(8,128)(2,1)}), bf16[8,32,1024]{2,1,0:T(8,128)(2,1)}, u32[]{:S(2)}, u32[]{:S(2)}) async-start(bf16[8,32,1024]{2,1,0:T(8,128)(2,1)} %broadcast_select_fusion.1), calls=%async_computation.1 | async-start | bytes 1048576 | tf_op jit(solution)/shard_map/all_to_all | solution.py:219

commit v8 on v3

--- a/solution.py
+++ b/solution.py
@@ -43,14 +43,15 @@
 
     @pl.when(n_live_ref[row] > 0)
     def _():
-        keep = keep_ref[0]
+        half_keep = keep_ref[0] * 0.5
         for h in range(heads):
             lo = h * head_dim
             q = q_ref[0, :, lo:lo + head_dim]
             k = kv_ref[0, :, lo:lo + head_dim]
             v = kv_ref[0, :, width + lo:width + lo + head_dim]
             s = lax.dot_general(q, k, (((1,), (1,)), ((), ())), preferred_element_type=jnp.float32)
-            w = (jax.nn.silu(s * scale) * keep).astype(jnp.bfloat16)
+            y = s * scale
+            w = (y * (1.0 + jnp.tanh(y * 0.5)) * half_keep).astype(jnp.bfloat16)
             o = jnp.dot(w, v, preferred_element_type=jnp.float32)
             o_ref[0, :, lo:lo + head_dim] = o.astype(o_ref.dtype)
 
@@ -194,9 +195,8 @@
 
     inputs = candidates.astype(jnp.float32)
     normed = layer_norm(inputs).astype(jnp.bfloat16).reshape(cand_rows * per_group, width)
-    projected = jax.nn.silu(jnp.dot(normed, w_uq, preferred_element_type=jnp.float32))
-    gates = projected[:, :width].reshape(cand_rows, per_group, width)
-    queries = projected[:, width:].astype(jnp.bfloat16).reshape(cand_rows, per_group, width)
+    queries = jax.nn.silu(jnp.dot(normed, w_uq[:, width:], preferred_element_type=jnp.float32))
+    queries = queries.astype(jnp.bfloat16).reshape(cand_rows, per_group, width)
     scale = head_dim ** (-0.5)
 
     q_pos = jnp.swapaxes(queries, 0, 1)
@@ -218,6 +218,8 @@
     a_in = lax.all_to_all(a_out, "group", split_axis=0, concat_axis=0, tiled=True)
     attn = jnp.swapaxes(a_in[receive_index], 0, 1).astype(jnp.float32)
 
+    gates = jax.nn.silu(jnp.dot(normed, w_uq[:, :width], preferred_element_type=jnp.float32))
+    gates = gates.reshape(cand_rows, per_group, width)
     gated = (layer_norm(attn) * gates).astype(jnp.bfloat16).reshape(cand_rows * per_group, width)
     result = jnp.dot(gated, w_out, preferred_element_type=jnp.float32) + inputs.reshape(
         cand_rows * per_group, width

time: 193 us -> 194 us (level)
  matrix products: 5.45 us -> 7.72 us
  local copies, waits for them, and re-layouts: 35.8 us -> 33.7 us
    reshape x3 -> x1, local copies, waits for them, and re-layouts: 2.68 us -> 0.29 us  [on_device(): queries = queries.astype(jnp.bfloat16).reshape(cand_rows, per_group, width)]
    dot_general x1 -> x2, matrix products: 3.82 us -> 6.09 us  [the longest x1 3.46 us: on_device(): jnp.dot(normed, w_uq[:, :width], preferred_element_type=jnp.float32)]
    unnamed x25 -> x23, local copies, waits for them, and re-layouts: 14.3 us -> 13.7 us
  transfers between devices with their start and end apart: 34 -> 34, of which waited for: 11 -> 11; matrix products, arithmetic and copies ran while one was open for 18% -> 19% of each run, Pallas kernels for 8% -> 8%
where the time goes in v8:
time: 194 us; the launch traced here: 193 us
  starting transfers between devices  64.5 us (33%)
  waiting for transfers between devices  53.8 us (28%)
  local copies, waits for them, and re-layouts  33.7 us (17%)
  other arithmetic  16.8 us (9%)
  Pallas kernels  15.9 us (8%)
  matrix products  7.72 us (4%)
    ppermute x32, starting transfers between devices, send(): return lax.ppermute(value, 'member', shift_perm(grid, axis, shift))  41.4 us
    ppermute x32, waiting for transfers between devices, send(): return lax.ppermute(value, 'member', shift_perm(grid, axis, shift))  39.2 us
    all_to_all x1, starting transfers between devices, on_device(): lax.all_to_all(a_out, 'group', split_axis=0, concat_axis=0, tiled=True)  17.1 us
    pallas_call x2, Pallas kernels, attend_local(): pl.pallas_call(kernel, out_shape=jax.ShapeDtypeStruct((rows, cands, width...  15.9 us
    unnamed x23, local copies, waits for them, and re-layouts  13.7 us
    all_to_all x1, waiting for transfers between devices, on_device(): lax.all_to_all(q_out, 'group', split_axis=0, concat_axis=0, tiled=True)  8.62 us
    all_to_all x1, waiting for transfers between devices, on_device(): lax.all_to_all(a_out, 'group', split_axis=0, concat_axis=0, tiled=True)  6.01 us
    all_to_all x1, starting transfers between devices, on_device(): lax.all_to_all(q_out, 'group', split_axis=0, concat_axis=0, tiled=True)  5.96 us
  transfers between devices with their start and end apart: 34, of which 11 were waited for; matrix products, arithmetic and copies ran while one was open for 19% of the time, Pallas kernels for 8%

profile of v8, /device:TPU:1, one launch (start us, length us, event | category | flops | bytes accessed | tf_op | source)
XLA Modules:
  0.0 192.9 jit_solution(16200823699311681493)
XLA Ops:
  0.0 1.0 fusion.36
  1.0 1.3 gather_fusion
  4.1 1.2 convert_reduce_fusion
  5.5 1.3 fusion.8
  7.0 2.6 %fusion.19 = bf16[32,8,1024]{2,1,0:T(8,128)(2,1)S(1)} fusion(bf16[1024,2048]{1,0:T(8,128)(2,1)} %param.12, bf16[32,8,1024]{2,1,0:T(8,128)(2,1)} %param.7, f32[32,8]{1,0:T(8,128)S(1)} %copy.37, f32[32,8]{1,0:T(8,128)S(1)} %copy.35), kind=kOutput, calls=%fused_computation.37 | convolution fusion | flops 539230208 | bytes 3147776 | tf_op jit(solution)/shard_map/dot_general | solution.py:198
  10.5 0.9 broadcast_select_fusion
  11.4 6.0 %all-to-all-start = ((bf16[8,32,1024]{2,1,0:T(8,128)(2,1)}), bf16[8,32,1024]{2,1,0:T(8,128)(2,1)S(1)}, u32[]{:S(2)}, u32[]{:S(2)}) async-start(bf16[8,32,1024]{2,1,0:T(8,128)(2,1)} %broadcast_select_fusion), calls=%async_computation | async-start | bytes 1048576 | tf_op jit(solution)/shard_map/all_to_all | solution.py:204
  18.1 8.6 %all-to-all-done = bf16[8,32,1024]{2,1,0:T(8,128)(2,1)S(1)} async-done(((bf16[8,32,1024]{2,1,0:T(8,128)(2,1)}), bf16[8,32,1024]{2,1,0:T(8,128)(2,1)S(1)}, u32[]{:S(2)}, u32[]{:S(2)}) %all-to-all-start) | async-done | bytes 524320 | tf_op jit(solution)/shard_map/all_to_all | solution.py:204
  27.3 1.2 constant_dynamic-update-slice_fusion.4
  28.5 1.2 collective-permute-start.1
  29.7 1.5 collective-permute-start
  31.2 3.8 %collective-permute-start.16 = (bf16[4,32,1024]{2,1,0:T(8,128)(2,1)S(1)}, bf16[4,32,1024]{2,1,0:T(8,128)(2,1)S(1)}, u32[]{:S(2)}, u32[]{:S(2)}) collective-permute-start(bf16[4,32,1024]{2,1,0:T(8,128)(2,1)S(1)} %get-tuple-element.36), channel_id=1, source_target_pairs={{0,12},{1,13},{2,14},{3,15},{4,0},{5,1},{6,2},{7,3},{8,4},{9,5},{1... | collective-permute-start | bytes 786440 | tf_op jit(solution)/shard_map/ppermute | solution.py:103
  35.0 1.6 collective-permute-done.1
  36.8 2.7 %collective-permute-start.3 = (bf16[4,16,1024]{2,1,0:T(8,128)(2,1)S(1)}, bf16[4,16,1024]{2,1,0:T(8,128)(2,1)S(1)}, u32[]{:S(2)}, u32[]{:S(2)}) collective-permute-start(bf16[4,16,1024]{2,1,0:T(8,128)(2,1)S(1)} %slice.176), channel_id=1, source_target_pairs={{0,3},{1,0},{2,1},{3,2},{4,7},{5,4},{6,5},{7,6},{8,11},{9,8},{10,9... | collective-permute-start | bytes 393224 | tf_op jit(solution)/shard_map/ppermute | solution.py:103
  39.5 2.7 %collective-permute-done.17 = bf16[4,32,1024]{2,1,0:T(8,128)(2,1)S(1)} collective-permute-done((bf16[4,32,1024]{2,1,0:T(8,128)(2,1)S(1)}, bf16[4,32,1024]{2,1,0:T(8,128)(2,1)S(1)}, u32[]{:S(2)}, u32[]{:S(2)}) %collective-permute-start.17) | collective-permute-done | bytes 262176 | tf_op jit(solution)/shard_map/ppermute | solution.py:103
  42.3 2.7 %collective-permute-start.19 = (bf16[4,16,1024]{2,1,0:T(8,128)(2,1)S(1)}, bf16[4,16,1024]{2,1,0:T(8,128)(2,1)S(1)}, u32[]{:S(2)}, u32[]{:S(2)}) collective-permute-start(bf16[4,16,1024]{2,1,0:T(8,128)(2,1)S(1)} %slice.191), channel_id=1, source_target_pairs={{0,12},{1,13},{2,14},{3,15},{4,0},{5,1},{6,2},{7,3},{8,4},{9,5},{1... | collective-permute-start | bytes 393224 | tf_op jit(solution)/shard_map/ppermute | solution.py:103
  45.1 0.9 constant_dynamic-update-slice_fusion.3
  47.5 0.9 constant_dynamic-update-slice_fusion
  48.4 0.9 constant_dynamic-update-slice_fusion.17
  49.2 2.7 %collective-permute-start.4 = (bf16[4,128,1024]{2,1,0:T(8,128)(2,1)}, bf16[4,128,1024]{2,1,0:T(8,128)(2,1)S(1)}, u32[]{:S(2)}, u32[]{:S(2)}) collective-permute-start(bf16[4,128,1024]{2,1,0:T(8,128)(2,1)} %get-tuple-element.37), channel_id=1, source_target_pairs={{0,12},{1,13},{2,14},{3,15},{4,0},{5,1},{6,2},{7,3},{8,4},{9,5},{1... | collective-permute-start | bytes 3145736 | tf_op jit(solution)/shard_map/ppermute | solution.py:103
  53.4 0.9 constant_dynamic-update-slice_fusion.14
  54.3 1.3 collective-permute-start.20
  55.8 2.5 %fusion.53 = (bf16[4,128,2048]{2,1,0:T(8,128)(2,1)}, bf16[4,128,2048]{2,1,0:T(8,128)(2,1)}) fusion(bf16[8,128,2048]{2,1,0:T(8,128)(2,1)S(1)} %copy-done.3), kind=kLoop, calls=%fused_computation.156 | loop fusion | bytes 8388608 | tf_op jit(solution)/shard_map/slice | solution.py:212
  58.3 13.0 %collective-permute-done.5 = bf16[4,128,1024]{2,1,0:T(8,128)(2,1)S(1)} collective-permute-done((bf16[4,128,1024]{2,1,0:T(8,128)(2,1)}, bf16[4,128,1024]{2,1,0:T(8,128)(2,1)S(1)}, u32[]{:S(2)}, u32[]{:S(2)}) %collective-permute-start.5) | collective-permute-done | bytes 1048608 | tf_op jit(solution)/shard_map/ppermute | solution.py:103
  72.1 2.7 %collective-permute-start.7 = (bf16[4,64,1024]{2,1,0:T(8,128)(2,1)S(1)}, bf16[4,64,1024]{2,1,0:T(8,128)(2,1)S(1)}, u32[]{:S(2)}, u32[]{:S(2)}) collective-permute-start(bf16[4,64,1024]{2,1,0:T(8,128)(2,1)S(1)} %slice.178), channel_id=1, source_target_pairs={{0,12},{1,13},{2,14},{3,15},{4,0},{5,1},{6,2},{7,3},{8,4},{9,5},{1... | collective-permute-start | bytes 1572872 | tf_op jit(solution)/shard_map/ppermute | solution.py:103
  75.5 2.2 %collective-permute-done.21 = bf16[4,128,1024]{2,1,0:T(8,128)(2,1)S(1)} collective-permute-done((bf16[4,128,1024]{2,1,0:T(8,128)(2,1)}, bf16[4,128,1024]{2,1,0:T(8,128)(2,1)S(1)}, u32[]{:S(2)}, u32[]{:S(2)}) %collective-permute-start.21) | collective-permute-done | bytes 1048608 | tf_op jit(solution)/shard_map/ppermute | solution.py:103
  77.7 0.8 slice.192
  78.5 0.8 slice.193
  79.4 2.7 %collective-permute-start.23 = (bf16[4,64,1024]{2,1,0:T(8,128)(2,1)}, bf16[4,64,1024]{2,1,0:T(8,128)(2,1)}, u32[]{:S(2)}, u32[]{:S(2)}) collective-permute-start(bf16[4,64,1024]{2,1,0:T(8,128)(2,1)} %slice.193), channel_id=1, source_target_pairs={{0,3},{1,0},{2,1},{3,2},{4,7},{5,4},{6,5},{7,6},{8,11},{9,8},{10,9... | collective-permute-start | bytes 1572872 | tf_op jit(solution)/shard_map/ppermute | solution.py:103
  82.0 1.1 constant_dynamic-update-slice_fusion.8
  83.1 1.1 constant_dynamic-update-slice_fusion.22
  84.2 0.8 constant_dynamic-update-slice_fusion.7
  85.1 0.8 constant_dynamic-update-slice_fusion.6
  85.9 1.1 constant_dynamic-update-slice_fusion.5.q_ref
  87.0 7.9 %shard_map.73 = bf16[4,512,1024]{2,1,0:T(8,128)(2,1)} custom-call(s32[4]{0:T(128)} %get-tuple-element.57.n_live_ref, bf16[4,512,1024]{2,1,0:T(8,128)(2,1)} %constant_dynamic-update-slice_fusion.5.q_ref, bf16[4,128,2048]{2,1,0:T(8,128)(2,1)} %get-tuple-element.17.kv_ref, f32[4,1,128]{2,1,0:T(1,128)} %get-tuple-element.53.keep_ref), custom_call_target="tpu_custom_call" | custom-call | flops 1073741824 | bytes 10485760 | tf_op jit(solution)/shard_map/pallas_call | solution.py:68
  94.9 2.3 %fusion.52 = (bf16[4,64,1024]{2,1,0:T(8,128)(2,1)}, bf16[4,64,1024]{2,1,0:T(8,128)(2,1)}) fusion(bf16[4,512,1024]{2,1,0:T(8,128)(2,1)} %shard_map.73), kind=kLoop, calls=%fused_computation.155 | loop fusion | bytes 2097152 | tf_op jit(solution)/shard_map/slice | solution.py:139
  97.2 1.5 collective-permute-start.8
  98.7 1.9 constant_dynamic-update-slice_fusion.21
  100.6 1.9 constant_dynamic-update-slice_fusion.20
  102.5 1.1 constant_dynamic-update-slice_fusion.19.q_ref
  103.5 8.0 %shard_map.74 = bf16[4,512,1024]{2,1,0:T(8,128)(2,1)} custom-call(s32[4]{0:T(128)} %get-tuple-element.58.n_live_ref, bf16[4,512,1024]{2,1,0:T(8,128)(2,1)} %constant_dynamic-update-slice_fusion.19.q_ref, bf16[4,128,2048]{2,1,0:T(8,128)(2,1)} %get-tuple-element.18.kv_ref, f32[4,1,128]{2,1,0:T(1,128)} %get-tuple-element.54.keep_ref), custom_call_target="tpu_custom_call" | custom-call | flops 1073741824 | bytes 10485760 | tf_op jit(solution)/shard_map/pallas_call | solution.py:68
  111.5 1.5 fusion.54
  113.0 2.7 %collective-permute-start.26 = (bf16[4,64,1024]{2,1,0:T(8,128)(2,1)S(1)}, bf16[4,64,1024]{2,1,0:T(8,128)(2,1)S(1)}, u32[]{:S(2)}, u32[]{:S(2)}) collective-permute-start(bf16[4,64,1024]{2,1,0:T(8,128)(2,1)S(1)} %get-tuple-element.22), channel_id=1, source_target_pairs={{0,3},{1,0},{2,1},{3,2},{4,7},{5,4},{6,5},{7,6},{8,11},{9,8},{10,9... | collective-permute-start | bytes 1572872 | tf_op jit(solution)/shard_map/ppermute | solution.py:103
  115.7 2.4 %add_convert_fusion.3 = (bf16[4,128,1024]{2,1,0:T(8,128)(2,1)S(1)}, bf16[4,128,1024]{2,1,0:T(8,128)(2,1)S(1)}) fusion(bf16[4,512,1024]{2,1,0:T(8,128)(2,1)} %shard_map.73, bf16[4,64,1024]{2,1,0:T(8,128)(2,1)} %collective-permute-done.8, bf16[4,64,1024]{2,1,0:T(8,128)(2,1)} %collective-permute-done.10), kind=kLoop, calls=%fused_computation.15 | loop fusion | flops 4194304 | bytes 5242880 | tf_op jit(solution)/shard_map/convert_element_type | solution.py:144
  118.3 1.3 collective-permute-start.9
  119.9 2.3 %collective-permute-done.24 = bf16[4,64,1024]{2,1,0:T(8,128)(2,1)S(1)} collective-permute-done((bf16[4,64,1024]{2,1,0:T(8,128)(2,1)S(1)}, bf16[4,64,1024]{2,1,0:T(8,128)(2,1)S(1)}, u32[]{:S(2)}, u32[]{:S(2)}) %collective-permute-start.24) | collective-permute-done | bytes 524320 | tf_op jit(solution)/shard_map/ppermute | solution.py:103
  123.0 2.7 %collective-permute-start.27 = (bf16[4,128,1024]{2,1,0:T(8,128)(2,1)S(1)}, bf16[4,128,1024]{2,1,0:T(8,128)(2,1)S(1)}, u32[]{:S(2)}, u32[]{:S(2)}) collective-permute-start(bf16[4,128,1024]{2,1,0:T(8,128)(2,1)S(1)} %get-tuple-element.20), channel_id=1, source_target_pairs={{0,3},{1,0},{2,1},{3,2},{4,7},{5,4},{6,5},{7,6},{8,11},{9,8},{10,9... | collective-permute-start | bytes 3145736 | tf_op jit(solution)/shard_map/ppermute | solution.py:103
  125.8 10.5 %collective-permute-done.11 = bf16[4,128,1024]{2,1,0:T(8,128)(2,1)S(1)} collective-permute-done((bf16[4,128,1024]{2,1,0:T(8,128)(2,1)S(1)}, bf16[4,128,1024]{2,1,0:T(8,128)(2,1)S(1)}, u32[]{:S(2)}, u32[]{:S(2)}) %collective-permute-start.11) | collective-permute-done | bytes 1048608 | tf_op jit(solution)/shard_map/ppermute | solution.py:103
  136.3 1.4 collective-permute-done.9
  137.6 1.7 fusion.50
  139.5 2.7 %collective-permute-start.14 = (bf16[4,16,1024]{2,1,0:T(8,128)(2,1)S(1)}, bf16[4,16,1024]{2,1,0:T(8,128)(2,1)S(1)}, u32[]{:S(2)}, u32[]{:S(2)}) collective-permute-start(bf16[4,16,1024]{2,1,0:T(8,128)(2,1)S(1)} %get-tuple-element.28), channel_id=1, source_target_pairs={{0,3},{1,0},{2,1},{3,2},{4,7},{5,4},{6,5},{7,6},{8,11},{9,8},{10,9... | collective-permute-start | bytes 393224 | tf_op jit(solution)/shard_map/ppermute | solution.py:103
  142.1 1.5 collective-permute-done.25
  144.5 2.7 %collective-permute-start.30 = (bf16[4,16,1024]{2,1,0:T(8,128)(2,1)S(1)}, bf16[4,16,1024]{2,1,0:T(8,128)(2,1)S(1)}, u32[]{:S(2)}, u32[]{:S(2)}) collective-permute-start(bf16[4,16,1024]{2,1,0:T(8,128)(2,1)S(1)} %get-tuple-element.30), channel_id=1, source_target_pairs={{0,12},{1,13},{2,14},{3,15},{4,0},{5,1},{6,2},{7,3},{8,4},{9,5},{1... | collective-permute-start | bytes 393224 | tf_op jit(solution)/shard_map/ppermute | solution.py:103
  147.4 3.0 %collective-permute-start.15 = (bf16[4,32,1024]{2,1,0:T(8,128)(2,1)S(1)}, bf16[4,32,1024]{2,1,0:T(8,128)(2,1)S(1)}, u32[]{:S(2)}, u32[]{:S(2)}) collective-permute-start(bf16[4,32,1024]{2,1,0:T(8,128)(2,1)S(1)} %get-tuple-element.24), channel_id=1, source_target_pairs={{0,3},{1,0},{2,1},{3,2},{4,7},{5,4},{6,5},{7,6},{8,11},{9,8},{10,9... | collective-permute-start | bytes 786440 | tf_op jit(solution)/shard_map/ppermute | solution.py:103
  150.5 2.7 %collective-permute-start.31 = (bf16[4,32,1024]{2,1,0:T(8,128)(2,1)S(1)}, bf16[4,32,1024]{2,1,0:T(8,128)(2,1)S(1)}, u32[]{:S(2)}, u32[]{:S(2)}) collective-permute-start(bf16[4,32,1024]{2,1,0:T(8,128)(2,1)S(1)} %get-tuple-element.26), channel_id=1, source_target_pairs={{0,12},{1,13},{2,14},{3,15},{4,0},{5,1},{6,2},{7,3},{8,4},{9,5},{1... | collective-permute-start | bytes 786440 | tf_op jit(solution)/shard_map/ppermute | solution.py:103
  153.2 3.9 %collective-permute-done.13 = bf16[4,32,1024]{2,1,0:T(8,128)(2,1)S(1)} collective-permute-done((bf16[4,32,1024]{2,1,0:T(8,128)(2,1)S(1)}, bf16[4,32,1024]{2,1,0:T(8,128)(2,1)S(1)}, u32[]{:S(2)}, u32[]{:S(2)}) %collective-permute-start.13) | collective-permute-done | bytes 262176 | tf_op jit(solution)/shard_map/ppermute | solution.py:103
  157.4 1.4 gather_fusion.6
  158.8 1.9 %broadcast_select_fusion.1 = bf16[8,32,1024]{2,1,0:T(8,128)(2,1)} fusion(bf16[8,32,1024]{2,1,0:T(8,128)(2,1)} %gather_fusion.6, pred[8]{0:T(512)(128)(4,1)S(1)} %fusion.40), kind=kLoop, calls=%fused_computation.58 | loop fusion | flops 262144 | bytes 1048584 | tf_op jit(solution)/shard_map/jit(_where)/select_n | solution.py:217
  160.7 17.1 %all-to-all-start.1 = ((bf16[8,32,1024]{2,1,0:T(8,128)(2,1)}), bf16[8,32,1024]{2,1,0:T(8,128)(2,1)}, u32[]{:S(2)}, u32[]{:S(2)}) async-start(bf16[8,32,1024]{2,1,0:T(8,128)(2,1)} %broadcast_select_fusion.1), calls=%async_computation.1 | async-start | bytes 1048576 | tf_op jit(solution)/shard_map/all_to_all | solution.py:218
  177.8 3.5 %multiply_bitcast_fusion = f32[32,8,1024]{2,1,0:T(8,128)} fusion(bf16[1024,2048]{1,0:T(8,128)(2,1)} %param.12, bf16[32,8,1024]{2,1,0:T(8,128)(2,1)S(1)} %copy-done.4, f32[32,8]{1,0:T(8,128)S(1)} %copy.37, f32[32,8]{1,0:T(8,128)S(1)} %copy.35), kind=kOutput, calls=%fused_computation.35 | convolution fusion | flops 538968064 | bytes 3672064 | tf_op jit(solution)/shard_map/dot_general | solution.py:221
  181.3 6.0 %all-to-all-done.1 = bf16[8,32,1024]{2,1,0:T(8,128)(2,1)} async-done(((bf16[8,32,1024]{2,1,0:T(8,128)(2,1)}), bf16[8,32,1024]{2,1,0:T(8,128)(2,1)}, u32[]{:S(2)}, u32[]{:S(2)}) %all-to-all-start.1) | async-done | bytes 524320 | tf_op jit(solution)/shard_map/all_to_all | solution.py:218
  187.3 1.6 gather_fusion.7
  189.4 1.9 fusion.14
  191.3 1.6 fusion.7
  (111 shorter events, 12.6 us)
Async XLA Ops:
  0.0 191.3 %copy-start = (bf16[1024,1024]{1,0:T(8,128)(2,1)S(1)}, bf16[1024,1024]{1,0:T(8,128)(2,1)}, u32[]{:S(2)}) copy-start(bf16[1024,1024]{1,0:T(8,128)(2,1)} %param.13) | copy-start | bytes 6291460
  9.6 7.8 %copy-start.1 = (s32[64]{0:T(128)S(1)}, s32[64]{0:T(128)}, u32[]{:S(2)}) copy-start(s32[64]{0:T(128)} %param.11) | copy-start | bytes 772
  11.4 15.3 %all-to-all-start = ((bf16[8,32,1024]{2,1,0:T(8,128)(2,1)}), bf16[8,32,1024]{2,1,0:T(8,128)(2,1)S(1)}, u32[]{:S(2)}, u32[]{:S(2)}) async-start(bf16[8,32,1024]{2,1,0:T(8,128)(2,1)} %broadcast_select_fusion), calls=%async_computation | async-start | bytes 1048576 | tf_op jit(solution)/shard_map/all_to_all | solution.py:204
  28.5 8.1 %collective-permute-start.1 = (bf16[4,32,1024]{2,1,0:T(8,128)(2,1)S(1)}, bf16[4,32,1024]{2,1,0:T(8,128)(2,1)S(1)}, u32[]{:S(2)}, u32[]{:S(2)}) collective-permute-start(bf16[4,32,1024]{2,1,0:T(8,128)(2,1)S(1)} %get-tuple-element.35), channel_id=1, source_target_pairs={{0,1},{1,2},{2,3},{3,0},{4,5},{5,6},{6,7},{7,4},{8,9},{9,10},{10,1... | collective-permute-start | bytes 786440 | tf_op jit(solution)/shard_map/ppermute | solution.py:103
  29.7 26.1 %copy-start.3 = (bf16[8,128,2048]{2,1,0:T(8,128)(2,1)S(1)}, bf16[8,128,2048]{2,1,0:T(8,128)(2,1)}, u32[]{:S(2)}) copy-start(bf16[8,128,2048]{2,1,0:T(8,128)(2,1)} %param.8) | copy-start | bytes 12582916
  29.7 7.0 %collective-permute-start = (bf16[4,32,1024]{2,1,0:T(8,128)(2,1)S(1)}, bf16[4,32,1024]{2,1,0:T(8,128)(2,1)S(1)}, u32[]{:S(2)}, u32[]{:S(2)}) collective-permute-start(bf16[4,32,1024]{2,1,0:T(8,128)(2,1)S(1)} %get-tuple-element.35), channel_id=1, source_target_pairs={{0,3},{1,0},{2,1},{3,2},{4,7},{5,4},{6,5},{7,6},{8,11},{9,8},{10,9... | collective-permute-start | bytes 786440 | tf_op jit(solution)/shard_map/ppermute | solution.py:103
  31.2 11.1 %collective-permute-start.16 = (bf16[4,32,1024]{2,1,0:T(8,128)(2,1)S(1)}, bf16[4,32,1024]{2,1,0:T(8,128)(2,1)S(1)}, u32[]{:S(2)}, u32[]{:S(2)}) collective-permute-start(bf16[4,32,1024]{2,1,0:T(8,128)(2,1)S(1)} %get-tuple-element.36), channel_id=1, source_target_pairs={{0,12},{1,13},{2,14},{3,15},{4,0},{5,1},{6,2},{7,3},{8,4},{9,5},{1... | collective-permute-start | bytes 786440 | tf_op jit(solution)/shard_map/ppermute | solution.py:103
  35.0 7.3 %collective-permute-start.17 = (bf16[4,32,1024]{2,1,0:T(8,128)(2,1)S(1)}, bf16[4,32,1024]{2,1,0:T(8,128)(2,1)S(1)}, u32[]{:S(2)}, u32[]{:S(2)}) collective-permute-start(bf16[4,32,1024]{2,1,0:T(8,128)(2,1)S(1)} %get-tuple-element.36), channel_id=1, source_target_pairs={{0,4},{1,5},{2,6},{3,7},{4,8},{5,9},{6,10},{7,11},{8,12},{9,13},{1... | collective-permute-start | bytes 786440 | tf_op jit(solution)/shard_map/ppermute | solution.py:103
  36.6 9.3 %collective-permute-start.2 = (bf16[4,16,1024]{2,1,0:T(8,128)(2,1)S(1)}, bf16[4,16,1024]{2,1,0:T(8,128)(2,1)S(1)}, u32[]{:S(2)}, u32[]{:S(2)}) collective-permute-start(bf16[4,16,1024]{2,1,0:T(8,128)(2,1)S(1)} %slice.175), channel_id=1, source_target_pairs={{0,1},{1,2},{2,3},{3,0},{4,5},{5,6},{6,7},{7,4},{8,9},{9,10},{10,1... | collective-permute-start | bytes 393224 | tf_op jit(solution)/shard_map/ppermute | solution.py:103
  36.8 10.0 %collective-permute-start.3 = (bf16[4,16,1024]{2,1,0:T(8,128)(2,1)S(1)}, bf16[4,16,1024]{2,1,0:T(8,128)(2,1)S(1)}, u32[]{:S(2)}, u32[]{:S(2)}) collective-permute-start(bf16[4,16,1024]{2,1,0:T(8,128)(2,1)S(1)} %slice.176), channel_id=1, source_target_pairs={{0,3},{1,0},{2,1},{3,2},{4,7},{5,4},{6,5},{7,6},{8,11},{9,8},{10,9... | collective-permute-start | bytes 393224 | tf_op jit(solution)/shard_map/ppermute | solution.py:103
  42.2 9.7 %collective-permute-start.18 = (bf16[4,16,1024]{2,1,0:T(8,128)(2,1)S(1)}, bf16[4,16,1024]{2,1,0:T(8,128)(2,1)S(1)}, u32[]{:S(2)}, u32[]{:S(2)}) collective-permute-start(bf16[4,16,1024]{2,1,0:T(8,128)(2,1)S(1)} %slice.190), channel_id=1, source_target_pairs={{0,4},{1,5},{2,6},{3,7},{4,8},{5,9},{6,10},{7,11},{8,12},{9,13},{1... | collective-permute-start | bytes 393224 | tf_op jit(solution)/shard_map/ppermute | solution.py:103
  42.3 10.3 %collective-permute-start.19 = (bf16[4,16,1024]{2,1,0:T(8,128)(2,1)S(1)}, bf16[4,16,1024]{2,1,0:T(8,128)(2,1)S(1)}, u32[]{:S(2)}, u32[]{:S(2)}) collective-permute-start(bf16[4,16,1024]{2,1,0:T(8,128)(2,1)S(1)} %slice.191), channel_id=1, source_target_pairs={{0,12},{1,13},{2,14},{3,15},{4,0},{5,1},{6,2},{7,3},{8,4},{9,5},{1... | collective-permute-start | bytes 393224 | tf_op jit(solution)/shard_map/ppermute | solution.py:103
  48.4 22.9 %collective-permute-start.5 = (bf16[4,128,1024]{2,1,0:T(8,128)(2,1)}, bf16[4,128,1024]{2,1,0:T(8,128)(2,1)S(1)}, u32[]{:S(2)}, u32[]{:S(2)}) collective-permute-start(bf16[4,128,1024]{2,1,0:T(8,128)(2,1)} %get-tuple-element.37), channel_id=1, source_target_pairs={{0,4},{1,5},{2,6},{3,7},{4,8},{5,9},{6,10},{7,11},{8,12},{9,13},{1... | collective-permute-start | bytes 3145736 | tf_op jit(solution)/shard_map/ppermute | solution.py:103
  49.2 22.8 %collective-permute-start.4 = (bf16[4,128,1024]{2,1,0:T(8,128)(2,1)}, bf16[4,128,1024]{2,1,0:T(8,128)(2,1)S(1)}, u32[]{:S(2)}, u32[]{:S(2)}) collective-permute-start(bf16[4,128,1024]{2,1,0:T(8,128)(2,1)} %get-tuple-element.37), channel_id=1, source_target_pairs={{0,12},{1,13},{2,14},{3,15},{4,0},{5,1},{6,2},{7,3},{8,4},{9,5},{1... | collective-permute-start | bytes 3145736 | tf_op jit(solution)/shard_map/ppermute | solution.py:103
  54.3 24.2 %collective-permute-start.20 = (bf16[4,128,1024]{2,1,0:T(8,128)(2,1)}, bf16[4,128,1024]{2,1,0:T(8,128)(2,1)S(1)}, u32[]{:S(2)}, u32[]{:S(2)}) collective-permute-start(bf16[4,128,1024]{2,1,0:T(8,128)(2,1)} %get-tuple-element.41), channel_id=1, source_target_pairs={{0,3},{1,0},{2,1},{3,2},{4,7},{5,4},{6,5},{7,6},{8,11},{9,8},{10,9... | collective-permute-start | bytes 3145736 | tf_op jit(solution)/shard_map/ppermute | solution.py:103
  55.6 22.1 %collective-permute-start.21 = (bf16[4,128,1024]{2,1,0:T(8,128)(2,1)}, bf16[4,128,1024]{2,1,0:T(8,128)(2,1)S(1)}, u32[]{:S(2)}, u32[]{:S(2)}) collective-permute-start(bf16[4,128,1024]{2,1,0:T(8,128)(2,1)} %get-tuple-element.41), channel_id=1, source_target_pairs={{0,1},{1,2},{2,3},{3,0},{4,5},{5,6},{6,7},{7,4},{8,9},{9,10},{10,1... | collective-permute-start | bytes 3145736 | tf_op jit(solution)/shard_map/ppermute | solution.py:103
  71.3 12.9 %collective-permute-start.6 = (bf16[4,64,1024]{2,1,0:T(8,128)(2,1)S(1)}, bf16[4,64,1024]{2,1,0:T(8,128)(2,1)S(1)}, u32[]{:S(2)}, u32[]{:S(2)}) collective-permute-start(bf16[4,64,1024]{2,1,0:T(8,128)(2,1)S(1)} %slice.177), channel_id=1, source_target_pairs={{0,4},{1,5},{2,6},{3,7},{4,8},{5,9},{6,10},{7,11},{8,12},{9,13},{1... | collective-permute-start | bytes 1572872 | tf_op jit(solution)/shard_map/ppermute | solution.py:103
  72.1 12.9 %collective-permute-start.7 = (bf16[4,64,1024]{2,1,0:T(8,128)(2,1)S(1)}, bf16[4,64,1024]{2,1,0:T(8,128)(2,1)S(1)}, u32[]{:S(2)}, u32[]{:S(2)}) collective-permute-start(bf16[4,64,1024]{2,1,0:T(8,128)(2,1)S(1)} %slice.178), channel_id=1, source_target_pairs={{0,12},{1,13},{2,14},{3,15},{4,0},{5,1},{6,2},{7,3},{8,4},{9,5},{1... | collective-permute-start | bytes 1572872 | tf_op jit(solution)/shard_map/ppermute | solution.py:103
  78.5 20.1 %collective-permute-start.22 = (bf16[4,64,1024]{2,1,0:T(8,128)(2,1)}, bf16[4,64,1024]{2,1,0:T(8,128)(2,1)}, u32[]{:S(2)}, u32[]{:S(2)}) collective-permute-start(bf16[4,64,1024]{2,1,0:T(8,128)(2,1)} %slice.192), channel_id=1, source_target_pairs={{0,1},{1,2},{2,3},{3,0},{4,5},{5,6},{6,7},{7,4},{8,9},{9,10},{10,1... | collective-permute-start | bytes 1572872 | tf_op jit(solution)/shard_map/ppermute | solution.py:103
  79.4 21.2 %collective-permute-start.23 = (bf16[4,64,1024]{2,1,0:T(8,128)(2,1)}, bf16[4,64,1024]{2,1,0:T(8,128)(2,1)}, u32[]{:S(2)}, u32[]{:S(2)}) collective-permute-start(bf16[4,64,1024]{2,1,0:T(8,128)(2,1)} %slice.193), channel_id=1, source_target_pairs={{0,3},{1,0},{2,1},{3,2},{4,7},{5,4},{6,5},{7,6},{8,11},{9,8},{10,9... | collective-permute-start | bytes 1572872 | tf_op jit(solution)/shard_map/ppermute | solution.py:103
  97.2 18.5 %collective-permute-start.10 = (bf16[4,64,1024]{2,1,0:T(8,128)(2,1)}, bf16[4,64,1024]{2,1,0:T(8,128)(2,1)}, u32[]{:S(2)}, u32[]{:S(2)}) collective-permute-start(bf16[4,64,1024]{2,1,0:T(8,128)(2,1)} %get-tuple-element.16), channel_id=1, source_target_pairs={{0,12},{1,13},{2,14},{3,15},{4,0},{5,1},{6,2},{7,3},{8,4},{9,5},{1... | collective-permute-start | bytes 1572872 | tf_op jit(solution)/shard_map/ppermute | solution.py:103
  97.2 18.5 %collective-permute-start.8 = (bf16[4,64,1024]{2,1,0:T(8,128)(2,1)}, bf16[4,64,1024]{2,1,0:T(8,128)(2,1)}, u32[]{:S(2)}, u32[]{:S(2)}) collective-permute-start(bf16[4,64,1024]{2,1,0:T(8,128)(2,1)} %get-tuple-element.15), channel_id=1, source_target_pairs={{0,4},{1,5},{2,6},{3,7},{4,8},{5,9},{6,10},{7,11},{8,12},{9,13},{1... | collective-permute-start | bytes 1572872 | tf_op jit(solution)/shard_map/ppermute | solution.py:103
  111.5 10.8 %copy-start.2 = (bf16[4,512,1024]{2,1,0:T(8,128)(2,1)S(1)}, bf16[4,512,1024]{2,1,0:T(8,128)(2,1)}, u32[]{:S(2)}) copy-start(bf16[4,512,1024]{2,1,0:T(8,128)(2,1)} %shard_map.74) | copy-start | bytes 12582916
  113.0 9.3 %collective-permute-start.24 = (bf16[4,64,1024]{2,1,0:T(8,128)(2,1)S(1)}, bf16[4,64,1024]{2,1,0:T(8,128)(2,1)S(1)}, u32[]{:S(2)}, u32[]{:S(2)}) collective-permute-start(bf16[4,64,1024]{2,1,0:T(8,128)(2,1)S(1)} %get-tuple-element.21), channel_id=1, source_target_pairs={{0,1},{1,2},{2,3},{3,0},{4,5},{5,6},{6,7},{7,4},{8,9},{9,10},{10,1... | collective-permute-start | bytes 1572872 | tf_op jit(solution)/shard_map/ppermute | solution.py:103
  113.0 9.2 %collective-permute-start.26 = (bf16[4,64,1024]{2,1,0:T(8,128)(2,1)S(1)}, bf16[4,64,1024]{2,1,0:T(8,128)(2,1)S(1)}, u32[]{:S(2)}, u32[]{:S(2)}) collective-permute-start(bf16[4,64,1024]{2,1,0:T(8,128)(2,1)S(1)} %get-tuple-element.22), channel_id=1, source_target_pairs={{0,3},{1,0},{2,1},{3,2},{4,7},{5,4},{6,5},{7,6},{8,11},{9,8},{10,9... | collective-permute-start | bytes 1572872 | tf_op jit(solution)/shard_map/ppermute | solution.py:103
  118.1 18.2 %collective-permute-start.11 = (bf16[4,128,1024]{2,1,0:T(8,128)(2,1)S(1)}, bf16[4,128,1024]{2,1,0:T(8,128)(2,1)S(1)}, u32[]{:S(2)}, u32[]{:S(2)}) collective-permute-start(bf16[4,128,1024]{2,1,0:T(8,128)(2,1)S(1)} %get-tuple-element.14), channel_id=1, source_target_pairs={{0,12},{1,13},{2,14},{3,15},{4,0},{5,1},{6,2},{7,3},{8,4},{9,5},{1... | collective-permute-start | bytes 3145736 | tf_op jit(solution)/shard_map/ppermute | solution.py:103
  118.3 19.4 %collective-permute-start.9 = (bf16[4,128,1024]{2,1,0:T(8,128)(2,1)S(1)}, bf16[4,128,1024]{2,1,0:T(8,128)(2,1)S(1)}, u32[]{:S(2)}, u32[]{:S(2)}) collective-permute-start(bf16[4,128,1024]{2,1,0:T(8,128)(2,1)S(1)} %get-tuple-element.13), channel_id=1, source_target_pairs={{0,4},{1,5},{2,6},{3,7},{4,8},{5,9},{6,10},{7,11},{8,12},{9,13},{1... | collective-permute-start | bytes 3145736 | tf_op jit(solution)/shard_map/ppermute | solution.py:103
  122.9 20.7 %collective-permute-start.25 = (bf16[4,128,1024]{2,1,0:T(8,128)(2,1)S(1)}, bf16[4,128,1024]{2,1,0:T(8,128)(2,1)S(1)}, u32[]{:S(2)}, u32[]{:S(2)}) collective-permute-start(bf16[4,128,1024]{2,1,0:T(8,128)(2,1)S(1)} %get-tuple-element.19), channel_id=1, source_target_pairs={{0,1},{1,2},{2,3},{3,0},{4,5},{5,6},{6,7},{7,4},{8,9},{9,10},{10,1... | collective-permute-start | bytes 3145736 | tf_op jit(solution)/shard_map/ppermute | solution.py:103
  123.0 20.7 %collective-permute-start.27 = (bf16[4,128,1024]{2,1,0:T(8,128)(2,1)S(1)}, bf16[4,128,1024]{2,1,0:T(8,128)(2,1)S(1)}, u32[]{:S(2)}, u32[]{:S(2)}) collective-permute-start(bf16[4,128,1024]{2,1,0:T(8,128)(2,1)S(1)} %get-tuple-element.20), channel_id=1, source_target_pairs={{0,3},{1,0},{2,1},{3,2},{4,7},{5,4},{6,5},{7,6},{8,11},{9,8},{10,9... | collective-permute-start | bytes 3145736 | tf_op jit(solution)/shard_map/ppermute | solution.py:103
  139.4 7.8 %collective-permute-start.12 = (bf16[4,16,1024]{2,1,0:T(8,128)(2,1)S(1)}, bf16[4,16,1024]{2,1,0:T(8,128)(2,1)S(1)}, u32[]{:S(2)}, u32[]{:S(2)}) collective-permute-start(bf16[4,16,1024]{2,1,0:T(8,128)(2,1)S(1)} %get-tuple-element.27), channel_id=1, source_target_pairs={{0,1},{1,2},{2,3},{3,0},{4,5},{5,6},{6,7},{7,4},{8,9},{9,10},{10,1... | collective-permute-start | bytes 393224 | tf_op jit(solution)/shard_map/ppermute | solution.py:103
  139.5 7.7 %collective-permute-start.14 = (bf16[4,16,1024]{2,1,0:T(8,128)(2,1)S(1)}, bf16[4,16,1024]{2,1,0:T(8,128)(2,1)S(1)}, u32[]{:S(2)}, u32[]{:S(2)}) collective-permute-start(bf16[4,16,1024]{2,1,0:T(8,128)(2,1)S(1)} %get-tuple-element.28), channel_id=1, source_target_pairs={{0,3},{1,0},{2,1},{3,2},{4,7},{5,4},{6,5},{7,6},{8,11},{9,8},{10,9... | collective-permute-start | bytes 393224 | tf_op jit(solution)/shard_map/ppermute | solution.py:103
  144.4 5.9 %collective-permute-start.28 = (bf16[4,16,1024]{2,1,0:T(8,128)(2,1)S(1)}, bf16[4,16,1024]{2,1,0:T(8,128)(2,1)S(1)}, u32[]{:S(2)}, u32[]{:S(2)}) collective-permute-start(bf16[4,16,1024]{2,1,0:T(8,128)(2,1)S(1)} %get-tuple-element.29), channel_id=1, source_target_pairs={{0,4},{1,5},{2,6},{3,7},{4,8},{5,9},{6,10},{7,11},{8,12},{9,13},{1... | collective-permute-start | bytes 393224 | tf_op jit(solution)/shard_map/ppermute | solution.py:103
  144.5 5.8 %collective-permute-start.30 = (bf16[4,16,1024]{2,1,0:T(8,128)(2,1)S(1)}, bf16[4,16,1024]{2,1,0:T(8,128)(2,1)S(1)}, u32[]{:S(2)}, u32[]{:S(2)}) collective-permute-start(bf16[4,16,1024]{2,1,0:T(8,128)(2,1)S(1)} %get-tuple-element.30), channel_id=1, source_target_pairs={{0,12},{1,13},{2,14},{3,15},{4,0},{5,1},{6,2},{7,3},{8,4},{9,5},{1... | collective-permute-start | bytes 393224 | tf_op jit(solution)/shard_map/ppermute | solution.py:103
  147.3 9.8 %collective-permute-start.13 = (bf16[4,32,1024]{2,1,0:T(8,128)(2,1)S(1)}, bf16[4,32,1024]{2,1,0:T(8,128)(2,1)S(1)}, u32[]{:S(2)}, u32[]{:S(2)}) collective-permute-start(bf16[4,32,1024]{2,1,0:T(8,128)(2,1)S(1)} %get-tuple-element.23), channel_id=1, source_target_pairs={{0,1},{1,2},{2,3},{3,0},{4,5},{5,6},{6,7},{7,4},{8,9},{9,10},{10,1... | collective-permute-start | bytes 786440 | tf_op jit(solution)/shard_map/ppermute | solution.py:103
  147.4 9.7 %collective-permute-start.15 = (bf16[4,32,1024]{2,1,0:T(8,128)(2,1)S(1)}, bf16[4,32,1024]{2,1,0:T(8,128)(2,1)S(1)}, u32[]{:S(2)}, u32[]{:S(2)}) collective-permute-start(bf16[4,32,1024]{2,1,0:T(8,128)(2,1)S(1)} %get-tuple-element.24), channel_id=1, source_target_pairs={{0,3},{1,0},{2,1},{3,2},{4,7},{5,4},{6,5},{7,6},{8,11},{9,8},{10,9... | collective-permute-start | bytes 786440 | tf_op jit(solution)/shard_map/ppermute | solution.py:103
  150.3 27.5 %copy-start.4 = (bf16[32,8,1024]{2,1,0:T(8,128)(2,1)S(1)}, bf16[32,8,1024]{2,1,0:T(8,128)(2,1)}, u32[]{:S(2)}) copy-start(bf16[32,8,1024]{2,1,0:T(8,128)(2,1)} %param.7) | copy-start | bytes 1572868
  150.4 6.8 %collective-permute-start.29 = (bf16[4,32,1024]{2,1,0:T(8,128)(2,1)S(1)}, bf16[4,32,1024]{2,1,0:T(8,128)(2,1)S(1)}, u32[]{:S(2)}, u32[]{:S(2)}) collective-permute-start(bf16[4,32,1024]{2,1,0:T(8,128)(2,1)S(1)} %get-tuple-element.25), channel_id=1, source_target_pairs={{0,4},{1,5},{2,6},{3,7},{4,8},{5,9},{6,10},{7,11},{8,12},{9,13},{1... | collective-permute-start | bytes 786440 | tf_op jit(solution)/shard_map/ppermute | solution.py:103
  150.5 6.7 %collective-permute-start.31 = (bf16[4,32,1024]{2,1,0:T(8,128)(2,1)S(1)}, bf16[4,32,1024]{2,1,0:T(8,128)(2,1)S(1)}, u32[]{:S(2)}, u32[]{:S(2)}) collective-permute-start(bf16[4,32,1024]{2,1,0:T(8,128)(2,1)S(1)} %get-tuple-element.26), channel_id=1, source_target_pairs={{0,12},{1,13},{2,14},{3,15},{4,0},{5,1},{6,2},{7,3},{8,4},{9,5},{1... | collective-permute-start | bytes 786440 | tf_op jit(solution)/shard_map/ppermute | solution.py:103
  160.7 26.6 %all-to-all-start.1 = ((bf16[8,32,1024]{2,1,0:T(8,128)(2,1)}), bf16[8,32,1024]{2,1,0:T(8,128)(2,1)}, u32[]{:S(2)}, u32[]{:S(2)}) async-start(bf16[8,32,1024]{2,1,0:T(8,128)(2,1)} %broadcast_select_fusion.1), calls=%async_computation.1 | async-start | bytes 1048576 | tf_op jit(solution)/shard_map/all_to_all | solution.py:218

commit v9 on v8

--- a/solution.py
+++ b/solution.py
@@ -33,9 +33,8 @@
     return (target, arrival, slot_of_pos)
 
 
-def attend_kernel(n_live_ref, q_ref, kv_ref, keep_ref, o_ref, *, heads, head_dim, scale):
+def attend_kernel(n_live_ref, q_ref, kv_ref, vk_ref, o_ref, *, heads, head_dim):
     row = pl.program_id(0)
-    width = heads * head_dim
 
     @pl.when(n_live_ref[row] <= 0)
     def _():
@@ -43,27 +42,26 @@
 
     @pl.when(n_live_ref[row] > 0)
     def _():
-        half_keep = keep_ref[0] * 0.5
         for h in range(heads):
             lo = h * head_dim
             q = q_ref[0, :, lo:lo + head_dim]
             k = kv_ref[0, :, lo:lo + head_dim]
-            v = kv_ref[0, :, width + lo:width + lo + head_dim]
-            s = lax.dot_general(q, k, (((1,), (1,)), ((), ())), preferred_element_type=jnp.float32)
-            y = s * scale
-            w = (y * (1.0 + jnp.tanh(y * 0.5)) * half_keep).astype(jnp.bfloat16)
+            v = vk_ref[0, :, lo:lo + head_dim]
+            t = lax.dot_general(q, k, (((1,), (1,)), ((), ())), preferred_element_type=jnp.float32)
+            w = (t * (1.0 + jnp.tanh(t))).astype(jnp.bfloat16)
             o = jnp.dot(w, v, preferred_element_type=jnp.float32)
             o_ref[0, :, lo:lo + head_dim] = o.astype(o_ref.dtype)
 
 
-def attend_local(queries, piece, live, first_event, scale, heads, out_dtype):
+def attend_local(queries, piece, live, first_event, heads, out_dtype):
     rows, cands, width = queries.shape
     count = piece.shape[1]
     head_dim = width // heads
     events = (first_event + jnp.arange(count)).astype(jnp.float32)
-    keep = ((events[None, :] < live[:, None]).astype(jnp.float32) / live[:, None])[:, None, :]
+    keep = (events[None, :] < live[:, None]).astype(jnp.float32) / live[:, None]
+    values = (piece[:, :, width:].astype(jnp.float32) * keep[:, :, None]).astype(jnp.bfloat16)
     n_live = jnp.clip(live.astype(jnp.int32) - first_event, 0, count).astype(jnp.int32)
-    kernel = functools.partial(attend_kernel, heads=heads, head_dim=head_dim, scale=scale)
+    kernel = functools.partial(attend_kernel, heads=heads, head_dim=head_dim)
     flops = 4 * rows * cands * count * width
     return pl.pallas_call(
         kernel,
@@ -73,8 +71,8 @@
             grid=(rows,),
             in_specs=[
                 pl.BlockSpec((1, cands, width), lambda r, n: (r, 0, 0)),
-                pl.BlockSpec((1, count, 2 * width), lambda r, n: (r, 0, 0)),
-                pl.BlockSpec((1, 1, count), lambda r, n: (r, 0, 0)),
+                pl.BlockSpec((1, count, width), lambda r, n: (r, 0, 0)),
+                pl.BlockSpec((1, count, width), lambda r, n: (r, 0, 0)),
             ],
             out_specs=pl.BlockSpec((1, cands, width), lambda r, n: (r, 0, 0)),
         ),
@@ -83,7 +81,7 @@
             transcendentals=rows * cands * count * heads,
             bytes_accessed=rows * (cands * width * 4 + count * width * 4),
         ),
-    )(n_live, queries, piece, keep)
+    )(n_live, queries, piece, values)
 
 
 def shift_perm(grid, axis, shift):
@@ -196,8 +194,7 @@
     inputs = candidates.astype(jnp.float32)
     normed = layer_norm(inputs).astype(jnp.bfloat16).reshape(cand_rows * per_group, width)
     queries = jax.nn.silu(jnp.dot(normed, w_uq[:, width:], preferred_element_type=jnp.float32))
-    queries = queries.astype(jnp.bfloat16).reshape(cand_rows, per_group, width)
-    scale = head_dim ** (-0.5)
+    queries = (queries * (0.5 * head_dim ** (-0.5))).astype(jnp.bfloat16).reshape(cand_rows, per_group, width)
 
     q_pos = jnp.swapaxes(queries, 0, 1)
     q_out = jnp.where(send_filled[:, None, None], q_pos[send_pos], jnp.zeros((), jnp.bfloat16))
@@ -209,7 +206,7 @@
     for rows_of, order in halves:
         q_all = torus_gather(q_rows[rows_of], grid, order)
         partial = attend_local(
-            q_all, kv_cache[rows_of], row_live[rows_of], member_now * count, scale, HEADS, jnp.bfloat16
+            q_all, kv_cache[rows_of], row_live[rows_of], member_now * count, HEADS, jnp.bfloat16
         )
         sums.append(torus_reduce(partial, grid, order))
     summed = jnp.concatenate(sums, axis=0).astype(jnp.bfloat16)

time: 194 us -> 192 us (0.990)
  no operation moved by 1% of the time
where the time goes in v9:
time: 192 us; the launch traced here: 191 us
  starting transfers between devices  64.5 us (34%)
  waiting for transfers between devices  52.5 us (27%)
  local copies, waits for them, and re-layouts  32.3 us (17%)
  other arithmetic  18 us (9%)
  Pallas kernels  15.5 us (8%)
  matrix products  7.74 us (4%)
    ppermute x32, starting transfers between devices, send(): return lax.ppermute(value, 'member', shift_perm(grid, axis, shift))  41.4 us
    ppermute x32, waiting for transfers between devices, send(): return lax.ppermute(value, 'member', shift_perm(grid, axis, shift))  37.9 us
    all_to_all x1, starting transfers between devices, on_device(): lax.all_to_all(a_out, 'group', split_axis=0, concat_axis=0, tiled=True)  17.1 us
    pallas_call x2, Pallas kernels, attend_local(): pl.pallas_call(kernel, out_shape=jax.ShapeDtypeStruct((rows, cands, width...  15.5 us
    unnamed x23, local copies, waits for them, and re-layouts  12.7 us
    all_to_all x1, waiting for transfers between devices, on_device(): lax.all_to_all(q_out, 'group', split_axis=0, concat_axis=0, tiled=True)  8.61 us
    all_to_all x1, waiting for transfers between devices, on_device(): lax.all_to_all(a_out, 'group', split_axis=0, concat_axis=0, tiled=True)  6.03 us
    all_to_all x1, starting transfers between devices, on_device(): lax.all_to_all(q_out, 'group', split_axis=0, concat_axis=0, tiled=True)  5.96 us
  transfers between devices with their start and end apart: 34, of which 11 were waited for; matrix products, arithmetic and copies ran while one was open for 19% of the time, Pallas kernels for 8%

profile of v9, /device:TPU:1, one launch (start us, length us, event | category | flops | bytes accessed | tf_op | source)
XLA Modules:
  0.0 191.1 jit_solution(83698162000683769)
XLA Ops:
  0.0 1.0 fusion.36
  1.0 1.3 gather_fusion
  4.1 1.2 convert_reduce_fusion
  5.5 1.3 fusion.8
  7.0 2.7 %fusion.19 = bf16[32,8,1024]{2,1,0:T(8,128)(2,1)S(1)} fusion(bf16[1024,2048]{1,0:T(8,128)(2,1)} %param.12, bf16[32,8,1024]{2,1,0:T(8,128)(2,1)} %param.7, f32[32,8]{1,0:T(8,128)S(1)} %copy.37, f32[32,8]{1,0:T(8,128)S(1)} %copy.35), kind=kOutput, calls=%fused_computation.39 | convolution fusion | flops 539492352 | bytes 3147776 | tf_op jit(solution)/shard_map/dot_general | solution.py:196
  10.5 0.9 broadcast_select_fusion
  11.4 6.0 %all-to-all-start = ((bf16[8,32,1024]{2,1,0:T(8,128)(2,1)}), bf16[8,32,1024]{2,1,0:T(8,128)(2,1)S(1)}, u32[]{:S(2)}, u32[]{:S(2)}) async-start(bf16[8,32,1024]{2,1,0:T(8,128)(2,1)} %broadcast_select_fusion), calls=%async_computation | async-start | bytes 1048576 | tf_op jit(solution)/shard_map/all_to_all | solution.py:201
  18.1 8.6 %all-to-all-done = bf16[8,32,1024]{2,1,0:T(8,128)(2,1)S(1)} async-done(((bf16[8,32,1024]{2,1,0:T(8,128)(2,1)}), bf16[8,32,1024]{2,1,0:T(8,128)(2,1)S(1)}, u32[]{:S(2)}, u32[]{:S(2)}) %all-to-all-start) | async-done | bytes 524320 | tf_op jit(solution)/shard_map/all_to_all | solution.py:201
  27.4 0.9 constant_dynamic-update-slice_fusion.4
  28.3 1.2 collective-permute-start.1
  29.6 1.5 collective-permute-start
  31.0 3.8 %collective-permute-start.16 = (bf16[4,32,1024]{2,1,0:T(8,128)(2,1)S(1)}, bf16[4,32,1024]{2,1,0:T(8,128)(2,1)S(1)}, u32[]{:S(2)}, u32[]{:S(2)}) collective-permute-start(bf16[4,32,1024]{2,1,0:T(8,128)(2,1)S(1)} %get-tuple-element.38), channel_id=1, source_target_pairs={{0,12},{1,13},{2,14},{3,15},{4,0},{5,1},{6,2},{7,3},{8,4},{9,5},{1... | collective-permute-start | bytes 786440 | tf_op jit(solution)/shard_map/ppermute | solution.py:101
  34.8 1.6 collective-permute-done.1
  36.6 2.7 %collective-permute-start.3 = (bf16[4,16,1024]{2,1,0:T(8,128)(2,1)S(1)}, bf16[4,16,1024]{2,1,0:T(8,128)(2,1)S(1)}, u32[]{:S(2)}, u32[]{:S(2)}) collective-permute-start(bf16[4,16,1024]{2,1,0:T(8,128)(2,1)S(1)} %slice.186), channel_id=1, source_target_pairs={{0,3},{1,0},{2,1},{3,2},{4,7},{5,4},{6,5},{7,6},{8,11},{9,8},{10,9... | collective-permute-start | bytes 393224 | tf_op jit(solution)/shard_map/ppermute | solution.py:101
  39.3 2.7 %collective-permute-done.17 = bf16[4,32,1024]{2,1,0:T(8,128)(2,1)S(1)} collective-permute-done((bf16[4,32,1024]{2,1,0:T(8,128)(2,1)S(1)}, bf16[4,32,1024]{2,1,0:T(8,128)(2,1)S(1)}, u32[]{:S(2)}, u32[]{:S(2)}) %collective-permute-start.17) | collective-permute-done | bytes 262176 | tf_op jit(solution)/shard_map/ppermute | solution.py:101
  42.2 2.7 %collective-permute-start.19 = (bf16[4,16,1024]{2,1,0:T(8,128)(2,1)S(1)}, bf16[4,16,1024]{2,1,0:T(8,128)(2,1)S(1)}, u32[]{:S(2)}, u32[]{:S(2)}) collective-permute-start(bf16[4,16,1024]{2,1,0:T(8,128)(2,1)S(1)} %slice.201), channel_id=1, source_target_pairs={{0,12},{1,13},{2,14},{3,15},{4,0},{5,1},{6,2},{7,3},{8,4},{9,5},{1... | collective-permute-start | bytes 393224 | tf_op jit(solution)/shard_map/ppermute | solution.py:101
  44.9 0.7 constant_dynamic-update-slice_fusion.3
  47.0 0.7 constant_dynamic-update-slice_fusion
  47.7 0.7 constant_dynamic-update-slice_fusion.17
  48.5 2.7 %collective-permute-start.4 = (bf16[4,128,1024]{2,1,0:T(8,128)(2,1)S(1)}, bf16[4,128,1024]{2,1,0:T(8,128)(2,1)S(1)}, u32[]{:S(2)}, u32[]{:S(2)}) collective-permute-start(bf16[4,128,1024]{2,1,0:T(8,128)(2,1)S(1)} %get-tuple-element.39), channel_id=1, source_target_pairs={{0,12},{1,13},{2,14},{3,15},{4,0},{5,1},{6,2},{7,3},{8,4},{9,5},{1... | collective-permute-start | bytes 3145736 | tf_op jit(solution)/shard_map/ppermute | solution.py:101
  52.5 0.7 constant_dynamic-update-slice_fusion.14
  53.2 1.3 collective-permute-start.20
  54.7 2.5 %fusion.51 = (bf16[4,128,2048]{2,1,0:T(8,128)(2,1)}, bf16[4,128,2048]{2,1,0:T(8,128)(2,1)}) fusion(bf16[8,128,2048]{2,1,0:T(8,128)(2,1)S(1)} %copy-done.3), kind=kLoop, calls=%fused_computation.156 | loop fusion | bytes 8388608 | tf_op jit(solution)/shard_map/slice | solution.py:209
  57.2 13.2 %collective-permute-done.5 = bf16[4,128,1024]{2,1,0:T(8,128)(2,1)S(1)} collective-permute-done((bf16[4,128,1024]{2,1,0:T(8,128)(2,1)S(1)}, bf16[4,128,1024]{2,1,0:T(8,128)(2,1)S(1)}, u32[]{:S(2)}, u32[]{:S(2)}) %collective-permute-start.5) | collective-permute-done | bytes 1048608 | tf_op jit(solution)/shard_map/ppermute | solution.py:101
  70.6 1.8 multiply_convert_fusion.1
  72.4 2.7 %collective-permute-start.7 = (bf16[4,64,1024]{2,1,0:T(8,128)(2,1)S(1)}, bf16[4,64,1024]{2,1,0:T(8,128)(2,1)S(1)}, u32[]{:S(2)}, u32[]{:S(2)}) collective-permute-start(bf16[4,64,1024]{2,1,0:T(8,128)(2,1)S(1)} %slice.188), channel_id=1, source_target_pairs={{0,12},{1,13},{2,14},{3,15},{4,0},{5,1},{6,2},{7,3},{8,4},{9,5},{1... | collective-permute-start | bytes 1572872 | tf_op jit(solution)/shard_map/ppermute | solution.py:101
  76.4 0.8 slice.202
  77.2 0.8 slice.203
  78.0 2.7 %collective-permute-start.23 = (bf16[4,64,1024]{2,1,0:T(8,128)(2,1)}, bf16[4,64,1024]{2,1,0:T(8,128)(2,1)}, u32[]{:S(2)}, u32[]{:S(2)}) collective-permute-start(bf16[4,64,1024]{2,1,0:T(8,128)(2,1)} %slice.203), channel_id=1, source_target_pairs={{0,3},{1,0},{2,1},{3,2},{4,7},{5,4},{6,5},{7,6},{8,11},{9,8},{10,9... | collective-permute-start | bytes 1572872 | tf_op jit(solution)/shard_map/ppermute | solution.py:101
  80.7 1.1 constant_dynamic-update-slice_fusion.8
  81.8 1.1 constant_dynamic-update-slice_fusion.22
  82.8 0.8 constant_dynamic-update-slice_fusion.7
  83.7 0.9 constant_dynamic-update-slice_fusion.6
  84.5 1.1 constant_dynamic-update-slice_fusion.5.q_ref
  85.6 7.7 %shard_map.73 = bf16[4,512,1024]{2,1,0:T(8,128)(2,1)} custom-call(s32[4]{0:T(128)} %get-tuple-element.59.n_live_ref, bf16[4,512,1024]{2,1,0:T(8,128)(2,1)} %constant_dynamic-update-slice_fusion.5.q_ref, bf16[4,128,2048]{2,1,0:T(8,128)(2,1)} %get-tuple-element.19.kv_ref, bf16[4,128,1024]{2,1,0:T(8,128)(2,1)} %get-tuple-element.17.vk_ref), custom_call_target="tpu_custom_call" | custom-call | flops 1073741824 | bytes 10485760 | tf_op jit(solution)/shard_map/pallas_call | solution.py:66
  93.3 2.2 %fusion.50 = (bf16[4,64,1024]{2,1,0:T(8,128)(2,1)}, bf16[4,64,1024]{2,1,0:T(8,128)(2,1)}) fusion(bf16[4,512,1024]{2,1,0:T(8,128)(2,1)} %shard_map.73), kind=kLoop, calls=%fused_computation.155 | loop fusion | bytes 2097152 | tf_op jit(solution)/shard_map/slice | solution.py:137
  96.2 0.8 collective-permute-start.8
  97.0 1.9 constant_dynamic-update-slice_fusion.21
  98.9 1.9 constant_dynamic-update-slice_fusion.20
  100.8 1.1 constant_dynamic-update-slice_fusion.19.q_ref
  101.9 7.8 %shard_map.74 = bf16[4,512,1024]{2,1,0:T(8,128)(2,1)} custom-call(s32[4]{0:T(128)} %get-tuple-element.60.n_live_ref, bf16[4,512,1024]{2,1,0:T(8,128)(2,1)} %constant_dynamic-update-slice_fusion.19.q_ref, bf16[4,128,2048]{2,1,0:T(8,128)(2,1)} %get-tuple-element.20.kv_ref, bf16[4,128,1024]{2,1,0:T(8,128)(2,1)} %get-tuple-element.18.vk_ref), custom_call_target="tpu_custom_call" | custom-call | flops 1073741824 | bytes 10485760 | tf_op jit(solution)/shard_map/pallas_call | solution.py:66
  109.6 1.5 fusion.52
  111.2 2.7 %collective-permute-start.26 = (bf16[4,64,1024]{2,1,0:T(8,128)(2,1)S(1)}, bf16[4,64,1024]{2,1,0:T(8,128)(2,1)S(1)}, u32[]{:S(2)}, u32[]{:S(2)}) collective-permute-start(bf16[4,64,1024]{2,1,0:T(8,128)(2,1)S(1)} %get-tuple-element.24), channel_id=1, source_target_pairs={{0,3},{1,0},{2,1},{3,2},{4,7},{5,4},{6,5},{7,6},{8,11},{9,8},{10,9... | collective-permute-start | bytes 1572872 | tf_op jit(solution)/shard_map/ppermute | solution.py:101
  113.9 2.4 %add_convert_fusion.3 = (bf16[4,128,1024]{2,1,0:T(8,128)(2,1)S(1)}, bf16[4,128,1024]{2,1,0:T(8,128)(2,1)S(1)}) fusion(bf16[4,512,1024]{2,1,0:T(8,128)(2,1)} %shard_map.73, bf16[4,64,1024]{2,1,0:T(8,128)(2,1)} %collective-permute-done.8, bf16[4,64,1024]{2,1,0:T(8,128)(2,1)} %collective-permute-done.10), kind=kLoop, calls=%fused_computation.16 | loop fusion | flops 4194304 | bytes 5242880 | tf_op jit(solution)/shard_map/convert_element_type | solution.py:142
  116.2 0.8 collective-permute-start.11
  118.1 2.3 %collective-permute-done.24 = bf16[4,64,1024]{2,1,0:T(8,128)(2,1)S(1)} collective-permute-done((bf16[4,64,1024]{2,1,0:T(8,128)(2,1)S(1)}, bf16[4,64,1024]{2,1,0:T(8,128)(2,1)S(1)}, u32[]{:S(2)}, u32[]{:S(2)}) %collective-permute-start.24) | collective-permute-done | bytes 524320 | tf_op jit(solution)/shard_map/ppermute | solution.py:101
  121.2 2.7 %collective-permute-start.27 = (bf16[4,128,1024]{2,1,0:T(8,128)(2,1)S(1)}, bf16[4,128,1024]{2,1,0:T(8,128)(2,1)S(1)}, u32[]{:S(2)}, u32[]{:S(2)}) collective-permute-start(bf16[4,128,1024]{2,1,0:T(8,128)(2,1)S(1)} %get-tuple-element.22), channel_id=1, source_target_pairs={{0,3},{1,0},{2,1},{3,2},{4,7},{5,4},{6,5},{7,6},{8,11},{9,8},{10,9... | collective-permute-start | bytes 3145736 | tf_op jit(solution)/shard_map/ppermute | solution.py:101
  123.9 10.5 %collective-permute-done.11 = bf16[4,128,1024]{2,1,0:T(8,128)(2,1)S(1)} collective-permute-done((bf16[4,128,1024]{2,1,0:T(8,128)(2,1)S(1)}, bf16[4,128,1024]{2,1,0:T(8,128)(2,1)S(1)}, u32[]{:S(2)}, u32[]{:S(2)}) %collective-permute-start.11) | collective-permute-done | bytes 1048608 | tf_op jit(solution)/shard_map/ppermute | solution.py:101
  134.4 1.8 collective-permute-done.9
  136.2 1.7 fusion.48
  138.0 2.7 %collective-permute-start.14 = (bf16[4,16,1024]{2,1,0:T(8,128)(2,1)S(1)}, bf16[4,16,1024]{2,1,0:T(8,128)(2,1)S(1)}, u32[]{:S(2)}, u32[]{:S(2)}) collective-permute-start(bf16[4,16,1024]{2,1,0:T(8,128)(2,1)S(1)} %get-tuple-element.30), channel_id=1, source_target_pairs={{0,3},{1,0},{2,1},{3,2},{4,7},{5,4},{6,5},{7,6},{8,11},{9,8},{10,9... | collective-permute-start | bytes 393224 | tf_op jit(solution)/shard_map/ppermute | solution.py:101
  140.7 1.1 collective-permute-done.25
  142.6 2.7 %collective-permute-start.30 = (bf16[4,16,1024]{2,1,0:T(8,128)(2,1)S(1)}, bf16[4,16,1024]{2,1,0:T(8,128)(2,1)S(1)}, u32[]{:S(2)}, u32[]{:S(2)}) collective-permute-start(bf16[4,16,1024]{2,1,0:T(8,128)(2,1)S(1)} %get-tuple-element.32), channel_id=1, source_target_pairs={{0,12},{1,13},{2,14},{3,15},{4,0},{5,1},{6,2},{7,3},{8,4},{9,5},{1... | collective-permute-start | bytes 393224 | tf_op jit(solution)/shard_map/ppermute | solution.py:101
  145.5 2.9 %collective-permute-start.15 = (bf16[4,32,1024]{2,1,0:T(8,128)(2,1)S(1)}, bf16[4,32,1024]{2,1,0:T(8,128)(2,1)S(1)}, u32[]{:S(2)}, u32[]{:S(2)}) collective-permute-start(bf16[4,32,1024]{2,1,0:T(8,128)(2,1)S(1)} %get-tuple-element.26), channel_id=1, source_target_pairs={{0,3},{1,0},{2,1},{3,2},{4,7},{5,4},{6,5},{7,6},{8,11},{9,8},{10,9... | collective-permute-start | bytes 786440 | tf_op jit(solution)/shard_map/ppermute | solution.py:101
  148.7 2.7 %collective-permute-start.31 = (bf16[4,32,1024]{2,1,0:T(8,128)(2,1)S(1)}, bf16[4,32,1024]{2,1,0:T(8,128)(2,1)S(1)}, u32[]{:S(2)}, u32[]{:S(2)}) collective-permute-start(bf16[4,32,1024]{2,1,0:T(8,128)(2,1)S(1)} %get-tuple-element.28), channel_id=1, source_target_pairs={{0,12},{1,13},{2,14},{3,15},{4,0},{5,1},{6,2},{7,3},{8,4},{9,5},{1... | collective-permute-start | bytes 786440 | tf_op jit(solution)/shard_map/ppermute | solution.py:101
  151.3 3.9 %collective-permute-done.13 = bf16[4,32,1024]{2,1,0:T(8,128)(2,1)S(1)} collective-permute-done((bf16[4,32,1024]{2,1,0:T(8,128)(2,1)S(1)}, bf16[4,32,1024]{2,1,0:T(8,128)(2,1)S(1)}, u32[]{:S(2)}, u32[]{:S(2)}) %collective-permute-start.13) | collective-permute-done | bytes 262176 | tf_op jit(solution)/shard_map/ppermute | solution.py:101
  155.5 1.4 gather_fusion.6
  156.9 1.9 %broadcast_select_fusion.1 = bf16[8,32,1024]{2,1,0:T(8,128)(2,1)} fusion(bf16[8,32,1024]{2,1,0:T(8,128)(2,1)} %gather_fusion.6, pred[8]{0:T(512)(128)(4,1)S(1)} %fusion.40), kind=kLoop, calls=%fused_computation.60 | loop fusion | flops 262144 | bytes 1048584 | tf_op jit(solution)/shard_map/jit(_where)/select_n | solution.py:214
  158.8 17.1 %all-to-all-start.1 = ((bf16[8,32,1024]{2,1,0:T(8,128)(2,1)}), bf16[8,32,1024]{2,1,0:T(8,128)(2,1)}, u32[]{:S(2)}, u32[]{:S(2)}) async-start(bf16[8,32,1024]{2,1,0:T(8,128)(2,1)} %broadcast_select_fusion.1), calls=%async_computation.1 | async-start | bytes 1048576 | tf_op jit(solution)/shard_map/all_to_all | solution.py:215
  176.0 3.4 %multiply_bitcast_fusion = f32[32,8,1024]{2,1,0:T(8,128)} fusion(bf16[1024,2048]{1,0:T(8,128)(2,1)} %param.12, bf16[32,8,1024]{2,1,0:T(8,128)(2,1)S(1)} %copy-done.4, f32[32,8]{1,0:T(8,128)S(1)} %copy.37, f32[32,8]{1,0:T(8,128)S(1)} %copy.35), kind=kOutput, calls=%fused_computation.37 | convolution fusion | flops 538968064 | bytes 3672064 | tf_op jit(solution)/shard_map/dot_general | solution.py:218
  179.4 6.0 %all-to-all-done.1 = bf16[8,32,1024]{2,1,0:T(8,128)(2,1)} async-done(((bf16[8,32,1024]{2,1,0:T(8,128)(2,1)}), bf16[8,32,1024]{2,1,0:T(8,128)(2,1)}, u32[]{:S(2)}, u32[]{:S(2)}) %all-to-all-start.1) | async-done | bytes 524320 | tf_op jit(solution)/shard_map/all_to_all | solution.py:215
  185.5 1.6 gather_fusion.7
  187.5 1.9 fusion.14
  189.4 1.6 fusion.7
  (111 shorter events, 13.4 us)
Async XLA Ops:
  0.0 189.4 %copy-start = (bf16[1024,1024]{1,0:T(8,128)(2,1)S(1)}, bf16[1024,1024]{1,0:T(8,128)(2,1)}, u32[]{:S(2)}) copy-start(bf16[1024,1024]{1,0:T(8,128)(2,1)} %param.13) | copy-start | bytes 6291460
  9.6 7.8 %copy-start.1 = (s32[64]{0:T(128)S(1)}, s32[64]{0:T(128)}, u32[]{:S(2)}) copy-start(s32[64]{0:T(128)} %param.11) | copy-start | bytes 772
  11.4 15.3 %all-to-all-start = ((bf16[8,32,1024]{2,1,0:T(8,128)(2,1)}), bf16[8,32,1024]{2,1,0:T(8,128)(2,1)S(1)}, u32[]{:S(2)}, u32[]{:S(2)}) async-start(bf16[8,32,1024]{2,1,0:T(8,128)(2,1)} %broadcast_select_fusion), calls=%async_computation | async-start | bytes 1048576 | tf_op jit(solution)/shard_map/all_to_all | solution.py:201
  27.3 27.4 %copy-start.3 = (bf16[8,128,2048]{2,1,0:T(8,128)(2,1)S(1)}, bf16[8,128,2048]{2,1,0:T(8,128)(2,1)}, u32[]{:S(2)}) copy-start(bf16[8,128,2048]{2,1,0:T(8,128)(2,1)} %param.8) | copy-start | bytes 12582916
  28.3 8.1 %collective-permute-start.1 = (bf16[4,32,1024]{2,1,0:T(8,128)(2,1)S(1)}, bf16[4,32,1024]{2,1,0:T(8,128)(2,1)S(1)}, u32[]{:S(2)}, u32[]{:S(2)}) collective-permute-start(bf16[4,32,1024]{2,1,0:T(8,128)(2,1)S(1)} %get-tuple-element.37), channel_id=1, source_target_pairs={{0,1},{1,2},{2,3},{3,0},{4,5},{5,6},{6,7},{7,4},{8,9},{9,10},{10,1... | collective-permute-start | bytes 786440 | tf_op jit(solution)/shard_map/ppermute | solution.py:101
  29.6 7.0 %collective-permute-start = (bf16[4,32,1024]{2,1,0:T(8,128)(2,1)S(1)}, bf16[4,32,1024]{2,1,0:T(8,128)(2,1)S(1)}, u32[]{:S(2)}, u32[]{:S(2)}) collective-permute-start(bf16[4,32,1024]{2,1,0:T(8,128)(2,1)S(1)} %get-tuple-element.37), channel_id=1, source_target_pairs={{0,3},{1,0},{2,1},{3,2},{4,7},{5,4},{6,5},{7,6},{8,11},{9,8},{10,9... | collective-permute-start | bytes 786440 | tf_op jit(solution)/shard_map/ppermute | solution.py:101
  31.0 11.1 %collective-permute-start.16 = (bf16[4,32,1024]{2,1,0:T(8,128)(2,1)S(1)}, bf16[4,32,1024]{2,1,0:T(8,128)(2,1)S(1)}, u32[]{:S(2)}, u32[]{:S(2)}) collective-permute-start(bf16[4,32,1024]{2,1,0:T(8,128)(2,1)S(1)} %get-tuple-element.38), channel_id=1, source_target_pairs={{0,12},{1,13},{2,14},{3,15},{4,0},{5,1},{6,2},{7,3},{8,4},{9,5},{1... | collective-permute-start | bytes 786440 | tf_op jit(solution)/shard_map/ppermute | solution.py:101
  34.8 7.3 %collective-permute-start.17 = (bf16[4,32,1024]{2,1,0:T(8,128)(2,1)S(1)}, bf16[4,32,1024]{2,1,0:T(8,128)(2,1)S(1)}, u32[]{:S(2)}, u32[]{:S(2)}) collective-permute-start(bf16[4,32,1024]{2,1,0:T(8,128)(2,1)S(1)} %get-tuple-element.38), channel_id=1, source_target_pairs={{0,4},{1,5},{2,6},{3,7},{4,8},{5,9},{6,10},{7,11},{8,12},{9,13},{1... | collective-permute-start | bytes 786440 | tf_op jit(solution)/shard_map/ppermute | solution.py:101
  36.4 9.2 %collective-permute-start.2 = (bf16[4,16,1024]{2,1,0:T(8,128)(2,1)S(1)}, bf16[4,16,1024]{2,1,0:T(8,128)(2,1)S(1)}, u32[]{:S(2)}, u32[]{:S(2)}) collective-permute-start(bf16[4,16,1024]{2,1,0:T(8,128)(2,1)S(1)} %slice.185), channel_id=1, source_target_pairs={{0,1},{1,2},{2,3},{3,0},{4,5},{5,6},{6,7},{7,4},{8,9},{9,10},{10,1... | collective-permute-start | bytes 393224 | tf_op jit(solution)/shard_map/ppermute | solution.py:101
  36.6 9.7 %collective-permute-start.3 = (bf16[4,16,1024]{2,1,0:T(8,128)(2,1)S(1)}, bf16[4,16,1024]{2,1,0:T(8,128)(2,1)S(1)}, u32[]{:S(2)}, u32[]{:S(2)}) collective-permute-start(bf16[4,16,1024]{2,1,0:T(8,128)(2,1)S(1)} %slice.186), channel_id=1, source_target_pairs={{0,3},{1,0},{2,1},{3,2},{4,7},{5,4},{6,5},{7,6},{8,11},{9,8},{10,9... | collective-permute-start | bytes 393224 | tf_op jit(solution)/shard_map/ppermute | solution.py:101
  42.1 9.1 %collective-permute-start.18 = (bf16[4,16,1024]{2,1,0:T(8,128)(2,1)S(1)}, bf16[4,16,1024]{2,1,0:T(8,128)(2,1)S(1)}, u32[]{:S(2)}, u32[]{:S(2)}) collective-permute-start(bf16[4,16,1024]{2,1,0:T(8,128)(2,1)S(1)} %slice.200), channel_id=1, source_target_pairs={{0,4},{1,5},{2,6},{3,7},{4,8},{5,9},{6,10},{7,11},{8,12},{9,13},{1... | collective-permute-start | bytes 393224 | tf_op jit(solution)/shard_map/ppermute | solution.py:101
  42.2 9.6 %collective-permute-start.19 = (bf16[4,16,1024]{2,1,0:T(8,128)(2,1)S(1)}, bf16[4,16,1024]{2,1,0:T(8,128)(2,1)S(1)}, u32[]{:S(2)}, u32[]{:S(2)}) collective-permute-start(bf16[4,16,1024]{2,1,0:T(8,128)(2,1)S(1)} %slice.201), channel_id=1, source_target_pairs={{0,12},{1,13},{2,14},{3,15},{4,0},{5,1},{6,2},{7,3},{8,4},{9,5},{1... | collective-permute-start | bytes 393224 | tf_op jit(solution)/shard_map/ppermute | solution.py:101
  47.7 22.7 %collective-permute-start.5 = (bf16[4,128,1024]{2,1,0:T(8,128)(2,1)S(1)}, bf16[4,128,1024]{2,1,0:T(8,128)(2,1)S(1)}, u32[]{:S(2)}, u32[]{:S(2)}) collective-permute-start(bf16[4,128,1024]{2,1,0:T(8,128)(2,1)S(1)} %get-tuple-element.39), channel_id=1, source_target_pairs={{0,4},{1,5},{2,6},{3,7},{4,8},{5,9},{6,10},{7,11},{8,12},{9,13},{1... | collective-permute-start | bytes 3145736 | tf_op jit(solution)/shard_map/ppermute | solution.py:101
  48.5 23.8 %collective-permute-start.4 = (bf16[4,128,1024]{2,1,0:T(8,128)(2,1)S(1)}, bf16[4,128,1024]{2,1,0:T(8,128)(2,1)S(1)}, u32[]{:S(2)}, u32[]{:S(2)}) collective-permute-start(bf16[4,128,1024]{2,1,0:T(8,128)(2,1)S(1)} %get-tuple-element.39), channel_id=1, source_target_pairs={{0,12},{1,13},{2,14},{3,15},{4,0},{5,1},{6,2},{7,3},{8,4},{9,5},{1... | collective-permute-start | bytes 3145736 | tf_op jit(solution)/shard_map/ppermute | solution.py:101
  53.2 24.0 %collective-permute-start.20 = (bf16[4,128,1024]{2,1,0:T(8,128)(2,1)S(1)}, bf16[4,128,1024]{2,1,0:T(8,128)(2,1)S(1)}, u32[]{:S(2)}, u32[]{:S(2)}) collective-permute-start(bf16[4,128,1024]{2,1,0:T(8,128)(2,1)S(1)} %get-tuple-element.43), channel_id=1, source_target_pairs={{0,3},{1,0},{2,1},{3,2},{4,7},{5,4},{6,5},{7,6},{8,11},{9,8},{10,9... | collective-permute-start | bytes 3145736 | tf_op jit(solution)/shard_map/ppermute | solution.py:101
  54.5 21.9 %collective-permute-start.21 = (bf16[4,128,1024]{2,1,0:T(8,128)(2,1)S(1)}, bf16[4,128,1024]{2,1,0:T(8,128)(2,1)S(1)}, u32[]{:S(2)}, u32[]{:S(2)}) collective-permute-start(bf16[4,128,1024]{2,1,0:T(8,128)(2,1)S(1)} %get-tuple-element.43), channel_id=1, source_target_pairs={{0,1},{1,2},{2,3},{3,0},{4,5},{5,6},{6,7},{7,4},{8,9},{9,10},{10,1... | collective-permute-start | bytes 3145736 | tf_op jit(solution)/shard_map/ppermute | solution.py:101
  70.5 12.4 %collective-permute-start.6 = (bf16[4,64,1024]{2,1,0:T(8,128)(2,1)S(1)}, bf16[4,64,1024]{2,1,0:T(8,128)(2,1)S(1)}, u32[]{:S(2)}, u32[]{:S(2)}) collective-permute-start(bf16[4,64,1024]{2,1,0:T(8,128)(2,1)S(1)} %slice.187), channel_id=1, source_target_pairs={{0,4},{1,5},{2,6},{3,7},{4,8},{5,9},{6,10},{7,11},{8,12},{9,13},{1... | collective-permute-start | bytes 1572872 | tf_op jit(solution)/shard_map/ppermute | solution.py:101
  72.4 11.3 %collective-permute-start.7 = (bf16[4,64,1024]{2,1,0:T(8,128)(2,1)S(1)}, bf16[4,64,1024]{2,1,0:T(8,128)(2,1)S(1)}, u32[]{:S(2)}, u32[]{:S(2)}) collective-permute-start(bf16[4,64,1024]{2,1,0:T(8,128)(2,1)S(1)} %slice.188), channel_id=1, source_target_pairs={{0,12},{1,13},{2,14},{3,15},{4,0},{5,1},{6,2},{7,3},{8,4},{9,5},{1... | collective-permute-start | bytes 1572872 | tf_op jit(solution)/shard_map/ppermute | solution.py:101
  77.2 19.8 %collective-permute-start.22 = (bf16[4,64,1024]{2,1,0:T(8,128)(2,1)}, bf16[4,64,1024]{2,1,0:T(8,128)(2,1)}, u32[]{:S(2)}, u32[]{:S(2)}) collective-permute-start(bf16[4,64,1024]{2,1,0:T(8,128)(2,1)} %slice.202), channel_id=1, source_target_pairs={{0,1},{1,2},{2,3},{3,0},{4,5},{5,6},{6,7},{7,4},{8,9},{9,10},{10,1... | collective-permute-start | bytes 1572872 | tf_op jit(solution)/shard_map/ppermute | solution.py:101
  78.0 20.9 %collective-permute-start.23 = (bf16[4,64,1024]{2,1,0:T(8,128)(2,1)}, bf16[4,64,1024]{2,1,0:T(8,128)(2,1)}, u32[]{:S(2)}, u32[]{:S(2)}) collective-permute-start(bf16[4,64,1024]{2,1,0:T(8,128)(2,1)} %slice.203), channel_id=1, source_target_pairs={{0,3},{1,0},{2,1},{3,2},{4,7},{5,4},{6,5},{7,6},{8,11},{9,8},{10,9... | collective-permute-start | bytes 1572872 | tf_op jit(solution)/shard_map/ppermute | solution.py:101
  95.6 18.3 %collective-permute-start.10 = (bf16[4,64,1024]{2,1,0:T(8,128)(2,1)}, bf16[4,64,1024]{2,1,0:T(8,128)(2,1)}, u32[]{:S(2)}, u32[]{:S(2)}) collective-permute-start(bf16[4,64,1024]{2,1,0:T(8,128)(2,1)} %get-tuple-element.16), channel_id=1, source_target_pairs={{0,12},{1,13},{2,14},{3,15},{4,0},{5,1},{6,2},{7,3},{8,4},{9,5},{1... | collective-permute-start | bytes 1572872 | tf_op jit(solution)/shard_map/ppermute | solution.py:101
  96.2 17.6 %collective-permute-start.8 = (bf16[4,64,1024]{2,1,0:T(8,128)(2,1)}, bf16[4,64,1024]{2,1,0:T(8,128)(2,1)}, u32[]{:S(2)}, u32[]{:S(2)}) collective-permute-start(bf16[4,64,1024]{2,1,0:T(8,128)(2,1)} %get-tuple-element.15), channel_id=1, source_target_pairs={{0,4},{1,5},{2,6},{3,7},{4,8},{5,9},{6,10},{7,11},{8,12},{9,13},{1... | collective-permute-start | bytes 1572872 | tf_op jit(solution)/shard_map/ppermute | solution.py:101
  109.6 10.8 %copy-start.2 = (bf16[4,512,1024]{2,1,0:T(8,128)(2,1)S(1)}, bf16[4,512,1024]{2,1,0:T(8,128)(2,1)}, u32[]{:S(2)}) copy-start(bf16[4,512,1024]{2,1,0:T(8,128)(2,1)} %shard_map.74) | copy-start | bytes 12582916
  111.1 9.3 %collective-permute-start.24 = (bf16[4,64,1024]{2,1,0:T(8,128)(2,1)S(1)}, bf16[4,64,1024]{2,1,0:T(8,128)(2,1)S(1)}, u32[]{:S(2)}, u32[]{:S(2)}) collective-permute-start(bf16[4,64,1024]{2,1,0:T(8,128)(2,1)S(1)} %get-tuple-element.23), channel_id=1, source_target_pairs={{0,1},{1,2},{2,3},{3,0},{4,5},{5,6},{6,7},{7,4},{8,9},{9,10},{10,1... | collective-permute-start | bytes 1572872 | tf_op jit(solution)/shard_map/ppermute | solution.py:101
  111.2 9.2 %collective-permute-start.26 = (bf16[4,64,1024]{2,1,0:T(8,128)(2,1)S(1)}, bf16[4,64,1024]{2,1,0:T(8,128)(2,1)S(1)}, u32[]{:S(2)}, u32[]{:S(2)}) collective-permute-start(bf16[4,64,1024]{2,1,0:T(8,128)(2,1)S(1)} %get-tuple-element.24), channel_id=1, source_target_pairs={{0,3},{1,0},{2,1},{3,2},{4,7},{5,4},{6,5},{7,6},{8,11},{9,8},{10,9... | collective-permute-start | bytes 1572872 | tf_op jit(solution)/shard_map/ppermute | solution.py:101
  116.2 18.2 %collective-permute-start.11 = (bf16[4,128,1024]{2,1,0:T(8,128)(2,1)S(1)}, bf16[4,128,1024]{2,1,0:T(8,128)(2,1)S(1)}, u32[]{:S(2)}, u32[]{:S(2)}) collective-permute-start(bf16[4,128,1024]{2,1,0:T(8,128)(2,1)S(1)} %get-tuple-element.14), channel_id=1, source_target_pairs={{0,12},{1,13},{2,14},{3,15},{4,0},{5,1},{6,2},{7,3},{8,4},{9,5},{1... | collective-permute-start | bytes 3145736 | tf_op jit(solution)/shard_map/ppermute | solution.py:101
  117.1 19.1 %collective-permute-start.9 = (bf16[4,128,1024]{2,1,0:T(8,128)(2,1)S(1)}, bf16[4,128,1024]{2,1,0:T(8,128)(2,1)S(1)}, u32[]{:S(2)}, u32[]{:S(2)}) collective-permute-start(bf16[4,128,1024]{2,1,0:T(8,128)(2,1)S(1)} %get-tuple-element.13), channel_id=1, source_target_pairs={{0,4},{1,5},{2,6},{3,7},{4,8},{5,9},{6,10},{7,11},{8,12},{9,13},{1... | collective-permute-start | bytes 3145736 | tf_op jit(solution)/shard_map/ppermute | solution.py:101
  121.1 20.7 %collective-permute-start.25 = (bf16[4,128,1024]{2,1,0:T(8,128)(2,1)S(1)}, bf16[4,128,1024]{2,1,0:T(8,128)(2,1)S(1)}, u32[]{:S(2)}, u32[]{:S(2)}) collective-permute-start(bf16[4,128,1024]{2,1,0:T(8,128)(2,1)S(1)} %get-tuple-element.21), channel_id=1, source_target_pairs={{0,1},{1,2},{2,3},{3,0},{4,5},{5,6},{6,7},{7,4},{8,9},{9,10},{10,1... | collective-permute-start | bytes 3145736 | tf_op jit(solution)/shard_map/ppermute | solution.py:101
  121.2 20.6 %collective-permute-start.27 = (bf16[4,128,1024]{2,1,0:T(8,128)(2,1)S(1)}, bf16[4,128,1024]{2,1,0:T(8,128)(2,1)S(1)}, u32[]{:S(2)}, u32[]{:S(2)}) collective-permute-start(bf16[4,128,1024]{2,1,0:T(8,128)(2,1)S(1)} %get-tuple-element.22), channel_id=1, source_target_pairs={{0,3},{1,0},{2,1},{3,2},{4,7},{5,4},{6,5},{7,6},{8,11},{9,8},{10,9... | collective-permute-start | bytes 3145736 | tf_op jit(solution)/shard_map/ppermute | solution.py:101
  137.9 7.3 %collective-permute-start.12 = (bf16[4,16,1024]{2,1,0:T(8,128)(2,1)S(1)}, bf16[4,16,1024]{2,1,0:T(8,128)(2,1)S(1)}, u32[]{:S(2)}, u32[]{:S(2)}) collective-permute-start(bf16[4,16,1024]{2,1,0:T(8,128)(2,1)S(1)} %get-tuple-element.29), channel_id=1, source_target_pairs={{0,1},{1,2},{2,3},{3,0},{4,5},{5,6},{6,7},{7,4},{8,9},{9,10},{10,1... | collective-permute-start | bytes 393224 | tf_op jit(solution)/shard_map/ppermute | solution.py:101
  138.0 7.3 %collective-permute-start.14 = (bf16[4,16,1024]{2,1,0:T(8,128)(2,1)S(1)}, bf16[4,16,1024]{2,1,0:T(8,128)(2,1)S(1)}, u32[]{:S(2)}, u32[]{:S(2)}) collective-permute-start(bf16[4,16,1024]{2,1,0:T(8,128)(2,1)S(1)} %get-tuple-element.30), channel_id=1, source_target_pairs={{0,3},{1,0},{2,1},{3,2},{4,7},{5,4},{6,5},{7,6},{8,11},{9,8},{10,9... | collective-permute-start | bytes 393224 | tf_op jit(solution)/shard_map/ppermute | solution.py:101
  142.5 5.9 %collective-permute-start.28 = (bf16[4,16,1024]{2,1,0:T(8,128)(2,1)S(1)}, bf16[4,16,1024]{2,1,0:T(8,128)(2,1)S(1)}, u32[]{:S(2)}, u32[]{:S(2)}) collective-permute-start(bf16[4,16,1024]{2,1,0:T(8,128)(2,1)S(1)} %get-tuple-element.31), channel_id=1, source_target_pairs={{0,4},{1,5},{2,6},{3,7},{4,8},{5,9},{6,10},{7,11},{8,12},{9,13},{1... | collective-permute-start | bytes 393224 | tf_op jit(solution)/shard_map/ppermute | solution.py:101
  142.6 5.8 %collective-permute-start.30 = (bf16[4,16,1024]{2,1,0:T(8,128)(2,1)S(1)}, bf16[4,16,1024]{2,1,0:T(8,128)(2,1)S(1)}, u32[]{:S(2)}, u32[]{:S(2)}) collective-permute-start(bf16[4,16,1024]{2,1,0:T(8,128)(2,1)S(1)} %get-tuple-element.32), channel_id=1, source_target_pairs={{0,12},{1,13},{2,14},{3,15},{4,0},{5,1},{6,2},{7,3},{8,4},{9,5},{1... | collective-permute-start | bytes 393224 | tf_op jit(solution)/shard_map/ppermute | solution.py:101
  145.4 9.8 %collective-permute-start.13 = (bf16[4,32,1024]{2,1,0:T(8,128)(2,1)S(1)}, bf16[4,32,1024]{2,1,0:T(8,128)(2,1)S(1)}, u32[]{:S(2)}, u32[]{:S(2)}) collective-permute-start(bf16[4,32,1024]{2,1,0:T(8,128)(2,1)S(1)} %get-tuple-element.25), channel_id=1, source_target_pairs={{0,1},{1,2},{2,3},{3,0},{4,5},{5,6},{6,7},{7,4},{8,9},{9,10},{10,1... | collective-permute-start | bytes 786440 | tf_op jit(solution)/shard_map/ppermute | solution.py:101
  145.5 9.7 %collective-permute-start.15 = (bf16[4,32,1024]{2,1,0:T(8,128)(2,1)S(1)}, bf16[4,32,1024]{2,1,0:T(8,128)(2,1)S(1)}, u32[]{:S(2)}, u32[]{:S(2)}) collective-permute-start(bf16[4,32,1024]{2,1,0:T(8,128)(2,1)S(1)} %get-tuple-element.26), channel_id=1, source_target_pairs={{0,3},{1,0},{2,1},{3,2},{4,7},{5,4},{6,5},{7,6},{8,11},{9,8},{10,9... | collective-permute-start | bytes 786440 | tf_op jit(solution)/shard_map/ppermute | solution.py:101
  148.4 27.5 %copy-start.4 = (bf16[32,8,1024]{2,1,0:T(8,128)(2,1)S(1)}, bf16[32,8,1024]{2,1,0:T(8,128)(2,1)}, u32[]{:S(2)}) copy-start(bf16[32,8,1024]{2,1,0:T(8,128)(2,1)} %param.7) | copy-start | bytes 1572868
  148.6 6.8 %collective-permute-start.29 = (bf16[4,32,1024]{2,1,0:T(8,128)(2,1)S(1)}, bf16[4,32,1024]{2,1,0:T(8,128)(2,1)S(1)}, u32[]{:S(2)}, u32[]{:S(2)}) collective-permute-start(bf16[4,32,1024]{2,1,0:T(8,128)(2,1)S(1)} %get-tuple-element.27), channel_id=1, source_target_pairs={{0,4},{1,5},{2,6},{3,7},{4,8},{5,9},{6,10},{7,11},{8,12},{9,13},{1... | collective-permute-start | bytes 786440 | tf_op jit(solution)/shard_map/ppermute | solution.py:101
  148.7 6.7 %collective-permute-start.31 = (bf16[4,32,1024]{2,1,0:T(8,128)(2,1)S(1)}, bf16[4,32,1024]{2,1,0:T(8,128)(2,1)S(1)}, u32[]{:S(2)}, u32[]{:S(2)}) collective-permute-start(bf16[4,32,1024]{2,1,0:T(8,128)(2,1)S(1)} %get-tuple-element.28), channel_id=1, source_target_pairs={{0,12},{1,13},{2,14},{3,15},{4,0},{5,1},{6,2},{7,3},{8,4},{9,5},{1... | collective-permute-start | bytes 786440 | tf_op jit(solution)/shard_map/ppermute | solution.py:101
  158.8 26.6 %all-to-all-start.1 = ((bf16[8,32,1024]{2,1,0:T(8,128)(2,1)}), bf16[8,32,1024]{2,1,0:T(8,128)(2,1)}, u32[]{:S(2)}, u32[]{:S(2)}) async-start(bf16[8,32,1024]{2,1,0:T(8,128)(2,1)} %broadcast_select_fusion.1), calls=%async_computation.1 | async-start | bytes 1048576 | tf_op jit(solution)/shard_map/all_to_all | solution.py:215

commit v10 on v9

--- a/solution.py
+++ b/solution.py
@@ -101,6 +101,20 @@
     return lax.ppermute(value, "member", shift_perm(grid, axis, shift))
 
 
+def direct_gather(block, grid, axis):
+    n = grid[axis]
+    return jnp.concatenate([block] + [send(block, grid, axis, -k) for k in range(1, n)], axis=1)
+
+
+def direct_reduce(parts, grid, axis):
+    n = grid[axis]
+    m = parts.shape[1] // n
+    out = parts[:, :m].astype(jnp.float32)
+    for k in range(1, n):
+        out = out + send(parts[:, k * m:(k + 1) * m].astype(jnp.bfloat16), grid, axis, k).astype(jnp.float32)
+    return out
+
+
 def ring_gather(block, grid, axis):
     n = grid[axis]
     slots = {0: block}
@@ -150,13 +164,13 @@
 
 def torus_gather(block, grid, order):
     rows, m, width = block.shape
-    out = ring_gather(block, grid, order[1])
+    out = direct_gather(block, grid, order[1])
     return ring_gather(out, grid, order[0])
 
 
 def torus_reduce(parts, grid, order):
-    out = ring_reduce(parts, grid, order[0])
-    return ring_reduce(out, grid, order[1])
+    out = ring_reduce(parts, grid, order[0]).astype(jnp.bfloat16)
+    return direct_reduce(out, grid, order[1])
 
 
 def on_device(grid, candidates, kv_cache, cache_request, rank_request, hist_blocks, w_uq, w_out):

time: 192 us -> 201 us (1.047)
  waiting for transfers between devices: 52.5 us -> 61.5 us
  starting transfers between devices: 64.5 us -> 62.1 us
    ppermute x32 -> x28, waiting for transfers between devices: 37.9 us -> 51.7 us  [send(): return lax.ppermute(value, 'member', shift_perm(grid, axis, shift))]
    all_to_all x1, waiting for transfers between devices: 8.61 us -> 3.76 us  [on_device(): lax.all_to_all(q_out, 'group', split_axis=0, concat_axis=0, tiled=True)]
    convert_element_type x0 -> x2, other arithmetic: none -> 2.5 us  [torus_reduce(): out = ring_reduce(parts, grid, order[0]).astype(jnp.bfloat16)]
    slice x1, local copies, waits for them, and re-layouts: 2.49 us -> 4.85 us  [on_device(): kv_cache[rows_of]]
    another operation x4 -> x2, other arithmetic: 2.62 us -> 0.34 us
    ppermute x32 -> x28, starting transfers between devices: 41.4 us -> 40 us  [send(): return lax.ppermute(value, 'member', shift_perm(grid, axis, shift))]
    unnamed x23 -> x22, local copies, waits for them, and re-layouts: 12.7 us -> 11.8 us
  transfers between devices with their start and end apart: 34 -> 30, of which waited for: 11 -> 13; matrix products, arithmetic and copies ran while one was open for 19% -> 19% of each run, Pallas kernels for 8% -> 8%
where the time goes in v10:
time: 201 us; the launch traced here: 199 us
  starting transfers between devices  62.1 us (31%)
  waiting for transfers between devices  61.5 us (31%)
  local copies, waits for them, and re-layouts  33.3 us (17%)
  other arithmetic  18.1 us (9%)
  Pallas kernels  15.5 us (8%)
  matrix products  7.73 us (4%)
    ppermute x28, waiting for transfers between devices, send(): return lax.ppermute(value, 'member', shift_perm(grid, axis, shift))  51.7 us
    ppermute x28, starting transfers between devices, send(): return lax.ppermute(value, 'member', shift_perm(grid, axis, shift))  40 us
    all_to_all x1, starting transfers between devices, on_device(): lax.all_to_all(a_out, 'group', split_axis=0, concat_axis=0, tiled=True)  16.1 us
    pallas_call x2, Pallas kernels, attend_local(): pl.pallas_call(kernel, out_shape=jax.ShapeDtypeStruct((rows, cands, width...  15.5 us
    unnamed x22, local copies, waits for them, and re-layouts  11.8 us
    all_to_all x1, waiting for transfers between devices, on_device(): lax.all_to_all(a_out, 'group', split_axis=0, concat_axis=0, tiled=True)  6.04 us
    all_to_all x1, starting transfers between devices, on_device(): lax.all_to_all(q_out, 'group', split_axis=0, concat_axis=0, tiled=True)  5.96 us
    slice x1, local copies, waits for them, and re-layouts, on_device(): kv_cache[rows_of]  4.85 us
  transfers between devices with their start and end apart: 30, of which 13 were waited for; matrix products, arithmetic and copies ran while one was open for 19% of the time, Pallas kernels for 8%

profile of v10, /device:TPU:1, one launch (start us, length us, event | category | flops | bytes accessed | tf_op | source)
XLA Modules:
  0.0 198.7 jit_solution(11969584957133822509)
XLA Ops:
  0.0 1.0 fusion.28
  1.0 1.3 gather_fusion
  4.1 1.2 convert_reduce_fusion
  5.5 1.3 fusion.8
  7.0 2.7 %fusion.19 = bf16[32,8,1024]{2,1,0:T(8,128)(2,1)S(1)} fusion(bf16[1024,2048]{1,0:T(8,128)(2,1)} %param.12, bf16[32,8,1024]{2,1,0:T(8,128)(2,1)} %param.7, f32[32,8]{1,0:T(8,128)S(1)} %copy.37, f32[32,8]{1,0:T(8,128)S(1)} %copy.35), kind=kOutput, calls=%fused_computation.41 | convolution fusion | flops 539492352 | bytes 3147776 | tf_op jit(solution)/shard_map/dot_general | solution.py:210
  10.5 0.9 broadcast_select_fusion
  11.4 6.0 %all-to-all-start = ((bf16[8,32,1024]{2,1,0:T(8,128)(2,1)}), bf16[8,32,1024]{2,1,0:T(8,128)(2,1)S(1)}, u32[]{:S(2)}, u32[]{:S(2)}) async-start(bf16[8,32,1024]{2,1,0:T(8,128)(2,1)} %broadcast_select_fusion), calls=%async_computation | async-start | bytes 1048576 | tf_op jit(solution)/shard_map/all_to_all | solution.py:215
  18.1 4.8 %fusion.41 = (bf16[4,128,2048]{2,1,0:T(8,128)(2,1)}, bf16[4,128,2048]{2,1,0:T(8,128)(2,1)}) fusion(bf16[8,128,2048]{2,1,0:T(8,128)(2,1)} %param.8), kind=kLoop, calls=%fused_computation.132 | loop fusion | bytes 8388608 | tf_op jit(solution)/shard_map/slice | solution.py:223
  23.0 3.8 %all-to-all-done = bf16[8,32,1024]{2,1,0:T(8,128)(2,1)S(1)} async-done(((bf16[8,32,1024]{2,1,0:T(8,128)(2,1)}), bf16[8,32,1024]{2,1,0:T(8,128)(2,1)S(1)}, u32[]{:S(2)}, u32[]{:S(2)}) %all-to-all-start) | async-done | bytes 524320 | tf_op jit(solution)/shard_map/all_to_all | solution.py:215
  27.4 0.9 fusion.45
  28.2 2.5 %collective-permute-start = (bf16[4,32,1024]{2,1,0:T(8,128)(2,1)S(1)}, bf16[4,32,1024]{2,1,0:T(8,128)(2,1)S(1)}, u32[]{:S(2)}, u32[]{:S(2)}) collective-permute-start(bf16[4,32,1024]{2,1,0:T(8,128)(2,1)S(1)} %get-tuple-element.27), channel_id=1, source_target_pairs={{0,3},{1,0},{2,1},{3,2},{4,7},{5,4},{6,5},{7,6},{8,11},{9,8},{10,9... | collective-permute-start | bytes 786440 | tf_op jit(solution)/shard_map/ppermute | solution.py:101
  31.9 3.8 %collective-permute-start.14 = (bf16[4,32,1024]{2,1,0:T(8,128)(2,1)S(1)}, bf16[4,32,1024]{2,1,0:T(8,128)(2,1)S(1)}, u32[]{:S(2)}, u32[]{:S(2)}) collective-permute-start(bf16[4,32,1024]{2,1,0:T(8,128)(2,1)S(1)} %get-tuple-element.30), channel_id=1, source_target_pairs={{0,12},{1,13},{2,14},{3,15},{4,0},{5,1},{6,2},{7,3},{8,4},{9,5},{1... | collective-permute-start | bytes 786440 | tf_op jit(solution)/shard_map/ppermute | solution.py:101
  36.2 1.6 collective-permute-start.16
  37.8 1.0 collective-permute-done.1
  38.9 7.2 %collective-permute-done.2 = bf16[4,32,1024]{2,1,0:T(8,128)(2,1)S(1)} collective-permute-done((bf16[4,32,1024]{2,1,0:T(8,128)(2,1)S(1)}, bf16[4,32,1024]{2,1,0:T(8,128)(2,1)S(1)}, u32[]{:S(2)}, u32[]{:S(2)}) %collective-permute-start.2) | collective-permute-done | bytes 262176 | tf_op jit(solution)/shard_map/ppermute | solution.py:101
  46.1 1.7 collective-permute-start.4
  47.9 2.1 %collective-permute-start.3 = (bf16[4,128,1024]{2,1,0:T(8,128)(2,1)S(1)}, bf16[4,128,1024]{2,1,0:T(8,128)(2,1)S(1)}, u32[]{:S(2)}, u32[]{:S(2)}) collective-permute-start(bf16[4,128,1024]{2,1,0:T(8,128)(2,1)S(1)} %pad_maximum_fusion), channel_id=1, source_target_pairs={{0,12},{1,13},{2,14},{3,15},{4,0},{5,1},{6,2},{7,3},{8,4},{9,5},{1... | collective-permute-start | bytes 3145736 | tf_op jit(solution)/shard_map/ppermute | solution.py:101
  50.2 2.4 %collective-permute-start.18 = (bf16[4,128,1024]{2,1,0:T(8,128)(2,1)S(1)}, bf16[4,128,1024]{2,1,0:T(8,128)(2,1)S(1)}, u32[]{:S(2)}, u32[]{:S(2)}) collective-permute-start(bf16[4,128,1024]{2,1,0:T(8,128)(2,1)S(1)} %pad_maximum_fusion.1), channel_id=1, source_target_pairs={{0,1},{1,2},{2,3},{3,0},{4,5},{5,6},{6,7},{7,4},{8,9},{9,10},{10,1... | collective-permute-start | bytes 3145736 | tf_op jit(solution)/shard_map/ppermute | solution.py:101
  53.3 1.8 multiply_convert_fusion.1
  57.2 15.8 %collective-permute-done.4 = bf16[4,128,1024]{2,1,0:T(8,128)(2,1)S(1)} collective-permute-done((bf16[4,128,1024]{2,1,0:T(8,128)(2,1)S(1)}, bf16[4,128,1024]{2,1,0:T(8,128)(2,1)S(1)}, u32[]{:S(2)}, u32[]{:S(2)}) %collective-permute-start.4) | collective-permute-done | bytes 1048608 | tf_op jit(solution)/shard_map/ppermute | solution.py:101
  73.9 2.7 %collective-permute-start.6 = (bf16[4,64,1024]{2,1,0:T(8,128)(2,1)S(1)}, bf16[4,64,1024]{2,1,0:T(8,128)(2,1)S(1)}, u32[]{:S(2)}, u32[]{:S(2)}) collective-permute-start(bf16[4,64,1024]{2,1,0:T(8,128)(2,1)S(1)} %slice.154), channel_id=1, source_target_pairs={{0,12},{1,13},{2,14},{3,15},{4,0},{5,1},{6,2},{7,3},{8,4},{9,5},{1... | collective-permute-start | bytes 1572872 | tf_op jit(solution)/shard_map/ppermute | solution.py:101
  76.6 0.7 constant_dynamic-update-slice_fusion.13
  78.1 0.8 slice.165
  78.9 1.9 collective-permute-start.19
  80.8 0.8 slice.166
  81.6 0.8 collective-permute-start.20
  82.4 1.0 constant_dynamic-update-slice_fusion.3
  83.4 1.0 constant_dynamic-update-slice_fusion.11
  84.5 2.4 %collective-permute-done.5 = bf16[4,64,1024]{2,1,0:T(8,128)(2,1)S(1)} collective-permute-done((bf16[4,64,1024]{2,1,0:T(8,128)(2,1)S(1)}, bf16[4,64,1024]{2,1,0:T(8,128)(2,1)S(1)}, u32[]{:S(2)}, u32[]{:S(2)}) %collective-permute-start.5) | collective-permute-done | bytes 524320 | tf_op jit(solution)/shard_map/ppermute | solution.py:101
  86.8 0.8 constant_dynamic-update-slice_fusion.2
  87.7 0.8 constant_dynamic-update-slice_fusion.1
  88.5 1.0 constant_dynamic-update-slice_fusion.q_ref
  89.5 7.7 %shard_map.73 = bf16[4,512,1024]{2,1,0:T(8,128)(2,1)} custom-call(s32[4]{0:T(128)} %get-tuple-element.35.n_live_ref, bf16[4,512,1024]{2,1,0:T(8,128)(2,1)} %constant_dynamic-update-slice_fusion.q_ref, bf16[4,128,2048]{2,1,0:T(8,128)(2,1)} %get-tuple-element.15.kv_ref, bf16[4,128,1024]{2,1,0:T(8,128)(2,1)} %get-tuple-element.13.vk_ref), custom_call_target="tpu_custom_call" | custom-call | flops 1073741824 | bytes 10485760 | tf_op jit(solution)/shard_map/pallas_call | solution.py:66
  97.3 2.2 %fusion.40 = (bf16[4,64,1024]{2,1,0:T(8,128)(2,1)}, bf16[4,64,1024]{2,1,0:T(8,128)(2,1)}) fusion(bf16[4,512,1024]{2,1,0:T(8,128)(2,1)} %shard_map.73), kind=kLoop, calls=%fused_computation.131 | loop fusion | bytes 2097152 | tf_op jit(solution)/shard_map/slice | solution.py:151
  99.5 2.7 %collective-permute-start.9 = (bf16[4,64,1024]{2,1,0:T(8,128)(2,1)}, bf16[4,64,1024]{2,1,0:T(8,128)(2,1)}, u32[]{:S(2)}, u32[]{:S(2)}) collective-permute-start(bf16[4,64,1024]{2,1,0:T(8,128)(2,1)} %get-tuple-element.12), channel_id=1, source_target_pairs={{0,12},{1,13},{2,14},{3,15},{4,0},{5,1},{6,2},{7,3},{8,4},{9,5},{1... | collective-permute-start | bytes 1572872 | tf_op jit(solution)/shard_map/ppermute | solution.py:101
  102.2 1.9 constant_dynamic-update-slice_fusion.10
  104.1 1.9 constant_dynamic-update-slice_fusion.9
  106.0 1.1 constant_dynamic-update-slice_fusion.8.q_ref
  107.1 7.8 %shard_map.74 = bf16[4,512,1024]{2,1,0:T(8,128)(2,1)} custom-call(s32[4]{0:T(128)} %get-tuple-element.36.n_live_ref, bf16[4,512,1024]{2,1,0:T(8,128)(2,1)} %constant_dynamic-update-slice_fusion.8.q_ref, bf16[4,128,2048]{2,1,0:T(8,128)(2,1)} %get-tuple-element.16.kv_ref, bf16[4,128,1024]{2,1,0:T(8,128)(2,1)} %get-tuple-element.14.vk_ref), custom_call_target="tpu_custom_call" | custom-call | flops 1073741824 | bytes 10485760 | tf_op jit(solution)/shard_map/pallas_call | solution.py:66
  114.9 1.5 fusion.42
  116.3 1.5 collective-permute-start.21
  117.9 1.2 collective-permute-start.23
  119.1 2.4 %add_convert_fusion.5 = (bf16[4,128,1024]{2,1,0:T(8,128)(2,1)S(1)}, bf16[4,128,1024]{2,1,0:T(8,128)(2,1)S(1)}) fusion(bf16[4,512,1024]{2,1,0:T(8,128)(2,1)} %shard_map.73, bf16[4,64,1024]{2,1,0:T(8,128)(2,1)} %collective-permute-done.7, bf16[4,64,1024]{2,1,0:T(8,128)(2,1)} %collective-permute-done.9), kind=kLoop, calls=%fused_computation.16 | loop fusion | flops 4194304 | bytes 5242880 | tf_op jit(solution)/shard_map/convert_element_type | solution.py:156
  121.5 1.5 collective-permute-start.8
  123.2 5.5 %collective-permute-done.21 = bf16[4,64,1024]{2,1,0:T(8,128)(2,1)S(1)} collective-permute-done((bf16[4,64,1024]{2,1,0:T(8,128)(2,1)S(1)}, bf16[4,64,1024]{2,1,0:T(8,128)(2,1)S(1)}, u32[]{:S(2)}, u32[]{:S(2)}) %collective-permute-start.21) | collective-permute-done | bytes 524320 | tf_op jit(solution)/shard_map/ppermute | solution.py:101
  129.5 2.7 %collective-permute-start.24 = (bf16[4,128,1024]{2,1,0:T(8,128)(2,1)S(1)}, bf16[4,128,1024]{2,1,0:T(8,128)(2,1)S(1)}, u32[]{:S(2)}, u32[]{:S(2)}) collective-permute-start(bf16[4,128,1024]{2,1,0:T(8,128)(2,1)S(1)} %get-tuple-element.18), channel_id=1, source_target_pairs={{0,3},{1,0},{2,1},{3,2},{4,7},{5,4},{6,5},{7,6},{8,11},{9,8},{10,9... | collective-permute-start | bytes 3145736 | tf_op jit(solution)/shard_map/ppermute | solution.py:101
  132.3 11.0 %collective-permute-done.10 = bf16[4,128,1024]{2,1,0:T(8,128)(2,1)S(1)} collective-permute-done((bf16[4,128,1024]{2,1,0:T(8,128)(2,1)S(1)}, bf16[4,128,1024]{2,1,0:T(8,128)(2,1)S(1)}, u32[]{:S(2)}, u32[]{:S(2)}) %collective-permute-start.10) | collective-permute-done | bytes 1048608 | tf_op jit(solution)/shard_map/ppermute | solution.py:101
  143.3 1.3 collective-permute-done.8
  144.6 1.9 add_convert_fusion.3
  146.6 1.5 collective-permute-start.12
  148.1 1.2 collective-permute-start.13
  149.3 2.6 %collective-permute-done.22 = bf16[4,128,1024]{2,1,0:T(8,128)(2,1)S(1)} collective-permute-done((bf16[4,128,1024]{2,1,0:T(8,128)(2,1)S(1)}, bf16[4,128,1024]{2,1,0:T(8,128)(2,1)S(1)}, u32[]{:S(2)}, u32[]{:S(2)}) %collective-permute-start.22) | collective-permute-done | bytes 1048608 | tf_op jit(solution)/shard_map/ppermute | solution.py:101
  152.7 4.0 %collective-permute-start.26 = (bf16[4,32,1024]{2,1,0:T(8,128)(2,1)S(1)}, bf16[4,32,1024]{2,1,0:T(8,128)(2,1)S(1)}, u32[]{:S(2)}, u32[]{:S(2)}) collective-permute-start(bf16[4,32,1024]{2,1,0:T(8,128)(2,1)S(1)} %get-tuple-element.26), channel_id=1, source_target_pairs={{0,8},{1,9},{2,10},{3,11},{4,12},{5,13},{6,14},{7,15},{8,0},{9,1},... | collective-permute-start | bytes 786440 | tf_op jit(solution)/shard_map/ppermute | solution.py:101
  156.7 0.9 collective-permute-done.11
  157.5 2.8 %collective-permute-start.27 = (bf16[4,32,1024]{2,1,0:T(8,128)(2,1)S(1)}, bf16[4,32,1024]{2,1,0:T(8,128)(2,1)S(1)}, u32[]{:S(2)}, u32[]{:S(2)}) collective-permute-start(bf16[4,32,1024]{2,1,0:T(8,128)(2,1)S(1)} %get-tuple-element.25), channel_id=1, source_target_pairs={{0,12},{1,13},{2,14},{3,15},{4,0},{5,1},{6,2},{7,3},{8,4},{9,5},{1... | collective-permute-start | bytes 786440 | tf_op jit(solution)/shard_map/ppermute | solution.py:101
  160.3 3.4 %collective-permute-done.12 = bf16[4,32,1024]{2,1,0:T(8,128)(2,1)S(1)} collective-permute-done((bf16[4,32,1024]{2,1,0:T(8,128)(2,1)S(1)}, bf16[4,32,1024]{2,1,0:T(8,128)(2,1)S(1)}, u32[]{:S(2)}, u32[]{:S(2)}) %collective-permute-start.12) | collective-permute-done | bytes 262176 | tf_op jit(solution)/shard_map/ppermute | solution.py:101
  164.2 1.4 gather_fusion.6
  165.5 1.9 broadcast_select_fusion.1
  167.5 16.1 %all-to-all-start.1 = ((bf16[8,32,1024]{2,1,0:T(8,128)(2,1)}), bf16[8,32,1024]{2,1,0:T(8,128)(2,1)}, u32[]{:S(2)}, u32[]{:S(2)}) async-start(bf16[8,32,1024]{2,1,0:T(8,128)(2,1)} %broadcast_select_fusion.1), calls=%async_computation.1 | async-start | bytes 1048576 | tf_op jit(solution)/shard_map/all_to_all | solution.py:229
  183.6 3.4 %multiply_bitcast_fusion = f32[32,8,1024]{2,1,0:T(8,128)} fusion(bf16[1024,2048]{1,0:T(8,128)(2,1)} %param.12, bf16[32,8,1024]{2,1,0:T(8,128)(2,1)S(1)} %copy-done.4, f32[32,8]{1,0:T(8,128)S(1)} %copy.37, f32[32,8]{1,0:T(8,128)S(1)} %copy.35), kind=kOutput, calls=%fused_computation.39 | convolution fusion | flops 538968064 | bytes 3672064 | tf_op jit(solution)/shard_map/dot_general | solution.py:232
  187.1 6.0 %all-to-all-done.1 = bf16[8,32,1024]{2,1,0:T(8,128)(2,1)} async-done(((bf16[8,32,1024]{2,1,0:T(8,128)(2,1)}), bf16[8,32,1024]{2,1,0:T(8,128)(2,1)}, u32[]{:S(2)}, u32[]{:S(2)}) %all-to-all-start.1) | async-done | bytes 524320 | tf_op jit(solution)/shard_map/all_to_all | solution.py:229
  193.1 1.6 gather_fusion.7
  195.2 1.9 fusion.14
  197.0 1.6 fusion.7
  (97 shorter events, 13.6 us)
Async XLA Ops:
  0.0 197.0 %copy-start = (bf16[1024,1024]{1,0:T(8,128)(2,1)S(1)}, bf16[1024,1024]{1,0:T(8,128)(2,1)}, u32[]{:S(2)}) copy-start(bf16[1024,1024]{1,0:T(8,128)(2,1)} %param.13) | copy-start | bytes 6291460
  9.6 7.9 %copy-start.1 = (s32[64]{0:T(128)S(1)}, s32[64]{0:T(128)}, u32[]{:S(2)}) copy-start(s32[64]{0:T(128)} %param.11) | copy-start | bytes 772
  11.4 15.3 %all-to-all-start = ((bf16[8,32,1024]{2,1,0:T(8,128)(2,1)}), bf16[8,32,1024]{2,1,0:T(8,128)(2,1)S(1)}, u32[]{:S(2)}, u32[]{:S(2)}) async-start(bf16[8,32,1024]{2,1,0:T(8,128)(2,1)} %broadcast_select_fusion), calls=%async_computation | async-start | bytes 1048576 | tf_op jit(solution)/shard_map/all_to_all | solution.py:215
  27.3 25.9 %copy-start.3 = (bf16[8,128,2048]{2,1,0:T(8,128)(2,1)S(1)}, bf16[8,128,2048]{2,1,0:T(8,128)(2,1)}, u32[]{:S(2)}) copy-start(bf16[8,128,2048]{2,1,0:T(8,128)(2,1)} %param.8) | copy-start | bytes 12582916
  28.2 8.0 %collective-permute-start = (bf16[4,32,1024]{2,1,0:T(8,128)(2,1)S(1)}, bf16[4,32,1024]{2,1,0:T(8,128)(2,1)S(1)}, u32[]{:S(2)}, u32[]{:S(2)}) collective-permute-start(bf16[4,32,1024]{2,1,0:T(8,128)(2,1)S(1)} %get-tuple-element.27), channel_id=1, source_target_pairs={{0,3},{1,0},{2,1},{3,2},{4,7},{5,4},{6,5},{7,6},{8,11},{9,8},{10,9... | collective-permute-start | bytes 786440 | tf_op jit(solution)/shard_map/ppermute | solution.py:101
  30.7 8.2 %collective-permute-start.1 = (bf16[4,32,1024]{2,1,0:T(8,128)(2,1)S(1)}, bf16[4,32,1024]{2,1,0:T(8,128)(2,1)S(1)}, u32[]{:S(2)}, u32[]{:S(2)}) collective-permute-start(bf16[4,32,1024]{2,1,0:T(8,128)(2,1)S(1)} %get-tuple-element.27), channel_id=1, source_target_pairs={{0,2},{1,3},{2,0},{3,1},{4,6},{5,7},{6,4},{7,5},{8,10},{9,11},{10,... | collective-permute-start | bytes 786440 | tf_op jit(solution)/shard_map/ppermute | solution.py:101
  31.2 14.8 %collective-permute-start.2 = (bf16[4,32,1024]{2,1,0:T(8,128)(2,1)S(1)}, bf16[4,32,1024]{2,1,0:T(8,128)(2,1)S(1)}, u32[]{:S(2)}, u32[]{:S(2)}) collective-permute-start(bf16[4,32,1024]{2,1,0:T(8,128)(2,1)S(1)} %get-tuple-element.27), channel_id=1, source_target_pairs={{0,1},{1,2},{2,3},{3,0},{4,5},{5,6},{6,7},{7,4},{8,9},{9,10},{10,1... | collective-permute-start | bytes 786440 | tf_op jit(solution)/shard_map/ppermute | solution.py:101
  31.9 18.2 %collective-permute-start.14 = (bf16[4,32,1024]{2,1,0:T(8,128)(2,1)S(1)}, bf16[4,32,1024]{2,1,0:T(8,128)(2,1)S(1)}, u32[]{:S(2)}, u32[]{:S(2)}) collective-permute-start(bf16[4,32,1024]{2,1,0:T(8,128)(2,1)S(1)} %get-tuple-element.30), channel_id=1, source_target_pairs={{0,12},{1,13},{2,14},{3,15},{4,0},{5,1},{6,2},{7,3},{8,4},{9,5},{1... | collective-permute-start | bytes 786440 | tf_op jit(solution)/shard_map/ppermute | solution.py:101
  35.7 14.4 %collective-permute-start.15 = (bf16[4,32,1024]{2,1,0:T(8,128)(2,1)S(1)}, bf16[4,32,1024]{2,1,0:T(8,128)(2,1)S(1)}, u32[]{:S(2)}, u32[]{:S(2)}) collective-permute-start(bf16[4,32,1024]{2,1,0:T(8,128)(2,1)S(1)} %get-tuple-element.30), channel_id=1, source_target_pairs={{0,8},{1,9},{2,10},{3,11},{4,12},{5,13},{6,14},{7,15},{8,0},{9,1},... | collective-permute-start | bytes 786440 | tf_op jit(solution)/shard_map/ppermute | solution.py:101
  36.2 13.9 %collective-permute-start.16 = (bf16[4,32,1024]{2,1,0:T(8,128)(2,1)S(1)}, bf16[4,32,1024]{2,1,0:T(8,128)(2,1)S(1)}, u32[]{:S(2)}, u32[]{:S(2)}) collective-permute-start(bf16[4,32,1024]{2,1,0:T(8,128)(2,1)S(1)} %get-tuple-element.30), channel_id=1, source_target_pairs={{0,4},{1,5},{2,6},{3,7},{4,8},{5,9},{6,10},{7,11},{8,12},{9,13},{1... | collective-permute-start | bytes 786440 | tf_op jit(solution)/shard_map/ppermute | solution.py:101
  46.1 26.9 %collective-permute-start.4 = (bf16[4,128,1024]{2,1,0:T(8,128)(2,1)S(1)}, bf16[4,128,1024]{2,1,0:T(8,128)(2,1)S(1)}, u32[]{:S(2)}, u32[]{:S(2)}) collective-permute-start(bf16[4,128,1024]{2,1,0:T(8,128)(2,1)S(1)} %pad_maximum_fusion), channel_id=1, source_target_pairs={{0,4},{1,5},{2,6},{3,7},{4,8},{5,9},{6,10},{7,11},{8,12},{9,13},{1... | collective-permute-start | bytes 3145736 | tf_op jit(solution)/shard_map/ppermute | solution.py:101
  47.9 25.9 %collective-permute-start.3 = (bf16[4,128,1024]{2,1,0:T(8,128)(2,1)S(1)}, bf16[4,128,1024]{2,1,0:T(8,128)(2,1)S(1)}, u32[]{:S(2)}, u32[]{:S(2)}) collective-permute-start(bf16[4,128,1024]{2,1,0:T(8,128)(2,1)S(1)} %pad_maximum_fusion), channel_id=1, source_target_pairs={{0,12},{1,13},{2,14},{3,15},{4,0},{5,1},{6,2},{7,3},{8,4},{9,5},{1... | collective-permute-start | bytes 3145736 | tf_op jit(solution)/shard_map/ppermute | solution.py:101
  50.2 30.6 %collective-permute-start.17 = (bf16[4,128,1024]{2,1,0:T(8,128)(2,1)S(1)}, bf16[4,128,1024]{2,1,0:T(8,128)(2,1)S(1)}, u32[]{:S(2)}, u32[]{:S(2)}) collective-permute-start(bf16[4,128,1024]{2,1,0:T(8,128)(2,1)S(1)} %pad_maximum_fusion.1), channel_id=1, source_target_pairs={{0,3},{1,0},{2,1},{3,2},{4,7},{5,4},{6,5},{7,6},{8,11},{9,8},{10,9... | collective-permute-start | bytes 3145736 | tf_op jit(solution)/shard_map/ppermute | solution.py:101
  50.2 27.8 %collective-permute-start.18 = (bf16[4,128,1024]{2,1,0:T(8,128)(2,1)S(1)}, bf16[4,128,1024]{2,1,0:T(8,128)(2,1)S(1)}, u32[]{:S(2)}, u32[]{:S(2)}) collective-permute-start(bf16[4,128,1024]{2,1,0:T(8,128)(2,1)S(1)} %pad_maximum_fusion.1), channel_id=1, source_target_pairs={{0,1},{1,2},{2,3},{3,0},{4,5},{5,6},{6,7},{7,4},{8,9},{9,10},{10,1... | collective-permute-start | bytes 3145736 | tf_op jit(solution)/shard_map/ppermute | solution.py:101
  73.0 13.8 %collective-permute-start.5 = (bf16[4,64,1024]{2,1,0:T(8,128)(2,1)S(1)}, bf16[4,64,1024]{2,1,0:T(8,128)(2,1)S(1)}, u32[]{:S(2)}, u32[]{:S(2)}) collective-permute-start(bf16[4,64,1024]{2,1,0:T(8,128)(2,1)S(1)} %slice.153), channel_id=1, source_target_pairs={{0,4},{1,5},{2,6},{3,7},{4,8},{5,9},{6,10},{7,11},{8,12},{9,13},{1... | collective-permute-start | bytes 1572872 | tf_op jit(solution)/shard_map/ppermute | solution.py:101
  73.9 13.8 %collective-permute-start.6 = (bf16[4,64,1024]{2,1,0:T(8,128)(2,1)S(1)}, bf16[4,64,1024]{2,1,0:T(8,128)(2,1)S(1)}, u32[]{:S(2)}, u32[]{:S(2)}) collective-permute-start(bf16[4,64,1024]{2,1,0:T(8,128)(2,1)S(1)} %slice.154), channel_id=1, source_target_pairs={{0,12},{1,13},{2,14},{3,15},{4,0},{5,1},{6,2},{7,3},{8,4},{9,5},{1... | collective-permute-start | bytes 1572872 | tf_op jit(solution)/shard_map/ppermute | solution.py:101
  78.9 23.3 %collective-permute-start.19 = (bf16[4,64,1024]{2,1,0:T(8,128)(2,1)}, bf16[4,64,1024]{2,1,0:T(8,128)(2,1)}, u32[]{:S(2)}, u32[]{:S(2)}) collective-permute-start(bf16[4,64,1024]{2,1,0:T(8,128)(2,1)} %slice.165), channel_id=1, source_target_pairs={{0,1},{1,2},{2,3},{3,0},{4,5},{5,6},{6,7},{7,4},{8,9},{9,10},{10,1... | collective-permute-start | bytes 1572872 | tf_op jit(solution)/shard_map/ppermute | solution.py:101
  81.6 22.5 %collective-permute-start.20 = (bf16[4,64,1024]{2,1,0:T(8,128)(2,1)}, bf16[4,64,1024]{2,1,0:T(8,128)(2,1)}, u32[]{:S(2)}, u32[]{:S(2)}) collective-permute-start(bf16[4,64,1024]{2,1,0:T(8,128)(2,1)} %slice.166), channel_id=1, source_target_pairs={{0,3},{1,0},{2,1},{3,2},{4,7},{5,4},{6,5},{7,6},{8,11},{9,8},{10,9... | collective-permute-start | bytes 1572872 | tf_op jit(solution)/shard_map/ppermute | solution.py:101
  99.5 19.6 %collective-permute-start.7 = (bf16[4,64,1024]{2,1,0:T(8,128)(2,1)}, bf16[4,64,1024]{2,1,0:T(8,128)(2,1)}, u32[]{:S(2)}, u32[]{:S(2)}) collective-permute-start(bf16[4,64,1024]{2,1,0:T(8,128)(2,1)} %get-tuple-element.11), channel_id=1, source_target_pairs={{0,4},{1,5},{2,6},{3,7},{4,8},{5,9},{6,10},{7,11},{8,12},{9,13},{1... | collective-permute-start | bytes 1572872 | tf_op jit(solution)/shard_map/ppermute | solution.py:101
  99.5 19.6 %collective-permute-start.9 = (bf16[4,64,1024]{2,1,0:T(8,128)(2,1)}, bf16[4,64,1024]{2,1,0:T(8,128)(2,1)}, u32[]{:S(2)}, u32[]{:S(2)}) collective-permute-start(bf16[4,64,1024]{2,1,0:T(8,128)(2,1)} %get-tuple-element.12), channel_id=1, source_target_pairs={{0,12},{1,13},{2,14},{3,15},{4,0},{5,1},{6,2},{7,3},{8,4},{9,5},{1... | collective-permute-start | bytes 1572872 | tf_op jit(solution)/shard_map/ppermute | solution.py:101
  114.9 13.8 %copy-start.2 = (bf16[4,512,1024]{2,1,0:T(8,128)(2,1)S(1)}, bf16[4,512,1024]{2,1,0:T(8,128)(2,1)}, u32[]{:S(2)}) copy-start(bf16[4,512,1024]{2,1,0:T(8,128)(2,1)} %shard_map.74) | copy-start | bytes 12582916
  116.3 12.4 %collective-permute-start.21 = (bf16[4,64,1024]{2,1,0:T(8,128)(2,1)S(1)}, bf16[4,64,1024]{2,1,0:T(8,128)(2,1)S(1)}, u32[]{:S(2)}, u32[]{:S(2)}) collective-permute-start(bf16[4,64,1024]{2,1,0:T(8,128)(2,1)S(1)} %get-tuple-element.19), channel_id=1, source_target_pairs={{0,1},{1,2},{2,3},{3,0},{4,5},{5,6},{6,7},{7,4},{8,9},{9,10},{10,1... | collective-permute-start | bytes 1572872 | tf_op jit(solution)/shard_map/ppermute | solution.py:101
  117.9 10.8 %collective-permute-start.23 = (bf16[4,64,1024]{2,1,0:T(8,128)(2,1)S(1)}, bf16[4,64,1024]{2,1,0:T(8,128)(2,1)S(1)}, u32[]{:S(2)}, u32[]{:S(2)}) collective-permute-start(bf16[4,64,1024]{2,1,0:T(8,128)(2,1)S(1)} %get-tuple-element.20), channel_id=1, source_target_pairs={{0,3},{1,0},{2,1},{3,2},{4,7},{5,4},{6,5},{7,6},{8,11},{9,8},{10,9... | collective-permute-start | bytes 1572872 | tf_op jit(solution)/shard_map/ppermute | solution.py:101
  121.5 21.8 %collective-permute-start.10 = (bf16[4,128,1024]{2,1,0:T(8,128)(2,1)S(1)}, bf16[4,128,1024]{2,1,0:T(8,128)(2,1)S(1)}, u32[]{:S(2)}, u32[]{:S(2)}) collective-permute-start(bf16[4,128,1024]{2,1,0:T(8,128)(2,1)S(1)} %get-tuple-element.10), channel_id=1, source_target_pairs={{0,12},{1,13},{2,14},{3,15},{4,0},{5,1},{6,2},{7,3},{8,4},{9,5},{1... | collective-permute-start | bytes 3145736 | tf_op jit(solution)/shard_map/ppermute | solution.py:101
  121.5 23.1 %collective-permute-start.8 = (bf16[4,128,1024]{2,1,0:T(8,128)(2,1)S(1)}, bf16[4,128,1024]{2,1,0:T(8,128)(2,1)S(1)}, u32[]{:S(2)}, u32[]{:S(2)}) collective-permute-start(bf16[4,128,1024]{2,1,0:T(8,128)(2,1)S(1)} %get-tuple-element.9), channel_id=1, source_target_pairs={{0,4},{1,5},{2,6},{3,7},{4,8},{5,9},{6,10},{7,11},{8,12},{9,13},{1... | collective-permute-start | bytes 3145736 | tf_op jit(solution)/shard_map/ppermute | solution.py:101
  129.4 22.5 %collective-permute-start.22 = (bf16[4,128,1024]{2,1,0:T(8,128)(2,1)S(1)}, bf16[4,128,1024]{2,1,0:T(8,128)(2,1)S(1)}, u32[]{:S(2)}, u32[]{:S(2)}) collective-permute-start(bf16[4,128,1024]{2,1,0:T(8,128)(2,1)S(1)} %get-tuple-element.17), channel_id=1, source_target_pairs={{0,1},{1,2},{2,3},{3,0},{4,5},{5,6},{6,7},{7,4},{8,9},{9,10},{10,1... | collective-permute-start | bytes 3145736 | tf_op jit(solution)/shard_map/ppermute | solution.py:101
  129.5 22.4 %collective-permute-start.24 = (bf16[4,128,1024]{2,1,0:T(8,128)(2,1)S(1)}, bf16[4,128,1024]{2,1,0:T(8,128)(2,1)S(1)}, u32[]{:S(2)}, u32[]{:S(2)}) collective-permute-start(bf16[4,128,1024]{2,1,0:T(8,128)(2,1)S(1)} %get-tuple-element.18), channel_id=1, source_target_pairs={{0,3},{1,0},{2,1},{3,2},{4,7},{5,4},{6,5},{7,6},{8,11},{9,8},{10,9... | collective-permute-start | bytes 3145736 | tf_op jit(solution)/shard_map/ppermute | solution.py:101
  146.5 11.0 %collective-permute-start.11 = (bf16[4,32,1024]{2,1,0:T(8,128)(2,1)S(1)}, bf16[4,32,1024]{2,1,0:T(8,128)(2,1)S(1)}, u32[]{:S(2)}, u32[]{:S(2)}) collective-permute-start(bf16[4,32,1024]{2,1,0:T(8,128)(2,1)S(1)} %get-tuple-element.21), channel_id=1, source_target_pairs={{0,1},{1,2},{2,3},{3,0},{4,5},{5,6},{6,7},{7,4},{8,9},{9,10},{10,1... | collective-permute-start | bytes 786440 | tf_op jit(solution)/shard_map/ppermute | solution.py:101
  146.6 17.1 %collective-permute-start.12 = (bf16[4,32,1024]{2,1,0:T(8,128)(2,1)S(1)}, bf16[4,32,1024]{2,1,0:T(8,128)(2,1)S(1)}, u32[]{:S(2)}, u32[]{:S(2)}) collective-permute-start(bf16[4,32,1024]{2,1,0:T(8,128)(2,1)S(1)} %get-tuple-element.23), channel_id=1, source_target_pairs={{0,2},{1,3},{2,0},{3,1},{4,6},{5,7},{6,4},{7,5},{8,10},{9,11},{10,... | collective-permute-start | bytes 786440 | tf_op jit(solution)/shard_map/ppermute | solution.py:101
  148.1 15.7 %collective-permute-start.13 = (bf16[4,32,1024]{2,1,0:T(8,128)(2,1)S(1)}, bf16[4,32,1024]{2,1,0:T(8,128)(2,1)S(1)}, u32[]{:S(2)}, u32[]{:S(2)}) collective-permute-start(bf16[4,32,1024]{2,1,0:T(8,128)(2,1)S(1)} %get-tuple-element.22), channel_id=1, source_target_pairs={{0,3},{1,0},{2,1},{3,2},{4,7},{5,4},{6,5},{7,6},{8,11},{9,8},{10,9... | collective-permute-start | bytes 786440 | tf_op jit(solution)/shard_map/ppermute | solution.py:101
  152.6 31.1 %copy-start.4 = (bf16[32,8,1024]{2,1,0:T(8,128)(2,1)S(1)}, bf16[32,8,1024]{2,1,0:T(8,128)(2,1)}, u32[]{:S(2)}) copy-start(bf16[32,8,1024]{2,1,0:T(8,128)(2,1)} %param.7) | copy-start | bytes 1572868
  152.6 11.3 %collective-permute-start.25 = (bf16[4,32,1024]{2,1,0:T(8,128)(2,1)S(1)}, bf16[4,32,1024]{2,1,0:T(8,128)(2,1)S(1)}, u32[]{:S(2)}, u32[]{:S(2)}) collective-permute-start(bf16[4,32,1024]{2,1,0:T(8,128)(2,1)S(1)} %get-tuple-element.24), channel_id=1, source_target_pairs={{0,4},{1,5},{2,6},{3,7},{4,8},{5,9},{6,10},{7,11},{8,12},{9,13},{1... | collective-permute-start | bytes 786440 | tf_op jit(solution)/shard_map/ppermute | solution.py:101
  152.7 11.2 %collective-permute-start.26 = (bf16[4,32,1024]{2,1,0:T(8,128)(2,1)S(1)}, bf16[4,32,1024]{2,1,0:T(8,128)(2,1)S(1)}, u32[]{:S(2)}, u32[]{:S(2)}) collective-permute-start(bf16[4,32,1024]{2,1,0:T(8,128)(2,1)S(1)} %get-tuple-element.26), channel_id=1, source_target_pairs={{0,8},{1,9},{2,10},{3,11},{4,12},{5,13},{6,14},{7,15},{8,0},{9,1},... | collective-permute-start | bytes 786440 | tf_op jit(solution)/shard_map/ppermute | solution.py:101
  157.5 6.4 %collective-permute-start.27 = (bf16[4,32,1024]{2,1,0:T(8,128)(2,1)S(1)}, bf16[4,32,1024]{2,1,0:T(8,128)(2,1)S(1)}, u32[]{:S(2)}, u32[]{:S(2)}) collective-permute-start(bf16[4,32,1024]{2,1,0:T(8,128)(2,1)S(1)} %get-tuple-element.25), channel_id=1, source_target_pairs={{0,12},{1,13},{2,14},{3,15},{4,0},{5,1},{6,2},{7,3},{8,4},{9,5},{1... | collective-permute-start | bytes 786440 | tf_op jit(solution)/shard_map/ppermute | solution.py:101
  167.5 25.6 %all-to-all-start.1 = ((bf16[8,32,1024]{2,1,0:T(8,128)(2,1)}), bf16[8,32,1024]{2,1,0:T(8,128)(2,1)}, u32[]{:S(2)}, u32[]{:S(2)}) async-start(bf16[8,32,1024]{2,1,0:T(8,128)(2,1)} %broadcast_select_fusion.1), calls=%async_computation.1 | async-start | bytes 1048576 | tf_op jit(solution)/shard_map/all_to_all | solution.py:229

commit v11 on v9

--- a/solution.py
+++ b/solution.py
@@ -193,13 +193,13 @@
 
     inputs = candidates.astype(jnp.float32)
     normed = layer_norm(inputs).astype(jnp.bfloat16).reshape(cand_rows * per_group, width)
-    queries = jax.nn.silu(jnp.dot(normed, w_uq[:, width:], preferred_element_type=jnp.float32))
-    queries = (queries * (0.5 * head_dim ** (-0.5))).astype(jnp.bfloat16).reshape(cand_rows, per_group, width)
-
-    q_pos = jnp.swapaxes(queries, 0, 1)
-    q_out = jnp.where(send_filled[:, None, None], q_pos[send_pos], jnp.zeros((), jnp.bfloat16))
-    q_in = lax.all_to_all(q_out, "group", split_axis=0, concat_axis=0, tiled=True)
-    q_rows = q_in[row_index]
+    c_pos = jnp.swapaxes(candidates, 0, 1)
+    c_out = jnp.where(send_filled[:, None, None], c_pos[send_pos], jnp.zeros((), candidates.dtype))
+    c_in = lax.all_to_all(c_out, "group", split_axis=0, concat_axis=0, tiled=True)
+    c_rows = c_in[row_index].reshape(-1, width)
+    q_normed = layer_norm(c_rows.astype(jnp.float32)).astype(jnp.bfloat16)
+    queries = jax.nn.silu(jnp.dot(q_normed, w_uq[:, width:], preferred_element_type=jnp.float32))
+    q_rows = (queries * (0.5 * head_dim ** (-0.5))).astype(jnp.bfloat16).reshape(per_group, cand_rows, width)
     split = per_group // 2
     halves = ((slice(0, split), (0, 1)), (slice(split, per_group), (1, 0)))
     sums = []

time: 192 us -> 206 us (1.073)
  local copies, waits for them, and re-layouts: 32.3 us -> 51.1 us
  waiting for transfers between devices: 52.5 us -> 46.7 us
    unnamed x23, local copies, waits for them, and re-layouts: 12.7 us -> 18.9 us
    all_to_all x1, waiting for transfers between devices: 8.61 us -> 5.03 us  [on_device(): lax.all_to_all(c_out, 'group', split_axis=0, concat_axis=0, tiled=True)]
    slice x4, local copies, waits for them, and re-layouts: 0.88 us -> 3.81 us  [ring_gather(): second = send(ahead[:, half:], grid, axis, -1)]
    slice x4, local copies, waits for them, and re-layouts: 0.88 us -> 3.78 us  [ring_gather(): first = send(behind[:, :half], grid, axis, 1)]
    concatenate x4, local copies, waits for them, and re-layouts: 3.64 us -> 6.34 us  [ring_gather(): return jnp.concatenate([slots[r] for r in range(n)], axis=1)]
    slice x1, local copies, waits for them, and re-layouts: 2.49 us -> 4.77 us  [on_device(): kv_cache[rows_of]]
    ppermute x32, waiting for transfers between devices: 37.9 us -> 35.7 us  [send(): return lax.ppermute(value, 'member', shift_perm(grid, axis, shift))]
  transfers between devices with their start and end apart: 34 -> 34, of which waited for: 11 -> 10; matrix products, arithmetic and copies ran while one was open for 19% -> 27% of each run, Pallas kernels for 8% -> 8%
where the time goes in v11:
time: 206 us; the launch traced here: 204 us
  starting transfers between devices  64 us (31%)
  local copies, waits for them, and re-layouts  51.1 us (25%)
  waiting for transfers between devices  46.7 us (23%)
  other arithmetic  19.1 us (9%)
  Pallas kernels  15.5 us (8%)
  matrix products  7.5 us (4%)
    ppermute x32, starting transfers between devices, send(): return lax.ppermute(value, 'member', shift_perm(grid, axis, shift))  40.9 us
    ppermute x32, waiting for transfers between devices, send(): return lax.ppermute(value, 'member', shift_perm(grid, axis, shift))  35.7 us
    unnamed x23, local copies, waits for them, and re-layouts  18.9 us
    all_to_all x1, starting transfers between devices, on_device(): lax.all_to_all(a_out, 'group', split_axis=0, concat_axis=0, tiled=True)  17.1 us
    pallas_call x2, Pallas kernels, attend_local(): pl.pallas_call(kernel, out_shape=jax.ShapeDtypeStruct((rows, cands, width...  15.5 us
    concatenate x4, local copies, waits for them, and re-layouts, ring_gather(): return jnp.concatenate([slots[r] for r in range(n)], axis=1)  6.34 us
    all_to_all x1, waiting for transfers between devices, on_device(): lax.all_to_all(a_out, 'group', split_axis=0, concat_axis=0, tiled=True)  5.97 us
    all_to_all x1, starting transfers between devices, on_device(): lax.all_to_all(c_out, 'group', split_axis=0, concat_axis=0, tiled=True)  5.96 us
  transfers between devices with their start and end apart: 34, of which 10 were waited for; matrix products, arithmetic and copies ran while one was open for 27% of the time, Pallas kernels for 8%

profile of v11, /device:TPU:1, one launch (start us, length us, event | category | flops | bytes accessed | tf_op | source)
XLA Modules:
  0.0 204.4 jit_solution(17542803817638332586)
XLA Ops:
  0.1 1.0 fusion.36
  1.1 1.3 gather_fusion
  4.2 1.3 copy.40
  5.5 1.4 gather_fusion.4
  6.9 1.9 broadcast_select_fusion
  8.8 6.0 %all-to-all-start = ((bf16[8,32,1024]{2,1,0:T(8,128)(2,1)}), bf16[8,32,1024]{2,1,0:T(8,128)(2,1)}, u32[]{:S(2)}, u32[]{:S(2)}) async-start(bf16[8,32,1024]{2,1,0:T(8,128)(2,1)} %broadcast_select_fusion), calls=%async_computation | async-start | bytes 1048576 | tf_op jit(solution)/shard_map/all_to_all | solution.py:198
  15.9 3.3 %multiply_convert_fusion.1 = (bf16[4,128,1024]{2,1,0:T(8,128)(2,1)}, bf16[4,128,1024]{2,1,0:T(8,128)(2,1)}) fusion(f32[4,128]{1,0:T(4,128)S(1)} %get-tuple-element.55, bf16[8,128,2048]{2,1,0:T(8,128)(2,1)} %param.8, f32[4,128]{1,0:T(4,128)S(1)} %get-tuple-element.56), kind=kLoop, calls=%fused_computation.17 | loop fusion | flops 3145728 | bytes 4198400 | tf_op jit(solution)/shard_map/convert_element_type | solution.py:62
  19.2 5.0 %all-to-all-done = bf16[8,32,1024]{2,1,0:T(8,128)(2,1)} async-done(((bf16[8,32,1024]{2,1,0:T(8,128)(2,1)}), bf16[8,32,1024]{2,1,0:T(8,128)(2,1)}, u32[]{:S(2)}, u32[]{:S(2)}) %all-to-all-start) | async-done | bytes 524320 | tf_op jit(solution)/shard_map/all_to_all | solution.py:198
  24.2 1.6 gather_fusion.5
  26.7 2.4 %multiply_convert_fusion.2 = bf16[256,1024]{1,0:T(8,128)(2,1)S(1)} fusion(bf16[256,1024]{1,0:T(8,128)(2,1)S(1)} %fusion.16, bf16[1024,2048]{1,0:T(8,128)(2,1)} %param.12), kind=kOutput, calls=%fused_computation.41 | convolution fusion | flops 538443776 | bytes 3145728 | tf_op jit(solution)/shard_map/dot_general | solution.py:201
  29.2 2.5 %collective-permute-start = (bf16[4,32,1024]{2,1,0:T(8,128)(2,1)S(1)}, bf16[4,32,1024]{2,1,0:T(8,128)(2,1)S(1)}, u32[]{:S(2)}, u32[]{:S(2)}) collective-permute-start(bf16[4,32,1024]{2,1,0:T(8,128)(2,1)S(1)} %bitcast.77), channel_id=1, source_target_pairs={{0,3},{1,0},{2,1},{3,2},{4,7},{5,4},{6,5},{7,6},{8,11},{9,8},{10,9... | collective-permute-start | bytes 786440 | tf_op jit(solution)/shard_map/ppermute | solution.py:101
  31.8 3.8 %collective-permute-start.16 = (bf16[4,32,1024]{2,1,0:T(8,128)(2,1)S(1)}, bf16[4,32,1024]{2,1,0:T(8,128)(2,1)S(1)}, u32[]{:S(2)}, u32[]{:S(2)}) collective-permute-start(bf16[4,32,1024]{2,1,0:T(8,128)(2,1)S(1)} %bitcast.74), channel_id=1, source_target_pairs={{0,12},{1,13},{2,14},{3,15},{4,0},{5,1},{6,2},{7,3},{8,4},{9,5},{1... | collective-permute-start | bytes 786440 | tf_op jit(solution)/shard_map/ppermute | solution.py:101
  35.5 0.9 constant_dynamic-update-slice_fusion.4
  37.3 2.3 %collective-permute-done.1 = bf16[4,32,1024]{2,1,0:T(8,128)(2,1)S(1)} collective-permute-done((bf16[4,32,1024]{2,1,0:T(8,128)(2,1)S(1)}, bf16[4,32,1024]{2,1,0:T(8,128)(2,1)S(1)}, u32[]{:S(2)}, u32[]{:S(2)}) %collective-permute-start.1) | collective-permute-done | bytes 262176 | tf_op jit(solution)/shard_map/ppermute | solution.py:101
  39.7 2.7 %collective-permute-start.3 = (bf16[4,16,1024]{2,1,0:T(8,128)(2,1)S(1)}, bf16[4,16,1024]{2,1,0:T(8,128)(2,1)S(1)}, u32[]{:S(2)}, u32[]{:S(2)}) collective-permute-start(bf16[4,16,1024]{2,1,0:T(8,128)(2,1)S(1)} %slice.194), channel_id=1, source_target_pairs={{0,3},{1,0},{2,1},{3,2},{4,7},{5,4},{6,5},{7,6},{8,11},{9,8},{10,9... | collective-permute-start | bytes 393224 | tf_op jit(solution)/shard_map/ppermute | solution.py:101
  43.1 1.1 collective-permute-start.18
  44.2 2.2 %collective-permute-start.19 = (bf16[4,16,1024]{2,1,0:T(8,128)(2,1)S(1)}, bf16[4,16,1024]{2,1,0:T(8,128)(2,1)S(1)}, u32[]{:S(2)}, u32[]{:S(2)}) collective-permute-start(bf16[4,16,1024]{2,1,0:T(8,128)(2,1)S(1)} %slice.209), channel_id=1, source_target_pairs={{0,12},{1,13},{2,14},{3,15},{4,0},{5,1},{6,2},{7,3},{8,4},{9,5},{1... | collective-permute-start | bytes 393224 | tf_op jit(solution)/shard_map/ppermute | solution.py:101
  46.4 0.9 constant_dynamic-update-slice_fusion.3
  49.6 0.9 constant_dynamic-update-slice_fusion
  50.5 1.4 collective-permute-start.4
  53.5 0.9 constant_dynamic-update-slice_fusion.14
  54.4 1.9 collective-permute-start.20
  57.0 4.8 %fusion.51 = (bf16[4,128,2048]{2,1,0:T(8,128)(2,1)}, bf16[4,128,2048]{2,1,0:T(8,128)(2,1)}) fusion(bf16[8,128,2048]{2,1,0:T(8,128)(2,1)} %param.8), kind=kLoop, calls=%fused_computation.164 | loop fusion | bytes 8388608 | tf_op jit(solution)/shard_map/slice | solution.py:209
  61.8 12.9 %collective-permute-done.5 = bf16[4,128,1024]{2,1,0:T(8,128)(2,1)} collective-permute-done((bf16[4,128,1024]{2,1,0:T(8,128)(2,1)}, bf16[4,128,1024]{2,1,0:T(8,128)(2,1)}, u32[]{:S(2)}, u32[]{:S(2)}) %collective-permute-start.5) | collective-permute-done | bytes 1048608 | tf_op jit(solution)/shard_map/ppermute | solution.py:101
  74.7 1.9 slice.195
  76.9 1.9 slice.196
  78.7 2.7 %collective-permute-start.7 = (bf16[4,64,1024]{2,1,0:T(8,128)(2,1)}, bf16[4,64,1024]{2,1,0:T(8,128)(2,1)}, u32[]{:S(2)}, u32[]{:S(2)}) collective-permute-start(bf16[4,64,1024]{2,1,0:T(8,128)(2,1)} %slice.196), channel_id=1, source_target_pairs={{0,12},{1,13},{2,14},{3,15},{4,0},{5,1},{6,2},{7,3},{8,4},{9,5},{1... | collective-permute-start | bytes 1572872 | tf_op jit(solution)/shard_map/ppermute | solution.py:101
  81.7 1.9 slice.210
  83.6 1.9 slice.211
  85.5 2.7 %collective-permute-start.23 = (bf16[4,64,1024]{2,1,0:T(8,128)(2,1)}, bf16[4,64,1024]{2,1,0:T(8,128)(2,1)}, u32[]{:S(2)}, u32[]{:S(2)}) collective-permute-start(bf16[4,64,1024]{2,1,0:T(8,128)(2,1)} %slice.211), channel_id=1, source_target_pairs={{0,3},{1,0},{2,1},{3,2},{4,7},{5,4},{6,5},{7,6},{8,11},{9,8},{10,9... | collective-permute-start | bytes 1572872 | tf_op jit(solution)/shard_map/ppermute | solution.py:101
  88.1 2.3 %constant_dynamic-update-slice_fusion.8 = bf16[4,512,1024]{2,1,0:T(8,128)(2,1)} fusion(bf16[4,512,1024]{2,1,0:T(8,128)(2,1)} %get-tuple-element.36, bf16[4,128,1024]{2,1,0:T(8,128)(2,1)} %collective-permute-done.4), kind=kLoop, calls=%fused_computation.75 | loop fusion | bytes 2097152
  90.4 2.3 %constant_dynamic-update-slice_fusion.22 = bf16[4,512,1024]{2,1,0:T(8,128)(2,1)} fusion(bf16[4,512,1024]{2,1,0:T(8,128)(2,1)} %get-tuple-element.42, bf16[4,128,1024]{2,1,0:T(8,128)(2,1)} %collective-permute-done.20), kind=kLoop, calls=%fused_computation.89 | loop fusion | bytes 2097152
  93.6 1.9 constant_dynamic-update-slice_fusion.6
  95.5 2.3 %constant_dynamic-update-slice_fusion.5.q_ref = bf16[4,512,1024]{2,1,0:T(8,128)(2,1)} fusion(bf16[4,512,1024]{2,1,0:T(8,128)(2,1)} %constant_dynamic-update-slice_fusion.6, bf16[4,128,1024]{2,1,0:T(8,128)(2,1)} %collective-permute-done.5), kind=kLoop, calls=%fused_computation.72 | loop fusion | bytes 2097152 | tf_op jit(solution)/shard_map/concatenate | solution.py:120
  97.7 7.7 %shard_map.73 = bf16[4,512,1024]{2,1,0:T(8,128)(2,1)} custom-call(s32[4]{0:T(128)} %get-tuple-element.59.n_live_ref, bf16[4,512,1024]{2,1,0:T(8,128)(2,1)} %constant_dynamic-update-slice_fusion.5.q_ref, bf16[4,128,2048]{2,1,0:T(8,128)(2,1)} %get-tuple-element.19.kv_ref, bf16[4,128,1024]{2,1,0:T(8,128)(2,1)} %get-tuple-element.17.vk_ref), custom_call_target="tpu_custom_call" | custom-call | flops 1073741824 | bytes 10485760 | tf_op jit(solution)/shard_map/pallas_call | solution.py:66
  105.5 2.2 %fusion.50 = (bf16[4,64,1024]{2,1,0:T(8,128)(2,1)}, bf16[4,64,1024]{2,1,0:T(8,128)(2,1)}) fusion(bf16[4,512,1024]{2,1,0:T(8,128)(2,1)} %shard_map.73), kind=kLoop, calls=%fused_computation.163 | loop fusion | bytes 2097152 | tf_op jit(solution)/shard_map/slice | solution.py:137
  107.7 1.5 collective-permute-start.8
  109.2 1.9 constant_dynamic-update-slice_fusion.21
  111.0 1.9 constant_dynamic-update-slice_fusion.20
  113.0 2.3 %constant_dynamic-update-slice_fusion.19.q_ref = bf16[4,512,1024]{2,1,0:T(8,128)(2,1)} fusion(bf16[4,512,1024]{2,1,0:T(8,128)(2,1)} %constant_dynamic-update-slice_fusion.20, bf16[4,128,1024]{2,1,0:T(8,128)(2,1)} %collective-permute-done.21), kind=kLoop, calls=%fused_computation.86 | loop fusion | bytes 2097152 | tf_op jit(solution)/shard_map/concatenate | solution.py:120
  115.3 7.8 %shard_map.74 = bf16[4,512,1024]{2,1,0:T(8,128)(2,1)} custom-call(s32[4]{0:T(128)} %get-tuple-element.60.n_live_ref, bf16[4,512,1024]{2,1,0:T(8,128)(2,1)} %constant_dynamic-update-slice_fusion.19.q_ref, bf16[4,128,2048]{2,1,0:T(8,128)(2,1)} %get-tuple-element.20.kv_ref, bf16[4,128,1024]{2,1,0:T(8,128)(2,1)} %get-tuple-element.18.vk_ref), custom_call_target="tpu_custom_call" | custom-call | flops 1073741824 | bytes 10485760 | tf_op jit(solution)/shard_map/pallas_call | solution.py:66
  123.1 1.4 fusion.52
  124.6 2.7 %collective-permute-start.26 = (bf16[4,64,1024]{2,1,0:T(8,128)(2,1)S(1)}, bf16[4,64,1024]{2,1,0:T(8,128)(2,1)S(1)}, u32[]{:S(2)}, u32[]{:S(2)}) collective-permute-start(bf16[4,64,1024]{2,1,0:T(8,128)(2,1)S(1)} %get-tuple-element.24), channel_id=1, source_target_pairs={{0,3},{1,0},{2,1},{3,2},{4,7},{5,4},{6,5},{7,6},{8,11},{9,8},{10,9... | collective-permute-start | bytes 1572872 | tf_op jit(solution)/shard_map/ppermute | solution.py:101
  127.2 2.2 %add_convert_fusion.3 = (bf16[4,128,1024]{2,1,0:T(8,128)(2,1)S(1)}, bf16[4,128,1024]{2,1,0:T(8,128)(2,1)S(1)}) fusion(bf16[4,512,1024]{2,1,0:T(8,128)(2,1)} %shard_map.73, bf16[4,64,1024]{2,1,0:T(8,128)(2,1)} %collective-permute-done.8, bf16[4,64,1024]{2,1,0:T(8,128)(2,1)S(1)} %collective-permute-done.10), kind=kLoop, calls=%fused_computation.16 | loop fusion | flops 4194304 | bytes 5242880 | tf_op jit(solution)/shard_map/convert_element_type | solution.py:142
  129.9 1.0 collective-permute-start.9
  131.1 2.7 %collective-permute-done.24 = bf16[4,64,1024]{2,1,0:T(8,128)(2,1)S(1)} collective-permute-done((bf16[4,64,1024]{2,1,0:T(8,128)(2,1)S(1)}, bf16[4,64,1024]{2,1,0:T(8,128)(2,1)S(1)}, u32[]{:S(2)}, u32[]{:S(2)}) %collective-permute-start.24) | collective-permute-done | bytes 524320 | tf_op jit(solution)/shard_map/ppermute | solution.py:101
  134.6 2.7 %collective-permute-start.27 = (bf16[4,128,1024]{2,1,0:T(8,128)(2,1)S(1)}, bf16[4,128,1024]{2,1,0:T(8,128)(2,1)S(1)}, u32[]{:S(2)}, u32[]{:S(2)}) collective-permute-start(bf16[4,128,1024]{2,1,0:T(8,128)(2,1)S(1)} %get-tuple-element.22), channel_id=1, source_target_pairs={{0,3},{1,0},{2,1},{3,2},{4,7},{5,4},{6,5},{7,6},{8,11},{9,8},{10,9... | collective-permute-start | bytes 3145736 | tf_op jit(solution)/shard_map/ppermute | solution.py:101
  137.3 10.3 %collective-permute-done.11 = bf16[4,128,1024]{2,1,0:T(8,128)(2,1)S(1)} collective-permute-done((bf16[4,128,1024]{2,1,0:T(8,128)(2,1)S(1)}, bf16[4,128,1024]{2,1,0:T(8,128)(2,1)S(1)}, u32[]{:S(2)}, u32[]{:S(2)}) %collective-permute-start.11) | collective-permute-done | bytes 1048608 | tf_op jit(solution)/shard_map/ppermute | solution.py:101
  147.6 1.3 collective-permute-done.9
  148.9 1.9 fusion.48
  150.9 2.7 %collective-permute-start.14 = (bf16[4,16,1024]{2,1,0:T(8,128)(2,1)S(1)}, bf16[4,16,1024]{2,1,0:T(8,128)(2,1)S(1)}, u32[]{:S(2)}, u32[]{:S(2)}) collective-permute-start(bf16[4,16,1024]{2,1,0:T(8,128)(2,1)S(1)} %get-tuple-element.30), channel_id=1, source_target_pairs={{0,3},{1,0},{2,1},{3,2},{4,7},{5,4},{6,5},{7,6},{8,11},{9,8},{10,9... | collective-permute-start | bytes 393224 | tf_op jit(solution)/shard_map/ppermute | solution.py:101
  153.6 1.6 collective-permute-done.25
  156.0 2.7 %collective-permute-start.30 = (bf16[4,16,1024]{2,1,0:T(8,128)(2,1)S(1)}, bf16[4,16,1024]{2,1,0:T(8,128)(2,1)S(1)}, u32[]{:S(2)}, u32[]{:S(2)}) collective-permute-start(bf16[4,16,1024]{2,1,0:T(8,128)(2,1)S(1)} %get-tuple-element.32), channel_id=1, source_target_pairs={{0,12},{1,13},{2,14},{3,15},{4,0},{5,1},{6,2},{7,3},{8,4},{9,5},{1... | collective-permute-start | bytes 393224 | tf_op jit(solution)/shard_map/ppermute | solution.py:101
  158.9 3.0 %collective-permute-start.15 = (bf16[4,32,1024]{2,1,0:T(8,128)(2,1)S(1)}, bf16[4,32,1024]{2,1,0:T(8,128)(2,1)S(1)}, u32[]{:S(2)}, u32[]{:S(2)}) collective-permute-start(bf16[4,32,1024]{2,1,0:T(8,128)(2,1)S(1)} %get-tuple-element.26), channel_id=1, source_target_pairs={{0,3},{1,0},{2,1},{3,2},{4,7},{5,4},{6,5},{7,6},{8,11},{9,8},{10,9... | collective-permute-start | bytes 786440 | tf_op jit(solution)/shard_map/ppermute | solution.py:101
  162.0 2.7 %collective-permute-start.31 = (bf16[4,32,1024]{2,1,0:T(8,128)(2,1)S(1)}, bf16[4,32,1024]{2,1,0:T(8,128)(2,1)S(1)}, u32[]{:S(2)}, u32[]{:S(2)}) collective-permute-start(bf16[4,32,1024]{2,1,0:T(8,128)(2,1)S(1)} %get-tuple-element.28), channel_id=1, source_target_pairs={{0,12},{1,13},{2,14},{3,15},{4,0},{5,1},{6,2},{7,3},{8,4},{9,5},{1... | collective-permute-start | bytes 786440 | tf_op jit(solution)/shard_map/ppermute | solution.py:101
  164.7 3.9 %collective-permute-done.13 = bf16[4,32,1024]{2,1,0:T(8,128)(2,1)S(1)} collective-permute-done((bf16[4,32,1024]{2,1,0:T(8,128)(2,1)S(1)}, bf16[4,32,1024]{2,1,0:T(8,128)(2,1)S(1)}, u32[]{:S(2)}, u32[]{:S(2)}) %collective-permute-start.13) | collective-permute-done | bytes 262176 | tf_op jit(solution)/shard_map/ppermute | solution.py:101
  168.9 1.4 gather_fusion.6
  170.3 1.9 broadcast_select_fusion.1
  172.2 17.1 %all-to-all-start.1 = ((bf16[8,32,1024]{2,1,0:T(8,128)(2,1)}), bf16[8,32,1024]{2,1,0:T(8,128)(2,1)}, u32[]{:S(2)}, u32[]{:S(2)}) async-start(bf16[8,32,1024]{2,1,0:T(8,128)(2,1)} %broadcast_select_fusion.1), calls=%async_computation.1 | async-start | bytes 1048576 | tf_op jit(solution)/shard_map/all_to_all | solution.py:215
  189.4 3.4 %multiply_bitcast_fusion = f32[32,8,1024]{2,1,0:T(8,128)} fusion(bf16[1024,2048]{1,0:T(8,128)(2,1)} %param.12, bf16[32,8,1024]{2,1,0:T(8,128)(2,1)S(1)} %copy-done.3, f32[32,8]{1,0:T(8,128)S(1)} %copy.31, f32[32,8]{1,0:T(8,128)S(1)} %copy.29), kind=kOutput, calls=%fused_computation.40 | convolution fusion | flops 538968064 | bytes 3672064 | tf_op jit(solution)/shard_map/dot_general | solution.py:218
  192.8 6.0 %all-to-all-done.1 = bf16[8,32,1024]{2,1,0:T(8,128)(2,1)} async-done(((bf16[8,32,1024]{2,1,0:T(8,128)(2,1)}), bf16[8,32,1024]{2,1,0:T(8,128)(2,1)}, u32[]{:S(2)}, u32[]{:S(2)}) %all-to-all-start.1) | async-done | bytes 524320 | tf_op jit(solution)/shard_map/all_to_all | solution.py:215
  198.8 1.6 gather_fusion.7
  200.9 1.9 fusion.14
  202.7 1.6 fusion.7
  (118 shorter events, 14.9 us)
Async XLA Ops:
  0.0 202.7 %copy-start = (bf16[1024,1024]{1,0:T(8,128)(2,1)S(1)}, bf16[1024,1024]{1,0:T(8,128)(2,1)}, u32[]{:S(2)}) copy-start(bf16[1024,1024]{1,0:T(8,128)(2,1)} %param.13) | copy-start | bytes 6291460
  0.0 14.8 %copy-start.3 = (bf16[32,8,1024]{2,1,0:T(8,128)(2,1)S(1)}, bf16[32,8,1024]{2,1,0:T(8,128)(2,1)}, u32[]{:S(2)}) copy-start(bf16[32,8,1024]{2,1,0:T(8,128)(2,1)} %param.7) | copy-start | bytes 1572868
  0.0 14.9 %copy-start.1 = (s32[64]{0:T(128)S(1)}, s32[64]{0:T(128)}, u32[]{:S(2)}) copy-start(s32[64]{0:T(128)} %param.11) | copy-start | bytes 772
  8.8 15.4 %all-to-all-start = ((bf16[8,32,1024]{2,1,0:T(8,128)(2,1)}), bf16[8,32,1024]{2,1,0:T(8,128)(2,1)}, u32[]{:S(2)}, u32[]{:S(2)}) async-start(bf16[8,32,1024]{2,1,0:T(8,128)(2,1)} %broadcast_select_fusion), calls=%async_computation | async-start | bytes 1048576 | tf_op jit(solution)/shard_map/all_to_all | solution.py:198
  29.2 10.5 %collective-permute-start = (bf16[4,32,1024]{2,1,0:T(8,128)(2,1)S(1)}, bf16[4,32,1024]{2,1,0:T(8,128)(2,1)S(1)}, u32[]{:S(2)}, u32[]{:S(2)}) collective-permute-start(bf16[4,32,1024]{2,1,0:T(8,128)(2,1)S(1)} %bitcast.77), channel_id=1, source_target_pairs={{0,3},{1,0},{2,1},{3,2},{4,7},{5,4},{6,5},{7,6},{8,11},{9,8},{10,9... | collective-permute-start | bytes 786440 | tf_op jit(solution)/shard_map/ppermute | solution.py:101
  31.8 7.8 %collective-permute-start.1 = (bf16[4,32,1024]{2,1,0:T(8,128)(2,1)S(1)}, bf16[4,32,1024]{2,1,0:T(8,128)(2,1)S(1)}, u32[]{:S(2)}, u32[]{:S(2)}) collective-permute-start(bf16[4,32,1024]{2,1,0:T(8,128)(2,1)S(1)} %bitcast.78), channel_id=1, source_target_pairs={{0,1},{1,2},{2,3},{3,0},{4,5},{5,6},{6,7},{7,4},{8,9},{9,10},{10,1... | collective-permute-start | bytes 786440 | tf_op jit(solution)/shard_map/ppermute | solution.py:101
  31.8 12.4 %collective-permute-start.16 = (bf16[4,32,1024]{2,1,0:T(8,128)(2,1)S(1)}, bf16[4,32,1024]{2,1,0:T(8,128)(2,1)S(1)}, u32[]{:S(2)}, u32[]{:S(2)}) collective-permute-start(bf16[4,32,1024]{2,1,0:T(8,128)(2,1)S(1)} %bitcast.74), channel_id=1, source_target_pairs={{0,12},{1,13},{2,14},{3,15},{4,0},{5,1},{6,2},{7,3},{8,4},{9,5},{1... | collective-permute-start | bytes 786440 | tf_op jit(solution)/shard_map/ppermute | solution.py:101
  35.5 7.5 %collective-permute-start.17 = (bf16[4,32,1024]{2,1,0:T(8,128)(2,1)S(1)}, bf16[4,32,1024]{2,1,0:T(8,128)(2,1)S(1)}, u32[]{:S(2)}, u32[]{:S(2)}) collective-permute-start(bf16[4,32,1024]{2,1,0:T(8,128)(2,1)S(1)} %bitcast.75), channel_id=1, source_target_pairs={{0,4},{1,5},{2,6},{3,7},{4,8},{5,9},{6,10},{7,11},{8,12},{9,13},{1... | collective-permute-start | bytes 786440 | tf_op jit(solution)/shard_map/ppermute | solution.py:101
  39.6 8.6 %collective-permute-start.2 = (bf16[4,16,1024]{2,1,0:T(8,128)(2,1)S(1)}, bf16[4,16,1024]{2,1,0:T(8,128)(2,1)S(1)}, u32[]{:S(2)}, u32[]{:S(2)}) collective-permute-start(bf16[4,16,1024]{2,1,0:T(8,128)(2,1)S(1)} %slice.193), channel_id=1, source_target_pairs={{0,1},{1,2},{2,3},{3,0},{4,5},{5,6},{6,7},{7,4},{8,9},{9,10},{10,1... | collective-permute-start | bytes 393224 | tf_op jit(solution)/shard_map/ppermute | solution.py:101
  39.7 9.2 %collective-permute-start.3 = (bf16[4,16,1024]{2,1,0:T(8,128)(2,1)S(1)}, bf16[4,16,1024]{2,1,0:T(8,128)(2,1)S(1)}, u32[]{:S(2)}, u32[]{:S(2)}) collective-permute-start(bf16[4,16,1024]{2,1,0:T(8,128)(2,1)S(1)} %slice.194), channel_id=1, source_target_pairs={{0,3},{1,0},{2,1},{3,2},{4,7},{5,4},{6,5},{7,6},{8,11},{9,8},{10,9... | collective-permute-start | bytes 393224 | tf_op jit(solution)/shard_map/ppermute | solution.py:101
  43.1 8.9 %collective-permute-start.18 = (bf16[4,16,1024]{2,1,0:T(8,128)(2,1)S(1)}, bf16[4,16,1024]{2,1,0:T(8,128)(2,1)S(1)}, u32[]{:S(2)}, u32[]{:S(2)}) collective-permute-start(bf16[4,16,1024]{2,1,0:T(8,128)(2,1)S(1)} %slice.208), channel_id=1, source_target_pairs={{0,4},{1,5},{2,6},{3,7},{4,8},{5,9},{6,10},{7,11},{8,12},{9,13},{1... | collective-permute-start | bytes 393224 | tf_op jit(solution)/shard_map/ppermute | solution.py:101
  44.2 8.6 %collective-permute-start.19 = (bf16[4,16,1024]{2,1,0:T(8,128)(2,1)S(1)}, bf16[4,16,1024]{2,1,0:T(8,128)(2,1)S(1)}, u32[]{:S(2)}, u32[]{:S(2)}) collective-permute-start(bf16[4,16,1024]{2,1,0:T(8,128)(2,1)S(1)} %slice.209), channel_id=1, source_target_pairs={{0,12},{1,13},{2,14},{3,15},{4,0},{5,1},{6,2},{7,3},{8,4},{9,5},{1... | collective-permute-start | bytes 393224 | tf_op jit(solution)/shard_map/ppermute | solution.py:101
  50.5 26.4 %collective-permute-start.4 = (bf16[4,128,1024]{2,1,0:T(8,128)(2,1)}, bf16[4,128,1024]{2,1,0:T(8,128)(2,1)}, u32[]{:S(2)}, u32[]{:S(2)}) collective-permute-start(bf16[4,128,1024]{2,1,0:T(8,128)(2,1)} %get-tuple-element.35), channel_id=1, source_target_pairs={{0,12},{1,13},{2,14},{3,15},{4,0},{5,1},{6,2},{7,3},{8,4},{9,5},{1... | collective-permute-start | bytes 3145736 | tf_op jit(solution)/shard_map/ppermute | solution.py:101
  51.9 22.7 %collective-permute-start.5 = (bf16[4,128,1024]{2,1,0:T(8,128)(2,1)}, bf16[4,128,1024]{2,1,0:T(8,128)(2,1)}, u32[]{:S(2)}, u32[]{:S(2)}) collective-permute-start(bf16[4,128,1024]{2,1,0:T(8,128)(2,1)} %get-tuple-element.35), channel_id=1, source_target_pairs={{0,4},{1,5},{2,6},{3,7},{4,8},{5,9},{6,10},{7,11},{8,12},{9,13},{1... | collective-permute-start | bytes 3145736 | tf_op jit(solution)/shard_map/ppermute | solution.py:101
  54.4 29.2 %collective-permute-start.20 = (bf16[4,128,1024]{2,1,0:T(8,128)(2,1)}, bf16[4,128,1024]{2,1,0:T(8,128)(2,1)}, u32[]{:S(2)}, u32[]{:S(2)}) collective-permute-start(bf16[4,128,1024]{2,1,0:T(8,128)(2,1)} %get-tuple-element.41), channel_id=1, source_target_pairs={{0,3},{1,0},{2,1},{3,2},{4,7},{5,4},{6,5},{7,6},{8,11},{9,8},{10,9... | collective-permute-start | bytes 3145736 | tf_op jit(solution)/shard_map/ppermute | solution.py:101
  56.3 25.4 %collective-permute-start.21 = (bf16[4,128,1024]{2,1,0:T(8,128)(2,1)}, bf16[4,128,1024]{2,1,0:T(8,128)(2,1)}, u32[]{:S(2)}, u32[]{:S(2)}) collective-permute-start(bf16[4,128,1024]{2,1,0:T(8,128)(2,1)} %get-tuple-element.41), channel_id=1, source_target_pairs={{0,1},{1,2},{2,3},{3,0},{4,5},{5,6},{6,7},{7,4},{8,9},{9,10},{10,1... | collective-permute-start | bytes 3145736 | tf_op jit(solution)/shard_map/ppermute | solution.py:101
  76.6 16.1 %collective-permute-start.6 = (bf16[4,64,1024]{2,1,0:T(8,128)(2,1)}, bf16[4,64,1024]{2,1,0:T(8,128)(2,1)S(1)}, u32[]{:S(2)}, u32[]{:S(2)}) collective-permute-start(bf16[4,64,1024]{2,1,0:T(8,128)(2,1)} %slice.195), channel_id=1, source_target_pairs={{0,4},{1,5},{2,6},{3,7},{4,8},{5,9},{6,10},{7,11},{8,12},{9,13},{1... | collective-permute-start | bytes 1572872 | tf_op jit(solution)/shard_map/ppermute | solution.py:101
  78.7 14.8 %collective-permute-start.7 = (bf16[4,64,1024]{2,1,0:T(8,128)(2,1)}, bf16[4,64,1024]{2,1,0:T(8,128)(2,1)}, u32[]{:S(2)}, u32[]{:S(2)}) collective-permute-start(bf16[4,64,1024]{2,1,0:T(8,128)(2,1)} %slice.196), channel_id=1, source_target_pairs={{0,12},{1,13},{2,14},{3,15},{4,0},{5,1},{6,2},{7,3},{8,4},{9,5},{1... | collective-permute-start | bytes 1572872 | tf_op jit(solution)/shard_map/ppermute | solution.py:101
  83.6 25.6 %collective-permute-start.22 = (bf16[4,64,1024]{2,1,0:T(8,128)(2,1)}, bf16[4,64,1024]{2,1,0:T(8,128)(2,1)}, u32[]{:S(2)}, u32[]{:S(2)}) collective-permute-start(bf16[4,64,1024]{2,1,0:T(8,128)(2,1)} %slice.210), channel_id=1, source_target_pairs={{0,1},{1,2},{2,3},{3,0},{4,5},{5,6},{6,7},{7,4},{8,9},{9,10},{10,1... | collective-permute-start | bytes 1572872 | tf_op jit(solution)/shard_map/ppermute | solution.py:101
  85.5 25.6 %collective-permute-start.23 = (bf16[4,64,1024]{2,1,0:T(8,128)(2,1)}, bf16[4,64,1024]{2,1,0:T(8,128)(2,1)}, u32[]{:S(2)}, u32[]{:S(2)}) collective-permute-start(bf16[4,64,1024]{2,1,0:T(8,128)(2,1)} %slice.211), channel_id=1, source_target_pairs={{0,3},{1,0},{2,1},{3,2},{4,7},{5,4},{6,5},{7,6},{8,11},{9,8},{10,9... | collective-permute-start | bytes 1572872 | tf_op jit(solution)/shard_map/ppermute | solution.py:101
  107.7 19.5 %collective-permute-start.10 = (bf16[4,64,1024]{2,1,0:T(8,128)(2,1)}, bf16[4,64,1024]{2,1,0:T(8,128)(2,1)S(1)}, u32[]{:S(2)}, u32[]{:S(2)}) collective-permute-start(bf16[4,64,1024]{2,1,0:T(8,128)(2,1)} %get-tuple-element.16), channel_id=1, source_target_pairs={{0,12},{1,13},{2,14},{3,15},{4,0},{5,1},{6,2},{7,3},{8,4},{9,5},{1... | collective-permute-start | bytes 1572872 | tf_op jit(solution)/shard_map/ppermute | solution.py:101
  107.7 19.5 %collective-permute-start.8 = (bf16[4,64,1024]{2,1,0:T(8,128)(2,1)}, bf16[4,64,1024]{2,1,0:T(8,128)(2,1)}, u32[]{:S(2)}, u32[]{:S(2)}) collective-permute-start(bf16[4,64,1024]{2,1,0:T(8,128)(2,1)} %get-tuple-element.15), channel_id=1, source_target_pairs={{0,4},{1,5},{2,6},{3,7},{4,8},{5,9},{6,10},{7,11},{8,12},{9,13},{1... | collective-permute-start | bytes 1572872 | tf_op jit(solution)/shard_map/ppermute | solution.py:101
  123.1 10.7 %copy-start.2 = (bf16[4,512,1024]{2,1,0:T(8,128)(2,1)S(1)}, bf16[4,512,1024]{2,1,0:T(8,128)(2,1)}, u32[]{:S(2)}) copy-start(bf16[4,512,1024]{2,1,0:T(8,128)(2,1)} %shard_map.74) | copy-start | bytes 12582916
  124.5 9.3 %collective-permute-start.24 = (bf16[4,64,1024]{2,1,0:T(8,128)(2,1)S(1)}, bf16[4,64,1024]{2,1,0:T(8,128)(2,1)S(1)}, u32[]{:S(2)}, u32[]{:S(2)}) collective-permute-start(bf16[4,64,1024]{2,1,0:T(8,128)(2,1)S(1)} %get-tuple-element.23), channel_id=1, source_target_pairs={{0,1},{1,2},{2,3},{3,0},{4,5},{5,6},{6,7},{7,4},{8,9},{9,10},{10,1... | collective-permute-start | bytes 1572872 | tf_op jit(solution)/shard_map/ppermute | solution.py:101
  124.6 9.2 %collective-permute-start.26 = (bf16[4,64,1024]{2,1,0:T(8,128)(2,1)S(1)}, bf16[4,64,1024]{2,1,0:T(8,128)(2,1)S(1)}, u32[]{:S(2)}, u32[]{:S(2)}) collective-permute-start(bf16[4,64,1024]{2,1,0:T(8,128)(2,1)S(1)} %get-tuple-element.24), channel_id=1, source_target_pairs={{0,3},{1,0},{2,1},{3,2},{4,7},{5,4},{6,5},{7,6},{8,11},{9,8},{10,9... | collective-permute-start | bytes 1572872 | tf_op jit(solution)/shard_map/ppermute | solution.py:101
  129.4 18.2 %collective-permute-start.11 = (bf16[4,128,1024]{2,1,0:T(8,128)(2,1)S(1)}, bf16[4,128,1024]{2,1,0:T(8,128)(2,1)S(1)}, u32[]{:S(2)}, u32[]{:S(2)}) collective-permute-start(bf16[4,128,1024]{2,1,0:T(8,128)(2,1)S(1)} %get-tuple-element.14), channel_id=1, source_target_pairs={{0,12},{1,13},{2,14},{3,15},{4,0},{5,1},{6,2},{7,3},{8,4},{9,5},{1... | collective-permute-start | bytes 3145736 | tf_op jit(solution)/shard_map/ppermute | solution.py:101
  129.9 18.9 %collective-permute-start.9 = (bf16[4,128,1024]{2,1,0:T(8,128)(2,1)S(1)}, bf16[4,128,1024]{2,1,0:T(8,128)(2,1)S(1)}, u32[]{:S(2)}, u32[]{:S(2)}) collective-permute-start(bf16[4,128,1024]{2,1,0:T(8,128)(2,1)S(1)} %get-tuple-element.13), channel_id=1, source_target_pairs={{0,4},{1,5},{2,6},{3,7},{4,8},{5,9},{6,10},{7,11},{8,12},{9,13},{1... | collective-permute-start | bytes 3145736 | tf_op jit(solution)/shard_map/ppermute | solution.py:101
  134.5 20.7 %collective-permute-start.25 = (bf16[4,128,1024]{2,1,0:T(8,128)(2,1)S(1)}, bf16[4,128,1024]{2,1,0:T(8,128)(2,1)S(1)}, u32[]{:S(2)}, u32[]{:S(2)}) collective-permute-start(bf16[4,128,1024]{2,1,0:T(8,128)(2,1)S(1)} %get-tuple-element.21), channel_id=1, source_target_pairs={{0,1},{1,2},{2,3},{3,0},{4,5},{5,6},{6,7},{7,4},{8,9},{9,10},{10,1... | collective-permute-start | bytes 3145736 | tf_op jit(solution)/shard_map/ppermute | solution.py:101
  134.6 20.6 %collective-permute-start.27 = (bf16[4,128,1024]{2,1,0:T(8,128)(2,1)S(1)}, bf16[4,128,1024]{2,1,0:T(8,128)(2,1)S(1)}, u32[]{:S(2)}, u32[]{:S(2)}) collective-permute-start(bf16[4,128,1024]{2,1,0:T(8,128)(2,1)S(1)} %get-tuple-element.22), channel_id=1, source_target_pairs={{0,3},{1,0},{2,1},{3,2},{4,7},{5,4},{6,5},{7,6},{8,11},{9,8},{10,9... | collective-permute-start | bytes 3145736 | tf_op jit(solution)/shard_map/ppermute | solution.py:101
  150.8 7.9 %collective-permute-start.12 = (bf16[4,16,1024]{2,1,0:T(8,128)(2,1)S(1)}, bf16[4,16,1024]{2,1,0:T(8,128)(2,1)S(1)}, u32[]{:S(2)}, u32[]{:S(2)}) collective-permute-start(bf16[4,16,1024]{2,1,0:T(8,128)(2,1)S(1)} %get-tuple-element.29), channel_id=1, source_target_pairs={{0,1},{1,2},{2,3},{3,0},{4,5},{5,6},{6,7},{7,4},{8,9},{9,10},{10,1... | collective-permute-start | bytes 393224 | tf_op jit(solution)/shard_map/ppermute | solution.py:101
  150.9 7.8 %collective-permute-start.14 = (bf16[4,16,1024]{2,1,0:T(8,128)(2,1)S(1)}, bf16[4,16,1024]{2,1,0:T(8,128)(2,1)S(1)}, u32[]{:S(2)}, u32[]{:S(2)}) collective-permute-start(bf16[4,16,1024]{2,1,0:T(8,128)(2,1)S(1)} %get-tuple-element.30), channel_id=1, source_target_pairs={{0,3},{1,0},{2,1},{3,2},{4,7},{5,4},{6,5},{7,6},{8,11},{9,8},{10,9... | collective-permute-start | bytes 393224 | tf_op jit(solution)/shard_map/ppermute | solution.py:101
  155.9 5.9 %collective-permute-start.28 = (bf16[4,16,1024]{2,1,0:T(8,128)(2,1)S(1)}, bf16[4,16,1024]{2,1,0:T(8,128)(2,1)S(1)}, u32[]{:S(2)}, u32[]{:S(2)}) collective-permute-start(bf16[4,16,1024]{2,1,0:T(8,128)(2,1)S(1)} %get-tuple-element.31), channel_id=1, source_target_pairs={{0,4},{1,5},{2,6},{3,7},{4,8},{5,9},{6,10},{7,11},{8,12},{9,13},{1... | collective-permute-start | bytes 393224 | tf_op jit(solution)/shard_map/ppermute | solution.py:101
  156.0 5.8 %collective-permute-start.30 = (bf16[4,16,1024]{2,1,0:T(8,128)(2,1)S(1)}, bf16[4,16,1024]{2,1,0:T(8,128)(2,1)S(1)}, u32[]{:S(2)}, u32[]{:S(2)}) collective-permute-start(bf16[4,16,1024]{2,1,0:T(8,128)(2,1)S(1)} %get-tuple-element.32), channel_id=1, source_target_pairs={{0,12},{1,13},{2,14},{3,15},{4,0},{5,1},{6,2},{7,3},{8,4},{9,5},{1... | collective-permute-start | bytes 393224 | tf_op jit(solution)/shard_map/ppermute | solution.py:101
  158.8 9.8 %collective-permute-start.13 = (bf16[4,32,1024]{2,1,0:T(8,128)(2,1)S(1)}, bf16[4,32,1024]{2,1,0:T(8,128)(2,1)S(1)}, u32[]{:S(2)}, u32[]{:S(2)}) collective-permute-start(bf16[4,32,1024]{2,1,0:T(8,128)(2,1)S(1)} %get-tuple-element.25), channel_id=1, source_target_pairs={{0,1},{1,2},{2,3},{3,0},{4,5},{5,6},{6,7},{7,4},{8,9},{9,10},{10,1... | collective-permute-start | bytes 786440 | tf_op jit(solution)/shard_map/ppermute | solution.py:101
  158.9 9.7 %collective-permute-start.15 = (bf16[4,32,1024]{2,1,0:T(8,128)(2,1)S(1)}, bf16[4,32,1024]{2,1,0:T(8,128)(2,1)S(1)}, u32[]{:S(2)}, u32[]{:S(2)}) collective-permute-start(bf16[4,32,1024]{2,1,0:T(8,128)(2,1)S(1)} %get-tuple-element.26), channel_id=1, source_target_pairs={{0,3},{1,0},{2,1},{3,2},{4,7},{5,4},{6,5},{7,6},{8,11},{9,8},{10,9... | collective-permute-start | bytes 786440 | tf_op jit(solution)/shard_map/ppermute | solution.py:101
  161.9 6.8 %collective-permute-start.29 = (bf16[4,32,1024]{2,1,0:T(8,128)(2,1)S(1)}, bf16[4,32,1024]{2,1,0:T(8,128)(2,1)S(1)}, u32[]{:S(2)}, u32[]{:S(2)}) collective-permute-start(bf16[4,32,1024]{2,1,0:T(8,128)(2,1)S(1)} %get-tuple-element.27), channel_id=1, source_target_pairs={{0,4},{1,5},{2,6},{3,7},{4,8},{5,9},{6,10},{7,11},{8,12},{9,13},{1... | collective-permute-start | bytes 786440 | tf_op jit(solution)/shard_map/ppermute | solution.py:101
  162.0 6.7 %collective-permute-start.31 = (bf16[4,32,1024]{2,1,0:T(8,128)(2,1)S(1)}, bf16[4,32,1024]{2,1,0:T(8,128)(2,1)S(1)}, u32[]{:S(2)}, u32[]{:S(2)}) collective-permute-start(bf16[4,32,1024]{2,1,0:T(8,128)(2,1)S(1)} %get-tuple-element.28), channel_id=1, source_target_pairs={{0,12},{1,13},{2,14},{3,15},{4,0},{5,1},{6,2},{7,3},{8,4},{9,5},{1... | collective-permute-start | bytes 786440 | tf_op jit(solution)/shard_map/ppermute | solution.py:101
  172.2 26.6 %all-to-all-start.1 = ((bf16[8,32,1024]{2,1,0:T(8,128)(2,1)}), bf16[8,32,1024]{2,1,0:T(8,128)(2,1)}, u32[]{:S(2)}, u32[]{:S(2)}) async-start(bf16[8,32,1024]{2,1,0:T(8,128)(2,1)} %broadcast_select_fusion.1), calls=%async_computation.1 | async-start | bytes 1048576 | tf_op jit(solution)/shard_map/all_to_all | solution.py:215

commit v12 on v9

--- a/solution.py
+++ b/solution.py
@@ -202,9 +202,12 @@
     q_rows = q_in[row_index]
     split = per_group // 2
     halves = ((slice(0, split), (0, 1)), (slice(split, per_group), (1, 0)))
+    inner_first = ring_gather(q_rows[halves[0][0]], grid, halves[0][1][1])
+    inner_first, rows_second = lax.optimization_barrier((inner_first, q_rows[halves[1][0]]))
+    inner_second = ring_gather(rows_second, grid, halves[1][1][1])
     sums = []
-    for rows_of, order in halves:
-        q_all = torus_gather(q_rows[rows_of], grid, order)
+    for (rows_of, order), inner in zip(halves, (inner_first, inner_second)):
+        q_all = ring_gather(inner, grid, order[0])
         partial = attend_local(
             q_all, kv_cache[rows_of], row_live[rows_of], member_now * count, HEADS, jnp.bfloat16
         )

time: 192 us -> 219 us (1.14)
  waiting for transfers between devices: 52.5 us -> 76.9 us
  starting transfers between devices: 64.5 us -> 67 us
    ppermute x32, waiting for transfers between devices: 37.9 us -> 62.3 us  [send(): return lax.ppermute(value, 'member', shift_perm(grid, axis, shift))]
    unnamed x23 -> x24, local copies, waits for them, and re-layouts: 12.7 us -> 11.6 us
  transfers between devices with their start and end apart: 34 -> 34, of which waited for: 11 -> 12; matrix products, arithmetic and copies ran while one was open for 19% -> 17% of each run, Pallas kernels for 8% -> 7%
where the time goes in v12:
time: 219 us; the launch traced here: 218 us
  waiting for transfers between devices  76.9 us (35%)
  starting transfers between devices  67 us (31%)
  local copies, waits for them, and re-layouts  30.6 us (14%)
  other arithmetic  19.5 us (9%)
  Pallas kernels  15.6 us (7%)
  matrix products  7.74 us (4%)
    ppermute x32, waiting for transfers between devices, send(): return lax.ppermute(value, 'member', shift_perm(grid, axis, shift))  62.3 us
    ppermute x32, starting transfers between devices, send(): return lax.ppermute(value, 'member', shift_perm(grid, axis, shift))  43.2 us
    all_to_all x1, starting transfers between devices, on_device(): lax.all_to_all(a_out, 'group', split_axis=0, concat_axis=0, tiled=True)  17.8 us
    pallas_call x2, Pallas kernels, attend_local(): pl.pallas_call(kernel, out_shape=jax.ShapeDtypeStruct((rows, cands, width...  15.6 us
    unnamed x24, local copies, waits for them, and re-layouts  11.6 us
    all_to_all x1, waiting for transfers between devices, on_device(): lax.all_to_all(q_out, 'group', split_axis=0, concat_axis=0, tiled=True)  8.61 us
    all_to_all x1, waiting for transfers between devices, on_device(): lax.all_to_all(a_out, 'group', split_axis=0, concat_axis=0, tiled=True)  6.03 us
    all_to_all x1, starting transfers between devices, on_device(): lax.all_to_all(q_out, 'group', split_axis=0, concat_axis=0, tiled=True)  5.96 us
  transfers between devices with their start and end apart: 34, of which 12 were waited for; matrix products, arithmetic and copies ran while one was open for 17% of the time, Pallas kernels for 7%

profile of v12, /device:TPU:1, one launch (start us, length us, event | category | flops | bytes accessed | tf_op | source)
XLA Modules:
  0.0 217.7 jit_solution(12374943259111190808)
XLA Ops:
  0.0 1.0 fusion.36
  1.0 1.3 gather_fusion
  4.1 1.2 convert_reduce_fusion
  5.5 1.3 fusion.8
  7.0 2.7 %fusion.19 = bf16[32,8,1024]{2,1,0:T(8,128)(2,1)S(1)} fusion(bf16[1024,2048]{1,0:T(8,128)(2,1)} %param.12, bf16[32,8,1024]{2,1,0:T(8,128)(2,1)} %param.7, f32[32,8]{1,0:T(8,128)S(1)} %copy.37, f32[32,8]{1,0:T(8,128)S(1)} %copy.35), kind=kOutput, calls=%fused_computation.39 | convolution fusion | flops 539492352 | bytes 3147776 | tf_op jit(solution)/shard_map/dot_general | solution.py:196
  10.5 0.9 broadcast_select_fusion
  11.4 6.0 %all-to-all-start = ((bf16[8,32,1024]{2,1,0:T(8,128)(2,1)}), bf16[8,32,1024]{2,1,0:T(8,128)(2,1)S(1)}, u32[]{:S(2)}, u32[]{:S(2)}) async-start(bf16[8,32,1024]{2,1,0:T(8,128)(2,1)} %broadcast_select_fusion), calls=%async_computation | async-start | bytes 1048576 | tf_op jit(solution)/shard_map/all_to_all | solution.py:201
  18.1 8.6 %all-to-all-done = bf16[8,32,1024]{2,1,0:T(8,128)(2,1)S(1)} async-done(((bf16[8,32,1024]{2,1,0:T(8,128)(2,1)}), bf16[8,32,1024]{2,1,0:T(8,128)(2,1)S(1)}, u32[]{:S(2)}, u32[]{:S(2)}) %all-to-all-start) | async-done | bytes 524320 | tf_op jit(solution)/shard_map/all_to_all | solution.py:201
  27.4 1.3 collective-permute-start.1
  28.7 1.5 collective-permute-start
  30.2 5.4 %collective-permute-done.1 = bf16[4,32,1024]{2,1,0:T(8,128)(2,1)S(1)} collective-permute-done((bf16[4,32,1024]{2,1,0:T(8,128)(2,1)S(1)}, bf16[4,32,1024]{2,1,0:T(8,128)(2,1)S(1)}, u32[]{:S(2)}, u32[]{:S(2)}) %collective-permute-start.1) | collective-permute-done | bytes 262176 | tf_op jit(solution)/shard_map/ppermute | solution.py:101
  35.8 2.7 %collective-permute-start.3 = (bf16[4,16,1024]{2,1,0:T(8,128)(2,1)S(1)}, bf16[4,16,1024]{2,1,0:T(8,128)(2,1)S(1)}, u32[]{:S(2)}, u32[]{:S(2)}) collective-permute-start(bf16[4,16,1024]{2,1,0:T(8,128)(2,1)S(1)} %slice.186), channel_id=1, source_target_pairs={{0,3},{1,0},{2,1},{3,2},{4,7},{5,4},{6,5},{7,6},{8,11},{9,8},{10,9... | collective-permute-start | bytes 393224 | tf_op jit(solution)/shard_map/ppermute | solution.py:101
  38.5 2.2 collective-permute-done.2
  40.8 3.8 %collective-permute-start.16 = (bf16[4,32,1024]{2,1,0:T(8,128)(2,1)S(1)}, bf16[4,32,1024]{2,1,0:T(8,128)(2,1)S(1)}, u32[]{:S(2)}, u32[]{:S(2)}) collective-permute-start(bf16[4,32,1024]{2,1,0:T(8,128)(2,1)S(1)} %get-tuple-element.8), channel_id=1, source_target_pairs={{0,12},{1,13},{2,14},{3,15},{4,0},{5,1},{6,2},{7,3},{8,4},{9,5},{1... | collective-permute-start | bytes 786440 | tf_op jit(solution)/shard_map/ppermute | solution.py:101
  44.6 3.3 %multiply_convert_fusion.1 = (bf16[4,128,1024]{2,1,0:T(8,128)(2,1)}, bf16[4,128,1024]{2,1,0:T(8,128)(2,1)}) fusion(f32[4,128]{1,0:T(4,128)S(1)} %get-tuple-element.50, bf16[8,128,2048]{2,1,0:T(8,128)(2,1)} %param.8, f32[4,128]{1,0:T(4,128)S(1)} %get-tuple-element.51), kind=kLoop, calls=%fused_computation.17 | loop fusion | flops 3145728 | bytes 4198400 | tf_op jit(solution)/shard_map/convert_element_type | solution.py:62
  47.9 2.7 %collective-permute-start.4 = (bf16[4,128,1024]{2,1,0:T(8,128)(2,1)S(1)}, bf16[4,128,1024]{2,1,0:T(8,128)(2,1)S(1)}, u32[]{:S(2)}, u32[]{:S(2)}) collective-permute-start(bf16[4,128,1024]{2,1,0:T(8,128)(2,1)S(1)} %constant_dynamic-update-slice_fusion), channel_id=1, source_target_pairs={{0,12},{1,13},{2,14},{3,15},{4,0},{5,1},{6,2},{7,3},{8,4},{9,5},{1... | collective-permute-start | bytes 3145736 | tf_op jit(solution)/shard_map/ppermute | solution.py:101
  51.9 2.7 %collective-permute-start.19 = (bf16[4,16,1024]{2,1,0:T(8,128)(2,1)S(1)}, bf16[4,16,1024]{2,1,0:T(8,128)(2,1)S(1)}, u32[]{:S(2)}, u32[]{:S(2)}) collective-permute-start(bf16[4,16,1024]{2,1,0:T(8,128)(2,1)S(1)} %slice.201), channel_id=1, source_target_pairs={{0,12},{1,13},{2,14},{3,15},{4,0},{5,1},{6,2},{7,3},{8,4},{9,5},{1... | collective-permute-start | bytes 393224 | tf_op jit(solution)/shard_map/ppermute | solution.py:101
  54.6 0.7 constant_dynamic-update-slice_fusion.13
  55.3 21.2 %collective-permute-done.18 = bf16[4,16,1024]{2,1,0:T(8,128)(2,1)S(1)} collective-permute-done((bf16[4,16,1024]{2,1,0:T(8,128)(2,1)S(1)}, bf16[4,16,1024]{2,1,0:T(8,128)(2,1)S(1)}, u32[]{:S(2)}, u32[]{:S(2)}) %collective-permute-start.18) | collective-permute-done | bytes 131104 | tf_op jit(solution)/shard_map/ppermute | solution.py:101
  78.0 0.7 constant_dynamic-update-slice_fusion.10
  78.7 3.1 %collective-permute-start.20 = (bf16[4,128,1024]{2,1,0:T(8,128)(2,1)S(1)}, bf16[4,128,1024]{2,1,0:T(8,128)(2,1)S(1)}, u32[]{:S(2)}, u32[]{:S(2)}) collective-permute-start(bf16[4,128,1024]{2,1,0:T(8,128)(2,1)S(1)} %get-tuple-element.40), channel_id=1, source_target_pairs={{0,3},{1,0},{2,1},{3,2},{4,7},{5,4},{6,5},{7,6},{8,11},{9,8},{10,9... | collective-permute-start | bytes 3145736 | tf_op jit(solution)/shard_map/ppermute | solution.py:101
  81.8 2.5 %fusion.51 = (bf16[4,128,2048]{2,1,0:T(8,128)(2,1)}, bf16[4,128,2048]{2,1,0:T(8,128)(2,1)}) fusion(bf16[8,128,2048]{2,1,0:T(8,128)(2,1)S(1)} %copy-done.3), kind=kLoop, calls=%fused_computation.152 | loop fusion | bytes 8388608 | tf_op jit(solution)/shard_map/slice | solution.py:212
  85.1 2.7 %collective-permute-start.7 = (bf16[4,64,1024]{2,1,0:T(8,128)(2,1)S(1)}, bf16[4,64,1024]{2,1,0:T(8,128)(2,1)S(1)}, u32[]{:S(2)}, u32[]{:S(2)}) collective-permute-start(bf16[4,64,1024]{2,1,0:T(8,128)(2,1)S(1)} %slice.189), channel_id=1, source_target_pairs={{0,12},{1,13},{2,14},{3,15},{4,0},{5,1},{6,2},{7,3},{8,4},{9,5},{1... | collective-permute-start | bytes 1572872 | tf_op jit(solution)/shard_map/ppermute | solution.py:101
  87.8 1.1 constant_dynamic-update-slice_fusion.9
  88.9 1.1 constant_dynamic-update-slice_fusion.8
  89.9 13.4 %collective-permute-done.21 = bf16[4,128,1024]{2,1,0:T(8,128)(2,1)S(1)} collective-permute-done((bf16[4,128,1024]{2,1,0:T(8,128)(2,1)S(1)}, bf16[4,128,1024]{2,1,0:T(8,128)(2,1)S(1)}, u32[]{:S(2)}, u32[]{:S(2)}) %collective-permute-start.21) | collective-permute-done | bytes 1048608 | tf_op jit(solution)/shard_map/ppermute | solution.py:101
  103.3 0.8 slice.202
  104.2 0.8 slice.203
  105.0 2.7 %collective-permute-start.23 = (bf16[4,64,1024]{2,1,0:T(8,128)(2,1)}, bf16[4,64,1024]{2,1,0:T(8,128)(2,1)}, u32[]{:S(2)}, u32[]{:S(2)}) collective-permute-start(bf16[4,64,1024]{2,1,0:T(8,128)(2,1)} %slice.203), channel_id=1, source_target_pairs={{0,3},{1,0},{2,1},{3,2},{4,7},{5,4},{6,5},{7,6},{8,11},{9,8},{10,9... | collective-permute-start | bytes 1572872 | tf_op jit(solution)/shard_map/ppermute | solution.py:101
  107.7 1.1 constant_dynamic-update-slice_fusion.18
  108.8 0.8 constant_dynamic-update-slice_fusion.7
  109.6 0.8 constant_dynamic-update-slice_fusion.6
  110.4 1.1 constant_dynamic-update-slice_fusion.5.q_ref
  111.5 7.7 %shard_map.73 = bf16[4,512,1024]{2,1,0:T(8,128)(2,1)} custom-call(s32[4]{0:T(128)} %get-tuple-element.54.n_live_ref, bf16[4,512,1024]{2,1,0:T(8,128)(2,1)} %constant_dynamic-update-slice_fusion.5.q_ref, bf16[4,128,2048]{2,1,0:T(8,128)(2,1)} %get-tuple-element.23.kv_ref, bf16[4,128,1024]{2,1,0:T(8,128)(2,1)} %get-tuple-element.21.vk_ref), custom_call_target="tpu_custom_call" | custom-call | flops 1073741824 | bytes 10485760 | tf_op jit(solution)/shard_map/pallas_call | solution.py:66
  119.2 2.2 %fusion.50 = (bf16[4,64,1024]{2,1,0:T(8,128)(2,1)}, bf16[4,64,1024]{2,1,0:T(8,128)(2,1)}) fusion(bf16[4,512,1024]{2,1,0:T(8,128)(2,1)} %shard_map.73), kind=kLoop, calls=%fused_computation.151 | loop fusion | bytes 2097152 | tf_op jit(solution)/shard_map/slice | solution.py:137
  121.5 1.5 collective-permute-start.8
  123.0 1.9 constant_dynamic-update-slice_fusion.17
  124.8 1.9 constant_dynamic-update-slice_fusion.16
  126.7 1.1 constant_dynamic-update-slice_fusion.15.q_ref
  127.8 7.8 %shard_map.74 = bf16[4,512,1024]{2,1,0:T(8,128)(2,1)} custom-call(s32[4]{0:T(128)} %get-tuple-element.55.n_live_ref, bf16[4,512,1024]{2,1,0:T(8,128)(2,1)} %constant_dynamic-update-slice_fusion.15.q_ref, bf16[4,128,2048]{2,1,0:T(8,128)(2,1)} %get-tuple-element.24.kv_ref, bf16[4,128,1024]{2,1,0:T(8,128)(2,1)} %get-tuple-element.22.vk_ref), custom_call_target="tpu_custom_call" | custom-call | flops 1073741824 | bytes 10485760 | tf_op jit(solution)/shard_map/pallas_call | solution.py:66
  135.6 1.5 fusion.52
  137.2 2.7 %collective-permute-start.26 = (bf16[4,64,1024]{2,1,0:T(8,128)(2,1)S(1)}, bf16[4,64,1024]{2,1,0:T(8,128)(2,1)S(1)}, u32[]{:S(2)}, u32[]{:S(2)}) collective-permute-start(bf16[4,64,1024]{2,1,0:T(8,128)(2,1)S(1)} %get-tuple-element.28), channel_id=1, source_target_pairs={{0,3},{1,0},{2,1},{3,2},{4,7},{5,4},{6,5},{7,6},{8,11},{9,8},{10,9... | collective-permute-start | bytes 1572872 | tf_op jit(solution)/shard_map/ppermute | solution.py:101
  139.9 2.4 %add_convert_fusion.3 = (bf16[4,128,1024]{2,1,0:T(8,128)(2,1)S(1)}, bf16[4,128,1024]{2,1,0:T(8,128)(2,1)S(1)}) fusion(bf16[4,512,1024]{2,1,0:T(8,128)(2,1)} %shard_map.73, bf16[4,64,1024]{2,1,0:T(8,128)(2,1)} %collective-permute-done.8, bf16[4,64,1024]{2,1,0:T(8,128)(2,1)} %collective-permute-done.10), kind=kLoop, calls=%fused_computation.16 | loop fusion | flops 4194304 | bytes 5242880 | tf_op jit(solution)/shard_map/convert_element_type | solution.py:142
  142.2 0.8 collective-permute-start.11
  143.0 0.8 collective-permute-start.9
  144.1 2.3 %collective-permute-done.24 = bf16[4,64,1024]{2,1,0:T(8,128)(2,1)S(1)} collective-permute-done((bf16[4,64,1024]{2,1,0:T(8,128)(2,1)S(1)}, bf16[4,64,1024]{2,1,0:T(8,128)(2,1)S(1)}, u32[]{:S(2)}, u32[]{:S(2)}) %collective-permute-start.24) | collective-permute-done | bytes 524320 | tf_op jit(solution)/shard_map/ppermute | solution.py:101
  147.2 2.7 %collective-permute-start.27 = (bf16[4,128,1024]{2,1,0:T(8,128)(2,1)S(1)}, bf16[4,128,1024]{2,1,0:T(8,128)(2,1)S(1)}, u32[]{:S(2)}, u32[]{:S(2)}) collective-permute-start(bf16[4,128,1024]{2,1,0:T(8,128)(2,1)S(1)} %get-tuple-element.26), channel_id=1, source_target_pairs={{0,3},{1,0},{2,1},{3,2},{4,7},{5,4},{6,5},{7,6},{8,11},{9,8},{10,9... | collective-permute-start | bytes 3145736 | tf_op jit(solution)/shard_map/ppermute | solution.py:101
  149.9 10.1 %collective-permute-done.11 = bf16[4,128,1024]{2,1,0:T(8,128)(2,1)S(1)} collective-permute-done((bf16[4,128,1024]{2,1,0:T(8,128)(2,1)S(1)}, bf16[4,128,1024]{2,1,0:T(8,128)(2,1)S(1)}, u32[]{:S(2)}, u32[]{:S(2)}) %collective-permute-start.11) | collective-permute-done | bytes 1048608 | tf_op jit(solution)/shard_map/ppermute | solution.py:101
  160.1 2.5 %collective-permute-done.9 = bf16[4,128,1024]{2,1,0:T(8,128)(2,1)S(1)} collective-permute-done((bf16[4,128,1024]{2,1,0:T(8,128)(2,1)S(1)}, bf16[4,128,1024]{2,1,0:T(8,128)(2,1)S(1)}, u32[]{:S(2)}, u32[]{:S(2)}) %collective-permute-start.9) | collective-permute-done | bytes 1048608 | tf_op jit(solution)/shard_map/ppermute | solution.py:101
  162.6 1.7 fusion.48
  164.4 2.7 %collective-permute-start.14 = (bf16[4,16,1024]{2,1,0:T(8,128)(2,1)S(1)}, bf16[4,16,1024]{2,1,0:T(8,128)(2,1)S(1)}, u32[]{:S(2)}, u32[]{:S(2)}) collective-permute-start(bf16[4,16,1024]{2,1,0:T(8,128)(2,1)S(1)} %get-tuple-element.34), channel_id=1, source_target_pairs={{0,3},{1,0},{2,1},{3,2},{4,7},{5,4},{6,5},{7,6},{8,11},{9,8},{10,9... | collective-permute-start | bytes 393224 | tf_op jit(solution)/shard_map/ppermute | solution.py:101
  167.1 0.8 collective-permute-done.25
  168.6 2.7 %collective-permute-start.30 = (bf16[4,16,1024]{2,1,0:T(8,128)(2,1)S(1)}, bf16[4,16,1024]{2,1,0:T(8,128)(2,1)S(1)}, u32[]{:S(2)}, u32[]{:S(2)}) collective-permute-start(bf16[4,16,1024]{2,1,0:T(8,128)(2,1)S(1)} %get-tuple-element.36), channel_id=1, source_target_pairs={{0,12},{1,13},{2,14},{3,15},{4,0},{5,1},{6,2},{7,3},{8,4},{9,5},{1... | collective-permute-start | bytes 393224 | tf_op jit(solution)/shard_map/ppermute | solution.py:101
  171.5 2.9 %collective-permute-start.15 = (bf16[4,32,1024]{2,1,0:T(8,128)(2,1)S(1)}, bf16[4,32,1024]{2,1,0:T(8,128)(2,1)S(1)}, u32[]{:S(2)}, u32[]{:S(2)}) collective-permute-start(bf16[4,32,1024]{2,1,0:T(8,128)(2,1)S(1)} %get-tuple-element.30), channel_id=1, source_target_pairs={{0,3},{1,0},{2,1},{3,2},{4,7},{5,4},{6,5},{7,6},{8,11},{9,8},{10,9... | collective-permute-start | bytes 786440 | tf_op jit(solution)/shard_map/ppermute | solution.py:101
  174.7 2.7 %collective-permute-start.31 = (bf16[4,32,1024]{2,1,0:T(8,128)(2,1)S(1)}, bf16[4,32,1024]{2,1,0:T(8,128)(2,1)S(1)}, u32[]{:S(2)}, u32[]{:S(2)}) collective-permute-start(bf16[4,32,1024]{2,1,0:T(8,128)(2,1)S(1)} %get-tuple-element.32), channel_id=1, source_target_pairs={{0,12},{1,13},{2,14},{3,15},{4,0},{5,1},{6,2},{7,3},{8,4},{9,5},{1... | collective-permute-start | bytes 786440 | tf_op jit(solution)/shard_map/ppermute | solution.py:101
  177.3 3.9 %collective-permute-done.13 = bf16[4,32,1024]{2,1,0:T(8,128)(2,1)S(1)} collective-permute-done((bf16[4,32,1024]{2,1,0:T(8,128)(2,1)S(1)}, bf16[4,32,1024]{2,1,0:T(8,128)(2,1)S(1)}, u32[]{:S(2)}, u32[]{:S(2)}) %collective-permute-start.13) | collective-permute-done | bytes 262176 | tf_op jit(solution)/shard_map/ppermute | solution.py:101
  181.5 1.4 gather_fusion.6
  182.9 1.9 broadcast_select_fusion.1
  184.9 17.8 %all-to-all-start.1 = ((bf16[8,32,1024]{2,1,0:T(8,128)(2,1)}), bf16[8,32,1024]{2,1,0:T(8,128)(2,1)}, u32[]{:S(2)}, u32[]{:S(2)}) async-start(bf16[8,32,1024]{2,1,0:T(8,128)(2,1)} %broadcast_select_fusion.1), calls=%async_computation.1 | async-start | bytes 1048576 | tf_op jit(solution)/shard_map/all_to_all | solution.py:218
  202.7 3.4 %multiply_bitcast_fusion = f32[32,8,1024]{2,1,0:T(8,128)} fusion(bf16[1024,2048]{1,0:T(8,128)(2,1)} %param.12, bf16[32,8,1024]{2,1,0:T(8,128)(2,1)S(1)} %copy-done.4, f32[32,8]{1,0:T(8,128)S(1)} %copy.37, f32[32,8]{1,0:T(8,128)S(1)} %copy.35), kind=kOutput, calls=%fused_computation.37 | convolution fusion | flops 538968064 | bytes 3672064 | tf_op jit(solution)/shard_map/dot_general | solution.py:221
  206.1 6.0 %all-to-all-done.1 = bf16[8,32,1024]{2,1,0:T(8,128)(2,1)} async-done(((bf16[8,32,1024]{2,1,0:T(8,128)(2,1)}), bf16[8,32,1024]{2,1,0:T(8,128)(2,1)}, u32[]{:S(2)}, u32[]{:S(2)}) %all-to-all-start.1) | async-done | bytes 524320 | tf_op jit(solution)/shard_map/all_to_all | solution.py:218
  212.2 1.6 gather_fusion.7
  214.2 1.9 fusion.14
  216.1 1.6 fusion.7
  (113 shorter events, 11.2 us)
Async XLA Ops:
  0.0 216.1 %copy-start = (bf16[1024,1024]{1,0:T(8,128)(2,1)S(1)}, bf16[1024,1024]{1,0:T(8,128)(2,1)}, u32[]{:S(2)}) copy-start(bf16[1024,1024]{1,0:T(8,128)(2,1)} %param.13) | copy-start | bytes 6291460
  9.6 7.8 %copy-start.1 = (s32[64]{0:T(128)S(1)}, s32[64]{0:T(128)}, u32[]{:S(2)}) copy-start(s32[64]{0:T(128)} %param.11) | copy-start | bytes 772
  11.4 15.3 %all-to-all-start = ((bf16[8,32,1024]{2,1,0:T(8,128)(2,1)}), bf16[8,32,1024]{2,1,0:T(8,128)(2,1)S(1)}, u32[]{:S(2)}, u32[]{:S(2)}) async-start(bf16[8,32,1024]{2,1,0:T(8,128)(2,1)} %broadcast_select_fusion), calls=%async_computation | async-start | bytes 1048576 | tf_op jit(solution)/shard_map/all_to_all | solution.py:201
  27.4 8.2 %collective-permute-start.1 = (bf16[4,32,1024]{2,1,0:T(8,128)(2,1)S(1)}, bf16[4,32,1024]{2,1,0:T(8,128)(2,1)S(1)}, u32[]{:S(2)}, u32[]{:S(2)}) collective-permute-start(bf16[4,32,1024]{2,1,0:T(8,128)(2,1)S(1)} %get-tuple-element.39), channel_id=1, source_target_pairs={{0,1},{1,2},{2,3},{3,0},{4,5},{5,6},{6,7},{7,4},{8,9},{9,10},{10,1... | collective-permute-start | bytes 786440 | tf_op jit(solution)/shard_map/ppermute | solution.py:101
  28.7 7.0 %collective-permute-start = (bf16[4,32,1024]{2,1,0:T(8,128)(2,1)S(1)}, bf16[4,32,1024]{2,1,0:T(8,128)(2,1)S(1)}, u32[]{:S(2)}, u32[]{:S(2)}) collective-permute-start(bf16[4,32,1024]{2,1,0:T(8,128)(2,1)S(1)} %get-tuple-element.39), channel_id=1, source_target_pairs={{0,3},{1,0},{2,1},{3,2},{4,7},{5,4},{6,5},{7,6},{8,11},{9,8},{10,9... | collective-permute-start | bytes 786440 | tf_op jit(solution)/shard_map/ppermute | solution.py:101
  35.6 5.1 %collective-permute-start.2 = (bf16[4,16,1024]{2,1,0:T(8,128)(2,1)S(1)}, bf16[4,16,1024]{2,1,0:T(8,128)(2,1)S(1)}, u32[]{:S(2)}, u32[]{:S(2)}) collective-permute-start(bf16[4,16,1024]{2,1,0:T(8,128)(2,1)S(1)} %slice.185), channel_id=1, source_target_pairs={{0,1},{1,2},{2,3},{3,0},{4,5},{5,6},{6,7},{7,4},{8,9},{9,10},{10,1... | collective-permute-start | bytes 393224 | tf_op jit(solution)/shard_map/ppermute | solution.py:101
  35.8 4.9 %collective-permute-start.3 = (bf16[4,16,1024]{2,1,0:T(8,128)(2,1)S(1)}, bf16[4,16,1024]{2,1,0:T(8,128)(2,1)S(1)}, u32[]{:S(2)}, u32[]{:S(2)}) collective-permute-start(bf16[4,16,1024]{2,1,0:T(8,128)(2,1)S(1)} %slice.186), channel_id=1, source_target_pairs={{0,3},{1,0},{2,1},{3,2},{4,7},{5,4},{6,5},{7,6},{8,11},{9,8},{10,9... | collective-permute-start | bytes 393224 | tf_op jit(solution)/shard_map/ppermute | solution.py:101
  40.7 41.1 %copy-start.3 = (bf16[8,128,2048]{2,1,0:T(8,128)(2,1)S(1)}, bf16[8,128,2048]{2,1,0:T(8,128)(2,1)}, u32[]{:S(2)}) copy-start(bf16[8,128,2048]{2,1,0:T(8,128)(2,1)} %param.8) | copy-start | bytes 12582916
  40.8 11.1 %collective-permute-start.16 = (bf16[4,32,1024]{2,1,0:T(8,128)(2,1)S(1)}, bf16[4,32,1024]{2,1,0:T(8,128)(2,1)S(1)}, u32[]{:S(2)}, u32[]{:S(2)}) collective-permute-start(bf16[4,32,1024]{2,1,0:T(8,128)(2,1)S(1)} %get-tuple-element.8), channel_id=1, source_target_pairs={{0,12},{1,13},{2,14},{3,15},{4,0},{5,1},{6,2},{7,3},{8,4},{9,5},{1... | collective-permute-start | bytes 786440 | tf_op jit(solution)/shard_map/ppermute | solution.py:101
  44.6 6.4 %collective-permute-start.17 = (bf16[4,32,1024]{2,1,0:T(8,128)(2,1)S(1)}, bf16[4,32,1024]{2,1,0:T(8,128)(2,1)S(1)}, u32[]{:S(2)}, u32[]{:S(2)}) collective-permute-start(bf16[4,32,1024]{2,1,0:T(8,128)(2,1)S(1)} %get-tuple-element.8), channel_id=1, source_target_pairs={{0,4},{1,5},{2,6},{3,7},{4,8},{5,9},{6,10},{7,11},{8,12},{9,13},{1... | collective-permute-start | bytes 786440 | tf_op jit(solution)/shard_map/ppermute | solution.py:101
  47.9 37.1 %collective-permute-start.4 = (bf16[4,128,1024]{2,1,0:T(8,128)(2,1)S(1)}, bf16[4,128,1024]{2,1,0:T(8,128)(2,1)S(1)}, u32[]{:S(2)}, u32[]{:S(2)}) collective-permute-start(bf16[4,128,1024]{2,1,0:T(8,128)(2,1)S(1)} %constant_dynamic-update-slice_fusion), channel_id=1, source_target_pairs={{0,12},{1,13},{2,14},{3,15},{4,0},{5,1},{6,2},{7,3},{8,4},{9,5},{1... | collective-permute-start | bytes 3145736 | tf_op jit(solution)/shard_map/ppermute | solution.py:101
  50.6 33.7 %collective-permute-start.5 = (bf16[4,128,1024]{2,1,0:T(8,128)(2,1)S(1)}, bf16[4,128,1024]{2,1,0:T(8,128)(2,1)S(1)}, u32[]{:S(2)}, u32[]{:S(2)}) collective-permute-start(bf16[4,128,1024]{2,1,0:T(8,128)(2,1)S(1)} %constant_dynamic-update-slice_fusion), channel_id=1, source_target_pairs={{0,4},{1,5},{2,6},{3,7},{4,8},{5,9},{6,10},{7,11},{8,12},{9,13},{1... | collective-permute-start | bytes 3145736 | tf_op jit(solution)/shard_map/ppermute | solution.py:101
  51.0 25.5 %collective-permute-start.18 = (bf16[4,16,1024]{2,1,0:T(8,128)(2,1)S(1)}, bf16[4,16,1024]{2,1,0:T(8,128)(2,1)S(1)}, u32[]{:S(2)}, u32[]{:S(2)}) collective-permute-start(bf16[4,16,1024]{2,1,0:T(8,128)(2,1)S(1)} %slice.200), channel_id=1, source_target_pairs={{0,4},{1,5},{2,6},{3,7},{4,8},{5,9},{6,10},{7,11},{8,12},{9,13},{1... | collective-permute-start | bytes 393224 | tf_op jit(solution)/shard_map/ppermute | solution.py:101
  51.9 25.4 %collective-permute-start.19 = (bf16[4,16,1024]{2,1,0:T(8,128)(2,1)S(1)}, bf16[4,16,1024]{2,1,0:T(8,128)(2,1)S(1)}, u32[]{:S(2)}, u32[]{:S(2)}) collective-permute-start(bf16[4,16,1024]{2,1,0:T(8,128)(2,1)S(1)} %slice.201), channel_id=1, source_target_pairs={{0,12},{1,13},{2,14},{3,15},{4,0},{5,1},{6,2},{7,3},{8,4},{9,5},{1... | collective-permute-start | bytes 393224 | tf_op jit(solution)/shard_map/ppermute | solution.py:101
  78.7 25.4 %collective-permute-start.20 = (bf16[4,128,1024]{2,1,0:T(8,128)(2,1)S(1)}, bf16[4,128,1024]{2,1,0:T(8,128)(2,1)S(1)}, u32[]{:S(2)}, u32[]{:S(2)}) collective-permute-start(bf16[4,128,1024]{2,1,0:T(8,128)(2,1)S(1)} %get-tuple-element.40), channel_id=1, source_target_pairs={{0,3},{1,0},{2,1},{3,2},{4,7},{5,4},{6,5},{7,6},{8,11},{9,8},{10,9... | collective-permute-start | bytes 3145736 | tf_op jit(solution)/shard_map/ppermute | solution.py:101
  81.8 21.5 %collective-permute-start.21 = (bf16[4,128,1024]{2,1,0:T(8,128)(2,1)S(1)}, bf16[4,128,1024]{2,1,0:T(8,128)(2,1)S(1)}, u32[]{:S(2)}, u32[]{:S(2)}) collective-permute-start(bf16[4,128,1024]{2,1,0:T(8,128)(2,1)S(1)} %get-tuple-element.40), channel_id=1, source_target_pairs={{0,1},{1,2},{2,3},{3,0},{4,5},{5,6},{6,7},{7,4},{8,9},{9,10},{10,1... | collective-permute-start | bytes 3145736 | tf_op jit(solution)/shard_map/ppermute | solution.py:101
  84.4 24.4 %collective-permute-start.6 = (bf16[4,64,1024]{2,1,0:T(8,128)(2,1)S(1)}, bf16[4,64,1024]{2,1,0:T(8,128)(2,1)S(1)}, u32[]{:S(2)}, u32[]{:S(2)}) collective-permute-start(bf16[4,64,1024]{2,1,0:T(8,128)(2,1)S(1)} %slice.188), channel_id=1, source_target_pairs={{0,4},{1,5},{2,6},{3,7},{4,8},{5,9},{6,10},{7,11},{8,12},{9,13},{1... | collective-permute-start | bytes 1572872 | tf_op jit(solution)/shard_map/ppermute | solution.py:101
  85.1 24.5 %collective-permute-start.7 = (bf16[4,64,1024]{2,1,0:T(8,128)(2,1)S(1)}, bf16[4,64,1024]{2,1,0:T(8,128)(2,1)S(1)}, u32[]{:S(2)}, u32[]{:S(2)}) collective-permute-start(bf16[4,64,1024]{2,1,0:T(8,128)(2,1)S(1)} %slice.189), channel_id=1, source_target_pairs={{0,12},{1,13},{2,14},{3,15},{4,0},{5,1},{6,2},{7,3},{8,4},{9,5},{1... | collective-permute-start | bytes 1572872 | tf_op jit(solution)/shard_map/ppermute | solution.py:101
  104.2 18.8 %collective-permute-start.22 = (bf16[4,64,1024]{2,1,0:T(8,128)(2,1)}, bf16[4,64,1024]{2,1,0:T(8,128)(2,1)}, u32[]{:S(2)}, u32[]{:S(2)}) collective-permute-start(bf16[4,64,1024]{2,1,0:T(8,128)(2,1)} %slice.202), channel_id=1, source_target_pairs={{0,1},{1,2},{2,3},{3,0},{4,5},{5,6},{6,7},{7,4},{8,9},{9,10},{10,1... | collective-permute-start | bytes 1572872 | tf_op jit(solution)/shard_map/ppermute | solution.py:101
  105.0 19.8 %collective-permute-start.23 = (bf16[4,64,1024]{2,1,0:T(8,128)(2,1)}, bf16[4,64,1024]{2,1,0:T(8,128)(2,1)}, u32[]{:S(2)}, u32[]{:S(2)}) collective-permute-start(bf16[4,64,1024]{2,1,0:T(8,128)(2,1)} %slice.203), channel_id=1, source_target_pairs={{0,3},{1,0},{2,1},{3,2},{4,7},{5,4},{6,5},{7,6},{8,11},{9,8},{10,9... | collective-permute-start | bytes 1572872 | tf_op jit(solution)/shard_map/ppermute | solution.py:101
  121.5 18.4 %collective-permute-start.10 = (bf16[4,64,1024]{2,1,0:T(8,128)(2,1)}, bf16[4,64,1024]{2,1,0:T(8,128)(2,1)}, u32[]{:S(2)}, u32[]{:S(2)}) collective-permute-start(bf16[4,64,1024]{2,1,0:T(8,128)(2,1)} %get-tuple-element.20), channel_id=1, source_target_pairs={{0,12},{1,13},{2,14},{3,15},{4,0},{5,1},{6,2},{7,3},{8,4},{9,5},{1... | collective-permute-start | bytes 1572872 | tf_op jit(solution)/shard_map/ppermute | solution.py:101
  121.5 18.4 %collective-permute-start.8 = (bf16[4,64,1024]{2,1,0:T(8,128)(2,1)}, bf16[4,64,1024]{2,1,0:T(8,128)(2,1)}, u32[]{:S(2)}, u32[]{:S(2)}) collective-permute-start(bf16[4,64,1024]{2,1,0:T(8,128)(2,1)} %get-tuple-element.19), channel_id=1, source_target_pairs={{0,4},{1,5},{2,6},{3,7},{4,8},{5,9},{6,10},{7,11},{8,12},{9,13},{1... | collective-permute-start | bytes 1572872 | tf_op jit(solution)/shard_map/ppermute | solution.py:101
  135.6 10.8 %copy-start.2 = (bf16[4,512,1024]{2,1,0:T(8,128)(2,1)S(1)}, bf16[4,512,1024]{2,1,0:T(8,128)(2,1)}, u32[]{:S(2)}) copy-start(bf16[4,512,1024]{2,1,0:T(8,128)(2,1)} %shard_map.74) | copy-start | bytes 12582916
  137.1 9.3 %collective-permute-start.24 = (bf16[4,64,1024]{2,1,0:T(8,128)(2,1)S(1)}, bf16[4,64,1024]{2,1,0:T(8,128)(2,1)S(1)}, u32[]{:S(2)}, u32[]{:S(2)}) collective-permute-start(bf16[4,64,1024]{2,1,0:T(8,128)(2,1)S(1)} %get-tuple-element.27), channel_id=1, source_target_pairs={{0,1},{1,2},{2,3},{3,0},{4,5},{5,6},{6,7},{7,4},{8,9},{9,10},{10,1... | collective-permute-start | bytes 1572872 | tf_op jit(solution)/shard_map/ppermute | solution.py:101
  137.2 9.2 %collective-permute-start.26 = (bf16[4,64,1024]{2,1,0:T(8,128)(2,1)S(1)}, bf16[4,64,1024]{2,1,0:T(8,128)(2,1)S(1)}, u32[]{:S(2)}, u32[]{:S(2)}) collective-permute-start(bf16[4,64,1024]{2,1,0:T(8,128)(2,1)S(1)} %get-tuple-element.28), channel_id=1, source_target_pairs={{0,3},{1,0},{2,1},{3,2},{4,7},{5,4},{6,5},{7,6},{8,11},{9,8},{10,9... | collective-permute-start | bytes 1572872 | tf_op jit(solution)/shard_map/ppermute | solution.py:101
  142.2 17.8 %collective-permute-start.11 = (bf16[4,128,1024]{2,1,0:T(8,128)(2,1)S(1)}, bf16[4,128,1024]{2,1,0:T(8,128)(2,1)S(1)}, u32[]{:S(2)}, u32[]{:S(2)}) collective-permute-start(bf16[4,128,1024]{2,1,0:T(8,128)(2,1)S(1)} %get-tuple-element.18), channel_id=1, source_target_pairs={{0,12},{1,13},{2,14},{3,15},{4,0},{5,1},{6,2},{7,3},{8,4},{9,5},{1... | collective-permute-start | bytes 3145736 | tf_op jit(solution)/shard_map/ppermute | solution.py:101
  143.0 19.6 %collective-permute-start.9 = (bf16[4,128,1024]{2,1,0:T(8,128)(2,1)S(1)}, bf16[4,128,1024]{2,1,0:T(8,128)(2,1)S(1)}, u32[]{:S(2)}, u32[]{:S(2)}) collective-permute-start(bf16[4,128,1024]{2,1,0:T(8,128)(2,1)S(1)} %get-tuple-element.17), channel_id=1, source_target_pairs={{0,4},{1,5},{2,6},{3,7},{4,8},{5,9},{6,10},{7,11},{8,12},{9,13},{1... | collective-permute-start | bytes 3145736 | tf_op jit(solution)/shard_map/ppermute | solution.py:101
  147.1 20.7 %collective-permute-start.25 = (bf16[4,128,1024]{2,1,0:T(8,128)(2,1)S(1)}, bf16[4,128,1024]{2,1,0:T(8,128)(2,1)S(1)}, u32[]{:S(2)}, u32[]{:S(2)}) collective-permute-start(bf16[4,128,1024]{2,1,0:T(8,128)(2,1)S(1)} %get-tuple-element.25), channel_id=1, source_target_pairs={{0,1},{1,2},{2,3},{3,0},{4,5},{5,6},{6,7},{7,4},{8,9},{9,10},{10,1... | collective-permute-start | bytes 3145736 | tf_op jit(solution)/shard_map/ppermute | solution.py:101
  147.2 20.7 %collective-permute-start.27 = (bf16[4,128,1024]{2,1,0:T(8,128)(2,1)S(1)}, bf16[4,128,1024]{2,1,0:T(8,128)(2,1)S(1)}, u32[]{:S(2)}, u32[]{:S(2)}) collective-permute-start(bf16[4,128,1024]{2,1,0:T(8,128)(2,1)S(1)} %get-tuple-element.26), channel_id=1, source_target_pairs={{0,3},{1,0},{2,1},{3,2},{4,7},{5,4},{6,5},{7,6},{8,11},{9,8},{10,9... | collective-permute-start | bytes 3145736 | tf_op jit(solution)/shard_map/ppermute | solution.py:101
  164.3 7.0 %collective-permute-start.12 = (bf16[4,16,1024]{2,1,0:T(8,128)(2,1)S(1)}, bf16[4,16,1024]{2,1,0:T(8,128)(2,1)S(1)}, u32[]{:S(2)}, u32[]{:S(2)}) collective-permute-start(bf16[4,16,1024]{2,1,0:T(8,128)(2,1)S(1)} %get-tuple-element.33), channel_id=1, source_target_pairs={{0,1},{1,2},{2,3},{3,0},{4,5},{5,6},{6,7},{7,4},{8,9},{9,10},{10,1... | collective-permute-start | bytes 393224 | tf_op jit(solution)/shard_map/ppermute | solution.py:101
  164.4 6.9 %collective-permute-start.14 = (bf16[4,16,1024]{2,1,0:T(8,128)(2,1)S(1)}, bf16[4,16,1024]{2,1,0:T(8,128)(2,1)S(1)}, u32[]{:S(2)}, u32[]{:S(2)}) collective-permute-start(bf16[4,16,1024]{2,1,0:T(8,128)(2,1)S(1)} %get-tuple-element.34), channel_id=1, source_target_pairs={{0,3},{1,0},{2,1},{3,2},{4,7},{5,4},{6,5},{7,6},{8,11},{9,8},{10,9... | collective-permute-start | bytes 393224 | tf_op jit(solution)/shard_map/ppermute | solution.py:101
  168.5 5.9 %collective-permute-start.28 = (bf16[4,16,1024]{2,1,0:T(8,128)(2,1)S(1)}, bf16[4,16,1024]{2,1,0:T(8,128)(2,1)S(1)}, u32[]{:S(2)}, u32[]{:S(2)}) collective-permute-start(bf16[4,16,1024]{2,1,0:T(8,128)(2,1)S(1)} %get-tuple-element.35), channel_id=1, source_target_pairs={{0,4},{1,5},{2,6},{3,7},{4,8},{5,9},{6,10},{7,11},{8,12},{9,13},{1... | collective-permute-start | bytes 393224 | tf_op jit(solution)/shard_map/ppermute | solution.py:101
  168.6 5.8 %collective-permute-start.30 = (bf16[4,16,1024]{2,1,0:T(8,128)(2,1)S(1)}, bf16[4,16,1024]{2,1,0:T(8,128)(2,1)S(1)}, u32[]{:S(2)}, u32[]{:S(2)}) collective-permute-start(bf16[4,16,1024]{2,1,0:T(8,128)(2,1)S(1)} %get-tuple-element.36), channel_id=1, source_target_pairs={{0,12},{1,13},{2,14},{3,15},{4,0},{5,1},{6,2},{7,3},{8,4},{9,5},{1... | collective-permute-start | bytes 393224 | tf_op jit(solution)/shard_map/ppermute | solution.py:101
  171.4 9.8 %collective-permute-start.13 = (bf16[4,32,1024]{2,1,0:T(8,128)(2,1)S(1)}, bf16[4,32,1024]{2,1,0:T(8,128)(2,1)S(1)}, u32[]{:S(2)}, u32[]{:S(2)}) collective-permute-start(bf16[4,32,1024]{2,1,0:T(8,128)(2,1)S(1)} %get-tuple-element.29), channel_id=1, source_target_pairs={{0,1},{1,2},{2,3},{3,0},{4,5},{5,6},{6,7},{7,4},{8,9},{9,10},{10,1... | collective-permute-start | bytes 786440 | tf_op jit(solution)/shard_map/ppermute | solution.py:101
  171.5 9.7 %collective-permute-start.15 = (bf16[4,32,1024]{2,1,0:T(8,128)(2,1)S(1)}, bf16[4,32,1024]{2,1,0:T(8,128)(2,1)S(1)}, u32[]{:S(2)}, u32[]{:S(2)}) collective-permute-start(bf16[4,32,1024]{2,1,0:T(8,128)(2,1)S(1)} %get-tuple-element.30), channel_id=1, source_target_pairs={{0,3},{1,0},{2,1},{3,2},{4,7},{5,4},{6,5},{7,6},{8,11},{9,8},{10,9... | collective-permute-start | bytes 786440 | tf_op jit(solution)/shard_map/ppermute | solution.py:101
  174.5 28.2 %copy-start.4 = (bf16[32,8,1024]{2,1,0:T(8,128)(2,1)S(1)}, bf16[32,8,1024]{2,1,0:T(8,128)(2,1)}, u32[]{:S(2)}) copy-start(bf16[32,8,1024]{2,1,0:T(8,128)(2,1)} %param.7) | copy-start | bytes 1572868
  174.6 6.8 %collective-permute-start.29 = (bf16[4,32,1024]{2,1,0:T(8,128)(2,1)S(1)}, bf16[4,32,1024]{2,1,0:T(8,128)(2,1)S(1)}, u32[]{:S(2)}, u32[]{:S(2)}) collective-permute-start(bf16[4,32,1024]{2,1,0:T(8,128)(2,1)S(1)} %get-tuple-element.31), channel_id=1, source_target_pairs={{0,4},{1,5},{2,6},{3,7},{4,8},{5,9},{6,10},{7,11},{8,12},{9,13},{1... | collective-permute-start | bytes 786440 | tf_op jit(solution)/shard_map/ppermute | solution.py:101
  174.7 6.7 %collective-permute-start.31 = (bf16[4,32,1024]{2,1,0:T(8,128)(2,1)S(1)}, bf16[4,32,1024]{2,1,0:T(8,128)(2,1)S(1)}, u32[]{:S(2)}, u32[]{:S(2)}) collective-permute-start(bf16[4,32,1024]{2,1,0:T(8,128)(2,1)S(1)} %get-tuple-element.32), channel_id=1, source_target_pairs={{0,12},{1,13},{2,14},{3,15},{4,0},{5,1},{6,2},{7,3},{8,4},{9,5},{1... | collective-permute-start | bytes 786440 | tf_op jit(solution)/shard_map/ppermute | solution.py:101
  184.9 27.3 %all-to-all-start.1 = ((bf16[8,32,1024]{2,1,0:T(8,128)(2,1)}), bf16[8,32,1024]{2,1,0:T(8,128)(2,1)}, u32[]{:S(2)}, u32[]{:S(2)}) async-start(bf16[8,32,1024]{2,1,0:T(8,128)(2,1)} %broadcast_select_fusion.1), calls=%async_computation.1 | async-start | bytes 1048576 | tf_op jit(solution)/shard_map/all_to_all | solution.py:218

commit v13 on v9

--- a/solution.py
+++ b/solution.py
@@ -33,55 +33,65 @@
     return (target, arrival, slot_of_pos)
 
 
-def attend_kernel(n_live_ref, q_ref, kv_ref, vk_ref, o_ref, *, heads, head_dim):
+def attend_kernel(n_live_ref, *refs, sets, heads, head_dim):
     row = pl.program_id(0)
-
-    @pl.when(n_live_ref[row] <= 0)
-    def _():
-        o_ref[...] = jnp.zeros(o_ref.shape, o_ref.dtype)
-
-    @pl.when(n_live_ref[row] > 0)
-    def _():
-        for h in range(heads):
-            lo = h * head_dim
-            q = q_ref[0, :, lo:lo + head_dim]
-            k = kv_ref[0, :, lo:lo + head_dim]
-            v = vk_ref[0, :, lo:lo + head_dim]
-            t = lax.dot_general(q, k, (((1,), (1,)), ((), ())), preferred_element_type=jnp.float32)
-            w = (t * (1.0 + jnp.tanh(t))).astype(jnp.bfloat16)
-            o = jnp.dot(w, v, preferred_element_type=jnp.float32)
-            o_ref[0, :, lo:lo + head_dim] = o.astype(o_ref.dtype)
-
-
-def attend_local(queries, piece, live, first_event, heads, out_dtype):
-    rows, cands, width = queries.shape
-    count = piece.shape[1]
+    rows = pl.num_programs(0)
+    for j in range(sets):
+        q_ref, kv_ref, vk_ref = refs[3 * j:3 * j + 3]
+        o_ref = refs[3 * sets + j]
+        live_here = n_live_ref[j * rows + row] > 0
+
+        @pl.when(jnp.logical_not(live_here))
+        def _():
+            o_ref[...] = jnp.zeros(o_ref.shape, o_ref.dtype)
+
+        @pl.when(live_here)
+        def _():
+            for h in range(heads):
+                lo = h * head_dim
+                q = q_ref[0, :, lo:lo + head_dim]
+                k = kv_ref[0, :, lo:lo + head_dim]
+                v = vk_ref[0, :, lo:lo + head_dim]
+                t = lax.dot_general(q, k, (((1,), (1,)), ((), ())), preferred_element_type=jnp.float32)
+                w = (t * (1.0 + jnp.tanh(t))).astype(jnp.bfloat16)
+                o = jnp.dot(w, v, preferred_element_type=jnp.float32)
+                o_ref[0, :, lo:lo + head_dim] = o.astype(o_ref.dtype)
+
+
+def attend_local(q_sets, kv_sets, live_sets, first_event, heads, out_dtype):
+    rows, cands, width = q_sets[0].shape
+    count = kv_sets[0].shape[1]
     head_dim = width // heads
     events = (first_event + jnp.arange(count)).astype(jnp.float32)
-    keep = (events[None, :] < live[:, None]).astype(jnp.float32) / live[:, None]
-    values = (piece[:, :, width:].astype(jnp.float32) * keep[:, :, None]).astype(jnp.bfloat16)
-    n_live = jnp.clip(live.astype(jnp.int32) - first_event, 0, count).astype(jnp.int32)
-    kernel = functools.partial(attend_kernel, heads=heads, head_dim=head_dim)
-    flops = 4 * rows * cands * count * width
+    operands, n_live = [], []
+    for queries, piece, live in zip(q_sets, kv_sets, live_sets):
+        keep = (events[None, :] < live[:, None]).astype(jnp.float32) / live[:, None]
+        values = (piece[:, :, width:].astype(jnp.float32) * keep[:, :, None]).astype(jnp.bfloat16)
+        operands += [queries, piece, values]
+        n_live.append(jnp.clip(live.astype(jnp.int32) - first_event, 0, count).astype(jnp.int32))
+    sets = len(q_sets)
+    kernel = functools.partial(attend_kernel, sets=sets, heads=heads, head_dim=head_dim)
+    flops = 4 * sets * rows * cands * count * width
+    set_specs = [
+        pl.BlockSpec((1, cands, width), lambda r, n: (r, 0, 0)),
+        pl.BlockSpec((1, count, width), lambda r, n: (r, 0, 0)),
+        pl.BlockSpec((1, count, width), lambda r, n: (r, 0, 0)),
+    ]
     return pl.pallas_call(
         kernel,
-        out_shape=jax.ShapeDtypeStruct((rows, cands, width), out_dtype),
+        out_shape=[jax.ShapeDtypeStruct((rows, cands, width), out_dtype) for _ in range(sets)],
         grid_spec=pltpu.PrefetchScalarGridSpec(
             num_scalar_prefetch=1,
             grid=(rows,),
-            in_specs=[
-                pl.BlockSpec((1, cands, width), lambda r, n: (r, 0, 0)),
-                pl.BlockSpec((1, count, width), lambda r, n: (r, 0, 0)),
-                pl.BlockSpec((1, count, width), lambda r, n: (r, 0, 0)),
-            ],
-            out_specs=pl.BlockSpec((1, cands, width), lambda r, n: (r, 0, 0)),
+            in_specs=set_specs * sets,
+            out_specs=[pl.BlockSpec((1, cands, width), lambda r, n: (r, 0, 0)) for _ in range(sets)],
         ),
         cost_estimate=pl.CostEstimate(
             flops=flops,
-            transcendentals=rows * cands * count * heads,
-            bytes_accessed=rows * (cands * width * 4 + count * width * 4),
+            transcendentals=sets * rows * cands * count * heads,
+            bytes_accessed=sets * rows * (cands * width * 4 + count * width * 4),
         ),
-    )(n_live, queries, piece, values)
+    )(jnp.concatenate(n_live), *operands)
 
 
 def shift_perm(grid, axis, shift):
@@ -202,13 +212,16 @@
     q_rows = q_in[row_index]
     split = per_group // 2
     halves = ((slice(0, split), (0, 1)), (slice(split, per_group), (1, 0)))
-    sums = []
-    for rows_of, order in halves:
-        q_all = torus_gather(q_rows[rows_of], grid, order)
-        partial = attend_local(
-            q_all, kv_cache[rows_of], row_live[rows_of], member_now * count, HEADS, jnp.bfloat16
-        )
-        sums.append(torus_reduce(partial, grid, order))
+    q_sets = [torus_gather(q_rows[rows_of], grid, order) for rows_of, order in halves]
+    partials = attend_local(
+        q_sets,
+        [kv_cache[rows_of] for rows_of, _ in halves],
+        [row_live[rows_of] for rows_of, _ in halves],
+        member_now * count,
+        HEADS,
+        jnp.bfloat16,
+    )
+    sums = [torus_reduce(partial, grid, order) for partial, (_, order) in zip(partials, halves)]
     summed = jnp.concatenate(sums, axis=0).astype(jnp.bfloat16)
 
     a_out = jnp.where(filled[:, None, None], summed[chosen], jnp.zeros((), summed.dtype))

time: 192 us -> 190 us (0.990)
  waiting for transfers between devices: 52.5 us -> 58.8 us
  local copies, waits for them, and re-layouts: 32.3 us -> 27.7 us
  Pallas kernels: 15.5 us -> 12.5 us
  other arithmetic: 18 us -> 15.2 us
  starting transfers between devices: 64.5 us -> 66.5 us
    ppermute x32, waiting for transfers between devices: 37.9 us -> 44.2 us  [send(): return lax.ppermute(value, 'member', shift_perm(grid, axis, shift))]
    pallas_call x2 -> x1, Pallas kernels: 15.5 us -> 12.5 us  [attend_local(): pl.pallas_call(kernel, out_shape=[jax.ShapeDtypeStruct((rows, cands, widt...]
    unnamed x23 -> x25, local copies, waits for them, and re-layouts: 12.7 us -> 10.6 us
  transfers between devices with their start and end apart: 34 -> 34, of which waited for: 11 -> 11; matrix products, arithmetic and copies ran while one was open for 19% -> 13% of each run, Pallas kernels for 8% -> 0%
where the time goes in v13:
time: 190 us; the launch traced here: 189 us
  starting transfers between devices  66.5 us (35%)
  waiting for transfers between devices  58.8 us (31%)
  local copies, waits for them, and re-layouts  27.7 us (15%)
  other arithmetic  15.2 us (8%)
  Pallas kernels  12.5 us (7%)
  matrix products  7.73 us (4%)
    ppermute x32, waiting for transfers between devices, send(): return lax.ppermute(value, 'member', shift_perm(grid, axis, shift))  44.2 us
    ppermute x32, starting transfers between devices, send(): return lax.ppermute(value, 'member', shift_perm(grid, axis, shift))  43.3 us
    all_to_all x1, starting transfers between devices, on_device(): lax.all_to_all(a_out, 'group', split_axis=0, concat_axis=0, tiled=True)  17.2 us
    pallas_call x1, Pallas kernels, attend_local(): pl.pallas_call(kernel, out_shape=[jax.ShapeDtypeStruct((rows, cands, widt...  12.5 us
    unnamed x25, local copies, waits for them, and re-layouts  10.6 us
    all_to_all x1, waiting for transfers between devices, on_device(): lax.all_to_all(q_out, 'group', split_axis=0, concat_axis=0, tiled=True)  8.53 us
    all_to_all x1, waiting for transfers between devices, on_device(): lax.all_to_all(a_out, 'group', split_axis=0, concat_axis=0, tiled=True)  6.04 us
    all_to_all x1, starting transfers between devices, on_device(): lax.all_to_all(q_out, 'group', split_axis=0, concat_axis=0, tiled=True)  5.96 us
  transfers between devices with their start and end apart: 34, of which 11 were waited for; matrix products, arithmetic and copies ran while one was open for 13% of the time, Pallas kernels for 0%

profile of v13, /device:TPU:1, one launch (start us, length us, event | category | flops | bytes accessed | tf_op | source)
XLA Modules:
  0.0 188.9 jit_solution(12808316363299086793)
XLA Ops:
  0.0 1.0 fusion.36
  1.0 1.3 gather_fusion
  4.1 1.2 convert_reduce_fusion
  5.5 1.3 fusion.8
  7.0 2.7 %fusion.19 = bf16[32,8,1024]{2,1,0:T(8,128)(2,1)S(1)} fusion(bf16[1024,2048]{1,0:T(8,128)(2,1)} %param.12, bf16[32,8,1024]{2,1,0:T(8,128)(2,1)} %param.7, f32[32,8]{1,0:T(8,128)S(1)} %copy.37, f32[32,8]{1,0:T(8,128)S(1)} %copy.35), kind=kOutput, calls=%fused_computation.39 | convolution fusion | flops 539492352 | bytes 3147776 | tf_op jit(solution)/shard_map/dot_general | solution.py:206
  10.5 0.9 broadcast_select_fusion
  11.4 6.0 %all-to-all-start = ((bf16[8,32,1024]{2,1,0:T(8,128)(2,1)}), bf16[8,32,1024]{2,1,0:T(8,128)(2,1)S(1)}, u32[]{:S(2)}, u32[]{:S(2)}) async-start(bf16[8,32,1024]{2,1,0:T(8,128)(2,1)} %broadcast_select_fusion), calls=%async_computation | async-start | bytes 1048576 | tf_op jit(solution)/shard_map/all_to_all | solution.py:211
  18.2 8.5 %all-to-all-done = bf16[8,32,1024]{2,1,0:T(8,128)(2,1)S(1)} async-done(((bf16[8,32,1024]{2,1,0:T(8,128)(2,1)}), bf16[8,32,1024]{2,1,0:T(8,128)(2,1)S(1)}, u32[]{:S(2)}, u32[]{:S(2)}) %all-to-all-start) | async-done | bytes 524320 | tf_op jit(solution)/shard_map/all_to_all | solution.py:211
  27.4 0.9 constant_dynamic-update-slice_fusion.18
  28.3 3.8 %collective-permute-start.8 = (bf16[4,32,1024]{2,1,0:T(8,128)(2,1)S(1)}, bf16[4,32,1024]{2,1,0:T(8,128)(2,1)S(1)}, u32[]{:S(2)}, u32[]{:S(2)}) collective-permute-start(bf16[4,32,1024]{2,1,0:T(8,128)(2,1)S(1)} %get-tuple-element.42), channel_id=1, source_target_pairs={{0,12},{1,13},{2,14},{3,15},{4,0},{5,1},{6,2},{7,3},{8,4},{9,5},{1... | collective-permute-start | bytes 786440 | tf_op jit(solution)/shard_map/ppermute | solution.py:111
  32.0 2.5 %collective-permute-start = (bf16[4,32,1024]{2,1,0:T(8,128)(2,1)S(1)}, bf16[4,32,1024]{2,1,0:T(8,128)(2,1)S(1)}, u32[]{:S(2)}, u32[]{:S(2)}) collective-permute-start(bf16[4,32,1024]{2,1,0:T(8,128)(2,1)S(1)} %get-tuple-element.41), channel_id=1, source_target_pairs={{0,3},{1,0},{2,1},{3,2},{4,7},{5,4},{6,5},{7,6},{8,11},{9,8},{10,9... | collective-permute-start | bytes 786440 | tf_op jit(solution)/shard_map/ppermute | solution.py:111
  34.6 5.3 %collective-permute-done.9 = bf16[4,32,1024]{2,1,0:T(8,128)(2,1)S(1)} collective-permute-done((bf16[4,32,1024]{2,1,0:T(8,128)(2,1)S(1)}, bf16[4,32,1024]{2,1,0:T(8,128)(2,1)S(1)}, u32[]{:S(2)}, u32[]{:S(2)}) %collective-permute-start.9) | collective-permute-done | bytes 262176 | tf_op jit(solution)/shard_map/ppermute | solution.py:111
  40.0 2.7 %collective-permute-start.11 = (bf16[4,16,1024]{2,1,0:T(8,128)(2,1)S(1)}, bf16[4,16,1024]{2,1,0:T(8,128)(2,1)S(1)}, u32[]{:S(2)}, u32[]{:S(2)}) collective-permute-start(bf16[4,16,1024]{2,1,0:T(8,128)(2,1)S(1)} %slice.191), channel_id=1, source_target_pairs={{0,12},{1,13},{2,14},{3,15},{4,0},{5,1},{6,2},{7,3},{8,4},{9,5},{1... | collective-permute-start | bytes 393224 | tf_op jit(solution)/shard_map/ppermute | solution.py:111
  42.7 1.3 collective-permute-start.2
  44.0 1.5 collective-permute-start.3
  45.5 0.8 constant_dynamic-update-slice_fusion.17
  46.3 0.8 constant_dynamic-update-slice_fusion.3
  48.4 0.7 constant_dynamic-update-slice_fusion.14
  49.1 1.3 collective-permute-start.12
  50.6 0.7 constant_dynamic-update-slice_fusion.2
  51.3 0.7 constant_dynamic-update-slice_fusion.1
  51.9 0.7 constant_dynamic-update-slice_fusion
  52.7 1.7 collective-permute-start.4
  54.4 1.8 multiply_convert_fusion
  56.2 2.5 %fusion.52 = (bf16[4,128,2048]{2,1,0:T(8,128)(2,1)}, bf16[4,128,2048]{2,1,0:T(8,128)(2,1)}) fusion(bf16[8,128,2048]{2,1,0:T(8,128)(2,1)S(1)} %copy-done.2), kind=kLoop, calls=%fused_computation.158 | loop fusion | bytes 8388608 | tf_op jit(solution)/shard_map/slice | solution.py:218
  58.7 14.1 %collective-permute-done.13 = bf16[4,128,1024]{2,1,0:T(8,128)(2,1)S(1)} collective-permute-done((bf16[4,128,1024]{2,1,0:T(8,128)(2,1)S(1)}, bf16[4,128,1024]{2,1,0:T(8,128)(2,1)S(1)}, u32[]{:S(2)}, u32[]{:S(2)}) %collective-permute-start.13) | collective-permute-done | bytes 1048608 | tf_op jit(solution)/shard_map/ppermute | solution.py:111
  73.0 2.7 %collective-permute-start.15 = (bf16[4,64,1024]{2,1,0:T(8,128)(2,1)S(1)}, bf16[4,64,1024]{2,1,0:T(8,128)(2,1)S(1)}, u32[]{:S(2)}, u32[]{:S(2)}) collective-permute-start(bf16[4,64,1024]{2,1,0:T(8,128)(2,1)S(1)} %slice.193), channel_id=1, source_target_pairs={{0,3},{1,0},{2,1},{3,2},{4,7},{5,4},{6,5},{7,6},{8,11},{9,8},{10,9... | collective-permute-start | bytes 1572872 | tf_op jit(solution)/shard_map/ppermute | solution.py:111
  76.6 2.9 %collective-permute-start.7 = (bf16[4,64,1024]{2,1,0:T(8,128)(2,1)S(1)}, bf16[4,64,1024]{2,1,0:T(8,128)(2,1)S(1)}, u32[]{:S(2)}, u32[]{:S(2)}) collective-permute-start(bf16[4,64,1024]{2,1,0:T(8,128)(2,1)S(1)} %slice.188), channel_id=1, source_target_pairs={{0,12},{1,13},{2,14},{3,15},{4,0},{5,1},{6,2},{7,3},{8,4},{9,5},{1... | collective-permute-start | bytes 1572872 | tf_op jit(solution)/shard_map/ppermute | solution.py:111
  79.5 1.1 constant_dynamic-update-slice_fusion.22
  80.5 1.0 constant_dynamic-update-slice_fusion.8
  81.6 1.7 collective-permute-done.14
  83.3 0.8 constant_dynamic-update-slice_fusion.21
  84.1 0.8 constant_dynamic-update-slice_fusion.20
  84.9 1.8 collective-permute-done.6
  86.8 0.8 constant_dynamic-update-slice_fusion.7
  87.6 1.0 constant_dynamic-update-slice_fusion.19.refs_3_
  88.6 0.8 constant_dynamic-update-slice_fusion.6
  89.5 1.1 constant_dynamic-update-slice_fusion.5.refs_0_
  90.6 12.5 %shard_map.73 = (bf16[4,512,1024]{2,1,0:T(8,128)(2,1)}, bf16[4,512,1024]{2,1,0:T(8,128)(2,1)}) custom-call(s32[8]{0:T(128)} %pad_add_fusion.n_live_ref, bf16[4,512,1024]{2,1,0:T(8,128)(2,1)} %constant_dynamic-update-slice_fusion.5.refs_0_, bf16[4,128,2048]{2,1,0:T(8,128)(2,1)} %get-tuple-element.28.refs_1_, bf16[4,128,1024]{2,1,0:T(8,128)(2,1)} %get-tuple-element.26.refs_2_, ...), custom_call_target="tpu_custom_call" | custom-call | flops 2147483648 | bytes 20971520 | tf_op jit(solution)/shard_map/pallas_call | solution.py:80
  103.0 1.5 fusion.50
  104.6 2.7 %collective-permute-start.18 = (bf16[4,64,1024]{2,1,0:T(8,128)(2,1)S(1)}, bf16[4,64,1024]{2,1,0:T(8,128)(2,1)S(1)}, u32[]{:S(2)}, u32[]{:S(2)}) collective-permute-start(bf16[4,64,1024]{2,1,0:T(8,128)(2,1)S(1)} %get-tuple-element.20), channel_id=1, source_target_pairs={{0,12},{1,13},{2,14},{3,15},{4,0},{5,1},{6,2},{7,3},{8,4},{9,5},{1... | collective-permute-start | bytes 1572872 | tf_op jit(solution)/shard_map/ppermute | solution.py:111
  107.2 1.3 fusion.51
  108.6 2.7 %collective-permute-start.26 = (bf16[4,64,1024]{2,1,0:T(8,128)(2,1)S(1)}, bf16[4,64,1024]{2,1,0:T(8,128)(2,1)S(1)}, u32[]{:S(2)}, u32[]{:S(2)}) collective-permute-start(bf16[4,64,1024]{2,1,0:T(8,128)(2,1)S(1)} %get-tuple-element.24), channel_id=1, source_target_pairs={{0,3},{1,0},{2,1},{3,2},{4,7},{5,4},{6,5},{7,6},{8,11},{9,8},{10,9... | collective-permute-start | bytes 1572872 | tf_op jit(solution)/shard_map/ppermute | solution.py:111
  111.3 2.5 %collective-permute-done.16 = bf16[4,64,1024]{2,1,0:T(8,128)(2,1)S(1)} collective-permute-done((bf16[4,64,1024]{2,1,0:T(8,128)(2,1)S(1)}, bf16[4,64,1024]{2,1,0:T(8,128)(2,1)S(1)}, u32[]{:S(2)}, u32[]{:S(2)}) %collective-permute-start.16) | collective-permute-done | bytes 524320 | tf_op jit(solution)/shard_map/ppermute | solution.py:111
  114.6 2.7 %collective-permute-start.19 = (bf16[4,128,1024]{2,1,0:T(8,128)(2,1)S(1)}, bf16[4,128,1024]{2,1,0:T(8,128)(2,1)S(1)}, u32[]{:S(2)}, u32[]{:S(2)}) collective-permute-start(bf16[4,128,1024]{2,1,0:T(8,128)(2,1)S(1)} %get-tuple-element.18), channel_id=1, source_target_pairs={{0,12},{1,13},{2,14},{3,15},{4,0},{5,1},{6,2},{7,3},{8,4},{9,5},{1... | collective-permute-start | bytes 3145736 | tf_op jit(solution)/shard_map/ppermute | solution.py:111
  118.2 0.7 add_convert_fusion.1
  118.9 2.7 %collective-permute-start.27 = (bf16[4,128,1024]{2,1,0:T(8,128)(2,1)S(1)}, bf16[4,128,1024]{2,1,0:T(8,128)(2,1)S(1)}, u32[]{:S(2)}, u32[]{:S(2)}) collective-permute-start(bf16[4,128,1024]{2,1,0:T(8,128)(2,1)S(1)} %get-tuple-element.22), channel_id=1, source_target_pairs={{0,3},{1,0},{2,1},{3,2},{4,7},{5,4},{6,5},{7,6},{8,11},{9,8},{10,9... | collective-permute-start | bytes 3145736 | tf_op jit(solution)/shard_map/ppermute | solution.py:111
  121.7 13.5 %collective-permute-done.17 = bf16[4,128,1024]{2,1,0:T(8,128)(2,1)S(1)} collective-permute-done((bf16[4,128,1024]{2,1,0:T(8,128)(2,1)S(1)}, bf16[4,128,1024]{2,1,0:T(8,128)(2,1)S(1)}, u32[]{:S(2)}, u32[]{:S(2)}) %collective-permute-start.17) | collective-permute-done | bytes 1048608 | tf_op jit(solution)/shard_map/ppermute | solution.py:111
  135.2 0.7 fusion.48
  136.0 2.8 %collective-permute-start.22 = (bf16[4,16,1024]{2,1,0:T(8,128)(2,1)S(1)}, bf16[4,16,1024]{2,1,0:T(8,128)(2,1)S(1)}, u32[]{:S(2)}, u32[]{:S(2)}) collective-permute-start(bf16[4,16,1024]{2,1,0:T(8,128)(2,1)S(1)} %get-tuple-element.34), channel_id=1, source_target_pairs={{0,3},{1,0},{2,1},{3,2},{4,7},{5,4},{6,5},{7,6},{8,11},{9,8},{10,9... | collective-permute-start | bytes 393224 | tf_op jit(solution)/shard_map/ppermute | solution.py:111
  138.8 0.8 collective-permute-done.25
  139.6 0.7 fusion.49
  140.4 2.7 %collective-permute-start.30 = (bf16[4,16,1024]{2,1,0:T(8,128)(2,1)S(1)}, bf16[4,16,1024]{2,1,0:T(8,128)(2,1)S(1)}, u32[]{:S(2)}, u32[]{:S(2)}) collective-permute-start(bf16[4,16,1024]{2,1,0:T(8,128)(2,1)S(1)} %get-tuple-element.36), channel_id=1, source_target_pairs={{0,12},{1,13},{2,14},{3,15},{4,0},{5,1},{6,2},{7,3},{8,4},{9,5},{1... | collective-permute-start | bytes 393224 | tf_op jit(solution)/shard_map/ppermute | solution.py:111
  143.8 2.4 %collective-permute-start.23 = (bf16[4,32,1024]{2,1,0:T(8,128)(2,1)S(1)}, bf16[4,32,1024]{2,1,0:T(8,128)(2,1)S(1)}, u32[]{:S(2)}, u32[]{:S(2)}) collective-permute-start(bf16[4,32,1024]{2,1,0:T(8,128)(2,1)S(1)} %get-tuple-element.30), channel_id=1, source_target_pairs={{0,3},{1,0},{2,1},{3,2},{4,7},{5,4},{6,5},{7,6},{8,11},{9,8},{10,9... | collective-permute-start | bytes 786440 | tf_op jit(solution)/shard_map/ppermute | solution.py:111
  146.4 2.7 %collective-permute-start.31 = (bf16[4,32,1024]{2,1,0:T(8,128)(2,1)S(1)}, bf16[4,32,1024]{2,1,0:T(8,128)(2,1)S(1)}, u32[]{:S(2)}, u32[]{:S(2)}) collective-permute-start(bf16[4,32,1024]{2,1,0:T(8,128)(2,1)S(1)} %get-tuple-element.32), channel_id=1, source_target_pairs={{0,12},{1,13},{2,14},{3,15},{4,0},{5,1},{6,2},{7,3},{8,4},{9,5},{1... | collective-permute-start | bytes 786440 | tf_op jit(solution)/shard_map/ppermute | solution.py:111
  149.1 3.9 %collective-permute-done.21 = bf16[4,32,1024]{2,1,0:T(8,128)(2,1)S(1)} collective-permute-done((bf16[4,32,1024]{2,1,0:T(8,128)(2,1)S(1)}, bf16[4,32,1024]{2,1,0:T(8,128)(2,1)S(1)}, u32[]{:S(2)}, u32[]{:S(2)}) %collective-permute-start.21) | collective-permute-done | bytes 262176 | tf_op jit(solution)/shard_map/ppermute | solution.py:111
  153.2 1.4 gather_fusion.6
  154.6 1.9 %broadcast_select_fusion.1 = bf16[8,32,1024]{2,1,0:T(8,128)(2,1)} fusion(bf16[8,32,1024]{2,1,0:T(8,128)(2,1)} %gather_fusion.6, pred[8]{0:T(512)(128)(4,1)S(1)} %fusion.40), kind=kLoop, calls=%fused_computation.60 | loop fusion | flops 262144 | bytes 1048584 | tf_op jit(solution)/shard_map/jit(_where)/select_n | solution.py:227
  156.6 17.2 %all-to-all-start.1 = ((bf16[8,32,1024]{2,1,0:T(8,128)(2,1)}), bf16[8,32,1024]{2,1,0:T(8,128)(2,1)}, u32[]{:S(2)}, u32[]{:S(2)}) async-start(bf16[8,32,1024]{2,1,0:T(8,128)(2,1)} %broadcast_select_fusion.1), calls=%async_computation.1 | async-start | bytes 1048576 | tf_op jit(solution)/shard_map/all_to_all | solution.py:228
  173.8 3.4 %multiply_bitcast_fusion = f32[32,8,1024]{2,1,0:T(8,128)} fusion(bf16[1024,2048]{1,0:T(8,128)(2,1)} %param.12, bf16[32,8,1024]{2,1,0:T(8,128)(2,1)S(1)} %copy-done.5, f32[32,8]{1,0:T(8,128)S(1)} %copy.37, f32[32,8]{1,0:T(8,128)S(1)} %copy.35), kind=kOutput, calls=%fused_computation.37 | convolution fusion | flops 538968064 | bytes 3672064 | tf_op jit(solution)/shard_map/dot_general | solution.py:231
  177.2 6.0 %all-to-all-done.1 = bf16[8,32,1024]{2,1,0:T(8,128)(2,1)} async-done(((bf16[8,32,1024]{2,1,0:T(8,128)(2,1)}), bf16[8,32,1024]{2,1,0:T(8,128)(2,1)}, u32[]{:S(2)}, u32[]{:S(2)}) %all-to-all-start.1) | async-done | bytes 524320 | tf_op jit(solution)/shard_map/all_to_all | solution.py:228
  183.3 1.6 gather_fusion.7
  185.3 1.9 fusion.14
  187.2 1.6 fusion.7
  (113 shorter events, 10.8 us)
Async XLA Ops:
  0.0 187.2 %copy-start = (bf16[1024,1024]{1,0:T(8,128)(2,1)S(1)}, bf16[1024,1024]{1,0:T(8,128)(2,1)}, u32[]{:S(2)}) copy-start(bf16[1024,1024]{1,0:T(8,128)(2,1)} %param.13) | copy-start | bytes 6291460
  9.6 7.9 %copy-start.1 = (s32[64]{0:T(128)S(1)}, s32[64]{0:T(128)}, u32[]{:S(2)}) copy-start(s32[64]{0:T(128)} %param.11) | copy-start | bytes 772
  11.4 15.3 %all-to-all-start = ((bf16[8,32,1024]{2,1,0:T(8,128)(2,1)}), bf16[8,32,1024]{2,1,0:T(8,128)(2,1)S(1)}, u32[]{:S(2)}, u32[]{:S(2)}) async-start(bf16[8,32,1024]{2,1,0:T(8,128)(2,1)} %broadcast_select_fusion), calls=%async_computation | async-start | bytes 1048576 | tf_op jit(solution)/shard_map/all_to_all | solution.py:211
  27.3 27.1 %copy-start.2 = (bf16[8,128,2048]{2,1,0:T(8,128)(2,1)S(1)}, bf16[8,128,2048]{2,1,0:T(8,128)(2,1)}, u32[]{:S(2)}) copy-start(bf16[8,128,2048]{2,1,0:T(8,128)(2,1)} %param.8) | copy-start | bytes 12582916
  28.3 11.7 %collective-permute-start.8 = (bf16[4,32,1024]{2,1,0:T(8,128)(2,1)S(1)}, bf16[4,32,1024]{2,1,0:T(8,128)(2,1)S(1)}, u32[]{:S(2)}, u32[]{:S(2)}) collective-permute-start(bf16[4,32,1024]{2,1,0:T(8,128)(2,1)S(1)} %get-tuple-element.42), channel_id=1, source_target_pairs={{0,12},{1,13},{2,14},{3,15},{4,0},{5,1},{6,2},{7,3},{8,4},{9,5},{1... | collective-permute-start | bytes 786440 | tf_op jit(solution)/shard_map/ppermute | solution.py:111
  32.0 7.8 %collective-permute-start.9 = (bf16[4,32,1024]{2,1,0:T(8,128)(2,1)S(1)}, bf16[4,32,1024]{2,1,0:T(8,128)(2,1)S(1)}, u32[]{:S(2)}, u32[]{:S(2)}) collective-permute-start(bf16[4,32,1024]{2,1,0:T(8,128)(2,1)S(1)} %get-tuple-element.42), channel_id=1, source_target_pairs={{0,4},{1,5},{2,6},{3,7},{4,8},{5,9},{6,10},{7,11},{8,12},{9,13},{1... | collective-permute-start | bytes 786440 | tf_op jit(solution)/shard_map/ppermute | solution.py:111
  32.0 12.0 %collective-permute-start = (bf16[4,32,1024]{2,1,0:T(8,128)(2,1)S(1)}, bf16[4,32,1024]{2,1,0:T(8,128)(2,1)S(1)}, u32[]{:S(2)}, u32[]{:S(2)}) collective-permute-start(bf16[4,32,1024]{2,1,0:T(8,128)(2,1)S(1)} %get-tuple-element.41), channel_id=1, source_target_pairs={{0,3},{1,0},{2,1},{3,2},{4,7},{5,4},{6,5},{7,6},{8,11},{9,8},{10,9... | collective-permute-start | bytes 786440 | tf_op jit(solution)/shard_map/ppermute | solution.py:111
  34.5 8.2 %collective-permute-start.1 = (bf16[4,32,1024]{2,1,0:T(8,128)(2,1)S(1)}, bf16[4,32,1024]{2,1,0:T(8,128)(2,1)S(1)}, u32[]{:S(2)}, u32[]{:S(2)}) collective-permute-start(bf16[4,32,1024]{2,1,0:T(8,128)(2,1)S(1)} %get-tuple-element.41), channel_id=1, source_target_pairs={{0,1},{1,2},{2,3},{3,0},{4,5},{5,6},{6,7},{7,4},{8,9},{9,10},{10,1... | collective-permute-start | bytes 786440 | tf_op jit(solution)/shard_map/ppermute | solution.py:111
  39.9 7.2 %collective-permute-start.10 = (bf16[4,16,1024]{2,1,0:T(8,128)(2,1)S(1)}, bf16[4,16,1024]{2,1,0:T(8,128)(2,1)S(1)}, u32[]{:S(2)}, u32[]{:S(2)}) collective-permute-start(bf16[4,16,1024]{2,1,0:T(8,128)(2,1)S(1)} %slice.190), channel_id=1, source_target_pairs={{0,4},{1,5},{2,6},{3,7},{4,8},{5,9},{6,10},{7,11},{8,12},{9,13},{1... | collective-permute-start | bytes 393224 | tf_op jit(solution)/shard_map/ppermute | solution.py:111
  40.0 7.7 %collective-permute-start.11 = (bf16[4,16,1024]{2,1,0:T(8,128)(2,1)S(1)}, bf16[4,16,1024]{2,1,0:T(8,128)(2,1)S(1)}, u32[]{:S(2)}, u32[]{:S(2)}) collective-permute-start(bf16[4,16,1024]{2,1,0:T(8,128)(2,1)S(1)} %slice.191), channel_id=1, source_target_pairs={{0,12},{1,13},{2,14},{3,15},{4,0},{5,1},{6,2},{7,3},{8,4},{9,5},{1... | collective-permute-start | bytes 393224 | tf_op jit(solution)/shard_map/ppermute | solution.py:111
  42.7 7.9 %collective-permute-start.2 = (bf16[4,16,1024]{2,1,0:T(8,128)(2,1)S(1)}, bf16[4,16,1024]{2,1,0:T(8,128)(2,1)S(1)}, u32[]{:S(2)}, u32[]{:S(2)}) collective-permute-start(bf16[4,16,1024]{2,1,0:T(8,128)(2,1)S(1)} %slice.185), channel_id=1, source_target_pairs={{0,1},{1,2},{2,3},{3,0},{4,5},{5,6},{6,7},{7,4},{8,9},{9,10},{10,1... | collective-permute-start | bytes 393224 | tf_op jit(solution)/shard_map/ppermute | solution.py:111
  44.0 7.3 %collective-permute-start.3 = (bf16[4,16,1024]{2,1,0:T(8,128)(2,1)S(1)}, bf16[4,16,1024]{2,1,0:T(8,128)(2,1)S(1)}, u32[]{:S(2)}, u32[]{:S(2)}) collective-permute-start(bf16[4,16,1024]{2,1,0:T(8,128)(2,1)S(1)} %slice.186), channel_id=1, source_target_pairs={{0,3},{1,0},{2,1},{3,2},{4,7},{5,4},{6,5},{7,6},{8,11},{9,8},{10,9... | collective-permute-start | bytes 393224 | tf_op jit(solution)/shard_map/ppermute | solution.py:111
  49.1 23.8 %collective-permute-start.12 = (bf16[4,128,1024]{2,1,0:T(8,128)(2,1)S(1)}, bf16[4,128,1024]{2,1,0:T(8,128)(2,1)S(1)}, u32[]{:S(2)}, u32[]{:S(2)}) collective-permute-start(bf16[4,128,1024]{2,1,0:T(8,128)(2,1)S(1)} %get-tuple-element.43), channel_id=1, source_target_pairs={{0,3},{1,0},{2,1},{3,2},{4,7},{5,4},{6,5},{7,6},{8,11},{9,8},{10,9... | collective-permute-start | bytes 3145736 | tf_op jit(solution)/shard_map/ppermute | solution.py:111
  50.4 22.4 %collective-permute-start.13 = (bf16[4,128,1024]{2,1,0:T(8,128)(2,1)S(1)}, bf16[4,128,1024]{2,1,0:T(8,128)(2,1)S(1)}, u32[]{:S(2)}, u32[]{:S(2)}) collective-permute-start(bf16[4,128,1024]{2,1,0:T(8,128)(2,1)S(1)} %get-tuple-element.43), channel_id=1, source_target_pairs={{0,1},{1,2},{2,3},{3,0},{4,5},{5,6},{6,7},{7,4},{8,9},{9,10},{10,1... | collective-permute-start | bytes 3145736 | tf_op jit(solution)/shard_map/ppermute | solution.py:111
  52.7 23.8 %collective-permute-start.4 = (bf16[4,128,1024]{2,1,0:T(8,128)(2,1)S(1)}, bf16[4,128,1024]{2,1,0:T(8,128)(2,1)S(1)}, u32[]{:S(2)}, u32[]{:S(2)}) collective-permute-start(bf16[4,128,1024]{2,1,0:T(8,128)(2,1)S(1)} %get-tuple-element.47), channel_id=1, source_target_pairs={{0,12},{1,13},{2,14},{3,15},{4,0},{5,1},{6,2},{7,3},{8,4},{9,5},{1... | collective-permute-start | bytes 3145736 | tf_op jit(solution)/shard_map/ppermute | solution.py:111
  54.4 21.9 %collective-permute-start.5 = (bf16[4,128,1024]{2,1,0:T(8,128)(2,1)S(1)}, bf16[4,128,1024]{2,1,0:T(8,128)(2,1)S(1)}, u32[]{:S(2)}, u32[]{:S(2)}) collective-permute-start(bf16[4,128,1024]{2,1,0:T(8,128)(2,1)S(1)} %get-tuple-element.47), channel_id=1, source_target_pairs={{0,4},{1,5},{2,6},{3,7},{4,8},{5,9},{6,10},{7,11},{8,12},{9,13},{1... | collective-permute-start | bytes 3145736 | tf_op jit(solution)/shard_map/ppermute | solution.py:111
  72.9 10.4 %collective-permute-start.14 = (bf16[4,64,1024]{2,1,0:T(8,128)(2,1)S(1)}, bf16[4,64,1024]{2,1,0:T(8,128)(2,1)S(1)}, u32[]{:S(2)}, u32[]{:S(2)}) collective-permute-start(bf16[4,64,1024]{2,1,0:T(8,128)(2,1)S(1)} %slice.192), channel_id=1, source_target_pairs={{0,1},{1,2},{2,3},{3,0},{4,5},{5,6},{6,7},{7,4},{8,9},{9,10},{10,1... | collective-permute-start | bytes 1572872 | tf_op jit(solution)/shard_map/ppermute | solution.py:111
  73.0 11.1 %collective-permute-start.15 = (bf16[4,64,1024]{2,1,0:T(8,128)(2,1)S(1)}, bf16[4,64,1024]{2,1,0:T(8,128)(2,1)S(1)}, u32[]{:S(2)}, u32[]{:S(2)}) collective-permute-start(bf16[4,64,1024]{2,1,0:T(8,128)(2,1)S(1)} %slice.193), channel_id=1, source_target_pairs={{0,3},{1,0},{2,1},{3,2},{4,7},{5,4},{6,5},{7,6},{8,11},{9,8},{10,9... | collective-permute-start | bytes 1572872 | tf_op jit(solution)/shard_map/ppermute | solution.py:111
  76.4 10.3 %collective-permute-start.6 = (bf16[4,64,1024]{2,1,0:T(8,128)(2,1)S(1)}, bf16[4,64,1024]{2,1,0:T(8,128)(2,1)S(1)}, u32[]{:S(2)}, u32[]{:S(2)}) collective-permute-start(bf16[4,64,1024]{2,1,0:T(8,128)(2,1)S(1)} %slice.187), channel_id=1, source_target_pairs={{0,4},{1,5},{2,6},{3,7},{4,8},{5,9},{6,10},{7,11},{8,12},{9,13},{1... | collective-permute-start | bytes 1572872 | tf_op jit(solution)/shard_map/ppermute | solution.py:111
  76.6 12.1 %collective-permute-start.7 = (bf16[4,64,1024]{2,1,0:T(8,128)(2,1)S(1)}, bf16[4,64,1024]{2,1,0:T(8,128)(2,1)S(1)}, u32[]{:S(2)}, u32[]{:S(2)}) collective-permute-start(bf16[4,64,1024]{2,1,0:T(8,128)(2,1)S(1)} %slice.188), channel_id=1, source_target_pairs={{0,12},{1,13},{2,14},{3,15},{4,0},{5,1},{6,2},{7,3},{8,4},{9,5},{1... | collective-permute-start | bytes 1572872 | tf_op jit(solution)/shard_map/ppermute | solution.py:111
  103.0 10.8 %copy-start.4 = (bf16[4,512,1024]{2,1,0:T(8,128)(2,1)S(1)}, bf16[4,512,1024]{2,1,0:T(8,128)(2,1)}, u32[]{:S(2)}) copy-start(bf16[4,512,1024]{2,1,0:T(8,128)(2,1)} %get-tuple-element.7) | copy-start | bytes 12582916
  104.5 13.7 %copy-start.3 = (bf16[4,512,1024]{2,1,0:T(8,128)(2,1)S(1)}, bf16[4,512,1024]{2,1,0:T(8,128)(2,1)}, u32[]{:S(2)}) copy-start(bf16[4,512,1024]{2,1,0:T(8,128)(2,1)} %get-tuple-element.8) | copy-start | bytes 12582916
  104.5 9.3 %collective-permute-start.16 = (bf16[4,64,1024]{2,1,0:T(8,128)(2,1)S(1)}, bf16[4,64,1024]{2,1,0:T(8,128)(2,1)S(1)}, u32[]{:S(2)}, u32[]{:S(2)}) collective-permute-start(bf16[4,64,1024]{2,1,0:T(8,128)(2,1)S(1)} %get-tuple-element.19), channel_id=1, source_target_pairs={{0,4},{1,5},{2,6},{3,7},{4,8},{5,9},{6,10},{7,11},{8,12},{9,13},{1... | collective-permute-start | bytes 1572872 | tf_op jit(solution)/shard_map/ppermute | solution.py:111
  104.6 9.2 %collective-permute-start.18 = (bf16[4,64,1024]{2,1,0:T(8,128)(2,1)S(1)}, bf16[4,64,1024]{2,1,0:T(8,128)(2,1)S(1)}, u32[]{:S(2)}, u32[]{:S(2)}) collective-permute-start(bf16[4,64,1024]{2,1,0:T(8,128)(2,1)S(1)} %get-tuple-element.20), channel_id=1, source_target_pairs={{0,12},{1,13},{2,14},{3,15},{4,0},{5,1},{6,2},{7,3},{8,4},{9,5},{1... | collective-permute-start | bytes 1572872 | tf_op jit(solution)/shard_map/ppermute | solution.py:111
  108.6 9.6 %collective-permute-start.24 = (bf16[4,64,1024]{2,1,0:T(8,128)(2,1)S(1)}, bf16[4,64,1024]{2,1,0:T(8,128)(2,1)S(1)}, u32[]{:S(2)}, u32[]{:S(2)}) collective-permute-start(bf16[4,64,1024]{2,1,0:T(8,128)(2,1)S(1)} %get-tuple-element.23), channel_id=1, source_target_pairs={{0,1},{1,2},{2,3},{3,0},{4,5},{5,6},{6,7},{7,4},{8,9},{9,10},{10,1... | collective-permute-start | bytes 1572872 | tf_op jit(solution)/shard_map/ppermute | solution.py:111
  108.6 9.5 %collective-permute-start.26 = (bf16[4,64,1024]{2,1,0:T(8,128)(2,1)S(1)}, bf16[4,64,1024]{2,1,0:T(8,128)(2,1)S(1)}, u32[]{:S(2)}, u32[]{:S(2)}) collective-permute-start(bf16[4,64,1024]{2,1,0:T(8,128)(2,1)S(1)} %get-tuple-element.24), channel_id=1, source_target_pairs={{0,3},{1,0},{2,1},{3,2},{4,7},{5,4},{6,5},{7,6},{8,11},{9,8},{10,9... | collective-permute-start | bytes 1572872 | tf_op jit(solution)/shard_map/ppermute | solution.py:111
  114.5 20.7 %collective-permute-start.17 = (bf16[4,128,1024]{2,1,0:T(8,128)(2,1)S(1)}, bf16[4,128,1024]{2,1,0:T(8,128)(2,1)S(1)}, u32[]{:S(2)}, u32[]{:S(2)}) collective-permute-start(bf16[4,128,1024]{2,1,0:T(8,128)(2,1)S(1)} %get-tuple-element.17), channel_id=1, source_target_pairs={{0,4},{1,5},{2,6},{3,7},{4,8},{5,9},{6,10},{7,11},{8,12},{9,13},{1... | collective-permute-start | bytes 3145736 | tf_op jit(solution)/shard_map/ppermute | solution.py:111
  114.6 20.7 %collective-permute-start.19 = (bf16[4,128,1024]{2,1,0:T(8,128)(2,1)S(1)}, bf16[4,128,1024]{2,1,0:T(8,128)(2,1)S(1)}, u32[]{:S(2)}, u32[]{:S(2)}) collective-permute-start(bf16[4,128,1024]{2,1,0:T(8,128)(2,1)S(1)} %get-tuple-element.18), channel_id=1, source_target_pairs={{0,12},{1,13},{2,14},{3,15},{4,0},{5,1},{6,2},{7,3},{8,4},{9,5},{1... | collective-permute-start | bytes 3145736 | tf_op jit(solution)/shard_map/ppermute | solution.py:111
  118.8 20.7 %collective-permute-start.25 = (bf16[4,128,1024]{2,1,0:T(8,128)(2,1)S(1)}, bf16[4,128,1024]{2,1,0:T(8,128)(2,1)S(1)}, u32[]{:S(2)}, u32[]{:S(2)}) collective-permute-start(bf16[4,128,1024]{2,1,0:T(8,128)(2,1)S(1)} %get-tuple-element.21), channel_id=1, source_target_pairs={{0,1},{1,2},{2,3},{3,0},{4,5},{5,6},{6,7},{7,4},{8,9},{9,10},{10,1... | collective-permute-start | bytes 3145736 | tf_op jit(solution)/shard_map/ppermute | solution.py:111
  118.9 20.7 %collective-permute-start.27 = (bf16[4,128,1024]{2,1,0:T(8,128)(2,1)S(1)}, bf16[4,128,1024]{2,1,0:T(8,128)(2,1)S(1)}, u32[]{:S(2)}, u32[]{:S(2)}) collective-permute-start(bf16[4,128,1024]{2,1,0:T(8,128)(2,1)S(1)} %get-tuple-element.22), channel_id=1, source_target_pairs={{0,3},{1,0},{2,1},{3,2},{4,7},{5,4},{6,5},{7,6},{8,11},{9,8},{10,9... | collective-permute-start | bytes 3145736 | tf_op jit(solution)/shard_map/ppermute | solution.py:111
  135.9 7.1 %collective-permute-start.20 = (bf16[4,16,1024]{2,1,0:T(8,128)(2,1)S(1)}, bf16[4,16,1024]{2,1,0:T(8,128)(2,1)S(1)}, u32[]{:S(2)}, u32[]{:S(2)}) collective-permute-start(bf16[4,16,1024]{2,1,0:T(8,128)(2,1)S(1)} %get-tuple-element.33), channel_id=1, source_target_pairs={{0,1},{1,2},{2,3},{3,0},{4,5},{5,6},{6,7},{7,4},{8,9},{9,10},{10,1... | collective-permute-start | bytes 393224 | tf_op jit(solution)/shard_map/ppermute | solution.py:111
  136.0 7.0 %collective-permute-start.22 = (bf16[4,16,1024]{2,1,0:T(8,128)(2,1)S(1)}, bf16[4,16,1024]{2,1,0:T(8,128)(2,1)S(1)}, u32[]{:S(2)}, u32[]{:S(2)}) collective-permute-start(bf16[4,16,1024]{2,1,0:T(8,128)(2,1)S(1)} %get-tuple-element.34), channel_id=1, source_target_pairs={{0,3},{1,0},{2,1},{3,2},{4,7},{5,4},{6,5},{7,6},{8,11},{9,8},{10,9... | collective-permute-start | bytes 393224 | tf_op jit(solution)/shard_map/ppermute | solution.py:111
  140.3 5.9 %collective-permute-start.28 = (bf16[4,16,1024]{2,1,0:T(8,128)(2,1)S(1)}, bf16[4,16,1024]{2,1,0:T(8,128)(2,1)S(1)}, u32[]{:S(2)}, u32[]{:S(2)}) collective-permute-start(bf16[4,16,1024]{2,1,0:T(8,128)(2,1)S(1)} %get-tuple-element.35), channel_id=1, source_target_pairs={{0,4},{1,5},{2,6},{3,7},{4,8},{5,9},{6,10},{7,11},{8,12},{9,13},{1... | collective-permute-start | bytes 393224 | tf_op jit(solution)/shard_map/ppermute | solution.py:111
  140.4 5.8 %collective-permute-start.30 = (bf16[4,16,1024]{2,1,0:T(8,128)(2,1)S(1)}, bf16[4,16,1024]{2,1,0:T(8,128)(2,1)S(1)}, u32[]{:S(2)}, u32[]{:S(2)}) collective-permute-start(bf16[4,16,1024]{2,1,0:T(8,128)(2,1)S(1)} %get-tuple-element.36), channel_id=1, source_target_pairs={{0,12},{1,13},{2,14},{3,15},{4,0},{5,1},{6,2},{7,3},{8,4},{9,5},{1... | collective-permute-start | bytes 393224 | tf_op jit(solution)/shard_map/ppermute | solution.py:111
  143.2 9.8 %collective-permute-start.21 = (bf16[4,32,1024]{2,1,0:T(8,128)(2,1)S(1)}, bf16[4,32,1024]{2,1,0:T(8,128)(2,1)S(1)}, u32[]{:S(2)}, u32[]{:S(2)}) collective-permute-start(bf16[4,32,1024]{2,1,0:T(8,128)(2,1)S(1)} %get-tuple-element.29), channel_id=1, source_target_pairs={{0,1},{1,2},{2,3},{3,0},{4,5},{5,6},{6,7},{7,4},{8,9},{9,10},{10,1... | collective-permute-start | bytes 786440 | tf_op jit(solution)/shard_map/ppermute | solution.py:111
  143.8 9.1 %collective-permute-start.23 = (bf16[4,32,1024]{2,1,0:T(8,128)(2,1)S(1)}, bf16[4,32,1024]{2,1,0:T(8,128)(2,1)S(1)}, u32[]{:S(2)}, u32[]{:S(2)}) collective-permute-start(bf16[4,32,1024]{2,1,0:T(8,128)(2,1)S(1)} %get-tuple-element.30), channel_id=1, source_target_pairs={{0,3},{1,0},{2,1},{3,2},{4,7},{5,4},{6,5},{7,6},{8,11},{9,8},{10,9... | collective-permute-start | bytes 786440 | tf_op jit(solution)/shard_map/ppermute | solution.py:111
  146.2 27.6 %copy-start.5 = (bf16[32,8,1024]{2,1,0:T(8,128)(2,1)S(1)}, bf16[32,8,1024]{2,1,0:T(8,128)(2,1)}, u32[]{:S(2)}) copy-start(bf16[32,8,1024]{2,1,0:T(8,128)(2,1)} %param.7) | copy-start | bytes 1572868
  146.3 6.7 %collective-permute-start.29 = (bf16[4,32,1024]{2,1,0:T(8,128)(2,1)S(1)}, bf16[4,32,1024]{2,1,0:T(8,128)(2,1)S(1)}, u32[]{:S(2)}, u32[]{:S(2)}) collective-permute-start(bf16[4,32,1024]{2,1,0:T(8,128)(2,1)S(1)} %get-tuple-element.31), channel_id=1, source_target_pairs={{0,4},{1,5},{2,6},{3,7},{4,8},{5,9},{6,10},{7,11},{8,12},{9,13},{1... | collective-permute-start | bytes 786440 | tf_op jit(solution)/shard_map/ppermute | solution.py:111
  146.4 6.7 %collective-permute-start.31 = (bf16[4,32,1024]{2,1,0:T(8,128)(2,1)S(1)}, bf16[4,32,1024]{2,1,0:T(8,128)(2,1)S(1)}, u32[]{:S(2)}, u32[]{:S(2)}) collective-permute-start(bf16[4,32,1024]{2,1,0:T(8,128)(2,1)S(1)} %get-tuple-element.32), channel_id=1, source_target_pairs={{0,12},{1,13},{2,14},{3,15},{4,0},{5,1},{6,2},{7,3},{8,4},{9,5},{1... | collective-permute-start | bytes 786440 | tf_op jit(solution)/shard_map/ppermute | solution.py:111
  156.6 26.7 %all-to-all-start.1 = ((bf16[8,32,1024]{2,1,0:T(8,128)(2,1)}), bf16[8,32,1024]{2,1,0:T(8,128)(2,1)}, u32[]{:S(2)}, u32[]{:S(2)}) async-start(bf16[8,32,1024]{2,1,0:T(8,128)(2,1)} %broadcast_select_fusion.1), calls=%async_computation.1 | async-start | bytes 1048576 | tf_op jit(solution)/shard_map/all_to_all | solution.py:228

commit v14 on v13

--- a/solution.py
+++ b/solution.py
@@ -58,7 +58,7 @@
                 o_ref[0, :, lo:lo + head_dim] = o.astype(o_ref.dtype)
 
 
-def attend_local(q_sets, kv_sets, live_sets, first_event, heads, out_dtype):
+def attend_local(q_sets, kv_sets, live_sets, active_sets, first_event, heads, out_dtype):
     rows, cands, width = q_sets[0].shape
     count = kv_sets[0].shape[1]
     head_dim = width // heads
@@ -69,6 +69,7 @@
         values = (piece[:, :, width:].astype(jnp.float32) * keep[:, :, None]).astype(jnp.bfloat16)
         operands += [queries, piece, values]
         n_live.append(jnp.clip(live.astype(jnp.int32) - first_event, 0, count).astype(jnp.int32))
+    n_live = [jnp.where(on, n, 0) for n, on in zip(n_live, active_sets)]
     sets = len(q_sets)
     kernel = functools.partial(attend_kernel, sets=sets, heads=heads, head_dim=head_dim)
     flops = 4 * sets * rows * cands * count * width
@@ -209,14 +210,17 @@
     q_pos = jnp.swapaxes(queries, 0, 1)
     q_out = jnp.where(send_filled[:, None, None], q_pos[send_pos], jnp.zeros((), jnp.bfloat16))
     q_in = lax.all_to_all(q_out, "group", split_axis=0, concat_axis=0, tiled=True)
-    q_rows = q_in[row_index]
-    split = per_group // 2
-    halves = ((slice(0, split), (0, 1)), (slice(split, per_group), (1, 0)))
-    q_sets = [torus_gather(q_rows[rows_of], grid, order) for rows_of, order in halves]
+    kv_slots = kv_cache[chosen]
+    live_slots = row_live[chosen]
+    slot_count = q_in.shape[0]
+    split = slot_count // 2
+    halves = ((slice(0, split), (0, 1)), (slice(split, slot_count), (1, 0)))
+    q_sets = [torus_gather(q_in[rows_of], grid, order) for rows_of, order in halves]
     partials = attend_local(
         q_sets,
-        [kv_cache[rows_of] for rows_of, _ in halves],
-        [row_live[rows_of] for rows_of, _ in halves],
+        [kv_slots[rows_of] for rows_of, _ in halves],
+        [live_slots[rows_of] for rows_of, _ in halves],
+        [filled[rows_of] for rows_of, _ in halves],
         member_now * count,
         HEADS,
         jnp.bfloat16,
@@ -224,8 +228,7 @@
     sums = [torus_reduce(partial, grid, order) for partial, (_, order) in zip(partials, halves)]
     summed = jnp.concatenate(sums, axis=0).astype(jnp.bfloat16)
 
-    a_out = jnp.where(filled[:, None, None], summed[chosen], jnp.zeros((), summed.dtype))
-    a_in = lax.all_to_all(a_out, "group", split_axis=0, concat_axis=0, tiled=True)
+    a_in = lax.all_to_all(summed, "group", split_axis=0, concat_axis=0, tiled=True)
     attn = jnp.swapaxes(a_in[receive_index], 0, 1).astype(jnp.float32)
 
     gates = jax.nn.silu(jnp.dot(normed, w_uq[:, :width], preferred_element_type=jnp.float32))

time: 190 us -> 185 us (0.974)
  waiting for transfers between devices: 58.8 us -> 51.2 us
  local copies, waits for them, and re-layouts: 27.7 us -> 30.8 us
    all_to_all x1, waiting for transfers between devices: 8.53 us -> 2.23 us  [on_device(): lax.all_to_all(q_out, 'group', split_axis=0, concat_axis=0, tiled=True)]
    gather x2, local copies, waits for them, and re-layouts: 1.95 us -> 5.63 us  [the longest x1 4.98 us: on_device(): kv_slots = kv_cache[chosen]]
    select_n x3 -> x2, other arithmetic: 2.02 us -> 0.08 us  [the longest x1 0.08 us: attend_local(): n_live = [jnp.where(on, n, 0) for n, on in zip(n_live, active_sets)]]
    unnamed x25 -> x27, local copies, waits for them, and re-layouts: 10.6 us -> 10.5 us
  transfers between devices with their start and end apart: 34 -> 34, of which waited for: 11 -> 11; matrix products, arithmetic and copies ran while one was open for 13% -> 18% of each run, Pallas kernels for 0% -> 0%
where the time goes in v14:
time: 185 us; the launch traced here: 184 us
  starting transfers between devices  66.2 us (36%)
  waiting for transfers between devices  51.2 us (28%)
  local copies, waits for them, and re-layouts  30.8 us (17%)
  other arithmetic  15.7 us (8%)
  Pallas kernels  12.5 us (7%)
  matrix products  7.71 us (4%)
    ppermute x32, starting transfers between devices, send(): return lax.ppermute(value, 'member', shift_perm(grid, axis, shift))  43.2 us
    ppermute x32, waiting for transfers between devices, send(): return lax.ppermute(value, 'member', shift_perm(grid, axis, shift))  42.9 us
    all_to_all x1, starting transfers between devices, on_device(): lax.all_to_all(summed, 'group', split_axis=0, concat_axis=0, tiled=True)  17 us
    pallas_call x1, Pallas kernels, attend_local(): pl.pallas_call(kernel, out_shape=[jax.ShapeDtypeStruct((rows, cands, widt...  12.5 us
    unnamed x27, local copies, waits for them, and re-layouts  10.5 us
    all_to_all x1, waiting for transfers between devices, on_device(): lax.all_to_all(summed, 'group', split_axis=0, concat_axis=0, tiled=True)  6.05 us
    all_to_all x1, starting transfers between devices, on_device(): lax.all_to_all(q_out, 'group', split_axis=0, concat_axis=0, tiled=True)  5.97 us
    gather x1, local copies, waits for them, and re-layouts, on_device(): kv_slots = kv_cache[chosen]  4.98 us
  transfers between devices with their start and end apart: 34, of which 11 were waited for; matrix products, arithmetic and copies ran while one was open for 18% of the time, Pallas kernels for 0%

profile of v14, /device:TPU:1, one launch (start us, length us, event | category | flops | bytes accessed | tf_op | source)
XLA Modules:
  0.0 184.4 jit_solution(11013608970461239583)
XLA Ops:
  0.0 1.0 fusion.36
  3.1 1.2 convert_reduce_fusion
  4.4 1.3 fusion.8
  5.9 2.7 %fusion.19 = bf16[32,8,1024]{2,1,0:T(8,128)(2,1)S(1)} fusion(bf16[1024,2048]{1,0:T(8,128)(2,1)} %param.12, bf16[32,8,1024]{2,1,0:T(8,128)(2,1)} %param.7, f32[32,8]{1,0:T(8,128)S(1)} %copy.37, f32[32,8]{1,0:T(8,128)S(1)} %copy.35), kind=kOutput, calls=%fused_computation.39 | convolution fusion | flops 539492352 | bytes 3147776 | tf_op jit(solution)/shard_map/dot_general | solution.py:207
  9.5 0.9 broadcast_select_fusion
  10.4 6.0 %all-to-all-start = ((bf16[8,32,1024]{2,1,0:T(8,128)(2,1)}), bf16[8,32,1024]{2,1,0:T(8,128)(2,1)S(1)}, u32[]{:S(2)}, u32[]{:S(2)}) async-start(bf16[8,32,1024]{2,1,0:T(8,128)(2,1)} %broadcast_select_fusion), calls=%async_computation | async-start | bytes 1048576 | tf_op jit(solution)/shard_map/all_to_all | solution.py:212
  18.4 5.0 %gather_fusion.6 = bf16[8,128,2048]{2,1,0:T(8,128)(2,1)} fusion(bf16[8,128,2048]{2,1,0:T(8,128)(2,1)} %param.8, s32[1024]{0:T(1024)S(1)} %get-tuple-element.64), kind=kCustom, calls=%fused_computation.6 | custom fusion | bytes 8388640 | tf_op jit(solution)/shard_map/gather | solution.py:213
  23.5 2.2 %all-to-all-done = bf16[8,32,1024]{2,1,0:T(8,128)(2,1)S(1)} async-done(((bf16[8,32,1024]{2,1,0:T(8,128)(2,1)}), bf16[8,32,1024]{2,1,0:T(8,128)(2,1)S(1)}, u32[]{:S(2)}, u32[]{:S(2)}) %all-to-all-start) | async-done | bytes 524320 | tf_op jit(solution)/shard_map/all_to_all | solution.py:212
  25.7 0.9 constant_dynamic-update-slice_fusion.18
  26.6 3.7 %collective-permute-start.8 = (bf16[4,32,1024]{2,1,0:T(8,128)(2,1)S(1)}, bf16[4,32,1024]{2,1,0:T(8,128)(2,1)S(1)}, u32[]{:S(2)}, u32[]{:S(2)}) collective-permute-start(bf16[4,32,1024]{2,1,0:T(8,128)(2,1)S(1)} %get-tuple-element.39), channel_id=1, source_target_pairs={{0,12},{1,13},{2,14},{3,15},{4,0},{5,1},{6,2},{7,3},{8,4},{9,5},{1... | collective-permute-start | bytes 786440 | tf_op jit(solution)/shard_map/ppermute | solution.py:112
  30.4 2.5 %collective-permute-start = (bf16[4,32,1024]{2,1,0:T(8,128)(2,1)S(1)}, bf16[4,32,1024]{2,1,0:T(8,128)(2,1)S(1)}, u32[]{:S(2)}, u32[]{:S(2)}) collective-permute-start(bf16[4,32,1024]{2,1,0:T(8,128)(2,1)S(1)} %get-tuple-element.40), channel_id=1, source_target_pairs={{0,3},{1,0},{2,1},{3,2},{4,7},{5,4},{6,5},{7,6},{8,11},{9,8},{10,9... | collective-permute-start | bytes 786440 | tf_op jit(solution)/shard_map/ppermute | solution.py:112
  32.8 3.4 %multiply_convert_fusion = (bf16[4,128,1024]{2,1,0:T(8,128)(2,1)}, bf16[4,128,1024]{2,1,0:T(8,128)(2,1)}) fusion(bf16[8,128,2048]{2,1,0:T(8,128)(2,1)} %gather_fusion.6, f32[4,128]{1,0:T(4,128)S(1)} %get-tuple-element.59, f32[4,128]{1,0:T(4,128)S(1)} %get-tuple-element.60), kind=kLoop, calls=%fused_computation.16 | loop fusion | flops 3145728 | bytes 4198400 | tf_op jit(solution)/shard_map/convert_element_type | solution.py:69
  36.3 1.9 %collective-permute-done.9 = bf16[4,32,1024]{2,1,0:T(8,128)(2,1)S(1)} collective-permute-done((bf16[4,32,1024]{2,1,0:T(8,128)(2,1)S(1)}, bf16[4,32,1024]{2,1,0:T(8,128)(2,1)S(1)}, u32[]{:S(2)}, u32[]{:S(2)}) %collective-permute-start.9) | collective-permute-done | bytes 262176 | tf_op jit(solution)/shard_map/ppermute | solution.py:112
  38.3 2.7 %collective-permute-start.11 = (bf16[4,16,1024]{2,1,0:T(8,128)(2,1)S(1)}, bf16[4,16,1024]{2,1,0:T(8,128)(2,1)S(1)}, u32[]{:S(2)}, u32[]{:S(2)}) collective-permute-start(bf16[4,16,1024]{2,1,0:T(8,128)(2,1)S(1)} %slice.205), channel_id=1, source_target_pairs={{0,12},{1,13},{2,14},{3,15},{4,0},{5,1},{6,2},{7,3},{8,4},{9,5},{1... | collective-permute-start | bytes 393224 | tf_op jit(solution)/shard_map/ppermute | solution.py:112
  41.0 1.3 collective-permute-start.2
  42.3 1.5 collective-permute-start.3
  43.9 0.8 constant_dynamic-update-slice_fusion.17
  44.6 0.8 constant_dynamic-update-slice_fusion.3
  46.7 0.7 constant_dynamic-update-slice_fusion.14
  47.5 1.3 collective-permute-start.12
  48.9 0.7 constant_dynamic-update-slice_fusion.2
  49.6 0.7 constant_dynamic-update-slice_fusion.1
  50.3 0.7 constant_dynamic-update-slice_fusion
  51.0 1.8 collective-permute-start.4
  52.9 2.5 %fusion.52 = (bf16[4,128,2048]{2,1,0:T(8,128)(2,1)}, bf16[4,128,2048]{2,1,0:T(8,128)(2,1)}) fusion(bf16[8,128,2048]{2,1,0:T(8,128)(2,1)S(1)} %copy-done.3), kind=kLoop, calls=%fused_computation.155 | loop fusion | bytes 8388608 | tf_op jit(solution)/shard_map/slice | solution.py:221
  55.4 15.8 %collective-permute-done.13 = bf16[4,128,1024]{2,1,0:T(8,128)(2,1)S(1)} collective-permute-done((bf16[4,128,1024]{2,1,0:T(8,128)(2,1)S(1)}, bf16[4,128,1024]{2,1,0:T(8,128)(2,1)S(1)}, u32[]{:S(2)}, u32[]{:S(2)}) %collective-permute-start.13) | collective-permute-done | bytes 1048608 | tf_op jit(solution)/shard_map/ppermute | solution.py:112
  71.3 2.7 %collective-permute-start.15 = (bf16[4,64,1024]{2,1,0:T(8,128)(2,1)S(1)}, bf16[4,64,1024]{2,1,0:T(8,128)(2,1)S(1)}, u32[]{:S(2)}, u32[]{:S(2)}) collective-permute-start(bf16[4,64,1024]{2,1,0:T(8,128)(2,1)S(1)} %slice.207), channel_id=1, source_target_pairs={{0,3},{1,0},{2,1},{3,2},{4,7},{5,4},{6,5},{7,6},{8,11},{9,8},{10,9... | collective-permute-start | bytes 1572872 | tf_op jit(solution)/shard_map/ppermute | solution.py:112
  74.9 2.9 %collective-permute-start.7 = (bf16[4,64,1024]{2,1,0:T(8,128)(2,1)S(1)}, bf16[4,64,1024]{2,1,0:T(8,128)(2,1)S(1)}, u32[]{:S(2)}, u32[]{:S(2)}) collective-permute-start(bf16[4,64,1024]{2,1,0:T(8,128)(2,1)S(1)} %slice.200), channel_id=1, source_target_pairs={{0,12},{1,13},{2,14},{3,15},{4,0},{5,1},{6,2},{7,3},{8,4},{9,5},{1... | collective-permute-start | bytes 1572872 | tf_op jit(solution)/shard_map/ppermute | solution.py:112
  77.8 1.1 constant_dynamic-update-slice_fusion.22
  78.9 1.0 constant_dynamic-update-slice_fusion.8
  79.9 1.7 collective-permute-done.14
  81.6 0.8 constant_dynamic-update-slice_fusion.21
  82.4 0.8 constant_dynamic-update-slice_fusion.20
  83.3 1.8 %collective-permute-done.6 = bf16[4,64,1024]{2,1,0:T(8,128)(2,1)S(1)} collective-permute-done((bf16[4,64,1024]{2,1,0:T(8,128)(2,1)S(1)}, bf16[4,64,1024]{2,1,0:T(8,128)(2,1)S(1)}, u32[]{:S(2)}, u32[]{:S(2)}) %collective-permute-start.6) | collective-permute-done | bytes 524320 | tf_op jit(solution)/shard_map/ppermute | solution.py:112
  85.1 0.8 constant_dynamic-update-slice_fusion.7
  85.9 1.0 constant_dynamic-update-slice_fusion.19.refs_3_
  87.0 0.8 constant_dynamic-update-slice_fusion.6
  87.8 1.1 constant_dynamic-update-slice_fusion.5.refs_0_
  88.9 12.5 %shard_map.73 = (bf16[4,512,1024]{2,1,0:T(8,128)(2,1)}, bf16[4,512,1024]{2,1,0:T(8,128)(2,1)}) custom-call(s32[8]{0:T(128)} %pad_add_fusion.n_live_ref, bf16[4,512,1024]{2,1,0:T(8,128)(2,1)} %constant_dynamic-update-slice_fusion.5.refs_0_, bf16[4,128,2048]{2,1,0:T(8,128)(2,1)} %get-tuple-element.26.refs_1_, bf16[4,128,1024]{2,1,0:T(8,128)(2,1)} %get-tuple-element.24.refs_2_, ...), custom_call_target="tpu_custom_call" | custom-call | flops 2147483648 | bytes 20971520 | tf_op jit(solution)/shard_map/pallas_call | solution.py:81
  101.4 1.5 fusion.50
  102.9 2.7 %collective-permute-start.18 = (bf16[4,64,1024]{2,1,0:T(8,128)(2,1)S(1)}, bf16[4,64,1024]{2,1,0:T(8,128)(2,1)S(1)}, u32[]{:S(2)}, u32[]{:S(2)}) collective-permute-start(bf16[4,64,1024]{2,1,0:T(8,128)(2,1)S(1)} %get-tuple-element.18), channel_id=1, source_target_pairs={{0,12},{1,13},{2,14},{3,15},{4,0},{5,1},{6,2},{7,3},{8,4},{9,5},{1... | collective-permute-start | bytes 1572872 | tf_op jit(solution)/shard_map/ppermute | solution.py:112
  105.6 1.3 fusion.51
  107.1 2.5 %collective-permute-start.26 = (bf16[4,64,1024]{2,1,0:T(8,128)(2,1)S(1)}, bf16[4,64,1024]{2,1,0:T(8,128)(2,1)S(1)}, u32[]{:S(2)}, u32[]{:S(2)}) collective-permute-start(bf16[4,64,1024]{2,1,0:T(8,128)(2,1)S(1)} %get-tuple-element.22), channel_id=1, source_target_pairs={{0,3},{1,0},{2,1},{3,2},{4,7},{5,4},{6,5},{7,6},{8,11},{9,8},{10,9... | collective-permute-start | bytes 1572872 | tf_op jit(solution)/shard_map/ppermute | solution.py:112
  109.6 2.5 %collective-permute-done.16 = bf16[4,64,1024]{2,1,0:T(8,128)(2,1)S(1)} collective-permute-done((bf16[4,64,1024]{2,1,0:T(8,128)(2,1)S(1)}, bf16[4,64,1024]{2,1,0:T(8,128)(2,1)S(1)}, u32[]{:S(2)}, u32[]{:S(2)}) %collective-permute-start.16) | collective-permute-done | bytes 524320 | tf_op jit(solution)/shard_map/ppermute | solution.py:112
  112.9 2.7 %collective-permute-start.19 = (bf16[4,128,1024]{2,1,0:T(8,128)(2,1)S(1)}, bf16[4,128,1024]{2,1,0:T(8,128)(2,1)S(1)}, u32[]{:S(2)}, u32[]{:S(2)}) collective-permute-start(bf16[4,128,1024]{2,1,0:T(8,128)(2,1)S(1)} %get-tuple-element.16), channel_id=1, source_target_pairs={{0,12},{1,13},{2,14},{3,15},{4,0},{5,1},{6,2},{7,3},{8,4},{9,5},{1... | collective-permute-start | bytes 3145736 | tf_op jit(solution)/shard_map/ppermute | solution.py:112
  115.7 0.8 collective-permute-done.24
  116.5 0.7 add_convert_fusion.1
  117.3 2.7 %collective-permute-start.27 = (bf16[4,128,1024]{2,1,0:T(8,128)(2,1)S(1)}, bf16[4,128,1024]{2,1,0:T(8,128)(2,1)S(1)}, u32[]{:S(2)}, u32[]{:S(2)}) collective-permute-start(bf16[4,128,1024]{2,1,0:T(8,128)(2,1)S(1)} %get-tuple-element.20), channel_id=1, source_target_pairs={{0,3},{1,0},{2,1},{3,2},{4,7},{5,4},{6,5},{7,6},{8,11},{9,8},{10,9... | collective-permute-start | bytes 3145736 | tf_op jit(solution)/shard_map/ppermute | solution.py:112
  120.0 13.5 %collective-permute-done.17 = bf16[4,128,1024]{2,1,0:T(8,128)(2,1)S(1)} collective-permute-done((bf16[4,128,1024]{2,1,0:T(8,128)(2,1)S(1)}, bf16[4,128,1024]{2,1,0:T(8,128)(2,1)S(1)}, u32[]{:S(2)}, u32[]{:S(2)}) %collective-permute-start.17) | collective-permute-done | bytes 1048608 | tf_op jit(solution)/shard_map/ppermute | solution.py:112
  133.6 0.7 fusion.48
  134.5 2.5 %collective-permute-start.22 = (bf16[4,16,1024]{2,1,0:T(8,128)(2,1)S(1)}, bf16[4,16,1024]{2,1,0:T(8,128)(2,1)S(1)}, u32[]{:S(2)}, u32[]{:S(2)}) collective-permute-start(bf16[4,16,1024]{2,1,0:T(8,128)(2,1)S(1)} %get-tuple-element.32), channel_id=1, source_target_pairs={{0,3},{1,0},{2,1},{3,2},{4,7},{5,4},{6,5},{7,6},{8,11},{9,8},{10,9... | collective-permute-start | bytes 393224 | tf_op jit(solution)/shard_map/ppermute | solution.py:112
  137.0 0.9 collective-permute-done.25
  137.9 0.7 fusion.49
  138.7 2.7 %collective-permute-start.30 = (bf16[4,16,1024]{2,1,0:T(8,128)(2,1)S(1)}, bf16[4,16,1024]{2,1,0:T(8,128)(2,1)S(1)}, u32[]{:S(2)}, u32[]{:S(2)}) collective-permute-start(bf16[4,16,1024]{2,1,0:T(8,128)(2,1)S(1)} %get-tuple-element.34), channel_id=1, source_target_pairs={{0,12},{1,13},{2,14},{3,15},{4,0},{5,1},{6,2},{7,3},{8,4},{9,5},{1... | collective-permute-start | bytes 393224 | tf_op jit(solution)/shard_map/ppermute | solution.py:112
  141.6 2.9 %collective-permute-start.23 = (bf16[4,32,1024]{2,1,0:T(8,128)(2,1)S(1)}, bf16[4,32,1024]{2,1,0:T(8,128)(2,1)S(1)}, u32[]{:S(2)}, u32[]{:S(2)}) collective-permute-start(bf16[4,32,1024]{2,1,0:T(8,128)(2,1)S(1)} %get-tuple-element.28), channel_id=1, source_target_pairs={{0,3},{1,0},{2,1},{3,2},{4,7},{5,4},{6,5},{7,6},{8,11},{9,8},{10,9... | collective-permute-start | bytes 786440 | tf_op jit(solution)/shard_map/ppermute | solution.py:112
  144.7 2.7 %collective-permute-start.31 = (bf16[4,32,1024]{2,1,0:T(8,128)(2,1)S(1)}, bf16[4,32,1024]{2,1,0:T(8,128)(2,1)S(1)}, u32[]{:S(2)}, u32[]{:S(2)}) collective-permute-start(bf16[4,32,1024]{2,1,0:T(8,128)(2,1)S(1)} %get-tuple-element.30), channel_id=1, source_target_pairs={{0,12},{1,13},{2,14},{3,15},{4,0},{5,1},{6,2},{7,3},{8,4},{9,5},{1... | collective-permute-start | bytes 786440 | tf_op jit(solution)/shard_map/ppermute | solution.py:112
  147.4 3.9 %collective-permute-done.21 = bf16[4,32,1024]{2,1,0:T(8,128)(2,1)S(1)} collective-permute-done((bf16[4,32,1024]{2,1,0:T(8,128)(2,1)S(1)}, bf16[4,32,1024]{2,1,0:T(8,128)(2,1)S(1)}, u32[]{:S(2)}, u32[]{:S(2)}) %collective-permute-start.21) | collective-permute-done | bytes 262176 | tf_op jit(solution)/shard_map/ppermute | solution.py:112
  151.5 0.8 pad_maximum_fusion
  152.4 17.0 %all-to-all-start.1 = ((bf16[8,32,1024]{2,1,0:T(8,128)(2,1)}), bf16[8,32,1024]{2,1,0:T(8,128)(2,1)}, u32[]{:S(2)}, u32[]{:S(2)}) async-start(bf16[8,32,1024]{2,1,0:T(8,128)(2,1)} %pad_maximum_fusion), calls=%async_computation.1 | async-start | bytes 1048576 | tf_op jit(solution)/shard_map/all_to_all | solution.py:231
  169.4 3.4 %multiply_bitcast_fusion = f32[32,8,1024]{2,1,0:T(8,128)} fusion(bf16[1024,2048]{1,0:T(8,128)(2,1)} %param.12, bf16[32,8,1024]{2,1,0:T(8,128)(2,1)S(1)} %copy-done.6, f32[32,8]{1,0:T(8,128)S(1)} %copy.37, f32[32,8]{1,0:T(8,128)S(1)} %copy.35), kind=kOutput, calls=%fused_computation.37 | convolution fusion | flops 538968064 | bytes 3672064 | tf_op jit(solution)/shard_map/dot_general | solution.py:234
  172.8 6.0 %all-to-all-done.1 = bf16[8,32,1024]{2,1,0:T(8,128)(2,1)} async-done(((bf16[8,32,1024]{2,1,0:T(8,128)(2,1)}), bf16[8,32,1024]{2,1,0:T(8,128)(2,1)}, u32[]{:S(2)}, u32[]{:S(2)}) %all-to-all-start.1) | async-done | bytes 524320 | tf_op jit(solution)/shard_map/all_to_all | solution.py:231
  178.8 1.6 gather_fusion.7
  180.9 1.9 %fusion.14 = bf16[32,8,1024]{2,0,1:T(8,128)(2,1)S(1)} fusion(bf16[8,32,1024]{2,1,0:T(8,128)(2,1)S(1)} %gather_fusion.7, f32[32,8,1024]{2,1,0:T(8,128)} %multiply_bitcast_fusion, f32[32,8]{0,1:T(8,128)S(1)} %add_rsqrt_fusion, f32[32,8]{0,1:T(8,128)S(1)} %broadcast_multiply_fusion), kind=kLoop, calls=%fused_computation.36 | loop fusion | flops 1310720 | bytes 2099200 | tf_op jit(solution)/shard_map/convert_element_type | solution.py:236
  182.8 1.6 fusion.7
  (113 shorter events, 10.6 us)
Async XLA Ops:
  0.0 182.8 %copy-start = (bf16[1024,1024]{1,0:T(8,128)(2,1)S(1)}, bf16[1024,1024]{1,0:T(8,128)(2,1)}, u32[]{:S(2)}) copy-start(bf16[1024,1024]{1,0:T(8,128)(2,1)} %param.13) | copy-start | bytes 6291460
  8.6 7.8 %copy-start.1 = (s32[64]{0:T(128)S(1)}, s32[64]{0:T(128)}, u32[]{:S(2)}) copy-start(s32[64]{0:T(128)} %param.9) | copy-start | bytes 772
  8.6 8.4 %copy-start.2 = (s32[64]{0:T(128)S(1)}, s32[64]{0:T(128)}, u32[]{:S(2)}) copy-start(s32[64]{0:T(128)} %param.11) | copy-start | bytes 772
  10.4 15.3 %all-to-all-start = ((bf16[8,32,1024]{2,1,0:T(8,128)(2,1)}), bf16[8,32,1024]{2,1,0:T(8,128)(2,1)S(1)}, u32[]{:S(2)}, u32[]{:S(2)}) async-start(bf16[8,32,1024]{2,1,0:T(8,128)(2,1)} %broadcast_select_fusion), calls=%async_computation | async-start | bytes 1048576 | tf_op jit(solution)/shard_map/all_to_all | solution.py:212
  26.6 11.7 %collective-permute-start.8 = (bf16[4,32,1024]{2,1,0:T(8,128)(2,1)S(1)}, bf16[4,32,1024]{2,1,0:T(8,128)(2,1)S(1)}, u32[]{:S(2)}, u32[]{:S(2)}) collective-permute-start(bf16[4,32,1024]{2,1,0:T(8,128)(2,1)S(1)} %get-tuple-element.39), channel_id=1, source_target_pairs={{0,12},{1,13},{2,14},{3,15},{4,0},{5,1},{6,2},{7,3},{8,4},{9,5},{1... | collective-permute-start | bytes 786440 | tf_op jit(solution)/shard_map/ppermute | solution.py:112
  30.4 7.8 %collective-permute-start.9 = (bf16[4,32,1024]{2,1,0:T(8,128)(2,1)S(1)}, bf16[4,32,1024]{2,1,0:T(8,128)(2,1)S(1)}, u32[]{:S(2)}, u32[]{:S(2)}) collective-permute-start(bf16[4,32,1024]{2,1,0:T(8,128)(2,1)S(1)} %get-tuple-element.39), channel_id=1, source_target_pairs={{0,4},{1,5},{2,6},{3,7},{4,8},{5,9},{6,10},{7,11},{8,12},{9,13},{1... | collective-permute-start | bytes 786440 | tf_op jit(solution)/shard_map/ppermute | solution.py:112
  30.4 12.0 %collective-permute-start = (bf16[4,32,1024]{2,1,0:T(8,128)(2,1)S(1)}, bf16[4,32,1024]{2,1,0:T(8,128)(2,1)S(1)}, u32[]{:S(2)}, u32[]{:S(2)}) collective-permute-start(bf16[4,32,1024]{2,1,0:T(8,128)(2,1)S(1)} %get-tuple-element.40), channel_id=1, source_target_pairs={{0,3},{1,0},{2,1},{3,2},{4,7},{5,4},{6,5},{7,6},{8,11},{9,8},{10,9... | collective-permute-start | bytes 786440 | tf_op jit(solution)/shard_map/ppermute | solution.py:112
  32.8 8.2 %collective-permute-start.1 = (bf16[4,32,1024]{2,1,0:T(8,128)(2,1)S(1)}, bf16[4,32,1024]{2,1,0:T(8,128)(2,1)S(1)}, u32[]{:S(2)}, u32[]{:S(2)}) collective-permute-start(bf16[4,32,1024]{2,1,0:T(8,128)(2,1)S(1)} %get-tuple-element.40), channel_id=1, source_target_pairs={{0,1},{1,2},{2,3},{3,0},{4,5},{5,6},{6,7},{7,4},{8,9},{9,10},{10,1... | collective-permute-start | bytes 786440 | tf_op jit(solution)/shard_map/ppermute | solution.py:112
  32.8 20.1 %copy-start.3 = (bf16[8,128,2048]{2,1,0:T(8,128)(2,1)S(1)}, bf16[8,128,2048]{2,1,0:T(8,128)(2,1)}, u32[]{:S(2)}) copy-start(bf16[8,128,2048]{2,1,0:T(8,128)(2,1)} %gather_fusion.6) | copy-start | bytes 12582916
  38.2 7.2 %collective-permute-start.10 = (bf16[4,16,1024]{2,1,0:T(8,128)(2,1)S(1)}, bf16[4,16,1024]{2,1,0:T(8,128)(2,1)S(1)}, u32[]{:S(2)}, u32[]{:S(2)}) collective-permute-start(bf16[4,16,1024]{2,1,0:T(8,128)(2,1)S(1)} %slice.204), channel_id=1, source_target_pairs={{0,4},{1,5},{2,6},{3,7},{4,8},{5,9},{6,10},{7,11},{8,12},{9,13},{1... | collective-permute-start | bytes 393224 | tf_op jit(solution)/shard_map/ppermute | solution.py:112
  38.3 7.7 %collective-permute-start.11 = (bf16[4,16,1024]{2,1,0:T(8,128)(2,1)S(1)}, bf16[4,16,1024]{2,1,0:T(8,128)(2,1)S(1)}, u32[]{:S(2)}, u32[]{:S(2)}) collective-permute-start(bf16[4,16,1024]{2,1,0:T(8,128)(2,1)S(1)} %slice.205), channel_id=1, source_target_pairs={{0,12},{1,13},{2,14},{3,15},{4,0},{5,1},{6,2},{7,3},{8,4},{9,5},{1... | collective-permute-start | bytes 393224 | tf_op jit(solution)/shard_map/ppermute | solution.py:112
  41.0 7.9 %collective-permute-start.2 = (bf16[4,16,1024]{2,1,0:T(8,128)(2,1)S(1)}, bf16[4,16,1024]{2,1,0:T(8,128)(2,1)S(1)}, u32[]{:S(2)}, u32[]{:S(2)}) collective-permute-start(bf16[4,16,1024]{2,1,0:T(8,128)(2,1)S(1)} %slice.197), channel_id=1, source_target_pairs={{0,1},{1,2},{2,3},{3,0},{4,5},{5,6},{6,7},{7,4},{8,9},{9,10},{10,1... | collective-permute-start | bytes 393224 | tf_op jit(solution)/shard_map/ppermute | solution.py:112
  42.3 7.3 %collective-permute-start.3 = (bf16[4,16,1024]{2,1,0:T(8,128)(2,1)S(1)}, bf16[4,16,1024]{2,1,0:T(8,128)(2,1)S(1)}, u32[]{:S(2)}, u32[]{:S(2)}) collective-permute-start(bf16[4,16,1024]{2,1,0:T(8,128)(2,1)S(1)} %slice.198), channel_id=1, source_target_pairs={{0,3},{1,0},{2,1},{3,2},{4,7},{5,4},{6,5},{7,6},{8,11},{9,8},{10,9... | collective-permute-start | bytes 393224 | tf_op jit(solution)/shard_map/ppermute | solution.py:112
  47.5 23.8 %collective-permute-start.12 = (bf16[4,128,1024]{2,1,0:T(8,128)(2,1)S(1)}, bf16[4,128,1024]{2,1,0:T(8,128)(2,1)S(1)}, u32[]{:S(2)}, u32[]{:S(2)}) collective-permute-start(bf16[4,128,1024]{2,1,0:T(8,128)(2,1)S(1)} %get-tuple-element.41), channel_id=1, source_target_pairs={{0,3},{1,0},{2,1},{3,2},{4,7},{5,4},{6,5},{7,6},{8,11},{9,8},{10,9... | collective-permute-start | bytes 3145736 | tf_op jit(solution)/shard_map/ppermute | solution.py:112
  48.7 22.4 %collective-permute-start.13 = (bf16[4,128,1024]{2,1,0:T(8,128)(2,1)S(1)}, bf16[4,128,1024]{2,1,0:T(8,128)(2,1)S(1)}, u32[]{:S(2)}, u32[]{:S(2)}) collective-permute-start(bf16[4,128,1024]{2,1,0:T(8,128)(2,1)S(1)} %get-tuple-element.41), channel_id=1, source_target_pairs={{0,1},{1,2},{2,3},{3,0},{4,5},{5,6},{6,7},{7,4},{8,9},{9,10},{10,1... | collective-permute-start | bytes 3145736 | tf_op jit(solution)/shard_map/ppermute | solution.py:112
  51.0 23.8 %collective-permute-start.4 = (bf16[4,128,1024]{2,1,0:T(8,128)(2,1)S(1)}, bf16[4,128,1024]{2,1,0:T(8,128)(2,1)S(1)}, u32[]{:S(2)}, u32[]{:S(2)}) collective-permute-start(bf16[4,128,1024]{2,1,0:T(8,128)(2,1)S(1)} %get-tuple-element.45), channel_id=1, source_target_pairs={{0,12},{1,13},{2,14},{3,15},{4,0},{5,1},{6,2},{7,3},{8,4},{9,5},{1... | collective-permute-start | bytes 3145736 | tf_op jit(solution)/shard_map/ppermute | solution.py:112
  52.8 21.9 %collective-permute-start.5 = (bf16[4,128,1024]{2,1,0:T(8,128)(2,1)S(1)}, bf16[4,128,1024]{2,1,0:T(8,128)(2,1)S(1)}, u32[]{:S(2)}, u32[]{:S(2)}) collective-permute-start(bf16[4,128,1024]{2,1,0:T(8,128)(2,1)S(1)} %get-tuple-element.45), channel_id=1, source_target_pairs={{0,4},{1,5},{2,6},{3,7},{4,8},{5,9},{6,10},{7,11},{8,12},{9,13},{1... | collective-permute-start | bytes 3145736 | tf_op jit(solution)/shard_map/ppermute | solution.py:112
  71.2 10.4 %collective-permute-start.14 = (bf16[4,64,1024]{2,1,0:T(8,128)(2,1)S(1)}, bf16[4,64,1024]{2,1,0:T(8,128)(2,1)S(1)}, u32[]{:S(2)}, u32[]{:S(2)}) collective-permute-start(bf16[4,64,1024]{2,1,0:T(8,128)(2,1)S(1)} %slice.206), channel_id=1, source_target_pairs={{0,1},{1,2},{2,3},{3,0},{4,5},{5,6},{6,7},{7,4},{8,9},{9,10},{10,1... | collective-permute-start | bytes 1572872 | tf_op jit(solution)/shard_map/ppermute | solution.py:112
  71.3 11.1 %collective-permute-start.15 = (bf16[4,64,1024]{2,1,0:T(8,128)(2,1)S(1)}, bf16[4,64,1024]{2,1,0:T(8,128)(2,1)S(1)}, u32[]{:S(2)}, u32[]{:S(2)}) collective-permute-start(bf16[4,64,1024]{2,1,0:T(8,128)(2,1)S(1)} %slice.207), channel_id=1, source_target_pairs={{0,3},{1,0},{2,1},{3,2},{4,7},{5,4},{6,5},{7,6},{8,11},{9,8},{10,9... | collective-permute-start | bytes 1572872 | tf_op jit(solution)/shard_map/ppermute | solution.py:112
  74.8 10.3 %collective-permute-start.6 = (bf16[4,64,1024]{2,1,0:T(8,128)(2,1)S(1)}, bf16[4,64,1024]{2,1,0:T(8,128)(2,1)S(1)}, u32[]{:S(2)}, u32[]{:S(2)}) collective-permute-start(bf16[4,64,1024]{2,1,0:T(8,128)(2,1)S(1)} %slice.199), channel_id=1, source_target_pairs={{0,4},{1,5},{2,6},{3,7},{4,8},{5,9},{6,10},{7,11},{8,12},{9,13},{1... | collective-permute-start | bytes 1572872 | tf_op jit(solution)/shard_map/ppermute | solution.py:112
  74.9 12.1 %collective-permute-start.7 = (bf16[4,64,1024]{2,1,0:T(8,128)(2,1)S(1)}, bf16[4,64,1024]{2,1,0:T(8,128)(2,1)S(1)}, u32[]{:S(2)}, u32[]{:S(2)}) collective-permute-start(bf16[4,64,1024]{2,1,0:T(8,128)(2,1)S(1)} %slice.200), channel_id=1, source_target_pairs={{0,12},{1,13},{2,14},{3,15},{4,0},{5,1},{6,2},{7,3},{8,4},{9,5},{1... | collective-permute-start | bytes 1572872 | tf_op jit(solution)/shard_map/ppermute | solution.py:112
  101.4 10.8 %copy-start.5 = (bf16[4,512,1024]{2,1,0:T(8,128)(2,1)S(1)}, bf16[4,512,1024]{2,1,0:T(8,128)(2,1)}, u32[]{:S(2)}) copy-start(bf16[4,512,1024]{2,1,0:T(8,128)(2,1)} %get-tuple-element.7) | copy-start | bytes 12582916
  102.8 13.7 %copy-start.4 = (bf16[4,512,1024]{2,1,0:T(8,128)(2,1)S(1)}, bf16[4,512,1024]{2,1,0:T(8,128)(2,1)}, u32[]{:S(2)}) copy-start(bf16[4,512,1024]{2,1,0:T(8,128)(2,1)} %get-tuple-element.8) | copy-start | bytes 12582916
  102.8 9.3 %collective-permute-start.16 = (bf16[4,64,1024]{2,1,0:T(8,128)(2,1)S(1)}, bf16[4,64,1024]{2,1,0:T(8,128)(2,1)S(1)}, u32[]{:S(2)}, u32[]{:S(2)}) collective-permute-start(bf16[4,64,1024]{2,1,0:T(8,128)(2,1)S(1)} %get-tuple-element.17), channel_id=1, source_target_pairs={{0,4},{1,5},{2,6},{3,7},{4,8},{5,9},{6,10},{7,11},{8,12},{9,13},{1... | collective-permute-start | bytes 1572872 | tf_op jit(solution)/shard_map/ppermute | solution.py:112
  102.9 9.2 %collective-permute-start.18 = (bf16[4,64,1024]{2,1,0:T(8,128)(2,1)S(1)}, bf16[4,64,1024]{2,1,0:T(8,128)(2,1)S(1)}, u32[]{:S(2)}, u32[]{:S(2)}) collective-permute-start(bf16[4,64,1024]{2,1,0:T(8,128)(2,1)S(1)} %get-tuple-element.18), channel_id=1, source_target_pairs={{0,12},{1,13},{2,14},{3,15},{4,0},{5,1},{6,2},{7,3},{8,4},{9,5},{1... | collective-permute-start | bytes 1572872 | tf_op jit(solution)/shard_map/ppermute | solution.py:112
  106.9 9.6 %collective-permute-start.24 = (bf16[4,64,1024]{2,1,0:T(8,128)(2,1)S(1)}, bf16[4,64,1024]{2,1,0:T(8,128)(2,1)S(1)}, u32[]{:S(2)}, u32[]{:S(2)}) collective-permute-start(bf16[4,64,1024]{2,1,0:T(8,128)(2,1)S(1)} %get-tuple-element.21), channel_id=1, source_target_pairs={{0,1},{1,2},{2,3},{3,0},{4,5},{5,6},{6,7},{7,4},{8,9},{9,10},{10,1... | collective-permute-start | bytes 1572872 | tf_op jit(solution)/shard_map/ppermute | solution.py:112
  107.1 9.4 %collective-permute-start.26 = (bf16[4,64,1024]{2,1,0:T(8,128)(2,1)S(1)}, bf16[4,64,1024]{2,1,0:T(8,128)(2,1)S(1)}, u32[]{:S(2)}, u32[]{:S(2)}) collective-permute-start(bf16[4,64,1024]{2,1,0:T(8,128)(2,1)S(1)} %get-tuple-element.22), channel_id=1, source_target_pairs={{0,3},{1,0},{2,1},{3,2},{4,7},{5,4},{6,5},{7,6},{8,11},{9,8},{10,9... | collective-permute-start | bytes 1572872 | tf_op jit(solution)/shard_map/ppermute | solution.py:112
  112.8 20.7 %collective-permute-start.17 = (bf16[4,128,1024]{2,1,0:T(8,128)(2,1)S(1)}, bf16[4,128,1024]{2,1,0:T(8,128)(2,1)S(1)}, u32[]{:S(2)}, u32[]{:S(2)}) collective-permute-start(bf16[4,128,1024]{2,1,0:T(8,128)(2,1)S(1)} %get-tuple-element.15), channel_id=1, source_target_pairs={{0,4},{1,5},{2,6},{3,7},{4,8},{5,9},{6,10},{7,11},{8,12},{9,13},{1... | collective-permute-start | bytes 3145736 | tf_op jit(solution)/shard_map/ppermute | solution.py:112
  112.9 20.6 %collective-permute-start.19 = (bf16[4,128,1024]{2,1,0:T(8,128)(2,1)S(1)}, bf16[4,128,1024]{2,1,0:T(8,128)(2,1)S(1)}, u32[]{:S(2)}, u32[]{:S(2)}) collective-permute-start(bf16[4,128,1024]{2,1,0:T(8,128)(2,1)S(1)} %get-tuple-element.16), channel_id=1, source_target_pairs={{0,12},{1,13},{2,14},{3,15},{4,0},{5,1},{6,2},{7,3},{8,4},{9,5},{1... | collective-permute-start | bytes 3145736 | tf_op jit(solution)/shard_map/ppermute | solution.py:112
  117.2 20.7 %collective-permute-start.25 = (bf16[4,128,1024]{2,1,0:T(8,128)(2,1)S(1)}, bf16[4,128,1024]{2,1,0:T(8,128)(2,1)S(1)}, u32[]{:S(2)}, u32[]{:S(2)}) collective-permute-start(bf16[4,128,1024]{2,1,0:T(8,128)(2,1)S(1)} %get-tuple-element.19), channel_id=1, source_target_pairs={{0,1},{1,2},{2,3},{3,0},{4,5},{5,6},{6,7},{7,4},{8,9},{9,10},{10,1... | collective-permute-start | bytes 3145736 | tf_op jit(solution)/shard_map/ppermute | solution.py:112
  117.3 20.6 %collective-permute-start.27 = (bf16[4,128,1024]{2,1,0:T(8,128)(2,1)S(1)}, bf16[4,128,1024]{2,1,0:T(8,128)(2,1)S(1)}, u32[]{:S(2)}, u32[]{:S(2)}) collective-permute-start(bf16[4,128,1024]{2,1,0:T(8,128)(2,1)S(1)} %get-tuple-element.20), channel_id=1, source_target_pairs={{0,3},{1,0},{2,1},{3,2},{4,7},{5,4},{6,5},{7,6},{8,11},{9,8},{10,9... | collective-permute-start | bytes 3145736 | tf_op jit(solution)/shard_map/ppermute | solution.py:112
  134.3 7.1 %collective-permute-start.20 = (bf16[4,16,1024]{2,1,0:T(8,128)(2,1)S(1)}, bf16[4,16,1024]{2,1,0:T(8,128)(2,1)S(1)}, u32[]{:S(2)}, u32[]{:S(2)}) collective-permute-start(bf16[4,16,1024]{2,1,0:T(8,128)(2,1)S(1)} %get-tuple-element.31), channel_id=1, source_target_pairs={{0,1},{1,2},{2,3},{3,0},{4,5},{5,6},{6,7},{7,4},{8,9},{9,10},{10,1... | collective-permute-start | bytes 393224 | tf_op jit(solution)/shard_map/ppermute | solution.py:112
  134.5 6.9 %collective-permute-start.22 = (bf16[4,16,1024]{2,1,0:T(8,128)(2,1)S(1)}, bf16[4,16,1024]{2,1,0:T(8,128)(2,1)S(1)}, u32[]{:S(2)}, u32[]{:S(2)}) collective-permute-start(bf16[4,16,1024]{2,1,0:T(8,128)(2,1)S(1)} %get-tuple-element.32), channel_id=1, source_target_pairs={{0,3},{1,0},{2,1},{3,2},{4,7},{5,4},{6,5},{7,6},{8,11},{9,8},{10,9... | collective-permute-start | bytes 393224 | tf_op jit(solution)/shard_map/ppermute | solution.py:112
  138.6 5.9 %collective-permute-start.28 = (bf16[4,16,1024]{2,1,0:T(8,128)(2,1)S(1)}, bf16[4,16,1024]{2,1,0:T(8,128)(2,1)S(1)}, u32[]{:S(2)}, u32[]{:S(2)}) collective-permute-start(bf16[4,16,1024]{2,1,0:T(8,128)(2,1)S(1)} %get-tuple-element.33), channel_id=1, source_target_pairs={{0,4},{1,5},{2,6},{3,7},{4,8},{5,9},{6,10},{7,11},{8,12},{9,13},{1... | collective-permute-start | bytes 393224 | tf_op jit(solution)/shard_map/ppermute | solution.py:112
  138.7 5.8 %collective-permute-start.30 = (bf16[4,16,1024]{2,1,0:T(8,128)(2,1)S(1)}, bf16[4,16,1024]{2,1,0:T(8,128)(2,1)S(1)}, u32[]{:S(2)}, u32[]{:S(2)}) collective-permute-start(bf16[4,16,1024]{2,1,0:T(8,128)(2,1)S(1)} %get-tuple-element.34), channel_id=1, source_target_pairs={{0,12},{1,13},{2,14},{3,15},{4,0},{5,1},{6,2},{7,3},{8,4},{9,5},{1... | collective-permute-start | bytes 393224 | tf_op jit(solution)/shard_map/ppermute | solution.py:112
  141.4 28.0 %copy-start.6 = (bf16[32,8,1024]{2,1,0:T(8,128)(2,1)S(1)}, bf16[32,8,1024]{2,1,0:T(8,128)(2,1)}, u32[]{:S(2)}) copy-start(bf16[32,8,1024]{2,1,0:T(8,128)(2,1)} %param.7) | copy-start | bytes 1572868
  141.5 9.8 %collective-permute-start.21 = (bf16[4,32,1024]{2,1,0:T(8,128)(2,1)S(1)}, bf16[4,32,1024]{2,1,0:T(8,128)(2,1)S(1)}, u32[]{:S(2)}, u32[]{:S(2)}) collective-permute-start(bf16[4,32,1024]{2,1,0:T(8,128)(2,1)S(1)} %get-tuple-element.27), channel_id=1, source_target_pairs={{0,1},{1,2},{2,3},{3,0},{4,5},{5,6},{6,7},{7,4},{8,9},{9,10},{10,1... | collective-permute-start | bytes 786440 | tf_op jit(solution)/shard_map/ppermute | solution.py:112
  141.6 9.7 %collective-permute-start.23 = (bf16[4,32,1024]{2,1,0:T(8,128)(2,1)S(1)}, bf16[4,32,1024]{2,1,0:T(8,128)(2,1)S(1)}, u32[]{:S(2)}, u32[]{:S(2)}) collective-permute-start(bf16[4,32,1024]{2,1,0:T(8,128)(2,1)S(1)} %get-tuple-element.28), channel_id=1, source_target_pairs={{0,3},{1,0},{2,1},{3,2},{4,7},{5,4},{6,5},{7,6},{8,11},{9,8},{10,9... | collective-permute-start | bytes 786440 | tf_op jit(solution)/shard_map/ppermute | solution.py:112
  144.7 6.7 %collective-permute-start.29 = (bf16[4,32,1024]{2,1,0:T(8,128)(2,1)S(1)}, bf16[4,32,1024]{2,1,0:T(8,128)(2,1)S(1)}, u32[]{:S(2)}, u32[]{:S(2)}) collective-permute-start(bf16[4,32,1024]{2,1,0:T(8,128)(2,1)S(1)} %get-tuple-element.29), channel_id=1, source_target_pairs={{0,4},{1,5},{2,6},{3,7},{4,8},{5,9},{6,10},{7,11},{8,12},{9,13},{1... | collective-permute-start | bytes 786440 | tf_op jit(solution)/shard_map/ppermute | solution.py:112
  144.7 6.7 %collective-permute-start.31 = (bf16[4,32,1024]{2,1,0:T(8,128)(2,1)S(1)}, bf16[4,32,1024]{2,1,0:T(8,128)(2,1)S(1)}, u32[]{:S(2)}, u32[]{:S(2)}) collective-permute-start(bf16[4,32,1024]{2,1,0:T(8,128)(2,1)S(1)} %get-tuple-element.30), channel_id=1, source_target_pairs={{0,12},{1,13},{2,14},{3,15},{4,0},{5,1},{6,2},{7,3},{8,4},{9,5},{1... | collective-permute-start | bytes 786440 | tf_op jit(solution)/shard_map/ppermute | solution.py:112
  152.4 26.5 %all-to-all-start.1 = ((bf16[8,32,1024]{2,1,0:T(8,128)(2,1)}), bf16[8,32,1024]{2,1,0:T(8,128)(2,1)}, u32[]{:S(2)}, u32[]{:S(2)}) async-start(bf16[8,32,1024]{2,1,0:T(8,128)(2,1)} %pad_maximum_fusion), calls=%async_computation.1 | async-start | bytes 1048576 | tf_op jit(solution)/shard_map/all_to_all | solution.py:231

commit v15 on v14

--- a/solution.py
+++ b/solution.py
@@ -204,11 +204,12 @@
 
     inputs = candidates.astype(jnp.float32)
     normed = layer_norm(inputs).astype(jnp.bfloat16).reshape(cand_rows * per_group, width)
-    queries = jax.nn.silu(jnp.dot(normed, w_uq[:, width:], preferred_element_type=jnp.float32))
-    queries = (queries * (0.5 * head_dim ** (-0.5))).astype(jnp.bfloat16).reshape(cand_rows, per_group, width)
-
-    q_pos = jnp.swapaxes(queries, 0, 1)
-    q_out = jnp.where(send_filled[:, None, None], q_pos[send_pos], jnp.zeros((), jnp.bfloat16))
+    c_send = jnp.take(candidates, send_pos, axis=1)
+    q_normed = layer_norm(c_send.astype(jnp.float32)).astype(jnp.bfloat16).reshape(-1, width)
+    queries = jax.nn.silu(jnp.dot(q_normed, w_uq[:, width:], preferred_element_type=jnp.float32))
+    queries = (queries * (0.5 * head_dim ** (-0.5))).astype(jnp.bfloat16).reshape(cand_rows, -1, width)
+
+    q_out = jnp.where(send_filled[:, None, None], jnp.swapaxes(queries, 0, 1), jnp.zeros((), jnp.bfloat16))
     q_in = lax.all_to_all(q_out, "group", split_axis=0, concat_axis=0, tiled=True)
     kv_slots = kv_cache[chosen]
     live_slots = row_live[chosen]

time: 185 us -> 188 us (1.016)
  other arithmetic: 15.7 us -> 22.5 us
  waiting for transfers between devices: 51.2 us -> 44.5 us
  local copies, waits for them, and re-layouts: 30.8 us -> 34.2 us
    ppermute x32, waiting for transfers between devices: 42.9 us -> 36.3 us  [send(): return lax.ppermute(value, 'member', shift_perm(grid, axis, shift))]
    convert_element_type x4, other arithmetic: 1.57 us -> 5.61 us  [ring_reduce(): acc_ahead.astype(jnp.bfloat16)]
    another operation x4, other arithmetic: 1.56 us -> 5.35 us
    gather x1, local copies, waits for them, and re-layouts: 0.58 us -> 2.6 us  [on_device(): c_send = jnp.take(candidates, send_pos, axis=1)]
    unnamed x27 -> x25, local copies, waits for them, and re-layouts: 10.5 us -> 10.7 us
  transfers between devices with their start and end apart: 34 -> 34, of which waited for: 11 -> 11; matrix products, arithmetic and copies ran while one was open for 18% -> 23% of each run, Pallas kernels for 0% -> 0%
where the time goes in v15:
time: 188 us
  starting transfers between devices  66.1 us (35%)
  waiting for transfers between devices  44.5 us (24%)
  local copies, waits for them, and re-layouts  34.2 us (18%)
  other arithmetic  22.5 us (12%)
  Pallas kernels  12.4 us (7%)
  matrix products  7.6 us (4%)
    ppermute x32, starting transfers between devices, send(): return lax.ppermute(value, 'member', shift_perm(grid, axis, shift))  43.1 us
    ppermute x32, waiting for transfers between devices, send(): return lax.ppermute(value, 'member', shift_perm(grid, axis, shift))  36.3 us
    all_to_all x1, starting transfers between devices, on_device(): lax.all_to_all(summed, 'group', split_axis=0, concat_axis=0, tiled=True)  17.1 us
    pallas_call x1, Pallas kernels, attend_local(): pl.pallas_call(kernel, out_shape=[jax.ShapeDtypeStruct((rows, cands, widt...  12.4 us
    unnamed x25, local copies, waits for them, and re-layouts  10.7 us
    all_to_all x1, waiting for transfers between devices, on_device(): lax.all_to_all(summed, 'group', split_axis=0, concat_axis=0, tiled=True)  5.97 us
    all_to_all x1, starting transfers between devices, on_device(): lax.all_to_all(q_out, 'group', split_axis=0, concat_axis=0, tiled=True)  5.96 us
    convert_element_type x4, other arithmetic, ring_reduce(): acc_ahead.astype(jnp.bfloat16)  5.61 us
  transfers between devices with their start and end apart: 34, of which 11 were waited for; matrix products, arithmetic and copies ran while one was open for 23% of the time, Pallas kernels for 0%

profile of v15, /device:TPU:1, one launch (start us, length us, event | category | flops | bytes accessed | tf_op | source)
XLA Modules:
  0.0 187.7 jit_solution(6335628282179694256)
XLA Ops:
  0.0 1.0 fusion.44
  3.0 2.6 %gather_fusion.5 = bf16[8,32,1024]{2,0,1:T(8,128)(2,1)S(1)} fusion(bf16[32,8,1024]{2,1,0:T(8,128)(2,1)} %param.7, s32[1024]{0:T(1024)S(1)} %get-tuple-element.63), kind=kCustom, calls=%fused_computation.5 | custom fusion | bytes 1048608 | tf_op jit(solution)/shard_map/jit(_take)/gather | solution.py:207
  6.9 2.5 %fusion.21 = bf16[32,8,1024]{2,1,0:T(8,128)(2,1)S(1)} fusion(bf16[1024,2048]{1,0:T(8,128)(2,1)} %param.12, bf16[8,32,1024]{2,0,1:T(8,128)(2,1)S(1)} %gather_fusion.5, f32[256]{0:T(256)S(1)} %rsqrt.28, f32[256]{0:T(256)S(1)} %div.93, pred[256]{0:T(512)(128)(4,1)S(1)} %broadcast_in_dim.127), kind=kOutput, calls=%fused_computation.44 | convolution fusion | flops 539754496 | bytes 3148032 | tf_op jit(solution)/shard_map/dot_general | solution.py:209
  9.5 1.4 fusion.36
  10.9 6.0 %all-to-all-start = ((bf16[8,32,1024]{2,1,0:T(8,128)(2,1)}), bf16[8,32,1024]{2,1,0:T(8,128)(2,1)S(1)}, u32[]{:S(2)}, u32[]{:S(2)}) async-start(bf16[8,32,1024]{2,1,0:T(8,128)(2,1)} %fusion.36), calls=%async_computation | async-start | bytes 1048576 | tf_op jit(solution)/shard_map/all_to_all | solution.py:213
  18.8 5.0 %gather_fusion.6 = bf16[8,128,2048]{2,1,0:T(8,128)(2,1)} fusion(bf16[8,128,2048]{2,1,0:T(8,128)(2,1)} %param.8, s32[1024]{0:T(1024)S(1)} %get-tuple-element.64), kind=kCustom, calls=%fused_computation.6 | custom fusion | bytes 8388640 | tf_op jit(solution)/shard_map/gather | solution.py:214
  23.9 2.3 %all-to-all-done = bf16[8,32,1024]{2,1,0:T(8,128)(2,1)S(1)} async-done(((bf16[8,32,1024]{2,1,0:T(8,128)(2,1)}), bf16[8,32,1024]{2,1,0:T(8,128)(2,1)S(1)}, u32[]{:S(2)}, u32[]{:S(2)}) %all-to-all-start) | async-done | bytes 524320 | tf_op jit(solution)/shard_map/all_to_all | solution.py:213
  26.2 0.9 constant_dynamic-update-slice_fusion.18
  27.1 3.7 %collective-permute-start.8 = (bf16[4,32,1024]{2,1,0:T(8,128)(2,1)S(1)}, bf16[4,32,1024]{2,1,0:T(8,128)(2,1)S(1)}, u32[]{:S(2)}, u32[]{:S(2)}) collective-permute-start(bf16[4,32,1024]{2,1,0:T(8,128)(2,1)S(1)} %get-tuple-element.39), channel_id=1, source_target_pairs={{0,12},{1,13},{2,14},{3,15},{4,0},{5,1},{6,2},{7,3},{8,4},{9,5},{1... | collective-permute-start | bytes 786440 | tf_op jit(solution)/shard_map/ppermute | solution.py:112
  30.8 2.5 %collective-permute-start = (bf16[4,32,1024]{2,1,0:T(8,128)(2,1)S(1)}, bf16[4,32,1024]{2,1,0:T(8,128)(2,1)S(1)}, u32[]{:S(2)}, u32[]{:S(2)}) collective-permute-start(bf16[4,32,1024]{2,1,0:T(8,128)(2,1)S(1)} %get-tuple-element.40), channel_id=1, source_target_pairs={{0,3},{1,0},{2,1},{3,2},{4,7},{5,4},{6,5},{7,6},{8,11},{9,8},{10,9... | collective-permute-start | bytes 786440 | tf_op jit(solution)/shard_map/ppermute | solution.py:112
  33.3 3.4 %multiply_convert_fusion = (bf16[4,128,1024]{2,1,0:T(8,128)(2,1)}, bf16[4,128,1024]{2,1,0:T(8,128)(2,1)}) fusion(bf16[8,128,2048]{2,1,0:T(8,128)(2,1)} %gather_fusion.6, f32[4,128]{1,0:T(4,128)S(1)} %get-tuple-element.59, f32[4,128]{1,0:T(4,128)S(1)} %get-tuple-element.60), kind=kLoop, calls=%fused_computation.16 | loop fusion | flops 3145728 | bytes 4198400 | tf_op jit(solution)/shard_map/convert_element_type | solution.py:69
  36.7 1.9 %collective-permute-done.9 = bf16[4,32,1024]{2,1,0:T(8,128)(2,1)S(1)} collective-permute-done((bf16[4,32,1024]{2,1,0:T(8,128)(2,1)S(1)}, bf16[4,32,1024]{2,1,0:T(8,128)(2,1)S(1)}, u32[]{:S(2)}, u32[]{:S(2)}) %collective-permute-start.9) | collective-permute-done | bytes 262176 | tf_op jit(solution)/shard_map/ppermute | solution.py:112
  38.8 2.7 %collective-permute-start.11 = (bf16[4,16,1024]{2,1,0:T(8,128)(2,1)S(1)}, bf16[4,16,1024]{2,1,0:T(8,128)(2,1)S(1)}, u32[]{:S(2)}, u32[]{:S(2)}) collective-permute-start(bf16[4,16,1024]{2,1,0:T(8,128)(2,1)S(1)} %slice.205), channel_id=1, source_target_pairs={{0,12},{1,13},{2,14},{3,15},{4,0},{5,1},{6,2},{7,3},{8,4},{9,5},{1... | collective-permute-start | bytes 393224 | tf_op jit(solution)/shard_map/ppermute | solution.py:112
  41.5 1.3 collective-permute-start.2
  42.8 1.5 collective-permute-start.3
  44.3 0.8 constant_dynamic-update-slice_fusion.17
  45.1 0.8 constant_dynamic-update-slice_fusion.3
  45.8 0.7 constant_dynamic-update-slice_fusion.16
  47.2 0.8 constant_dynamic-update-slice_fusion.14
  48.0 1.3 collective-permute-start.12
  50.1 0.7 constant_dynamic-update-slice_fusion.1
  50.8 0.7 constant_dynamic-update-slice_fusion
  51.6 1.8 collective-permute-start.4
  53.4 2.5 %fusion.61 = (bf16[4,128,2048]{2,1,0:T(8,128)(2,1)}, bf16[4,128,2048]{2,1,0:T(8,128)(2,1)}) fusion(bf16[8,128,2048]{2,1,0:T(8,128)(2,1)S(1)} %copy-done.4), kind=kLoop, calls=%fused_computation.173 | loop fusion | bytes 8388608 | tf_op jit(solution)/shard_map/slice | solution.py:222
  55.9 15.7 %collective-permute-done.13 = bf16[4,128,1024]{2,1,0:T(8,128)(2,1)S(1)} collective-permute-done((bf16[4,128,1024]{2,1,0:T(8,128)(2,1)S(1)}, bf16[4,128,1024]{2,1,0:T(8,128)(2,1)S(1)}, u32[]{:S(2)}, u32[]{:S(2)}) %collective-permute-start.13) | collective-permute-done | bytes 1048608 | tf_op jit(solution)/shard_map/ppermute | solution.py:112
  71.8 2.7 %collective-permute-start.15 = (bf16[4,64,1024]{2,1,0:T(8,128)(2,1)S(1)}, bf16[4,64,1024]{2,1,0:T(8,128)(2,1)S(1)}, u32[]{:S(2)}, u32[]{:S(2)}) collective-permute-start(bf16[4,64,1024]{2,1,0:T(8,128)(2,1)S(1)} %slice.207), channel_id=1, source_target_pairs={{0,3},{1,0},{2,1},{3,2},{4,7},{5,4},{6,5},{7,6},{8,11},{9,8},{10,9... | collective-permute-start | bytes 1572872 | tf_op jit(solution)/shard_map/ppermute | solution.py:112
  75.4 2.9 %collective-permute-start.7 = (bf16[4,64,1024]{2,1,0:T(8,128)(2,1)S(1)}, bf16[4,64,1024]{2,1,0:T(8,128)(2,1)S(1)}, u32[]{:S(2)}, u32[]{:S(2)}) collective-permute-start(bf16[4,64,1024]{2,1,0:T(8,128)(2,1)S(1)} %slice.200), channel_id=1, source_target_pairs={{0,12},{1,13},{2,14},{3,15},{4,0},{5,1},{6,2},{7,3},{8,4},{9,5},{1... | collective-permute-start | bytes 1572872 | tf_op jit(solution)/shard_map/ppermute | solution.py:112
  78.3 1.1 constant_dynamic-update-slice_fusion.22
  79.4 1.1 constant_dynamic-update-slice_fusion.8
  80.5 1.6 collective-permute-done.14
  82.1 0.8 constant_dynamic-update-slice_fusion.21
  83.0 0.9 constant_dynamic-update-slice_fusion.20
  83.8 1.8 collective-permute-done.6
  85.6 0.8 constant_dynamic-update-slice_fusion.7
  86.5 1.1 constant_dynamic-update-slice_fusion.19.refs_3_
  87.6 0.8 constant_dynamic-update-slice_fusion.6
  88.4 1.1 constant_dynamic-update-slice_fusion.5.refs_0_
  89.5 12.4 %shard_map.73 = (bf16[4,512,1024]{2,1,0:T(8,128)(2,1)}, bf16[4,512,1024]{2,1,0:T(8,128)(2,1)}) custom-call(s32[8]{0:T(128)} %pad_add_fusion.n_live_ref, bf16[4,512,1024]{2,1,0:T(8,128)(2,1)} %constant_dynamic-update-slice_fusion.5.refs_0_, bf16[4,128,2048]{2,1,0:T(8,128)(2,1)} %get-tuple-element.26.refs_1_, bf16[4,128,1024]{2,1,0:T(8,128)(2,1)} %get-tuple-element.24.refs_2_, ...), custom_call_target="tpu_custom_call" | custom-call | flops 2147483648 | bytes 20971520 | tf_op jit(solution)/shard_map/pallas_call | solution.py:81
  101.8 1.5 fusion.59
  103.4 2.7 %collective-permute-start.18 = (bf16[4,64,1024]{2,1,0:T(8,128)(2,1)S(1)}, bf16[4,64,1024]{2,1,0:T(8,128)(2,1)S(1)}, u32[]{:S(2)}, u32[]{:S(2)}) collective-permute-start(bf16[4,64,1024]{2,1,0:T(8,128)(2,1)S(1)} %get-tuple-element.18), channel_id=1, source_target_pairs={{0,12},{1,13},{2,14},{3,15},{4,0},{5,1},{6,2},{7,3},{8,4},{9,5},{1... | collective-permute-start | bytes 1572872 | tf_op jit(solution)/shard_map/ppermute | solution.py:112
  106.0 2.2 %fusion.60 = (bf16[4,64,1024]{2,1,0:T(8,128)(2,1)}, bf16[4,64,1024]{2,1,0:T(8,128)(2,1)}) fusion(bf16[4,512,1024]{2,1,0:T(8,128)(2,1)} %get-tuple-element.8), kind=kLoop, calls=%fused_computation.172 | loop fusion | bytes 2097152 | tf_op jit(solution)/shard_map/slice | solution.py:148
  108.3 2.7 %collective-permute-start.26 = (bf16[4,64,1024]{2,1,0:T(8,128)(2,1)}, bf16[4,64,1024]{2,1,0:T(8,128)(2,1)}, u32[]{:S(2)}, u32[]{:S(2)}) collective-permute-start(bf16[4,64,1024]{2,1,0:T(8,128)(2,1)} %get-tuple-element.22), channel_id=1, source_target_pairs={{0,3},{1,0},{2,1},{3,2},{4,7},{5,4},{6,5},{7,6},{8,11},{9,8},{10,9... | collective-permute-start | bytes 1572872 | tf_op jit(solution)/shard_map/ppermute | solution.py:112
  111.0 1.7 collective-permute-done.16
  112.6 1.8 add_convert_fusion.3
  114.4 2.7 %collective-permute-start.19 = (bf16[4,128,1024]{2,1,0:T(8,128)(2,1)}, bf16[4,128,1024]{2,1,0:T(8,128)(2,1)}, u32[]{:S(2)}, u32[]{:S(2)}) collective-permute-start(bf16[4,128,1024]{2,1,0:T(8,128)(2,1)} %get-tuple-element.16), channel_id=1, source_target_pairs={{0,12},{1,13},{2,14},{3,15},{4,0},{5,1},{6,2},{7,3},{8,4},{9,5},{1... | collective-permute-start | bytes 3145736 | tf_op jit(solution)/shard_map/ppermute | solution.py:112
  118.0 3.6 %add_convert_fusion.1 = (bf16[4,128,1024]{2,1,0:T(8,128)(2,1)}, bf16[4,128,1024]{2,1,0:T(8,128)(2,1)}) fusion(bf16[4,64,1024]{2,1,0:T(8,128)(2,1)S(1)} %collective-permute-done.24, bf16[4,512,1024]{2,1,0:T(8,128)(2,1)} %get-tuple-element.8, bf16[4,64,1024]{2,1,0:T(8,128)(2,1)} %collective-permute-done.26), kind=kLoop, calls=%fused_computation.12 | loop fusion | flops 4194304 | bytes 5242880 | tf_op jit(solution)/shard_map/convert_element_type | solution.py:153
  121.6 2.7 %collective-permute-start.27 = (bf16[4,128,1024]{2,1,0:T(8,128)(2,1)}, bf16[4,128,1024]{2,1,0:T(8,128)(2,1)}, u32[]{:S(2)}, u32[]{:S(2)}) collective-permute-start(bf16[4,128,1024]{2,1,0:T(8,128)(2,1)} %get-tuple-element.20), channel_id=1, source_target_pairs={{0,3},{1,0},{2,1},{3,2},{4,7},{5,4},{6,5},{7,6},{8,11},{9,8},{10,9... | collective-permute-start | bytes 3145736 | tf_op jit(solution)/shard_map/ppermute | solution.py:112
  124.7 9.3 %collective-permute-done.17 = bf16[4,128,1024]{2,1,0:T(8,128)(2,1)} collective-permute-done((bf16[4,128,1024]{2,1,0:T(8,128)(2,1)}, bf16[4,128,1024]{2,1,0:T(8,128)(2,1)}, u32[]{:S(2)}, u32[]{:S(2)}) %collective-permute-start.17) | collective-permute-done | bytes 1048608 | tf_op jit(solution)/shard_map/ppermute | solution.py:112
  134.1 2.6 %fusion.57 = (bf16[4,128,1024]{2,1,0:T(8,128)(2,1)S(1)}, f32[4,128,1024]{2,1,0:T(8,128)S(1)}) fusion(bf16[4,128,1024]{2,1,0:T(8,128)(2,1)} %collective-permute-done.19, bf16[4,128,1024]{2,1,0:T(8,128)(2,1)} %collective-permute-done.17, bf16[4,512,1024]{2,1,0:T(8,128)(2,1)} %get-tuple-element.7), kind=kLoop, calls=%fused_computation.169 | loop fusion | flops 3145728 | bytes 6291456 | tf_op jit(solution)/shard_map/convert.20
  136.7 2.7 %collective-permute-start.22 = (bf16[4,16,1024]{2,1,0:T(8,128)(2,1)S(1)}, bf16[4,16,1024]{2,1,0:T(8,128)(2,1)S(1)}, u32[]{:S(2)}, u32[]{:S(2)}) collective-permute-start(bf16[4,16,1024]{2,1,0:T(8,128)(2,1)S(1)} %get-tuple-element.32), channel_id=1, source_target_pairs={{0,3},{1,0},{2,1},{3,2},{4,7},{5,4},{6,5},{7,6},{8,11},{9,8},{10,9... | collective-permute-start | bytes 393224 | tf_op jit(solution)/shard_map/ppermute | solution.py:112
  139.4 2.6 %fusion.58 = (bf16[4,128,1024]{2,1,0:T(8,128)(2,1)S(1)}, f32[4,128,1024]{2,1,0:T(8,128)S(1)}) fusion(bf16[4,128,1024]{2,1,0:T(8,128)(2,1)} %collective-permute-done.27, bf16[4,128,1024]{2,1,0:T(8,128)(2,1)} %collective-permute-done.25, bf16[4,512,1024]{2,1,0:T(8,128)(2,1)} %get-tuple-element.8), kind=kLoop, calls=%fused_computation.170 | loop fusion | flops 3145728 | bytes 6291456 | tf_op jit(solution)/shard_map/convert.19
  142.1 3.0 %collective-permute-start.30 = (bf16[4,16,1024]{2,1,0:T(8,128)(2,1)S(1)}, bf16[4,16,1024]{2,1,0:T(8,128)(2,1)S(1)}, u32[]{:S(2)}, u32[]{:S(2)}) collective-permute-start(bf16[4,16,1024]{2,1,0:T(8,128)(2,1)S(1)} %get-tuple-element.34), channel_id=1, source_target_pairs={{0,12},{1,13},{2,14},{3,15},{4,0},{5,1},{6,2},{7,3},{8,4},{9,5},{1... | collective-permute-start | bytes 393224 | tf_op jit(solution)/shard_map/ppermute | solution.py:112
  145.3 2.7 %collective-permute-start.23 = (bf16[4,32,1024]{2,1,0:T(8,128)(2,1)S(1)}, bf16[4,32,1024]{2,1,0:T(8,128)(2,1)S(1)}, u32[]{:S(2)}, u32[]{:S(2)}) collective-permute-start(bf16[4,32,1024]{2,1,0:T(8,128)(2,1)S(1)} %get-tuple-element.28), channel_id=1, source_target_pairs={{0,3},{1,0},{2,1},{3,2},{4,7},{5,4},{6,5},{7,6},{8,11},{9,8},{10,9... | collective-permute-start | bytes 786440 | tf_op jit(solution)/shard_map/ppermute | solution.py:112
  148.1 0.7 collective-permute-start.29
  148.8 2.2 %collective-permute-start.31 = (bf16[4,32,1024]{2,1,0:T(8,128)(2,1)S(1)}, bf16[4,32,1024]{2,1,0:T(8,128)(2,1)S(1)}, u32[]{:S(2)}, u32[]{:S(2)}) collective-permute-start(bf16[4,32,1024]{2,1,0:T(8,128)(2,1)S(1)} %get-tuple-element.30), channel_id=1, source_target_pairs={{0,12},{1,13},{2,14},{3,15},{4,0},{5,1},{6,2},{7,3},{8,4},{9,5},{1... | collective-permute-start | bytes 786440 | tf_op jit(solution)/shard_map/ppermute | solution.py:112
  151.0 2.5 %collective-permute-done.21 = bf16[4,32,1024]{2,1,0:T(8,128)(2,1)S(1)} collective-permute-done((bf16[4,32,1024]{2,1,0:T(8,128)(2,1)S(1)}, bf16[4,32,1024]{2,1,0:T(8,128)(2,1)S(1)}, u32[]{:S(2)}, u32[]{:S(2)}) %collective-permute-start.21) | collective-permute-done | bytes 262176 | tf_op jit(solution)/shard_map/ppermute | solution.py:112
  153.7 0.9 collective-permute-done.29
  154.7 0.8 pad_maximum_fusion
  155.5 17.1 %all-to-all-start.1 = ((bf16[8,32,1024]{2,1,0:T(8,128)(2,1)}), bf16[8,32,1024]{2,1,0:T(8,128)(2,1)}, u32[]{:S(2)}, u32[]{:S(2)}) async-start(bf16[8,32,1024]{2,1,0:T(8,128)(2,1)} %pad_maximum_fusion), calls=%async_computation.1 | async-start | bytes 1048576 | tf_op jit(solution)/shard_map/all_to_all | solution.py:232
  172.7 3.4 %multiply_bitcast_fusion = f32[32,8,1024]{2,1,0:T(8,128)} fusion(bf16[1024,2048]{1,0:T(8,128)(2,1)} %param.12, bf16[32,8,1024]{2,1,0:T(8,128)(2,1)S(1)} %copy-done.3, f32[32,8]{1,0:T(8,128)S(1)} %copy.47, f32[32,8]{1,0:T(8,128)S(1)} %copy.45), kind=kOutput, calls=%fused_computation.41 | convolution fusion | flops 538968064 | bytes 3672064 | tf_op jit(solution)/shard_map/dot_general | solution.py:235
  176.1 6.0 %all-to-all-done.1 = bf16[8,32,1024]{2,1,0:T(8,128)(2,1)} async-done(((bf16[8,32,1024]{2,1,0:T(8,128)(2,1)}), bf16[8,32,1024]{2,1,0:T(8,128)(2,1)}, u32[]{:S(2)}, u32[]{:S(2)}) %all-to-all-start.1) | async-done | bytes 524320 | tf_op jit(solution)/shard_map/all_to_all | solution.py:232
  182.1 1.6 gather_fusion.7
  184.2 1.9 fusion.16
  186.0 1.6 fusion.7
  (123 shorter events, 10.8 us)
Async XLA Ops:
  0.0 186.0 %copy-start = (bf16[1024,1024]{1,0:T(8,128)(2,1)S(1)}, bf16[1024,1024]{1,0:T(8,128)(2,1)}, u32[]{:S(2)}) copy-start(bf16[1024,1024]{1,0:T(8,128)(2,1)} %param.13) | copy-start | bytes 6291460
  6.9 9.9 %copy-start.1 = (s32[64]{0:T(128)S(1)}, s32[64]{0:T(128)}, u32[]{:S(2)}) copy-start(s32[64]{0:T(128)} %param.9) | copy-start | bytes 772
  6.9 10.6 %copy-start.2 = (s32[64]{0:T(128)S(1)}, s32[64]{0:T(128)}, u32[]{:S(2)}) copy-start(s32[64]{0:T(128)} %param.11) | copy-start | bytes 772
  10.9 15.3 %all-to-all-start = ((bf16[8,32,1024]{2,1,0:T(8,128)(2,1)}), bf16[8,32,1024]{2,1,0:T(8,128)(2,1)S(1)}, u32[]{:S(2)}, u32[]{:S(2)}) async-start(bf16[8,32,1024]{2,1,0:T(8,128)(2,1)} %fusion.36), calls=%async_computation | async-start | bytes 1048576 | tf_op jit(solution)/shard_map/all_to_all | solution.py:213
  27.1 11.7 %collective-permute-start.8 = (bf16[4,32,1024]{2,1,0:T(8,128)(2,1)S(1)}, bf16[4,32,1024]{2,1,0:T(8,128)(2,1)S(1)}, u32[]{:S(2)}, u32[]{:S(2)}) collective-permute-start(bf16[4,32,1024]{2,1,0:T(8,128)(2,1)S(1)} %get-tuple-element.39), channel_id=1, source_target_pairs={{0,12},{1,13},{2,14},{3,15},{4,0},{5,1},{6,2},{7,3},{8,4},{9,5},{1... | collective-permute-start | bytes 786440 | tf_op jit(solution)/shard_map/ppermute | solution.py:112
  30.8 7.8 %collective-permute-start.9 = (bf16[4,32,1024]{2,1,0:T(8,128)(2,1)S(1)}, bf16[4,32,1024]{2,1,0:T(8,128)(2,1)S(1)}, u32[]{:S(2)}, u32[]{:S(2)}) collective-permute-start(bf16[4,32,1024]{2,1,0:T(8,128)(2,1)S(1)} %get-tuple-element.39), channel_id=1, source_target_pairs={{0,4},{1,5},{2,6},{3,7},{4,8},{5,9},{6,10},{7,11},{8,12},{9,13},{1... | collective-permute-start | bytes 786440 | tf_op jit(solution)/shard_map/ppermute | solution.py:112
  30.8 12.0 %collective-permute-start = (bf16[4,32,1024]{2,1,0:T(8,128)(2,1)S(1)}, bf16[4,32,1024]{2,1,0:T(8,128)(2,1)S(1)}, u32[]{:S(2)}, u32[]{:S(2)}) collective-permute-start(bf16[4,32,1024]{2,1,0:T(8,128)(2,1)S(1)} %get-tuple-element.40), channel_id=1, source_target_pairs={{0,3},{1,0},{2,1},{3,2},{4,7},{5,4},{6,5},{7,6},{8,11},{9,8},{10,9... | collective-permute-start | bytes 786440 | tf_op jit(solution)/shard_map/ppermute | solution.py:112
  33.3 8.2 %collective-permute-start.1 = (bf16[4,32,1024]{2,1,0:T(8,128)(2,1)S(1)}, bf16[4,32,1024]{2,1,0:T(8,128)(2,1)S(1)}, u32[]{:S(2)}, u32[]{:S(2)}) collective-permute-start(bf16[4,32,1024]{2,1,0:T(8,128)(2,1)S(1)} %get-tuple-element.40), channel_id=1, source_target_pairs={{0,1},{1,2},{2,3},{3,0},{4,5},{5,6},{6,7},{7,4},{8,9},{9,10},{10,1... | collective-permute-start | bytes 786440 | tf_op jit(solution)/shard_map/ppermute | solution.py:112
  33.3 20.1 %copy-start.4 = (bf16[8,128,2048]{2,1,0:T(8,128)(2,1)S(1)}, bf16[8,128,2048]{2,1,0:T(8,128)(2,1)}, u32[]{:S(2)}) copy-start(bf16[8,128,2048]{2,1,0:T(8,128)(2,1)} %gather_fusion.6) | copy-start | bytes 12582916
  38.6 7.2 %collective-permute-start.10 = (bf16[4,16,1024]{2,1,0:T(8,128)(2,1)S(1)}, bf16[4,16,1024]{2,1,0:T(8,128)(2,1)S(1)}, u32[]{:S(2)}, u32[]{:S(2)}) collective-permute-start(bf16[4,16,1024]{2,1,0:T(8,128)(2,1)S(1)} %slice.204), channel_id=1, source_target_pairs={{0,4},{1,5},{2,6},{3,7},{4,8},{5,9},{6,10},{7,11},{8,12},{9,13},{1... | collective-permute-start | bytes 393224 | tf_op jit(solution)/shard_map/ppermute | solution.py:112
  38.8 7.8 %collective-permute-start.11 = (bf16[4,16,1024]{2,1,0:T(8,128)(2,1)S(1)}, bf16[4,16,1024]{2,1,0:T(8,128)(2,1)S(1)}, u32[]{:S(2)}, u32[]{:S(2)}) collective-permute-start(bf16[4,16,1024]{2,1,0:T(8,128)(2,1)S(1)} %slice.205), channel_id=1, source_target_pairs={{0,12},{1,13},{2,14},{3,15},{4,0},{5,1},{6,2},{7,3},{8,4},{9,5},{1... | collective-permute-start | bytes 393224 | tf_op jit(solution)/shard_map/ppermute | solution.py:112
  41.5 8.0 %collective-permute-start.2 = (bf16[4,16,1024]{2,1,0:T(8,128)(2,1)S(1)}, bf16[4,16,1024]{2,1,0:T(8,128)(2,1)S(1)}, u32[]{:S(2)}, u32[]{:S(2)}) collective-permute-start(bf16[4,16,1024]{2,1,0:T(8,128)(2,1)S(1)} %slice.197), channel_id=1, source_target_pairs={{0,1},{1,2},{2,3},{3,0},{4,5},{5,6},{6,7},{7,4},{8,9},{9,10},{10,1... | collective-permute-start | bytes 393224 | tf_op jit(solution)/shard_map/ppermute | solution.py:112
  42.8 7.3 %collective-permute-start.3 = (bf16[4,16,1024]{2,1,0:T(8,128)(2,1)S(1)}, bf16[4,16,1024]{2,1,0:T(8,128)(2,1)S(1)}, u32[]{:S(2)}, u32[]{:S(2)}) collective-permute-start(bf16[4,16,1024]{2,1,0:T(8,128)(2,1)S(1)} %slice.198), channel_id=1, source_target_pairs={{0,3},{1,0},{2,1},{3,2},{4,7},{5,4},{6,5},{7,6},{8,11},{9,8},{10,9... | collective-permute-start | bytes 393224 | tf_op jit(solution)/shard_map/ppermute | solution.py:112
  48.0 23.8 %collective-permute-start.12 = (bf16[4,128,1024]{2,1,0:T(8,128)(2,1)S(1)}, bf16[4,128,1024]{2,1,0:T(8,128)(2,1)S(1)}, u32[]{:S(2)}, u32[]{:S(2)}) collective-permute-start(bf16[4,128,1024]{2,1,0:T(8,128)(2,1)S(1)} %get-tuple-element.41), channel_id=1, source_target_pairs={{0,3},{1,0},{2,1},{3,2},{4,7},{5,4},{6,5},{7,6},{8,11},{9,8},{10,9... | collective-permute-start | bytes 3145736 | tf_op jit(solution)/shard_map/ppermute | solution.py:112
  49.2 22.4 %collective-permute-start.13 = (bf16[4,128,1024]{2,1,0:T(8,128)(2,1)S(1)}, bf16[4,128,1024]{2,1,0:T(8,128)(2,1)S(1)}, u32[]{:S(2)}, u32[]{:S(2)}) collective-permute-start(bf16[4,128,1024]{2,1,0:T(8,128)(2,1)S(1)} %get-tuple-element.41), channel_id=1, source_target_pairs={{0,1},{1,2},{2,3},{3,0},{4,5},{5,6},{6,7},{7,4},{8,9},{9,10},{10,1... | collective-permute-start | bytes 3145736 | tf_op jit(solution)/shard_map/ppermute | solution.py:112
  51.6 23.8 %collective-permute-start.4 = (bf16[4,128,1024]{2,1,0:T(8,128)(2,1)S(1)}, bf16[4,128,1024]{2,1,0:T(8,128)(2,1)S(1)}, u32[]{:S(2)}, u32[]{:S(2)}) collective-permute-start(bf16[4,128,1024]{2,1,0:T(8,128)(2,1)S(1)} %get-tuple-element.45), channel_id=1, source_target_pairs={{0,12},{1,13},{2,14},{3,15},{4,0},{5,1},{6,2},{7,3},{8,4},{9,5},{1... | collective-permute-start | bytes 3145736 | tf_op jit(solution)/shard_map/ppermute | solution.py:112
  53.3 21.9 %collective-permute-start.5 = (bf16[4,128,1024]{2,1,0:T(8,128)(2,1)S(1)}, bf16[4,128,1024]{2,1,0:T(8,128)(2,1)S(1)}, u32[]{:S(2)}, u32[]{:S(2)}) collective-permute-start(bf16[4,128,1024]{2,1,0:T(8,128)(2,1)S(1)} %get-tuple-element.45), channel_id=1, source_target_pairs={{0,4},{1,5},{2,6},{3,7},{4,8},{5,9},{6,10},{7,11},{8,12},{9,13},{1... | collective-permute-start | bytes 3145736 | tf_op jit(solution)/shard_map/ppermute | solution.py:112
  71.7 10.4 %collective-permute-start.14 = (bf16[4,64,1024]{2,1,0:T(8,128)(2,1)S(1)}, bf16[4,64,1024]{2,1,0:T(8,128)(2,1)S(1)}, u32[]{:S(2)}, u32[]{:S(2)}) collective-permute-start(bf16[4,64,1024]{2,1,0:T(8,128)(2,1)S(1)} %slice.206), channel_id=1, source_target_pairs={{0,1},{1,2},{2,3},{3,0},{4,5},{5,6},{6,7},{7,4},{8,9},{9,10},{10,1... | collective-permute-start | bytes 1572872 | tf_op jit(solution)/shard_map/ppermute | solution.py:112
  71.8 11.1 %collective-permute-start.15 = (bf16[4,64,1024]{2,1,0:T(8,128)(2,1)S(1)}, bf16[4,64,1024]{2,1,0:T(8,128)(2,1)S(1)}, u32[]{:S(2)}, u32[]{:S(2)}) collective-permute-start(bf16[4,64,1024]{2,1,0:T(8,128)(2,1)S(1)} %slice.207), channel_id=1, source_target_pairs={{0,3},{1,0},{2,1},{3,2},{4,7},{5,4},{6,5},{7,6},{8,11},{9,8},{10,9... | collective-permute-start | bytes 1572872 | tf_op jit(solution)/shard_map/ppermute | solution.py:112
  75.3 10.3 %collective-permute-start.6 = (bf16[4,64,1024]{2,1,0:T(8,128)(2,1)S(1)}, bf16[4,64,1024]{2,1,0:T(8,128)(2,1)S(1)}, u32[]{:S(2)}, u32[]{:S(2)}) collective-permute-start(bf16[4,64,1024]{2,1,0:T(8,128)(2,1)S(1)} %slice.199), channel_id=1, source_target_pairs={{0,4},{1,5},{2,6},{3,7},{4,8},{5,9},{6,10},{7,11},{8,12},{9,13},{1... | collective-permute-start | bytes 1572872 | tf_op jit(solution)/shard_map/ppermute | solution.py:112
  75.4 12.1 %collective-permute-start.7 = (bf16[4,64,1024]{2,1,0:T(8,128)(2,1)S(1)}, bf16[4,64,1024]{2,1,0:T(8,128)(2,1)S(1)}, u32[]{:S(2)}, u32[]{:S(2)}) collective-permute-start(bf16[4,64,1024]{2,1,0:T(8,128)(2,1)S(1)} %slice.200), channel_id=1, source_target_pairs={{0,12},{1,13},{2,14},{3,15},{4,0},{5,1},{6,2},{7,3},{8,4},{9,5},{1... | collective-permute-start | bytes 1572872 | tf_op jit(solution)/shard_map/ppermute | solution.py:112
  101.8 10.8 %copy-start.5 = (bf16[4,512,1024]{2,1,0:T(8,128)(2,1)S(1)}, bf16[4,512,1024]{2,1,0:T(8,128)(2,1)}, u32[]{:S(2)}) copy-start(bf16[4,512,1024]{2,1,0:T(8,128)(2,1)} %get-tuple-element.7) | copy-start | bytes 12582916
  103.3 13.8 %copy-start.3 = (bf16[32,8,1024]{2,1,0:T(8,128)(2,1)S(1)}, bf16[32,8,1024]{2,1,0:T(8,128)(2,1)}, u32[]{:S(2)}) copy-start(bf16[32,8,1024]{2,1,0:T(8,128)(2,1)} %param.7) | copy-start | bytes 1572868
  103.3 9.3 %collective-permute-start.16 = (bf16[4,64,1024]{2,1,0:T(8,128)(2,1)S(1)}, bf16[4,64,1024]{2,1,0:T(8,128)(2,1)S(1)}, u32[]{:S(2)}, u32[]{:S(2)}) collective-permute-start(bf16[4,64,1024]{2,1,0:T(8,128)(2,1)S(1)} %get-tuple-element.17), channel_id=1, source_target_pairs={{0,4},{1,5},{2,6},{3,7},{4,8},{5,9},{6,10},{7,11},{8,12},{9,13},{1... | collective-permute-start | bytes 1572872 | tf_op jit(solution)/shard_map/ppermute | solution.py:112
  103.4 9.2 %collective-permute-start.18 = (bf16[4,64,1024]{2,1,0:T(8,128)(2,1)S(1)}, bf16[4,64,1024]{2,1,0:T(8,128)(2,1)S(1)}, u32[]{:S(2)}, u32[]{:S(2)}) collective-permute-start(bf16[4,64,1024]{2,1,0:T(8,128)(2,1)S(1)} %get-tuple-element.18), channel_id=1, source_target_pairs={{0,12},{1,13},{2,14},{3,15},{4,0},{5,1},{6,2},{7,3},{8,4},{9,5},{1... | collective-permute-start | bytes 1572872 | tf_op jit(solution)/shard_map/ppermute | solution.py:112
  108.3 9.7 %collective-permute-start.24 = (bf16[4,64,1024]{2,1,0:T(8,128)(2,1)}, bf16[4,64,1024]{2,1,0:T(8,128)(2,1)S(1)}, u32[]{:S(2)}, u32[]{:S(2)}) collective-permute-start(bf16[4,64,1024]{2,1,0:T(8,128)(2,1)} %get-tuple-element.21), channel_id=1, source_target_pairs={{0,1},{1,2},{2,3},{3,0},{4,5},{5,6},{6,7},{7,4},{8,9},{9,10},{10,1... | collective-permute-start | bytes 1572872 | tf_op jit(solution)/shard_map/ppermute | solution.py:112
  108.3 9.7 %collective-permute-start.26 = (bf16[4,64,1024]{2,1,0:T(8,128)(2,1)}, bf16[4,64,1024]{2,1,0:T(8,128)(2,1)}, u32[]{:S(2)}, u32[]{:S(2)}) collective-permute-start(bf16[4,64,1024]{2,1,0:T(8,128)(2,1)} %get-tuple-element.22), channel_id=1, source_target_pairs={{0,3},{1,0},{2,1},{3,2},{4,7},{5,4},{6,5},{7,6},{8,11},{9,8},{10,9... | collective-permute-start | bytes 1572872 | tf_op jit(solution)/shard_map/ppermute | solution.py:112
  114.4 19.6 %collective-permute-start.17 = (bf16[4,128,1024]{2,1,0:T(8,128)(2,1)}, bf16[4,128,1024]{2,1,0:T(8,128)(2,1)}, u32[]{:S(2)}, u32[]{:S(2)}) collective-permute-start(bf16[4,128,1024]{2,1,0:T(8,128)(2,1)} %get-tuple-element.15), channel_id=1, source_target_pairs={{0,4},{1,5},{2,6},{3,7},{4,8},{5,9},{6,10},{7,11},{8,12},{9,13},{1... | collective-permute-start | bytes 3145736 | tf_op jit(solution)/shard_map/ppermute | solution.py:112
  114.4 19.6 %collective-permute-start.19 = (bf16[4,128,1024]{2,1,0:T(8,128)(2,1)}, bf16[4,128,1024]{2,1,0:T(8,128)(2,1)}, u32[]{:S(2)}, u32[]{:S(2)}) collective-permute-start(bf16[4,128,1024]{2,1,0:T(8,128)(2,1)} %get-tuple-element.16), channel_id=1, source_target_pairs={{0,12},{1,13},{2,14},{3,15},{4,0},{5,1},{6,2},{7,3},{8,4},{9,5},{1... | collective-permute-start | bytes 3145736 | tf_op jit(solution)/shard_map/ppermute | solution.py:112
  121.6 17.8 %collective-permute-start.25 = (bf16[4,128,1024]{2,1,0:T(8,128)(2,1)}, bf16[4,128,1024]{2,1,0:T(8,128)(2,1)}, u32[]{:S(2)}, u32[]{:S(2)}) collective-permute-start(bf16[4,128,1024]{2,1,0:T(8,128)(2,1)} %get-tuple-element.19), channel_id=1, source_target_pairs={{0,1},{1,2},{2,3},{3,0},{4,5},{5,6},{6,7},{7,4},{8,9},{9,10},{10,1... | collective-permute-start | bytes 3145736 | tf_op jit(solution)/shard_map/ppermute | solution.py:112
  121.6 17.8 %collective-permute-start.27 = (bf16[4,128,1024]{2,1,0:T(8,128)(2,1)}, bf16[4,128,1024]{2,1,0:T(8,128)(2,1)}, u32[]{:S(2)}, u32[]{:S(2)}) collective-permute-start(bf16[4,128,1024]{2,1,0:T(8,128)(2,1)} %get-tuple-element.20), channel_id=1, source_target_pairs={{0,3},{1,0},{2,1},{3,2},{4,7},{5,4},{6,5},{7,6},{8,11},{9,8},{10,9... | collective-permute-start | bytes 3145736 | tf_op jit(solution)/shard_map/ppermute | solution.py:112
  136.7 8.5 %collective-permute-start.20 = (bf16[4,16,1024]{2,1,0:T(8,128)(2,1)S(1)}, bf16[4,16,1024]{2,1,0:T(8,128)(2,1)S(1)}, u32[]{:S(2)}, u32[]{:S(2)}) collective-permute-start(bf16[4,16,1024]{2,1,0:T(8,128)(2,1)S(1)} %get-tuple-element.31), channel_id=1, source_target_pairs={{0,1},{1,2},{2,3},{3,0},{4,5},{5,6},{6,7},{7,4},{8,9},{9,10},{10,1... | collective-permute-start | bytes 393224 | tf_op jit(solution)/shard_map/ppermute | solution.py:112
  136.7 8.4 %collective-permute-start.22 = (bf16[4,16,1024]{2,1,0:T(8,128)(2,1)S(1)}, bf16[4,16,1024]{2,1,0:T(8,128)(2,1)S(1)}, u32[]{:S(2)}, u32[]{:S(2)}) collective-permute-start(bf16[4,16,1024]{2,1,0:T(8,128)(2,1)S(1)} %get-tuple-element.32), channel_id=1, source_target_pairs={{0,3},{1,0},{2,1},{3,2},{4,7},{5,4},{6,5},{7,6},{8,11},{9,8},{10,9... | collective-permute-start | bytes 393224 | tf_op jit(solution)/shard_map/ppermute | solution.py:112
  142.0 6.0 %collective-permute-start.28 = (bf16[4,16,1024]{2,1,0:T(8,128)(2,1)S(1)}, bf16[4,16,1024]{2,1,0:T(8,128)(2,1)S(1)}, u32[]{:S(2)}, u32[]{:S(2)}) collective-permute-start(bf16[4,16,1024]{2,1,0:T(8,128)(2,1)S(1)} %get-tuple-element.33), channel_id=1, source_target_pairs={{0,4},{1,5},{2,6},{3,7},{4,8},{5,9},{6,10},{7,11},{8,12},{9,13},{1... | collective-permute-start | bytes 393224 | tf_op jit(solution)/shard_map/ppermute | solution.py:112
  142.1 5.9 %collective-permute-start.30 = (bf16[4,16,1024]{2,1,0:T(8,128)(2,1)S(1)}, bf16[4,16,1024]{2,1,0:T(8,128)(2,1)S(1)}, u32[]{:S(2)}, u32[]{:S(2)}) collective-permute-start(bf16[4,16,1024]{2,1,0:T(8,128)(2,1)S(1)} %get-tuple-element.34), channel_id=1, source_target_pairs={{0,12},{1,13},{2,14},{3,15},{4,0},{5,1},{6,2},{7,3},{8,4},{9,5},{1... | collective-permute-start | bytes 393224 | tf_op jit(solution)/shard_map/ppermute | solution.py:112
  145.2 8.3 %collective-permute-start.21 = (bf16[4,32,1024]{2,1,0:T(8,128)(2,1)S(1)}, bf16[4,32,1024]{2,1,0:T(8,128)(2,1)S(1)}, u32[]{:S(2)}, u32[]{:S(2)}) collective-permute-start(bf16[4,32,1024]{2,1,0:T(8,128)(2,1)S(1)} %get-tuple-element.27), channel_id=1, source_target_pairs={{0,1},{1,2},{2,3},{3,0},{4,5},{5,6},{6,7},{7,4},{8,9},{9,10},{10,1... | collective-permute-start | bytes 786440 | tf_op jit(solution)/shard_map/ppermute | solution.py:112
  145.3 8.2 %collective-permute-start.23 = (bf16[4,32,1024]{2,1,0:T(8,128)(2,1)S(1)}, bf16[4,32,1024]{2,1,0:T(8,128)(2,1)S(1)}, u32[]{:S(2)}, u32[]{:S(2)}) collective-permute-start(bf16[4,32,1024]{2,1,0:T(8,128)(2,1)S(1)} %get-tuple-element.28), channel_id=1, source_target_pairs={{0,3},{1,0},{2,1},{3,2},{4,7},{5,4},{6,5},{7,6},{8,11},{9,8},{10,9... | collective-permute-start | bytes 786440 | tf_op jit(solution)/shard_map/ppermute | solution.py:112
  148.1 6.5 %collective-permute-start.29 = (bf16[4,32,1024]{2,1,0:T(8,128)(2,1)S(1)}, bf16[4,32,1024]{2,1,0:T(8,128)(2,1)S(1)}, u32[]{:S(2)}, u32[]{:S(2)}) collective-permute-start(bf16[4,32,1024]{2,1,0:T(8,128)(2,1)S(1)} %get-tuple-element.29), channel_id=1, source_target_pairs={{0,4},{1,5},{2,6},{3,7},{4,8},{5,9},{6,10},{7,11},{8,12},{9,13},{1... | collective-permute-start | bytes 786440 | tf_op jit(solution)/shard_map/ppermute | solution.py:112
  148.8 5.8 %collective-permute-start.31 = (bf16[4,32,1024]{2,1,0:T(8,128)(2,1)S(1)}, bf16[4,32,1024]{2,1,0:T(8,128)(2,1)S(1)}, u32[]{:S(2)}, u32[]{:S(2)}) collective-permute-start(bf16[4,32,1024]{2,1,0:T(8,128)(2,1)S(1)} %get-tuple-element.30), channel_id=1, source_target_pairs={{0,12},{1,13},{2,14},{3,15},{4,0},{5,1},{6,2},{7,3},{8,4},{9,5},{1... | collective-permute-start | bytes 786440 | tf_op jit(solution)/shard_map/ppermute | solution.py:112
  155.5 26.5 %all-to-all-start.1 = ((bf16[8,32,1024]{2,1,0:T(8,128)(2,1)}), bf16[8,32,1024]{2,1,0:T(8,128)(2,1)}, u32[]{:S(2)}, u32[]{:S(2)}) async-start(bf16[8,32,1024]{2,1,0:T(8,128)(2,1)} %pad_maximum_fusion), calls=%async_computation.1 | async-start | bytes 1048576 | tf_op jit(solution)/shard_map/all_to_all | solution.py:232

commit v16 on v14

--- a/solution.py
+++ b/solution.py
@@ -58,15 +58,19 @@
                 o_ref[0, :, lo:lo + head_dim] = o.astype(o_ref.dtype)
 
 
-def attend_local(q_sets, kv_sets, live_sets, active_sets, first_event, heads, out_dtype):
+def masked_values(piece, live, first_event):
+    count, width = piece.shape[1], piece.shape[2] // 2
+    events = (first_event + jnp.arange(count)).astype(jnp.float32)
+    keep = (events[None, :] < live[:, None]).astype(jnp.float32) / live[:, None]
+    return (piece[:, :, width:].astype(jnp.float32) * keep[:, :, None]).astype(jnp.bfloat16)
+
+
+def attend_local(q_sets, kv_sets, vk_sets, live_sets, active_sets, first_event, heads, out_dtype):
     rows, cands, width = q_sets[0].shape
     count = kv_sets[0].shape[1]
     head_dim = width // heads
-    events = (first_event + jnp.arange(count)).astype(jnp.float32)
     operands, n_live = [], []
-    for queries, piece, live in zip(q_sets, kv_sets, live_sets):
-        keep = (events[None, :] < live[:, None]).astype(jnp.float32) / live[:, None]
-        values = (piece[:, :, width:].astype(jnp.float32) * keep[:, :, None]).astype(jnp.bfloat16)
+    for queries, piece, values, live in zip(q_sets, kv_sets, vk_sets, live_sets):
         operands += [queries, piece, values]
         n_live.append(jnp.clip(live.astype(jnp.int32) - first_event, 0, count).astype(jnp.int32))
     n_live = [jnp.where(on, n, 0) for n, on in zip(n_live, active_sets)]
@@ -211,6 +215,7 @@
     q_out = jnp.where(send_filled[:, None, None], q_pos[send_pos], jnp.zeros((), jnp.bfloat16))
     q_in = lax.all_to_all(q_out, "group", split_axis=0, concat_axis=0, tiled=True)
     kv_slots = kv_cache[chosen]
+    vk_slots = masked_values(kv_cache, row_live, member_now * count)[chosen]
     live_slots = row_live[chosen]
     slot_count = q_in.shape[0]
     split = slot_count // 2
@@ -219,6 +224,7 @@
     partials = attend_local(
         q_sets,
         [kv_slots[rows_of] for rows_of, _ in halves],
+        [vk_slots[rows_of] for rows_of, _ in halves],
         [live_slots[rows_of] for rows_of, _ in halves],
         [filled[rows_of] for rows_of, _ in halves],
         member_now * count,

time: 185 us -> 191 us (1.032)
  local copies, waits for them, and re-layouts: 30.8 us -> 38.1 us
  starting transfers between devices: 66.2 us -> 64 us
    gather x0 -> x1, local copies, waits for them, and re-layouts: none -> 3.64 us  [on_device(): vk_slots = masked_values(kv_cache, row_live, member_now * count)[chosen]]
    ppermute x32, waiting for transfers between devices: 42.9 us -> 46.1 us  [send(): return lax.ppermute(value, 'member', shift_perm(grid, axis, shift))]
    slice x1, local copies, waits for them, and re-layouts: 0.07 us -> 3.09 us  [on_device(): vk_slots[rows_of]]
    all_to_all x1, waiting for transfers between devices: 2.23 us -> 0.01 us  [on_device(): lax.all_to_all(q_out, 'group', split_axis=0, concat_axis=0, tiled=True)]
    unnamed x27 -> x25, local copies, waits for them, and re-layouts: 10.5 us -> 10.5 us
  transfers between devices with their start and end apart: 34 -> 34, of which waited for: 11 -> 11; matrix products, arithmetic and copies ran while one was open for 18% -> 21% of each run, Pallas kernels for 0% -> 0%
where the time goes in v16:
time: 191 us; the launch traced here: 190 us
  starting transfers between devices  64 us (34%)
  waiting for transfers between devices  52.1 us (27%)
  local copies, waits for them, and re-layouts  38.1 us (20%)
  other arithmetic  15.6 us (8%)
  Pallas kernels  12.4 us (6%)
  matrix products  7.73 us (4%)
    ppermute x32, waiting for transfers between devices, send(): return lax.ppermute(value, 'member', shift_perm(grid, axis, shift))  46.1 us
    ppermute x32, starting transfers between devices, send(): return lax.ppermute(value, 'member', shift_perm(grid, axis, shift))  42.9 us
    all_to_all x1, starting transfers between devices, on_device(): lax.all_to_all(summed, 'group', split_axis=0, concat_axis=0, tiled=True)  15.1 us
    pallas_call x1, Pallas kernels, attend_local(): pl.pallas_call(kernel, out_shape=[jax.ShapeDtypeStruct((rows, cands, widt...  12.4 us
    unnamed x25, local copies, waits for them, and re-layouts  10.5 us
    all_to_all x1, waiting for transfers between devices, on_device(): lax.all_to_all(summed, 'group', split_axis=0, concat_axis=0, tiled=True)  6.01 us
    all_to_all x1, starting transfers between devices, on_device(): lax.all_to_all(q_out, 'group', split_axis=0, concat_axis=0, tiled=True)  5.96 us
    gather x1, local copies, waits for them, and re-layouts, on_device(): kv_slots = kv_cache[chosen]  4.97 us
  transfers between devices with their start and end apart: 34, of which 11 were waited for; matrix products, arithmetic and copies ran while one was open for 21% of the time, Pallas kernels for 0%

profile of v16, /device:TPU:1, one launch (start us, length us, event | category | flops | bytes accessed | tf_op | source)
XLA Modules:
  0.0 190.4 jit_solution(5028362259180981881)
XLA Ops:
  0.0 1.0 fusion.36
  1.0 1.3 gather_fusion
  4.1 1.2 convert_reduce_fusion
  5.5 1.3 fusion.8
  7.0 2.7 %fusion.19 = bf16[32,8,1024]{2,1,0:T(8,128)(2,1)S(1)} fusion(bf16[1024,2048]{1,0:T(8,128)(2,1)} %param.12, bf16[32,8,1024]{2,1,0:T(8,128)(2,1)} %param.7, f32[32,8]{1,0:T(8,128)S(1)} %copy.37, f32[32,8]{1,0:T(8,128)S(1)} %copy.35), kind=kOutput, calls=%fused_computation.39 | convolution fusion | flops 539492352 | bytes 3147776 | tf_op jit(solution)/shard_map/dot_general | solution.py:211
  10.5 0.9 broadcast_select_fusion
  11.4 6.0 %all-to-all-start = ((bf16[8,32,1024]{2,1,0:T(8,128)(2,1)}), bf16[8,32,1024]{2,1,0:T(8,128)(2,1)S(1)}, u32[]{:S(2)}, u32[]{:S(2)}) async-start(bf16[8,32,1024]{2,1,0:T(8,128)(2,1)} %broadcast_select_fusion), calls=%async_computation | async-start | bytes 1048576 | tf_op jit(solution)/shard_map/all_to_all | solution.py:216
  19.0 5.0 %gather_fusion.6 = bf16[8,128,2048]{2,1,0:T(8,128)(2,1)} fusion(bf16[8,128,2048]{2,1,0:T(8,128)(2,1)} %param.8, s32[1024]{0:T(1024)S(1)} %pad_clamp_fusion.3), kind=kCustom, calls=%fused_computation.6 | custom fusion | bytes 8388640 | tf_op jit(solution)/shard_map/gather | solution.py:217
  24.1 3.4 %multiply_convert_fusion = bf16[8,128,1024]{2,1,0:T(8,128)(2,1)} fusion(f32[8,128]{1,0:T(8,128)S(1)} %convert_divide_fusion, bf16[8,128,2048]{2,1,0:T(8,128)(2,1)} %param.8), kind=kLoop, calls=%fused_computation.9 | loop fusion | flops 3145728 | bytes 4198400 | tf_op jit(solution)/shard_map/convert_element_type | solution.py:65
  27.4 3.6 %gather_fusion.7 = bf16[8,128,1024]{2,1,0:T(8,128)(2,1)} fusion(bf16[8,128,1024]{2,1,0:T(8,128)(2,1)} %multiply_convert_fusion, s32[1024]{0:T(1024)S(1)} %pad_clamp_fusion.3), kind=kCustom, calls=%fused_computation.7 | custom fusion | bytes 4194336 | tf_op jit(solution)/shard_map/gather | solution.py:218
  31.1 0.9 constant_dynamic-update-slice_fusion.18
  32.0 3.8 %collective-permute-start.8 = (bf16[4,32,1024]{2,1,0:T(8,128)(2,1)S(1)}, bf16[4,32,1024]{2,1,0:T(8,128)(2,1)S(1)}, u32[]{:S(2)}, u32[]{:S(2)}) collective-permute-start(bf16[4,32,1024]{2,1,0:T(8,128)(2,1)S(1)} %get-tuple-element.39), channel_id=1, source_target_pairs={{0,12},{1,13},{2,14},{3,15},{4,0},{5,1},{6,2},{7,3},{8,4},{9,5},{1... | collective-permute-start | bytes 786440 | tf_op jit(solution)/shard_map/ppermute | solution.py:116
  35.7 2.5 %collective-permute-start = (bf16[4,32,1024]{2,1,0:T(8,128)(2,1)S(1)}, bf16[4,32,1024]{2,1,0:T(8,128)(2,1)S(1)}, u32[]{:S(2)}, u32[]{:S(2)}) collective-permute-start(bf16[4,32,1024]{2,1,0:T(8,128)(2,1)S(1)} %get-tuple-element.40), channel_id=1, source_target_pairs={{0,3},{1,0},{2,1},{3,2},{4,7},{5,4},{6,5},{7,6},{8,11},{9,8},{10,9... | collective-permute-start | bytes 786440 | tf_op jit(solution)/shard_map/ppermute | solution.py:116
  38.2 3.1 %fusion.53 = (bf16[4,128,1024]{2,1,0:T(8,128)(2,1)}, bf16[4,128,1024]{2,1,0:T(8,128)(2,1)}) fusion(bf16[8,128,1024]{2,1,0:T(8,128)(2,1)} %gather_fusion.7), kind=kLoop, calls=%fused_computation.155 | loop fusion | bytes 4194304 | tf_op jit(solution)/shard_map/slice | solution.py:227
  41.3 3.2 %collective-permute-done.9 = bf16[4,32,1024]{2,1,0:T(8,128)(2,1)S(1)} collective-permute-done((bf16[4,32,1024]{2,1,0:T(8,128)(2,1)S(1)}, bf16[4,32,1024]{2,1,0:T(8,128)(2,1)S(1)}, u32[]{:S(2)}, u32[]{:S(2)}) %collective-permute-start.9) | collective-permute-done | bytes 262176 | tf_op jit(solution)/shard_map/ppermute | solution.py:116
  44.6 2.7 %collective-permute-start.11 = (bf16[4,16,1024]{2,1,0:T(8,128)(2,1)S(1)}, bf16[4,16,1024]{2,1,0:T(8,128)(2,1)S(1)}, u32[]{:S(2)}, u32[]{:S(2)}) collective-permute-start(bf16[4,16,1024]{2,1,0:T(8,128)(2,1)S(1)} %slice.209), channel_id=1, source_target_pairs={{0,12},{1,13},{2,14},{3,15},{4,0},{5,1},{6,2},{7,3},{8,4},{9,5},{1... | collective-permute-start | bytes 393224 | tf_op jit(solution)/shard_map/ppermute | solution.py:116
  47.4 1.3 collective-permute-start.2
  48.7 1.5 collective-permute-start.3
  50.2 0.7 constant_dynamic-update-slice_fusion.17
  51.0 0.7 constant_dynamic-update-slice_fusion.3
  53.0 0.7 constant_dynamic-update-slice_fusion.14
  53.8 1.3 collective-permute-start.12
  55.3 0.7 constant_dynamic-update-slice_fusion.2
  56.6 0.7 constant_dynamic-update-slice_fusion
  57.4 1.8 collective-permute-start.4
  59.2 2.5 %fusion.52 = (bf16[4,128,2048]{2,1,0:T(8,128)(2,1)}, bf16[4,128,2048]{2,1,0:T(8,128)(2,1)}) fusion(bf16[8,128,2048]{2,1,0:T(8,128)(2,1)S(1)} %copy-done.2), kind=kLoop, calls=%fused_computation.154 | loop fusion | bytes 8388608 | tf_op jit(solution)/shard_map/slice | solution.py:226
  61.7 16.7 %collective-permute-done.13 = bf16[4,128,1024]{2,1,0:T(8,128)(2,1)S(1)} collective-permute-done((bf16[4,128,1024]{2,1,0:T(8,128)(2,1)S(1)}, bf16[4,128,1024]{2,1,0:T(8,128)(2,1)S(1)}, u32[]{:S(2)}, u32[]{:S(2)}) %collective-permute-start.13) | collective-permute-done | bytes 1048608 | tf_op jit(solution)/shard_map/ppermute | solution.py:116
  78.6 2.7 %collective-permute-start.15 = (bf16[4,64,1024]{2,1,0:T(8,128)(2,1)S(1)}, bf16[4,64,1024]{2,1,0:T(8,128)(2,1)S(1)}, u32[]{:S(2)}, u32[]{:S(2)}) collective-permute-start(bf16[4,64,1024]{2,1,0:T(8,128)(2,1)S(1)} %slice.211), channel_id=1, source_target_pairs={{0,3},{1,0},{2,1},{3,2},{4,7},{5,4},{6,5},{7,6},{8,11},{9,8},{10,9... | collective-permute-start | bytes 1572872 | tf_op jit(solution)/shard_map/ppermute | solution.py:116
  82.2 2.9 %collective-permute-start.7 = (bf16[4,64,1024]{2,1,0:T(8,128)(2,1)S(1)}, bf16[4,64,1024]{2,1,0:T(8,128)(2,1)S(1)}, u32[]{:S(2)}, u32[]{:S(2)}) collective-permute-start(bf16[4,64,1024]{2,1,0:T(8,128)(2,1)S(1)} %slice.204), channel_id=1, source_target_pairs={{0,12},{1,13},{2,14},{3,15},{4,0},{5,1},{6,2},{7,3},{8,4},{9,5},{1... | collective-permute-start | bytes 1572872 | tf_op jit(solution)/shard_map/ppermute | solution.py:116
  85.1 1.1 constant_dynamic-update-slice_fusion.22
  86.2 1.1 constant_dynamic-update-slice_fusion.8
  87.2 2.6 %collective-permute-done.14 = bf16[4,64,1024]{2,1,0:T(8,128)(2,1)S(1)} collective-permute-done((bf16[4,64,1024]{2,1,0:T(8,128)(2,1)S(1)}, bf16[4,64,1024]{2,1,0:T(8,128)(2,1)S(1)}, u32[]{:S(2)}, u32[]{:S(2)}) %collective-permute-start.14) | collective-permute-done | bytes 524320 | tf_op jit(solution)/shard_map/ppermute | solution.py:116
  89.9 0.8 constant_dynamic-update-slice_fusion.21
  90.7 0.8 constant_dynamic-update-slice_fusion.20
  91.5 1.4 collective-permute-done.6
  92.9 0.8 constant_dynamic-update-slice_fusion.7
  93.7 1.1 constant_dynamic-update-slice_fusion.19.refs_3_
  94.8 0.9 constant_dynamic-update-slice_fusion.6
  95.6 1.1 constant_dynamic-update-slice_fusion.5.refs_0_
  96.7 12.4 %shard_map.73 = (bf16[4,512,1024]{2,1,0:T(8,128)(2,1)}, bf16[4,512,1024]{2,1,0:T(8,128)(2,1)}) custom-call(s32[8]{0:T(128)} %pad_add_fusion.n_live_ref, bf16[4,512,1024]{2,1,0:T(8,128)(2,1)} %constant_dynamic-update-slice_fusion.5.refs_0_, bf16[4,128,2048]{2,1,0:T(8,128)(2,1)} %get-tuple-element.24.refs_1_, bf16[4,128,1024]{2,1,0:T(8,128)(2,1)} %get-tuple-element.30.refs_2_, ...), custom_call_target="tpu_custom_call" | custom-call | flops 2147483648 | bytes 20971520 | tf_op jit(solution)/shard_map/pallas_call | solution.py:85
  109.2 1.4 fusion.50
  110.7 2.7 %collective-permute-start.18 = (bf16[4,64,1024]{2,1,0:T(8,128)(2,1)S(1)}, bf16[4,64,1024]{2,1,0:T(8,128)(2,1)S(1)}, u32[]{:S(2)}, u32[]{:S(2)}) collective-permute-start(bf16[4,64,1024]{2,1,0:T(8,128)(2,1)S(1)} %get-tuple-element.18), channel_id=1, source_target_pairs={{0,12},{1,13},{2,14},{3,15},{4,0},{5,1},{6,2},{7,3},{8,4},{9,5},{1... | collective-permute-start | bytes 1572872 | tf_op jit(solution)/shard_map/ppermute | solution.py:116
  113.3 1.3 fusion.51
  115.0 2.3 %collective-permute-start.26 = (bf16[4,64,1024]{2,1,0:T(8,128)(2,1)S(1)}, bf16[4,64,1024]{2,1,0:T(8,128)(2,1)S(1)}, u32[]{:S(2)}, u32[]{:S(2)}) collective-permute-start(bf16[4,64,1024]{2,1,0:T(8,128)(2,1)S(1)} %get-tuple-element.22), channel_id=1, source_target_pairs={{0,3},{1,0},{2,1},{3,2},{4,7},{5,4},{6,5},{7,6},{8,11},{9,8},{10,9... | collective-permute-start | bytes 1572872 | tf_op jit(solution)/shard_map/ppermute | solution.py:116
  117.4 3.2 %collective-permute-done.16 = bf16[4,64,1024]{2,1,0:T(8,128)(2,1)S(1)} collective-permute-done((bf16[4,64,1024]{2,1,0:T(8,128)(2,1)S(1)}, bf16[4,64,1024]{2,1,0:T(8,128)(2,1)S(1)}, u32[]{:S(2)}, u32[]{:S(2)}) %collective-permute-start.16) | collective-permute-done | bytes 524320 | tf_op jit(solution)/shard_map/ppermute | solution.py:116
  121.2 2.7 %collective-permute-start.19 = (bf16[4,128,1024]{2,1,0:T(8,128)(2,1)S(1)}, bf16[4,128,1024]{2,1,0:T(8,128)(2,1)S(1)}, u32[]{:S(2)}, u32[]{:S(2)}) collective-permute-start(bf16[4,128,1024]{2,1,0:T(8,128)(2,1)S(1)} %get-tuple-element.16), channel_id=1, source_target_pairs={{0,12},{1,13},{2,14},{3,15},{4,0},{5,1},{6,2},{7,3},{8,4},{9,5},{1... | collective-permute-start | bytes 3145736 | tf_op jit(solution)/shard_map/ppermute | solution.py:116
  124.2 0.7 add_convert_fusion.1
  125.2 2.5 %collective-permute-start.27 = (bf16[4,128,1024]{2,1,0:T(8,128)(2,1)S(1)}, bf16[4,128,1024]{2,1,0:T(8,128)(2,1)S(1)}, u32[]{:S(2)}, u32[]{:S(2)}) collective-permute-start(bf16[4,128,1024]{2,1,0:T(8,128)(2,1)S(1)} %get-tuple-element.20), channel_id=1, source_target_pairs={{0,3},{1,0},{2,1},{3,2},{4,7},{5,4},{6,5},{7,6},{8,11},{9,8},{10,9... | collective-permute-start | bytes 3145736 | tf_op jit(solution)/shard_map/ppermute | solution.py:116
  127.7 14.4 %collective-permute-done.17 = bf16[4,128,1024]{2,1,0:T(8,128)(2,1)S(1)} collective-permute-done((bf16[4,128,1024]{2,1,0:T(8,128)(2,1)S(1)}, bf16[4,128,1024]{2,1,0:T(8,128)(2,1)S(1)}, u32[]{:S(2)}, u32[]{:S(2)}) %collective-permute-start.17) | collective-permute-done | bytes 1048608 | tf_op jit(solution)/shard_map/ppermute | solution.py:116
  142.2 0.7 fusion.48
  143.5 2.1 %collective-permute-start.22 = (bf16[4,16,1024]{2,1,0:T(8,128)(2,1)S(1)}, bf16[4,16,1024]{2,1,0:T(8,128)(2,1)S(1)}, u32[]{:S(2)}, u32[]{:S(2)}) collective-permute-start(bf16[4,16,1024]{2,1,0:T(8,128)(2,1)S(1)} %get-tuple-element.32), channel_id=1, source_target_pairs={{0,3},{1,0},{2,1},{3,2},{4,7},{5,4},{6,5},{7,6},{8,11},{9,8},{10,9... | collective-permute-start | bytes 393224 | tf_op jit(solution)/shard_map/ppermute | solution.py:116
  145.7 0.7 fusion.49
  146.5 2.7 %collective-permute-start.30 = (bf16[4,16,1024]{2,1,0:T(8,128)(2,1)S(1)}, bf16[4,16,1024]{2,1,0:T(8,128)(2,1)S(1)}, u32[]{:S(2)}, u32[]{:S(2)}) collective-permute-start(bf16[4,16,1024]{2,1,0:T(8,128)(2,1)S(1)} %get-tuple-element.34), channel_id=1, source_target_pairs={{0,12},{1,13},{2,14},{3,15},{4,0},{5,1},{6,2},{7,3},{8,4},{9,5},{1... | collective-permute-start | bytes 393224 | tf_op jit(solution)/shard_map/ppermute | solution.py:116
  149.9 2.7 %collective-permute-start.23 = (bf16[4,32,1024]{2,1,0:T(8,128)(2,1)S(1)}, bf16[4,32,1024]{2,1,0:T(8,128)(2,1)S(1)}, u32[]{:S(2)}, u32[]{:S(2)}) collective-permute-start(bf16[4,32,1024]{2,1,0:T(8,128)(2,1)S(1)} %get-tuple-element.26), channel_id=1, source_target_pairs={{0,3},{1,0},{2,1},{3,2},{4,7},{5,4},{6,5},{7,6},{8,11},{9,8},{10,9... | collective-permute-start | bytes 786440 | tf_op jit(solution)/shard_map/ppermute | solution.py:116
  152.8 2.7 %collective-permute-start.31 = (bf16[4,32,1024]{2,1,0:T(8,128)(2,1)S(1)}, bf16[4,32,1024]{2,1,0:T(8,128)(2,1)S(1)}, u32[]{:S(2)}, u32[]{:S(2)}) collective-permute-start(bf16[4,32,1024]{2,1,0:T(8,128)(2,1)S(1)} %get-tuple-element.28), channel_id=1, source_target_pairs={{0,12},{1,13},{2,14},{3,15},{4,0},{5,1},{6,2},{7,3},{8,4},{9,5},{1... | collective-permute-start | bytes 786440 | tf_op jit(solution)/shard_map/ppermute | solution.py:116
  155.5 2.3 %collective-permute-done.21 = bf16[4,32,1024]{2,1,0:T(8,128)(2,1)S(1)} collective-permute-done((bf16[4,32,1024]{2,1,0:T(8,128)(2,1)S(1)}, bf16[4,32,1024]{2,1,0:T(8,128)(2,1)S(1)}, u32[]{:S(2)}, u32[]{:S(2)}) %collective-permute-start.21) | collective-permute-done | bytes 262176 | tf_op jit(solution)/shard_map/ppermute | solution.py:116
  158.0 1.3 collective-permute-done.29
  159.4 0.8 pad_maximum_fusion
  160.2 15.1 %all-to-all-start.1 = ((bf16[8,32,1024]{2,1,0:T(8,128)(2,1)}), bf16[8,32,1024]{2,1,0:T(8,128)(2,1)}, u32[]{:S(2)}, u32[]{:S(2)}) async-start(bf16[8,32,1024]{2,1,0:T(8,128)(2,1)} %pad_maximum_fusion), calls=%async_computation.1 | async-start | bytes 1048576 | tf_op jit(solution)/shard_map/all_to_all | solution.py:237
  175.3 3.4 %multiply_bitcast_fusion = f32[32,8,1024]{2,1,0:T(8,128)} fusion(bf16[1024,2048]{1,0:T(8,128)(2,1)} %param.12, bf16[32,8,1024]{2,1,0:T(8,128)(2,1)S(1)} %copy-done.5, f32[32,8]{1,0:T(8,128)S(1)} %copy.37, f32[32,8]{1,0:T(8,128)S(1)} %copy.35), kind=kOutput, calls=%fused_computation.37 | convolution fusion | flops 538968064 | bytes 3672064 | tf_op jit(solution)/shard_map/dot_general | solution.py:240
  178.8 6.0 %all-to-all-done.1 = bf16[8,32,1024]{2,1,0:T(8,128)(2,1)} async-done(((bf16[8,32,1024]{2,1,0:T(8,128)(2,1)}), bf16[8,32,1024]{2,1,0:T(8,128)(2,1)}, u32[]{:S(2)}, u32[]{:S(2)}) %all-to-all-start.1) | async-done | bytes 524320 | tf_op jit(solution)/shard_map/all_to_all | solution.py:237
  184.8 1.6 gather_fusion.8
  186.9 1.9 fusion.14
  188.7 1.6 fusion.7
  (111 shorter events, 12.2 us)
Async XLA Ops:
  0.0 188.7 %copy-start = (bf16[1024,1024]{1,0:T(8,128)(2,1)S(1)}, bf16[1024,1024]{1,0:T(8,128)(2,1)}, u32[]{:S(2)}) copy-start(bf16[1024,1024]{1,0:T(8,128)(2,1)} %param.13) | copy-start | bytes 6291460
  9.6 8.1 %copy-start.1 = (s32[64]{0:T(128)S(1)}, s32[64]{0:T(128)}, u32[]{:S(2)}) copy-start(s32[64]{0:T(128)} %param.11) | copy-start | bytes 772
  11.4 19.7 %all-to-all-start = ((bf16[8,32,1024]{2,1,0:T(8,128)(2,1)}), bf16[8,32,1024]{2,1,0:T(8,128)(2,1)S(1)}, u32[]{:S(2)}, u32[]{:S(2)}) async-start(bf16[8,32,1024]{2,1,0:T(8,128)(2,1)} %broadcast_select_fusion), calls=%async_computation | async-start | bytes 1048576 | tf_op jit(solution)/shard_map/all_to_all | solution.py:216
  32.0 12.7 %collective-permute-start.8 = (bf16[4,32,1024]{2,1,0:T(8,128)(2,1)S(1)}, bf16[4,32,1024]{2,1,0:T(8,128)(2,1)S(1)}, u32[]{:S(2)}, u32[]{:S(2)}) collective-permute-start(bf16[4,32,1024]{2,1,0:T(8,128)(2,1)S(1)} %get-tuple-element.39), channel_id=1, source_target_pairs={{0,12},{1,13},{2,14},{3,15},{4,0},{5,1},{6,2},{7,3},{8,4},{9,5},{1... | collective-permute-start | bytes 786440 | tf_op jit(solution)/shard_map/ppermute | solution.py:116
  35.7 8.8 %collective-permute-start.9 = (bf16[4,32,1024]{2,1,0:T(8,128)(2,1)S(1)}, bf16[4,32,1024]{2,1,0:T(8,128)(2,1)S(1)}, u32[]{:S(2)}, u32[]{:S(2)}) collective-permute-start(bf16[4,32,1024]{2,1,0:T(8,128)(2,1)S(1)} %get-tuple-element.39), channel_id=1, source_target_pairs={{0,4},{1,5},{2,6},{3,7},{4,8},{5,9},{6,10},{7,11},{8,12},{9,13},{1... | collective-permute-start | bytes 786440 | tf_op jit(solution)/shard_map/ppermute | solution.py:116
  35.7 23.5 %copy-start.2 = (bf16[8,128,2048]{2,1,0:T(8,128)(2,1)S(1)}, bf16[8,128,2048]{2,1,0:T(8,128)(2,1)}, u32[]{:S(2)}) copy-start(bf16[8,128,2048]{2,1,0:T(8,128)(2,1)} %gather_fusion.6) | copy-start | bytes 12582916
  35.7 12.9 %collective-permute-start = (bf16[4,32,1024]{2,1,0:T(8,128)(2,1)S(1)}, bf16[4,32,1024]{2,1,0:T(8,128)(2,1)S(1)}, u32[]{:S(2)}, u32[]{:S(2)}) collective-permute-start(bf16[4,32,1024]{2,1,0:T(8,128)(2,1)S(1)} %get-tuple-element.40), channel_id=1, source_target_pairs={{0,3},{1,0},{2,1},{3,2},{4,7},{5,4},{6,5},{7,6},{8,11},{9,8},{10,9... | collective-permute-start | bytes 786440 | tf_op jit(solution)/shard_map/ppermute | solution.py:116
  38.2 9.2 %collective-permute-start.1 = (bf16[4,32,1024]{2,1,0:T(8,128)(2,1)S(1)}, bf16[4,32,1024]{2,1,0:T(8,128)(2,1)S(1)}, u32[]{:S(2)}, u32[]{:S(2)}) collective-permute-start(bf16[4,32,1024]{2,1,0:T(8,128)(2,1)S(1)} %get-tuple-element.40), channel_id=1, source_target_pairs={{0,1},{1,2},{2,3},{3,0},{4,5},{5,6},{6,7},{7,4},{8,9},{9,10},{10,1... | collective-permute-start | bytes 786440 | tf_op jit(solution)/shard_map/ppermute | solution.py:116
  44.5 7.2 %collective-permute-start.10 = (bf16[4,16,1024]{2,1,0:T(8,128)(2,1)S(1)}, bf16[4,16,1024]{2,1,0:T(8,128)(2,1)S(1)}, u32[]{:S(2)}, u32[]{:S(2)}) collective-permute-start(bf16[4,16,1024]{2,1,0:T(8,128)(2,1)S(1)} %slice.208), channel_id=1, source_target_pairs={{0,4},{1,5},{2,6},{3,7},{4,8},{5,9},{6,10},{7,11},{8,12},{9,13},{1... | collective-permute-start | bytes 393224 | tf_op jit(solution)/shard_map/ppermute | solution.py:116
  44.6 7.7 %collective-permute-start.11 = (bf16[4,16,1024]{2,1,0:T(8,128)(2,1)S(1)}, bf16[4,16,1024]{2,1,0:T(8,128)(2,1)S(1)}, u32[]{:S(2)}, u32[]{:S(2)}) collective-permute-start(bf16[4,16,1024]{2,1,0:T(8,128)(2,1)S(1)} %slice.209), channel_id=1, source_target_pairs={{0,12},{1,13},{2,14},{3,15},{4,0},{5,1},{6,2},{7,3},{8,4},{9,5},{1... | collective-permute-start | bytes 393224 | tf_op jit(solution)/shard_map/ppermute | solution.py:116
  47.4 7.9 %collective-permute-start.2 = (bf16[4,16,1024]{2,1,0:T(8,128)(2,1)S(1)}, bf16[4,16,1024]{2,1,0:T(8,128)(2,1)S(1)}, u32[]{:S(2)}, u32[]{:S(2)}) collective-permute-start(bf16[4,16,1024]{2,1,0:T(8,128)(2,1)S(1)} %slice.201), channel_id=1, source_target_pairs={{0,1},{1,2},{2,3},{3,0},{4,5},{5,6},{6,7},{7,4},{8,9},{9,10},{10,1... | collective-permute-start | bytes 393224 | tf_op jit(solution)/shard_map/ppermute | solution.py:116
  48.7 7.2 %collective-permute-start.3 = (bf16[4,16,1024]{2,1,0:T(8,128)(2,1)S(1)}, bf16[4,16,1024]{2,1,0:T(8,128)(2,1)S(1)}, u32[]{:S(2)}, u32[]{:S(2)}) collective-permute-start(bf16[4,16,1024]{2,1,0:T(8,128)(2,1)S(1)} %slice.202), channel_id=1, source_target_pairs={{0,3},{1,0},{2,1},{3,2},{4,7},{5,4},{6,5},{7,6},{8,11},{9,8},{10,9... | collective-permute-start | bytes 393224 | tf_op jit(solution)/shard_map/ppermute | solution.py:116
  53.8 24.8 %collective-permute-start.12 = (bf16[4,128,1024]{2,1,0:T(8,128)(2,1)S(1)}, bf16[4,128,1024]{2,1,0:T(8,128)(2,1)S(1)}, u32[]{:S(2)}, u32[]{:S(2)}) collective-permute-start(bf16[4,128,1024]{2,1,0:T(8,128)(2,1)S(1)} %get-tuple-element.41), channel_id=1, source_target_pairs={{0,3},{1,0},{2,1},{3,2},{4,7},{5,4},{6,5},{7,6},{8,11},{9,8},{10,9... | collective-permute-start | bytes 3145736 | tf_op jit(solution)/shard_map/ppermute | solution.py:116
  55.1 23.4 %collective-permute-start.13 = (bf16[4,128,1024]{2,1,0:T(8,128)(2,1)S(1)}, bf16[4,128,1024]{2,1,0:T(8,128)(2,1)S(1)}, u32[]{:S(2)}, u32[]{:S(2)}) collective-permute-start(bf16[4,128,1024]{2,1,0:T(8,128)(2,1)S(1)} %get-tuple-element.41), channel_id=1, source_target_pairs={{0,1},{1,2},{2,3},{3,0},{4,5},{5,6},{6,7},{7,4},{8,9},{9,10},{10,1... | collective-permute-start | bytes 3145736 | tf_op jit(solution)/shard_map/ppermute | solution.py:116
  57.4 24.8 %collective-permute-start.4 = (bf16[4,128,1024]{2,1,0:T(8,128)(2,1)S(1)}, bf16[4,128,1024]{2,1,0:T(8,128)(2,1)S(1)}, u32[]{:S(2)}, u32[]{:S(2)}) collective-permute-start(bf16[4,128,1024]{2,1,0:T(8,128)(2,1)S(1)} %get-tuple-element.45), channel_id=1, source_target_pairs={{0,12},{1,13},{2,14},{3,15},{4,0},{5,1},{6,2},{7,3},{8,4},{9,5},{1... | collective-permute-start | bytes 3145736 | tf_op jit(solution)/shard_map/ppermute | solution.py:116
  59.1 22.9 %collective-permute-start.5 = (bf16[4,128,1024]{2,1,0:T(8,128)(2,1)S(1)}, bf16[4,128,1024]{2,1,0:T(8,128)(2,1)S(1)}, u32[]{:S(2)}, u32[]{:S(2)}) collective-permute-start(bf16[4,128,1024]{2,1,0:T(8,128)(2,1)S(1)} %get-tuple-element.45), channel_id=1, source_target_pairs={{0,4},{1,5},{2,6},{3,7},{4,8},{5,9},{6,10},{7,11},{8,12},{9,13},{1... | collective-permute-start | bytes 3145736 | tf_op jit(solution)/shard_map/ppermute | solution.py:116
  78.5 11.4 %collective-permute-start.14 = (bf16[4,64,1024]{2,1,0:T(8,128)(2,1)S(1)}, bf16[4,64,1024]{2,1,0:T(8,128)(2,1)S(1)}, u32[]{:S(2)}, u32[]{:S(2)}) collective-permute-start(bf16[4,64,1024]{2,1,0:T(8,128)(2,1)S(1)} %slice.210), channel_id=1, source_target_pairs={{0,1},{1,2},{2,3},{3,0},{4,5},{5,6},{6,7},{7,4},{8,9},{9,10},{10,1... | collective-permute-start | bytes 1572872 | tf_op jit(solution)/shard_map/ppermute | solution.py:116
  78.6 12.1 %collective-permute-start.15 = (bf16[4,64,1024]{2,1,0:T(8,128)(2,1)S(1)}, bf16[4,64,1024]{2,1,0:T(8,128)(2,1)S(1)}, u32[]{:S(2)}, u32[]{:S(2)}) collective-permute-start(bf16[4,64,1024]{2,1,0:T(8,128)(2,1)S(1)} %slice.211), channel_id=1, source_target_pairs={{0,3},{1,0},{2,1},{3,2},{4,7},{5,4},{6,5},{7,6},{8,11},{9,8},{10,9... | collective-permute-start | bytes 1572872 | tf_op jit(solution)/shard_map/ppermute | solution.py:116
  82.0 10.8 %collective-permute-start.6 = (bf16[4,64,1024]{2,1,0:T(8,128)(2,1)S(1)}, bf16[4,64,1024]{2,1,0:T(8,128)(2,1)S(1)}, u32[]{:S(2)}, u32[]{:S(2)}) collective-permute-start(bf16[4,64,1024]{2,1,0:T(8,128)(2,1)S(1)} %slice.203), channel_id=1, source_target_pairs={{0,4},{1,5},{2,6},{3,7},{4,8},{5,9},{6,10},{7,11},{8,12},{9,13},{1... | collective-permute-start | bytes 1572872 | tf_op jit(solution)/shard_map/ppermute | solution.py:116
  82.2 12.6 %collective-permute-start.7 = (bf16[4,64,1024]{2,1,0:T(8,128)(2,1)S(1)}, bf16[4,64,1024]{2,1,0:T(8,128)(2,1)S(1)}, u32[]{:S(2)}, u32[]{:S(2)}) collective-permute-start(bf16[4,64,1024]{2,1,0:T(8,128)(2,1)S(1)} %slice.204), channel_id=1, source_target_pairs={{0,12},{1,13},{2,14},{3,15},{4,0},{5,1},{6,2},{7,3},{8,4},{9,5},{1... | collective-permute-start | bytes 1572872 | tf_op jit(solution)/shard_map/ppermute | solution.py:116
  109.2 11.4 %copy-start.4 = (bf16[4,512,1024]{2,1,0:T(8,128)(2,1)S(1)}, bf16[4,512,1024]{2,1,0:T(8,128)(2,1)}, u32[]{:S(2)}) copy-start(bf16[4,512,1024]{2,1,0:T(8,128)(2,1)} %get-tuple-element.7) | copy-start | bytes 12582916
  110.6 13.6 %copy-start.3 = (bf16[4,512,1024]{2,1,0:T(8,128)(2,1)S(1)}, bf16[4,512,1024]{2,1,0:T(8,128)(2,1)}, u32[]{:S(2)}) copy-start(bf16[4,512,1024]{2,1,0:T(8,128)(2,1)} %get-tuple-element.8) | copy-start | bytes 12582916
  110.6 10.0 %collective-permute-start.16 = (bf16[4,64,1024]{2,1,0:T(8,128)(2,1)S(1)}, bf16[4,64,1024]{2,1,0:T(8,128)(2,1)S(1)}, u32[]{:S(2)}, u32[]{:S(2)}) collective-permute-start(bf16[4,64,1024]{2,1,0:T(8,128)(2,1)S(1)} %get-tuple-element.17), channel_id=1, source_target_pairs={{0,4},{1,5},{2,6},{3,7},{4,8},{5,9},{6,10},{7,11},{8,12},{9,13},{1... | collective-permute-start | bytes 1572872 | tf_op jit(solution)/shard_map/ppermute | solution.py:116
  110.7 9.9 %collective-permute-start.18 = (bf16[4,64,1024]{2,1,0:T(8,128)(2,1)S(1)}, bf16[4,64,1024]{2,1,0:T(8,128)(2,1)S(1)}, u32[]{:S(2)}, u32[]{:S(2)}) collective-permute-start(bf16[4,64,1024]{2,1,0:T(8,128)(2,1)S(1)} %get-tuple-element.18), channel_id=1, source_target_pairs={{0,12},{1,13},{2,14},{3,15},{4,0},{5,1},{6,2},{7,3},{8,4},{9,5},{1... | collective-permute-start | bytes 1572872 | tf_op jit(solution)/shard_map/ppermute | solution.py:116
  114.6 9.6 %collective-permute-start.24 = (bf16[4,64,1024]{2,1,0:T(8,128)(2,1)S(1)}, bf16[4,64,1024]{2,1,0:T(8,128)(2,1)S(1)}, u32[]{:S(2)}, u32[]{:S(2)}) collective-permute-start(bf16[4,64,1024]{2,1,0:T(8,128)(2,1)S(1)} %get-tuple-element.21), channel_id=1, source_target_pairs={{0,1},{1,2},{2,3},{3,0},{4,5},{5,6},{6,7},{7,4},{8,9},{9,10},{10,1... | collective-permute-start | bytes 1572872 | tf_op jit(solution)/shard_map/ppermute | solution.py:116
  115.0 9.2 %collective-permute-start.26 = (bf16[4,64,1024]{2,1,0:T(8,128)(2,1)S(1)}, bf16[4,64,1024]{2,1,0:T(8,128)(2,1)S(1)}, u32[]{:S(2)}, u32[]{:S(2)}) collective-permute-start(bf16[4,64,1024]{2,1,0:T(8,128)(2,1)S(1)} %get-tuple-element.22), channel_id=1, source_target_pairs={{0,3},{1,0},{2,1},{3,2},{4,7},{5,4},{6,5},{7,6},{8,11},{9,8},{10,9... | collective-permute-start | bytes 1572872 | tf_op jit(solution)/shard_map/ppermute | solution.py:116
  121.2 21.0 %collective-permute-start.17 = (bf16[4,128,1024]{2,1,0:T(8,128)(2,1)S(1)}, bf16[4,128,1024]{2,1,0:T(8,128)(2,1)S(1)}, u32[]{:S(2)}, u32[]{:S(2)}) collective-permute-start(bf16[4,128,1024]{2,1,0:T(8,128)(2,1)S(1)} %get-tuple-element.15), channel_id=1, source_target_pairs={{0,4},{1,5},{2,6},{3,7},{4,8},{5,9},{6,10},{7,11},{8,12},{9,13},{1... | collective-permute-start | bytes 3145736 | tf_op jit(solution)/shard_map/ppermute | solution.py:116
  121.2 20.9 %collective-permute-start.19 = (bf16[4,128,1024]{2,1,0:T(8,128)(2,1)S(1)}, bf16[4,128,1024]{2,1,0:T(8,128)(2,1)S(1)}, u32[]{:S(2)}, u32[]{:S(2)}) collective-permute-start(bf16[4,128,1024]{2,1,0:T(8,128)(2,1)S(1)} %get-tuple-element.16), channel_id=1, source_target_pairs={{0,12},{1,13},{2,14},{3,15},{4,0},{5,1},{6,2},{7,3},{8,4},{9,5},{1... | collective-permute-start | bytes 3145736 | tf_op jit(solution)/shard_map/ppermute | solution.py:116
  124.9 20.8 %collective-permute-start.25 = (bf16[4,128,1024]{2,1,0:T(8,128)(2,1)S(1)}, bf16[4,128,1024]{2,1,0:T(8,128)(2,1)S(1)}, u32[]{:S(2)}, u32[]{:S(2)}) collective-permute-start(bf16[4,128,1024]{2,1,0:T(8,128)(2,1)S(1)} %get-tuple-element.19), channel_id=1, source_target_pairs={{0,1},{1,2},{2,3},{3,0},{4,5},{5,6},{6,7},{7,4},{8,9},{9,10},{10,1... | collective-permute-start | bytes 3145736 | tf_op jit(solution)/shard_map/ppermute | solution.py:116
  125.2 20.4 %collective-permute-start.27 = (bf16[4,128,1024]{2,1,0:T(8,128)(2,1)S(1)}, bf16[4,128,1024]{2,1,0:T(8,128)(2,1)S(1)}, u32[]{:S(2)}, u32[]{:S(2)}) collective-permute-start(bf16[4,128,1024]{2,1,0:T(8,128)(2,1)S(1)} %get-tuple-element.20), channel_id=1, source_target_pairs={{0,3},{1,0},{2,1},{3,2},{4,7},{5,4},{6,5},{7,6},{8,11},{9,8},{10,9... | collective-permute-start | bytes 3145736 | tf_op jit(solution)/shard_map/ppermute | solution.py:116
  142.9 6.8 %collective-permute-start.20 = (bf16[4,16,1024]{2,1,0:T(8,128)(2,1)S(1)}, bf16[4,16,1024]{2,1,0:T(8,128)(2,1)S(1)}, u32[]{:S(2)}, u32[]{:S(2)}) collective-permute-start(bf16[4,16,1024]{2,1,0:T(8,128)(2,1)S(1)} %get-tuple-element.31), channel_id=1, source_target_pairs={{0,1},{1,2},{2,3},{3,0},{4,5},{5,6},{6,7},{7,4},{8,9},{9,10},{10,1... | collective-permute-start | bytes 393224 | tf_op jit(solution)/shard_map/ppermute | solution.py:116
  143.5 6.2 %collective-permute-start.22 = (bf16[4,16,1024]{2,1,0:T(8,128)(2,1)S(1)}, bf16[4,16,1024]{2,1,0:T(8,128)(2,1)S(1)}, u32[]{:S(2)}, u32[]{:S(2)}) collective-permute-start(bf16[4,16,1024]{2,1,0:T(8,128)(2,1)S(1)} %get-tuple-element.32), channel_id=1, source_target_pairs={{0,3},{1,0},{2,1},{3,2},{4,7},{5,4},{6,5},{7,6},{8,11},{9,8},{10,9... | collective-permute-start | bytes 393224 | tf_op jit(solution)/shard_map/ppermute | solution.py:116
  146.4 6.2 %collective-permute-start.28 = (bf16[4,16,1024]{2,1,0:T(8,128)(2,1)S(1)}, bf16[4,16,1024]{2,1,0:T(8,128)(2,1)S(1)}, u32[]{:S(2)}, u32[]{:S(2)}) collective-permute-start(bf16[4,16,1024]{2,1,0:T(8,128)(2,1)S(1)} %get-tuple-element.33), channel_id=1, source_target_pairs={{0,4},{1,5},{2,6},{3,7},{4,8},{5,9},{6,10},{7,11},{8,12},{9,13},{1... | collective-permute-start | bytes 393224 | tf_op jit(solution)/shard_map/ppermute | solution.py:116
  146.5 6.1 %collective-permute-start.30 = (bf16[4,16,1024]{2,1,0:T(8,128)(2,1)S(1)}, bf16[4,16,1024]{2,1,0:T(8,128)(2,1)S(1)}, u32[]{:S(2)}, u32[]{:S(2)}) collective-permute-start(bf16[4,16,1024]{2,1,0:T(8,128)(2,1)S(1)} %get-tuple-element.34), channel_id=1, source_target_pairs={{0,12},{1,13},{2,14},{3,15},{4,0},{5,1},{6,2},{7,3},{8,4},{9,5},{1... | collective-permute-start | bytes 393224 | tf_op jit(solution)/shard_map/ppermute | solution.py:116
  149.7 25.6 %copy-start.5 = (bf16[32,8,1024]{2,1,0:T(8,128)(2,1)S(1)}, bf16[32,8,1024]{2,1,0:T(8,128)(2,1)}, u32[]{:S(2)}) copy-start(bf16[32,8,1024]{2,1,0:T(8,128)(2,1)} %param.7) | copy-start | bytes 1572868
  149.8 8.0 %collective-permute-start.21 = (bf16[4,32,1024]{2,1,0:T(8,128)(2,1)S(1)}, bf16[4,32,1024]{2,1,0:T(8,128)(2,1)S(1)}, u32[]{:S(2)}, u32[]{:S(2)}) collective-permute-start(bf16[4,32,1024]{2,1,0:T(8,128)(2,1)S(1)} %get-tuple-element.25), channel_id=1, source_target_pairs={{0,1},{1,2},{2,3},{3,0},{4,5},{5,6},{6,7},{7,4},{8,9},{9,10},{10,1... | collective-permute-start | bytes 786440 | tf_op jit(solution)/shard_map/ppermute | solution.py:116
  149.9 7.9 %collective-permute-start.23 = (bf16[4,32,1024]{2,1,0:T(8,128)(2,1)S(1)}, bf16[4,32,1024]{2,1,0:T(8,128)(2,1)S(1)}, u32[]{:S(2)}, u32[]{:S(2)}) collective-permute-start(bf16[4,32,1024]{2,1,0:T(8,128)(2,1)S(1)} %get-tuple-element.26), channel_id=1, source_target_pairs={{0,3},{1,0},{2,1},{3,2},{4,7},{5,4},{6,5},{7,6},{8,11},{9,8},{10,9... | collective-permute-start | bytes 786440 | tf_op jit(solution)/shard_map/ppermute | solution.py:116
  152.8 6.5 %collective-permute-start.29 = (bf16[4,32,1024]{2,1,0:T(8,128)(2,1)S(1)}, bf16[4,32,1024]{2,1,0:T(8,128)(2,1)S(1)}, u32[]{:S(2)}, u32[]{:S(2)}) collective-permute-start(bf16[4,32,1024]{2,1,0:T(8,128)(2,1)S(1)} %get-tuple-element.27), channel_id=1, source_target_pairs={{0,4},{1,5},{2,6},{3,7},{4,8},{5,9},{6,10},{7,11},{8,12},{9,13},{1... | collective-permute-start | bytes 786440 | tf_op jit(solution)/shard_map/ppermute | solution.py:116
  152.8 6.4 %collective-permute-start.31 = (bf16[4,32,1024]{2,1,0:T(8,128)(2,1)S(1)}, bf16[4,32,1024]{2,1,0:T(8,128)(2,1)S(1)}, u32[]{:S(2)}, u32[]{:S(2)}) collective-permute-start(bf16[4,32,1024]{2,1,0:T(8,128)(2,1)S(1)} %get-tuple-element.28), channel_id=1, source_target_pairs={{0,12},{1,13},{2,14},{3,15},{4,0},{5,1},{6,2},{7,3},{8,4},{9,5},{1... | collective-permute-start | bytes 786440 | tf_op jit(solution)/shard_map/ppermute | solution.py:116
  160.2 24.6 %all-to-all-start.1 = ((bf16[8,32,1024]{2,1,0:T(8,128)(2,1)}), bf16[8,32,1024]{2,1,0:T(8,128)(2,1)}, u32[]{:S(2)}, u32[]{:S(2)}) async-start(bf16[8,32,1024]{2,1,0:T(8,128)(2,1)} %pad_maximum_fusion), calls=%async_computation.1 | async-start | bytes 1048576 | tf_op jit(solution)/shard_map/all_to_all | solution.py:237

commit v17 on v14

--- a/solution.py
+++ b/solution.py
@@ -112,7 +112,7 @@
     return lax.ppermute(value, "member", shift_perm(grid, axis, shift))
 
 
-def ring_gather(block, grid, axis):
+def ring_gather(block, grid, axis, split_far=True):
     n = grid[axis]
     slots = {0: block}
     ahead, behind = block, block
@@ -123,6 +123,8 @@
     if n % 2 == 0:
         if n == 2:
             slots[1] = send(block, grid, axis, -1)
+        elif not split_far:
+            slots[n // 2] = send(behind, grid, axis, 1)
         else:
             half = block.shape[1] // 2
             first = send(behind[:, :half], grid, axis, 1)
@@ -131,7 +133,7 @@
     return jnp.concatenate([slots[r] for r in range(n)], axis=1)
 
 
-def ring_reduce(parts, grid, axis):
+def ring_reduce(parts, grid, axis, split_far=True):
     n = grid[axis]
     rows, total, width = parts.shape
     m = total // n
@@ -142,7 +144,9 @@
         return slots[0] + send(slots[1].astype(jnp.bfloat16), grid, axis, 1).astype(jnp.float32)
     top = (n - 1) // 2
     acc_ahead, acc_behind = slots[top], slots[n - top]
-    if n % 2 == 0:
+    if n % 2 == 0 and not split_far:
+        acc_ahead = acc_ahead + send(slots[n // 2].astype(jnp.bfloat16), grid, axis, 1).astype(jnp.float32)
+    elif n % 2 == 0:
         half = m // 2
         far = slots[n // 2].astype(jnp.bfloat16)
         got_first = send(far[:, :half], grid, axis, 1).astype(jnp.float32)
@@ -161,13 +165,13 @@
 
 def torus_gather(block, grid, order):
     rows, m, width = block.shape
-    out = ring_gather(block, grid, order[1])
+    out = ring_gather(block, grid, order[1], split_far=False)
     return ring_gather(out, grid, order[0])
 
 
 def torus_reduce(parts, grid, order):
     out = ring_reduce(parts, grid, order[0])
-    return ring_reduce(out, grid, order[1])
+    return ring_reduce(out, grid, order[1], split_far=False)
 
 
 def on_device(grid, candidates, kv_cache, cache_request, rank_request, hist_blocks, w_uq, w_out):

time: 185 us -> 190 us (1.027)
  waiting for transfers between devices: 51.2 us -> 68.7 us
  starting transfers between devices: 66.2 us -> 54.9 us
    ppermute x32 -> x28, waiting for transfers between devices: 42.9 us -> 62.7 us  [send(): return lax.ppermute(value, 'member', shift_perm(grid, axis, shift))]
    ppermute x32 -> x28, starting transfers between devices: 43.2 us -> 34.1 us  [send(): return lax.ppermute(value, 'member', shift_perm(grid, axis, shift))]
    slice x1, local copies, waits for them, and re-layouts: 2.5 us -> 4.74 us  [on_device(): kv_slots[rows_of]]
    all_to_all x1, waiting for transfers between devices: 2.23 us -> 0.01 us  [on_device(): lax.all_to_all(q_out, 'group', split_axis=0, concat_axis=0, tiled=True)]
    all_to_all x1, starting transfers between devices: 17 us -> 14.8 us  [on_device(): lax.all_to_all(summed, 'group', split_axis=0, concat_axis=0, tiled=True)]
    unnamed x27 -> x26, local copies, waits for them, and re-layouts: 10.5 us -> 9.77 us
  transfers between devices with their start and end apart: 34 -> 30, of which waited for: 11 -> 16; matrix products, arithmetic and copies ran while one was open for 18% -> 17% of each run, Pallas kernels for 0% -> 0%
where the time goes in v17:
time: 190 us
  waiting for transfers between devices  68.7 us (36%)
  starting transfers between devices  54.9 us (29%)
  local copies, waits for them, and re-layouts  31.5 us (17%)
  other arithmetic  14 us (7%)
  Pallas kernels  12.4 us (7%)
  matrix products  7.74 us (4%)
    ppermute x28, waiting for transfers between devices, send(): return lax.ppermute(value, 'member', shift_perm(grid, axis, shift))  62.7 us
    ppermute x28, starting transfers between devices, send(): return lax.ppermute(value, 'member', shift_perm(grid, axis, shift))  34.1 us
    all_to_all x1, starting transfers between devices, on_device(): lax.all_to_all(summed, 'group', split_axis=0, concat_axis=0, tiled=True)  14.8 us
    pallas_call x1, Pallas kernels, attend_local(): pl.pallas_call(kernel, out_shape=[jax.ShapeDtypeStruct((rows, cands, widt...  12.4 us
    unnamed x26, local copies, waits for them, and re-layouts  9.77 us
    all_to_all x1, waiting for transfers between devices, on_device(): lax.all_to_all(summed, 'group', split_axis=0, concat_axis=0, tiled=True)  6.03 us
    all_to_all x1, starting transfers between devices, on_device(): lax.all_to_all(q_out, 'group', split_axis=0, concat_axis=0, tiled=True)  5.97 us
    gather x1, local copies, waits for them, and re-layouts, on_device(): kv_slots = kv_cache[chosen]  4.94 us
  transfers between devices with their start and end apart: 30, of which 16 were waited for; matrix products, arithmetic and copies ran while one was open for 17% of the time, Pallas kernels for 0%

profile of v17, /device:TPU:1, one launch (start us, length us, event | category | flops | bytes accessed | tf_op | source)
XLA Modules:
  0.0 189.8 jit_solution(3070835874470786141)
XLA Ops:
  0.0 1.0 fusion.34
  1.4 0.6 gather_fusion.3
  2.1 0.6 gather_fusion.4
  3.1 1.2 convert_reduce_fusion
  4.4 1.3 fusion.8
  5.9 2.7 %fusion.19 = bf16[32,8,1024]{2,1,0:T(8,128)(2,1)S(1)} fusion(bf16[1024,2048]{1,0:T(8,128)(2,1)} %param.12, bf16[32,8,1024]{2,1,0:T(8,128)(2,1)} %param.7, f32[32,8]{1,0:T(8,128)S(1)} %copy.37, f32[32,8]{1,0:T(8,128)S(1)} %copy.35), kind=kOutput, calls=%fused_computation.41 | convolution fusion | flops 539492352 | bytes 3147776 | tf_op jit(solution)/shard_map/dot_general | solution.py:211
  9.5 0.9 broadcast_select_fusion
  10.4 6.0 %all-to-all-start = ((bf16[8,32,1024]{2,1,0:T(8,128)(2,1)}), bf16[8,32,1024]{2,1,0:T(8,128)(2,1)S(1)}, u32[]{:S(2)}, u32[]{:S(2)}) async-start(bf16[8,32,1024]{2,1,0:T(8,128)(2,1)} %broadcast_select_fusion), calls=%async_computation | async-start | bytes 1048576 | tf_op jit(solution)/shard_map/all_to_all | solution.py:216
  17.7 4.9 %gather_fusion.6 = bf16[8,128,2048]{2,1,0:T(8,128)(2,1)} fusion(bf16[8,128,2048]{2,1,0:T(8,128)(2,1)} %param.8, s32[1024]{0:T(1024)S(1)} %get-tuple-element.42), kind=kCustom, calls=%fused_computation.6 | custom fusion | bytes 8388640 | tf_op jit(solution)/shard_map/gather | solution.py:217
  22.6 4.7 %fusion.50 = (bf16[4,128,2048]{2,1,0:T(8,128)(2,1)}, bf16[4,128,2048]{2,1,0:T(8,128)(2,1)}) fusion(bf16[8,128,2048]{2,1,0:T(8,128)(2,1)} %gather_fusion.6), kind=kLoop, calls=%fused_computation.141 | loop fusion | bytes 8388608 | tf_op jit(solution)/shard_map/slice | solution.py:225
  27.4 0.9 fusion.53
  28.2 1.6 collective-permute-start.8
  30.7 2.1 %collective-permute-start.7 = (bf16[4,32,1024]{2,1,0:T(8,128)(2,1)S(1)}, bf16[4,32,1024]{2,1,0:T(8,128)(2,1)S(1)}, u32[]{:S(2)}, u32[]{:S(2)}) collective-permute-start(bf16[4,32,1024]{2,1,0:T(8,128)(2,1)S(1)} %get-tuple-element.31), channel_id=1, source_target_pairs={{0,12},{1,13},{2,14},{3,15},{4,0},{5,1},{6,2},{7,3},{8,4},{9,5},{1... | collective-permute-start | bytes 786440 | tf_op jit(solution)/shard_map/ppermute | solution.py:112
  32.9 1.2 collective-permute-start.1
  34.1 4.6 %collective-permute-done.8 = bf16[4,32,1024]{2,1,0:T(8,128)(2,1)S(1)} collective-permute-done((bf16[4,32,1024]{2,1,0:T(8,128)(2,1)S(1)}, bf16[4,32,1024]{2,1,0:T(8,128)(2,1)S(1)}, u32[]{:S(2)}, u32[]{:S(2)}) %collective-permute-start.8) | collective-permute-done | bytes 262176 | tf_op jit(solution)/shard_map/ppermute | solution.py:112
  38.8 2.5 %collective-permute-start = (bf16[4,32,1024]{2,1,0:T(8,128)(2,1)S(1)}, bf16[4,32,1024]{2,1,0:T(8,128)(2,1)S(1)}, u32[]{:S(2)}, u32[]{:S(2)}) collective-permute-start(bf16[4,32,1024]{2,1,0:T(8,128)(2,1)S(1)} %get-tuple-element.34), channel_id=1, source_target_pairs={{0,3},{1,0},{2,1},{3,2},{4,7},{5,4},{6,5},{7,6},{8,11},{9,8},{10,9... | collective-permute-start | bytes 786440 | tf_op jit(solution)/shard_map/ppermute | solution.py:112
  41.6 5.5 %collective-permute-done.9 = bf16[4,32,1024]{2,1,0:T(8,128)(2,1)S(1)} collective-permute-done((bf16[4,32,1024]{2,1,0:T(8,128)(2,1)S(1)}, bf16[4,32,1024]{2,1,0:T(8,128)(2,1)S(1)}, u32[]{:S(2)}, u32[]{:S(2)}) %collective-permute-start.9) | collective-permute-done | bytes 262176 | tf_op jit(solution)/shard_map/ppermute | solution.py:112
  47.2 2.6 %collective-permute-start.10 = (bf16[4,128,1024]{2,1,0:T(8,128)(2,1)S(1)}, bf16[4,128,1024]{2,1,0:T(8,128)(2,1)S(1)}, u32[]{:S(2)}, u32[]{:S(2)}) collective-permute-start(bf16[4,128,1024]{2,1,0:T(8,128)(2,1)S(1)} %pad_maximum_fusion.1), channel_id=1, source_target_pairs={{0,3},{1,0},{2,1},{3,2},{4,7},{5,4},{6,5},{7,6},{8,11},{9,8},{10,9... | collective-permute-start | bytes 3145736 | tf_op jit(solution)/shard_map/ppermute | solution.py:112
  49.9 2.0 %collective-permute-start.3 = (bf16[4,128,1024]{2,1,0:T(8,128)(2,1)S(1)}, bf16[4,128,1024]{2,1,0:T(8,128)(2,1)S(1)}, u32[]{:S(2)}, u32[]{:S(2)}) collective-permute-start(bf16[4,128,1024]{2,1,0:T(8,128)(2,1)S(1)} %pad_maximum_fusion), channel_id=1, source_target_pairs={{0,12},{1,13},{2,14},{3,15},{4,0},{5,1},{6,2},{7,3},{8,4},{9,5},{1... | collective-permute-start | bytes 3145736 | tf_op jit(solution)/shard_map/ppermute | solution.py:112
  52.6 1.7 multiply_convert_fusion
  54.3 0.7 constant_dynamic-update-slice_fusion.14
  55.0 0.7 constant_dynamic-update-slice_fusion.6
  55.8 0.7 constant_dynamic-update-slice_fusion.13
  56.5 17.5 %collective-permute-done.11 = bf16[4,128,1024]{2,1,0:T(8,128)(2,1)S(1)} collective-permute-done((bf16[4,128,1024]{2,1,0:T(8,128)(2,1)S(1)}, bf16[4,128,1024]{2,1,0:T(8,128)(2,1)S(1)}, u32[]{:S(2)}, u32[]{:S(2)}) %collective-permute-start.11) | collective-permute-done | bytes 1048608 | tf_op jit(solution)/shard_map/ppermute | solution.py:112
  74.1 0.7 constant_dynamic-update-slice_fusion.12
  74.9 2.7 %collective-permute-start.13 = (bf16[4,64,1024]{2,1,0:T(8,128)(2,1)S(1)}, bf16[4,64,1024]{2,1,0:T(8,128)(2,1)S(1)}, u32[]{:S(2)}, u32[]{:S(2)}) collective-permute-start(bf16[4,64,1024]{2,1,0:T(8,128)(2,1)S(1)} %slice.175), channel_id=1, source_target_pairs={{0,3},{1,0},{2,1},{3,2},{4,7},{5,4},{6,5},{7,6},{8,11},{9,8},{10,9... | collective-permute-start | bytes 1572872 | tf_op jit(solution)/shard_map/ppermute | solution.py:112
  77.6 0.7 constant_dynamic-update-slice_fusion.5
  78.3 0.7 constant_dynamic-update-slice_fusion.4
  79.2 2.7 %collective-permute-start.6 = (bf16[4,64,1024]{2,1,0:T(8,128)(2,1)S(1)}, bf16[4,64,1024]{2,1,0:T(8,128)(2,1)S(1)}, u32[]{:S(2)}, u32[]{:S(2)}) collective-permute-start(bf16[4,64,1024]{2,1,0:T(8,128)(2,1)S(1)} %slice.170), channel_id=1, source_target_pairs={{0,12},{1,13},{2,14},{3,15},{4,0},{5,1},{6,2},{7,3},{8,4},{9,5},{1... | collective-permute-start | bytes 1572872 | tf_op jit(solution)/shard_map/ppermute | solution.py:112
  81.9 1.0 constant_dynamic-update-slice_fusion.11
  82.9 1.0 constant_dynamic-update-slice_fusion.3
  84.0 2.2 %collective-permute-done.12 = bf16[4,64,1024]{2,1,0:T(8,128)(2,1)S(1)} collective-permute-done((bf16[4,64,1024]{2,1,0:T(8,128)(2,1)S(1)}, bf16[4,64,1024]{2,1,0:T(8,128)(2,1)S(1)}, u32[]{:S(2)}, u32[]{:S(2)}) %collective-permute-start.12) | collective-permute-done | bytes 524320 | tf_op jit(solution)/shard_map/ppermute | solution.py:112
  86.2 0.9 constant_dynamic-update-slice_fusion.10
  87.1 0.8 constant_dynamic-update-slice_fusion.9
  87.9 2.8 %collective-permute-done.5 = bf16[4,64,1024]{2,1,0:T(8,128)(2,1)S(1)} collective-permute-done((bf16[4,64,1024]{2,1,0:T(8,128)(2,1)S(1)}, bf16[4,64,1024]{2,1,0:T(8,128)(2,1)S(1)}, u32[]{:S(2)}, u32[]{:S(2)}) %collective-permute-start.5) | collective-permute-done | bytes 524320 | tf_op jit(solution)/shard_map/ppermute | solution.py:112
  90.7 0.9 constant_dynamic-update-slice_fusion.2
  91.5 1.1 constant_dynamic-update-slice_fusion.8.refs_3_
  92.6 0.8 constant_dynamic-update-slice_fusion.1
  93.4 1.0 constant_dynamic-update-slice_fusion.refs_0_
  94.5 12.4 %shard_map.73 = (bf16[4,512,1024]{2,1,0:T(8,128)(2,1)}, bf16[4,512,1024]{2,1,0:T(8,128)(2,1)}) custom-call(s32[8]{0:T(128)} %pad_add_fusion.n_live_ref, bf16[4,512,1024]{2,1,0:T(8,128)(2,1)} %constant_dynamic-update-slice_fusion.refs_0_, bf16[4,128,2048]{2,1,0:T(8,128)(2,1)} %get-tuple-element.26.refs_1_, bf16[4,128,1024]{2,1,0:T(8,128)(2,1)} %get-tuple-element.24.refs_2_, ...), custom_call_target="tpu_custom_call" | custom-call | flops 2147483648 | bytes 20971520 | tf_op jit(solution)/shard_map/pallas_call | solution.py:81
  106.9 1.5 fusion.48
  108.7 2.7 %collective-permute-start.16 = (bf16[4,64,1024]{2,1,0:T(8,128)(2,1)S(1)}, bf16[4,64,1024]{2,1,0:T(8,128)(2,1)S(1)}, u32[]{:S(2)}, u32[]{:S(2)}) collective-permute-start(bf16[4,64,1024]{2,1,0:T(8,128)(2,1)S(1)} %get-tuple-element.18), channel_id=1, source_target_pairs={{0,12},{1,13},{2,14},{3,15},{4,0},{5,1},{6,2},{7,3},{8,4},{9,5},{1... | collective-permute-start | bytes 1572872 | tf_op jit(solution)/shard_map/ppermute | solution.py:112
  111.3 1.3 fusion.49
  112.7 2.7 %collective-permute-start.23 = (bf16[4,64,1024]{2,1,0:T(8,128)(2,1)S(1)}, bf16[4,64,1024]{2,1,0:T(8,128)(2,1)S(1)}, u32[]{:S(2)}, u32[]{:S(2)}) collective-permute-start(bf16[4,64,1024]{2,1,0:T(8,128)(2,1)S(1)} %get-tuple-element.22), channel_id=1, source_target_pairs={{0,3},{1,0},{2,1},{3,2},{4,7},{5,4},{6,5},{7,6},{8,11},{9,8},{10,9... | collective-permute-start | bytes 1572872 | tf_op jit(solution)/shard_map/ppermute | solution.py:112
  115.4 4.0 %collective-permute-done.14 = bf16[4,64,1024]{2,1,0:T(8,128)(2,1)S(1)} collective-permute-done((bf16[4,64,1024]{2,1,0:T(8,128)(2,1)S(1)}, bf16[4,64,1024]{2,1,0:T(8,128)(2,1)S(1)}, u32[]{:S(2)}, u32[]{:S(2)}) %collective-permute-start.14) | collective-permute-done | bytes 524320 | tf_op jit(solution)/shard_map/ppermute | solution.py:112
  119.3 0.7 add_convert_fusion.3
  120.1 2.7 %collective-permute-start.17 = (bf16[4,128,1024]{2,1,0:T(8,128)(2,1)S(1)}, bf16[4,128,1024]{2,1,0:T(8,128)(2,1)S(1)}, u32[]{:S(2)}, u32[]{:S(2)}) collective-permute-start(bf16[4,128,1024]{2,1,0:T(8,128)(2,1)S(1)} %get-tuple-element.16), channel_id=1, source_target_pairs={{0,12},{1,13},{2,14},{3,15},{4,0},{5,1},{6,2},{7,3},{8,4},{9,5},{1... | collective-permute-start | bytes 3145736 | tf_op jit(solution)/shard_map/ppermute | solution.py:112
  122.8 0.7 add_convert_fusion.1
  123.6 2.7 %collective-permute-start.24 = (bf16[4,128,1024]{2,1,0:T(8,128)(2,1)S(1)}, bf16[4,128,1024]{2,1,0:T(8,128)(2,1)S(1)}, u32[]{:S(2)}, u32[]{:S(2)}) collective-permute-start(bf16[4,128,1024]{2,1,0:T(8,128)(2,1)S(1)} %get-tuple-element.20), channel_id=1, source_target_pairs={{0,3},{1,0},{2,1},{3,2},{4,7},{5,4},{6,5},{7,6},{8,11},{9,8},{10,9... | collective-permute-start | bytes 3145736 | tf_op jit(solution)/shard_map/ppermute | solution.py:112
  126.3 14.9 %collective-permute-done.15 = bf16[4,128,1024]{2,1,0:T(8,128)(2,1)S(1)} collective-permute-done((bf16[4,128,1024]{2,1,0:T(8,128)(2,1)S(1)}, bf16[4,128,1024]{2,1,0:T(8,128)(2,1)S(1)}, u32[]{:S(2)}, u32[]{:S(2)}) %collective-permute-start.15) | collective-permute-done | bytes 1048608 | tf_op jit(solution)/shard_map/ppermute | solution.py:112
  141.2 0.7 fusion.46
  142.0 2.5 %collective-permute-done.22 = bf16[4,128,1024]{2,1,0:T(8,128)(2,1)S(1)} collective-permute-done((bf16[4,128,1024]{2,1,0:T(8,128)(2,1)S(1)}, bf16[4,128,1024]{2,1,0:T(8,128)(2,1)S(1)}, u32[]{:S(2)}, u32[]{:S(2)}) %collective-permute-start.22) | collective-permute-done | bytes 1048608 | tf_op jit(solution)/shard_map/ppermute | solution.py:112
  144.4 0.7 fusion.47
  145.3 2.5 %collective-permute-start.20 = (bf16[4,32,1024]{2,1,0:T(8,128)(2,1)S(1)}, bf16[4,32,1024]{2,1,0:T(8,128)(2,1)S(1)}, u32[]{:S(2)}, u32[]{:S(2)}) collective-permute-start(bf16[4,32,1024]{2,1,0:T(8,128)(2,1)S(1)} %get-tuple-element.28), channel_id=1, source_target_pairs={{0,3},{1,0},{2,1},{3,2},{4,7},{5,4},{6,5},{7,6},{8,11},{9,8},{10,9... | collective-permute-start | bytes 786440 | tf_op jit(solution)/shard_map/ppermute | solution.py:112
  147.7 2.6 %collective-permute-start.27 = (bf16[4,32,1024]{2,1,0:T(8,128)(2,1)S(1)}, bf16[4,32,1024]{2,1,0:T(8,128)(2,1)S(1)}, u32[]{:S(2)}, u32[]{:S(2)}) collective-permute-start(bf16[4,32,1024]{2,1,0:T(8,128)(2,1)S(1)} %get-tuple-element.30), channel_id=1, source_target_pairs={{0,12},{1,13},{2,14},{3,15},{4,0},{5,1},{6,2},{7,3},{8,4},{9,5},{1... | collective-permute-start | bytes 786440 | tf_op jit(solution)/shard_map/ppermute | solution.py:112
  150.3 1.2 collective-permute-done.18
  152.4 6.4 %collective-permute-done.19 = bf16[4,32,1024]{2,1,0:T(8,128)(2,1)S(1)} collective-permute-done((bf16[4,32,1024]{2,1,0:T(8,128)(2,1)S(1)}, bf16[4,32,1024]{2,1,0:T(8,128)(2,1)S(1)}, u32[]{:S(2)}, u32[]{:S(2)}) %collective-permute-start.19) | collective-permute-done | bytes 262176 | tf_op jit(solution)/shard_map/ppermute | solution.py:112
  159.1 0.8 pad_maximum_fusion.2
  159.9 14.8 %all-to-all-start.1 = ((bf16[8,32,1024]{2,1,0:T(8,128)(2,1)}), bf16[8,32,1024]{2,1,0:T(8,128)(2,1)}, u32[]{:S(2)}, u32[]{:S(2)}) async-start(bf16[8,32,1024]{2,1,0:T(8,128)(2,1)} %pad_maximum_fusion.2), calls=%async_computation.1 | async-start | bytes 1048576 | tf_op jit(solution)/shard_map/all_to_all | solution.py:235
  174.8 3.4 %multiply_bitcast_fusion = f32[32,8,1024]{2,1,0:T(8,128)} fusion(bf16[1024,2048]{1,0:T(8,128)(2,1)} %param.12, bf16[32,8,1024]{2,1,0:T(8,128)(2,1)S(1)} %copy-done.6, f32[32,8]{1,0:T(8,128)S(1)} %copy.37, f32[32,8]{1,0:T(8,128)S(1)} %copy.35), kind=kOutput, calls=%fused_computation.39 | convolution fusion | flops 538968064 | bytes 3672064 | tf_op jit(solution)/shard_map/dot_general | solution.py:238
  178.2 6.0 %all-to-all-done.1 = bf16[8,32,1024]{2,1,0:T(8,128)(2,1)} async-done(((bf16[8,32,1024]{2,1,0:T(8,128)(2,1)}), bf16[8,32,1024]{2,1,0:T(8,128)(2,1)}, u32[]{:S(2)}, u32[]{:S(2)}) %all-to-all-start.1) | async-done | bytes 524320 | tf_op jit(solution)/shard_map/all_to_all | solution.py:235
  184.2 1.6 gather_fusion.7
  186.3 1.9 fusion.14
  188.2 1.6 fusion.7
  (101 shorter events, 8.1 us)
Async XLA Ops:
  0.0 188.2 %copy-start = (bf16[1024,1024]{1,0:T(8,128)(2,1)S(1)}, bf16[1024,1024]{1,0:T(8,128)(2,1)}, u32[]{:S(2)}) copy-start(bf16[1024,1024]{1,0:T(8,128)(2,1)} %param.13) | copy-start | bytes 6291460
  8.6 7.8 %copy-start.1 = (s32[64]{0:T(128)S(1)}, s32[64]{0:T(128)}, u32[]{:S(2)}) copy-start(s32[64]{0:T(128)} %param.9) | copy-start | bytes 772
  8.6 8.4 %copy-start.2 = (s32[64]{0:T(128)S(1)}, s32[64]{0:T(128)}, u32[]{:S(2)}) copy-start(s32[64]{0:T(128)} %param.11) | copy-start | bytes 772
  10.4 17.0 %all-to-all-start = ((bf16[8,32,1024]{2,1,0:T(8,128)(2,1)}), bf16[8,32,1024]{2,1,0:T(8,128)(2,1)S(1)}, u32[]{:S(2)}, u32[]{:S(2)}) async-start(bf16[8,32,1024]{2,1,0:T(8,128)(2,1)} %broadcast_select_fusion), calls=%async_computation | async-start | bytes 1048576 | tf_op jit(solution)/shard_map/all_to_all | solution.py:216
  28.2 10.4 %collective-permute-start.8 = (bf16[4,32,1024]{2,1,0:T(8,128)(2,1)S(1)}, bf16[4,32,1024]{2,1,0:T(8,128)(2,1)S(1)}, u32[]{:S(2)}, u32[]{:S(2)}) collective-permute-start(bf16[4,32,1024]{2,1,0:T(8,128)(2,1)S(1)} %get-tuple-element.31), channel_id=1, source_target_pairs={{0,4},{1,5},{2,6},{3,7},{4,8},{5,9},{6,10},{7,11},{8,12},{9,13},{1... | collective-permute-start | bytes 786440 | tf_op jit(solution)/shard_map/ppermute | solution.py:112
  30.6 21.9 %copy-start.3 = (bf16[8,128,2048]{2,1,0:T(8,128)(2,1)S(1)}, bf16[8,128,2048]{2,1,0:T(8,128)(2,1)}, u32[]{:S(2)}) copy-start(bf16[8,128,2048]{2,1,0:T(8,128)(2,1)} %gather_fusion.6) | copy-start | bytes 12582916
  30.7 10.9 %collective-permute-start.7 = (bf16[4,32,1024]{2,1,0:T(8,128)(2,1)S(1)}, bf16[4,32,1024]{2,1,0:T(8,128)(2,1)S(1)}, u32[]{:S(2)}, u32[]{:S(2)}) collective-permute-start(bf16[4,32,1024]{2,1,0:T(8,128)(2,1)S(1)} %get-tuple-element.31), channel_id=1, source_target_pairs={{0,12},{1,13},{2,14},{3,15},{4,0},{5,1},{6,2},{7,3},{8,4},{9,5},{1... | collective-permute-start | bytes 786440 | tf_op jit(solution)/shard_map/ppermute | solution.py:112
  32.9 8.8 %collective-permute-start.1 = (bf16[4,32,1024]{2,1,0:T(8,128)(2,1)S(1)}, bf16[4,32,1024]{2,1,0:T(8,128)(2,1)S(1)}, u32[]{:S(2)}, u32[]{:S(2)}) collective-permute-start(bf16[4,32,1024]{2,1,0:T(8,128)(2,1)S(1)} %get-tuple-element.34), channel_id=1, source_target_pairs={{0,1},{1,2},{2,3},{3,0},{4,5},{5,6},{6,7},{7,4},{8,9},{9,10},{10,1... | collective-permute-start | bytes 786440 | tf_op jit(solution)/shard_map/ppermute | solution.py:112
  38.7 8.5 %collective-permute-start.9 = (bf16[4,32,1024]{2,1,0:T(8,128)(2,1)S(1)}, bf16[4,32,1024]{2,1,0:T(8,128)(2,1)S(1)}, u32[]{:S(2)}, u32[]{:S(2)}) collective-permute-start(bf16[4,32,1024]{2,1,0:T(8,128)(2,1)S(1)} %collective-permute-done.8), channel_id=1, source_target_pairs={{0,4},{1,5},{2,6},{3,7},{4,8},{5,9},{6,10},{7,11},{8,12},{9,13},{1... | collective-permute-start | bytes 786440 | tf_op jit(solution)/shard_map/ppermute | solution.py:112
  38.8 11.1 %collective-permute-start = (bf16[4,32,1024]{2,1,0:T(8,128)(2,1)S(1)}, bf16[4,32,1024]{2,1,0:T(8,128)(2,1)S(1)}, u32[]{:S(2)}, u32[]{:S(2)}) collective-permute-start(bf16[4,32,1024]{2,1,0:T(8,128)(2,1)S(1)} %get-tuple-element.34), channel_id=1, source_target_pairs={{0,3},{1,0},{2,1},{3,2},{4,7},{5,4},{6,5},{7,6},{8,11},{9,8},{10,9... | collective-permute-start | bytes 786440 | tf_op jit(solution)/shard_map/ppermute | solution.py:112
  41.6 8.2 %collective-permute-start.2 = (bf16[4,32,1024]{2,1,0:T(8,128)(2,1)S(1)}, bf16[4,32,1024]{2,1,0:T(8,128)(2,1)S(1)}, u32[]{:S(2)}, u32[]{:S(2)}) collective-permute-start(bf16[4,32,1024]{2,1,0:T(8,128)(2,1)S(1)} %collective-permute-done.1), channel_id=1, source_target_pairs={{0,1},{1,2},{2,3},{3,0},{4,5},{5,6},{6,7},{7,4},{8,9},{9,10},{10,1... | collective-permute-start | bytes 786440 | tf_op jit(solution)/shard_map/ppermute | solution.py:112
  47.2 27.6 %collective-permute-start.10 = (bf16[4,128,1024]{2,1,0:T(8,128)(2,1)S(1)}, bf16[4,128,1024]{2,1,0:T(8,128)(2,1)S(1)}, u32[]{:S(2)}, u32[]{:S(2)}) collective-permute-start(bf16[4,128,1024]{2,1,0:T(8,128)(2,1)S(1)} %pad_maximum_fusion.1), channel_id=1, source_target_pairs={{0,3},{1,0},{2,1},{3,2},{4,7},{5,4},{6,5},{7,6},{8,11},{9,8},{10,9... | collective-permute-start | bytes 3145736 | tf_op jit(solution)/shard_map/ppermute | solution.py:112
  49.8 24.2 %collective-permute-start.11 = (bf16[4,128,1024]{2,1,0:T(8,128)(2,1)S(1)}, bf16[4,128,1024]{2,1,0:T(8,128)(2,1)S(1)}, u32[]{:S(2)}, u32[]{:S(2)}) collective-permute-start(bf16[4,128,1024]{2,1,0:T(8,128)(2,1)S(1)} %pad_maximum_fusion.1), channel_id=1, source_target_pairs={{0,1},{1,2},{2,3},{3,0},{4,5},{5,6},{6,7},{7,4},{8,9},{9,10},{10,1... | collective-permute-start | bytes 3145736 | tf_op jit(solution)/shard_map/ppermute | solution.py:112
  49.9 29.2 %collective-permute-start.3 = (bf16[4,128,1024]{2,1,0:T(8,128)(2,1)S(1)}, bf16[4,128,1024]{2,1,0:T(8,128)(2,1)S(1)}, u32[]{:S(2)}, u32[]{:S(2)}) collective-permute-start(bf16[4,128,1024]{2,1,0:T(8,128)(2,1)S(1)} %pad_maximum_fusion), channel_id=1, source_target_pairs={{0,12},{1,13},{2,14},{3,15},{4,0},{5,1},{6,2},{7,3},{8,4},{9,5},{1... | collective-permute-start | bytes 3145736 | tf_op jit(solution)/shard_map/ppermute | solution.py:112
  52.0 27.0 %collective-permute-start.4 = (bf16[4,128,1024]{2,1,0:T(8,128)(2,1)S(1)}, bf16[4,128,1024]{2,1,0:T(8,128)(2,1)S(1)}, u32[]{:S(2)}, u32[]{:S(2)}) collective-permute-start(bf16[4,128,1024]{2,1,0:T(8,128)(2,1)S(1)} %pad_maximum_fusion), channel_id=1, source_target_pairs={{0,4},{1,5},{2,6},{3,7},{4,8},{5,9},{6,10},{7,11},{8,12},{9,13},{1... | collective-permute-start | bytes 3145736 | tf_op jit(solution)/shard_map/ppermute | solution.py:112
  74.0 12.2 %collective-permute-start.12 = (bf16[4,64,1024]{2,1,0:T(8,128)(2,1)S(1)}, bf16[4,64,1024]{2,1,0:T(8,128)(2,1)S(1)}, u32[]{:S(2)}, u32[]{:S(2)}) collective-permute-start(bf16[4,64,1024]{2,1,0:T(8,128)(2,1)S(1)} %slice.174), channel_id=1, source_target_pairs={{0,1},{1,2},{2,3},{3,0},{4,5},{5,6},{6,7},{7,4},{8,9},{9,10},{10,1... | collective-permute-start | bytes 1572872 | tf_op jit(solution)/shard_map/ppermute | solution.py:112
  74.9 12.2 %collective-permute-start.13 = (bf16[4,64,1024]{2,1,0:T(8,128)(2,1)S(1)}, bf16[4,64,1024]{2,1,0:T(8,128)(2,1)S(1)}, u32[]{:S(2)}, u32[]{:S(2)}) collective-permute-start(bf16[4,64,1024]{2,1,0:T(8,128)(2,1)S(1)} %slice.175), channel_id=1, source_target_pairs={{0,3},{1,0},{2,1},{3,2},{4,7},{5,4},{6,5},{7,6},{8,11},{9,8},{10,9... | collective-permute-start | bytes 1572872 | tf_op jit(solution)/shard_map/ppermute | solution.py:112
  79.1 11.6 %collective-permute-start.5 = (bf16[4,64,1024]{2,1,0:T(8,128)(2,1)S(1)}, bf16[4,64,1024]{2,1,0:T(8,128)(2,1)S(1)}, u32[]{:S(2)}, u32[]{:S(2)}) collective-permute-start(bf16[4,64,1024]{2,1,0:T(8,128)(2,1)S(1)} %slice.169), channel_id=1, source_target_pairs={{0,4},{1,5},{2,6},{3,7},{4,8},{5,9},{6,10},{7,11},{8,12},{9,13},{1... | collective-permute-start | bytes 1572872 | tf_op jit(solution)/shard_map/ppermute | solution.py:112
  79.2 13.4 %collective-permute-start.6 = (bf16[4,64,1024]{2,1,0:T(8,128)(2,1)S(1)}, bf16[4,64,1024]{2,1,0:T(8,128)(2,1)S(1)}, u32[]{:S(2)}, u32[]{:S(2)}) collective-permute-start(bf16[4,64,1024]{2,1,0:T(8,128)(2,1)S(1)} %slice.170), channel_id=1, source_target_pairs={{0,12},{1,13},{2,14},{3,15},{4,0},{5,1},{6,2},{7,3},{8,4},{9,5},{1... | collective-permute-start | bytes 1572872 | tf_op jit(solution)/shard_map/ppermute | solution.py:112
  106.9 12.4 %copy-start.5 = (bf16[4,512,1024]{2,1,0:T(8,128)(2,1)S(1)}, bf16[4,512,1024]{2,1,0:T(8,128)(2,1)}, u32[]{:S(2)}) copy-start(bf16[4,512,1024]{2,1,0:T(8,128)(2,1)} %get-tuple-element.7) | copy-start | bytes 12582916
  108.4 14.5 %copy-start.4 = (bf16[4,512,1024]{2,1,0:T(8,128)(2,1)S(1)}, bf16[4,512,1024]{2,1,0:T(8,128)(2,1)}, u32[]{:S(2)}) copy-start(bf16[4,512,1024]{2,1,0:T(8,128)(2,1)} %get-tuple-element.8) | copy-start | bytes 12582916
  108.4 10.9 %collective-permute-start.14 = (bf16[4,64,1024]{2,1,0:T(8,128)(2,1)S(1)}, bf16[4,64,1024]{2,1,0:T(8,128)(2,1)S(1)}, u32[]{:S(2)}, u32[]{:S(2)}) collective-permute-start(bf16[4,64,1024]{2,1,0:T(8,128)(2,1)S(1)} %get-tuple-element.17), channel_id=1, source_target_pairs={{0,4},{1,5},{2,6},{3,7},{4,8},{5,9},{6,10},{7,11},{8,12},{9,13},{1... | collective-permute-start | bytes 1572872 | tf_op jit(solution)/shard_map/ppermute | solution.py:112
  108.7 10.7 %collective-permute-start.16 = (bf16[4,64,1024]{2,1,0:T(8,128)(2,1)S(1)}, bf16[4,64,1024]{2,1,0:T(8,128)(2,1)S(1)}, u32[]{:S(2)}, u32[]{:S(2)}) collective-permute-start(bf16[4,64,1024]{2,1,0:T(8,128)(2,1)S(1)} %get-tuple-element.18), channel_id=1, source_target_pairs={{0,12},{1,13},{2,14},{3,15},{4,0},{5,1},{6,2},{7,3},{8,4},{9,5},{1... | collective-permute-start | bytes 1572872 | tf_op jit(solution)/shard_map/ppermute | solution.py:112
  112.6 10.2 %collective-permute-start.21 = (bf16[4,64,1024]{2,1,0:T(8,128)(2,1)S(1)}, bf16[4,64,1024]{2,1,0:T(8,128)(2,1)S(1)}, u32[]{:S(2)}, u32[]{:S(2)}) collective-permute-start(bf16[4,64,1024]{2,1,0:T(8,128)(2,1)S(1)} %get-tuple-element.21), channel_id=1, source_target_pairs={{0,1},{1,2},{2,3},{3,0},{4,5},{5,6},{6,7},{7,4},{8,9},{9,10},{10,1... | collective-permute-start | bytes 1572872 | tf_op jit(solution)/shard_map/ppermute | solution.py:112
  112.7 10.1 %collective-permute-start.23 = (bf16[4,64,1024]{2,1,0:T(8,128)(2,1)S(1)}, bf16[4,64,1024]{2,1,0:T(8,128)(2,1)S(1)}, u32[]{:S(2)}, u32[]{:S(2)}) collective-permute-start(bf16[4,64,1024]{2,1,0:T(8,128)(2,1)S(1)} %get-tuple-element.22), channel_id=1, source_target_pairs={{0,3},{1,0},{2,1},{3,2},{4,7},{5,4},{6,5},{7,6},{8,11},{9,8},{10,9... | collective-permute-start | bytes 1572872 | tf_op jit(solution)/shard_map/ppermute | solution.py:112
  120.0 21.1 %collective-permute-start.15 = (bf16[4,128,1024]{2,1,0:T(8,128)(2,1)S(1)}, bf16[4,128,1024]{2,1,0:T(8,128)(2,1)S(1)}, u32[]{:S(2)}, u32[]{:S(2)}) collective-permute-start(bf16[4,128,1024]{2,1,0:T(8,128)(2,1)S(1)} %get-tuple-element.15), channel_id=1, source_target_pairs={{0,4},{1,5},{2,6},{3,7},{4,8},{5,9},{6,10},{7,11},{8,12},{9,13},{1... | collective-permute-start | bytes 3145736 | tf_op jit(solution)/shard_map/ppermute | solution.py:112
  120.1 21.1 %collective-permute-start.17 = (bf16[4,128,1024]{2,1,0:T(8,128)(2,1)S(1)}, bf16[4,128,1024]{2,1,0:T(8,128)(2,1)S(1)}, u32[]{:S(2)}, u32[]{:S(2)}) collective-permute-start(bf16[4,128,1024]{2,1,0:T(8,128)(2,1)S(1)} %get-tuple-element.16), channel_id=1, source_target_pairs={{0,12},{1,13},{2,14},{3,15},{4,0},{5,1},{6,2},{7,3},{8,4},{9,5},{1... | collective-permute-start | bytes 3145736 | tf_op jit(solution)/shard_map/ppermute | solution.py:112
  123.5 20.9 %collective-permute-start.22 = (bf16[4,128,1024]{2,1,0:T(8,128)(2,1)S(1)}, bf16[4,128,1024]{2,1,0:T(8,128)(2,1)S(1)}, u32[]{:S(2)}, u32[]{:S(2)}) collective-permute-start(bf16[4,128,1024]{2,1,0:T(8,128)(2,1)S(1)} %get-tuple-element.19), channel_id=1, source_target_pairs={{0,1},{1,2},{2,3},{3,0},{4,5},{5,6},{6,7},{7,4},{8,9},{9,10},{10,1... | collective-permute-start | bytes 3145736 | tf_op jit(solution)/shard_map/ppermute | solution.py:112
  123.6 20.8 %collective-permute-start.24 = (bf16[4,128,1024]{2,1,0:T(8,128)(2,1)S(1)}, bf16[4,128,1024]{2,1,0:T(8,128)(2,1)S(1)}, u32[]{:S(2)}, u32[]{:S(2)}) collective-permute-start(bf16[4,128,1024]{2,1,0:T(8,128)(2,1)S(1)} %get-tuple-element.20), channel_id=1, source_target_pairs={{0,3},{1,0},{2,1},{3,2},{4,7},{5,4},{6,5},{7,6},{8,11},{9,8},{10,9... | collective-permute-start | bytes 3145736 | tf_op jit(solution)/shard_map/ppermute | solution.py:112
  141.9 9.6 %collective-permute-start.18 = (bf16[4,32,1024]{2,1,0:T(8,128)(2,1)S(1)}, bf16[4,32,1024]{2,1,0:T(8,128)(2,1)S(1)}, u32[]{:S(2)}, u32[]{:S(2)}) collective-permute-start(bf16[4,32,1024]{2,1,0:T(8,128)(2,1)S(1)} %get-tuple-element.27), channel_id=1, source_target_pairs={{0,1},{1,2},{2,3},{3,0},{4,5},{5,6},{6,7},{7,4},{8,9},{9,10},{10,1... | collective-permute-start | bytes 786440 | tf_op jit(solution)/shard_map/ppermute | solution.py:112
  145.1 29.6 %copy-start.6 = (bf16[32,8,1024]{2,1,0:T(8,128)(2,1)S(1)}, bf16[32,8,1024]{2,1,0:T(8,128)(2,1)}, u32[]{:S(2)}) copy-start(bf16[32,8,1024]{2,1,0:T(8,128)(2,1)} %param.7) | copy-start | bytes 1572868
  145.2 6.8 %collective-permute-start.25 = (bf16[4,32,1024]{2,1,0:T(8,128)(2,1)S(1)}, bf16[4,32,1024]{2,1,0:T(8,128)(2,1)S(1)}, u32[]{:S(2)}, u32[]{:S(2)}) collective-permute-start(bf16[4,32,1024]{2,1,0:T(8,128)(2,1)S(1)} %get-tuple-element.29), channel_id=1, source_target_pairs={{0,4},{1,5},{2,6},{3,7},{4,8},{5,9},{6,10},{7,11},{8,12},{9,13},{1... | collective-permute-start | bytes 786440 | tf_op jit(solution)/shard_map/ppermute | solution.py:112
  145.3 7.1 %collective-permute-start.20 = (bf16[4,32,1024]{2,1,0:T(8,128)(2,1)S(1)}, bf16[4,32,1024]{2,1,0:T(8,128)(2,1)S(1)}, u32[]{:S(2)}, u32[]{:S(2)}) collective-permute-start(bf16[4,32,1024]{2,1,0:T(8,128)(2,1)S(1)} %get-tuple-element.28), channel_id=1, source_target_pairs={{0,3},{1,0},{2,1},{3,2},{4,7},{5,4},{6,5},{7,6},{8,11},{9,8},{10,9... | collective-permute-start | bytes 786440 | tf_op jit(solution)/shard_map/ppermute | solution.py:112
  147.7 11.1 %collective-permute-start.27 = (bf16[4,32,1024]{2,1,0:T(8,128)(2,1)S(1)}, bf16[4,32,1024]{2,1,0:T(8,128)(2,1)S(1)}, u32[]{:S(2)}, u32[]{:S(2)}) collective-permute-start(bf16[4,32,1024]{2,1,0:T(8,128)(2,1)S(1)} %get-tuple-element.30), channel_id=1, source_target_pairs={{0,12},{1,13},{2,14},{3,15},{4,0},{5,1},{6,2},{7,3},{8,4},{9,5},{1... | collective-permute-start | bytes 786440 | tf_op jit(solution)/shard_map/ppermute | solution.py:112
  151.6 7.2 %collective-permute-start.19 = (bf16[4,32,1024]{2,1,0:T(8,128)(2,1)S(1)}, bf16[4,32,1024]{2,1,0:T(8,128)(2,1)S(1)}, u32[]{:S(2)}, u32[]{:S(2)}) collective-permute-start(bf16[4,32,1024]{2,1,0:T(8,128)(2,1)S(1)} %fusion.26), channel_id=1, source_target_pairs={{0,1},{1,2},{2,3},{3,0},{4,5},{5,6},{6,7},{7,4},{8,9},{9,10},{10,1... | collective-permute-start | bytes 786440 | tf_op jit(solution)/shard_map/ppermute | solution.py:112
  152.1 6.9 %collective-permute-start.26 = (bf16[4,32,1024]{2,1,0:T(8,128)(2,1)S(1)}, bf16[4,32,1024]{2,1,0:T(8,128)(2,1)S(1)}, u32[]{:S(2)}, u32[]{:S(2)}) collective-permute-start(bf16[4,32,1024]{2,1,0:T(8,128)(2,1)S(1)} %fusion.23), channel_id=1, source_target_pairs={{0,4},{1,5},{2,6},{3,7},{4,8},{5,9},{6,10},{7,11},{8,12},{9,13},{1... | collective-permute-start | bytes 786440 | tf_op jit(solution)/shard_map/ppermute | solution.py:112
  159.9 24.3 %all-to-all-start.1 = ((bf16[8,32,1024]{2,1,0:T(8,128)(2,1)}), bf16[8,32,1024]{2,1,0:T(8,128)(2,1)}, u32[]{:S(2)}, u32[]{:S(2)}) async-start(bf16[8,32,1024]{2,1,0:T(8,128)(2,1)} %pad_maximum_fusion.2), calls=%async_computation.1 | async-start | bytes 1048576 | tf_op jit(solution)/shard_map/all_to_all | solution.py:235
